TPU v7x, 512 devices: a whole 4x8x8 slice. The times are simulated.
512 devices in a mesh: docs: 128 (over y, z, core), grp: 4 (over x).
Axes of the slice: x: 4, y: 8, z: 8, core: 2. Of those that a mesh axis runs over, the one named last changes fastest.
Arguments:
- embeddings: bfloat16 [131072, 1024], P(('docs', 'grp')), may hold values from -6 to 6
- projection: bfloat16 [1024, 512], replicated, may hold values from -0.1875 to 0.1875
- phase_code: int32 [1], replicated, may hold values from 0 to 1023
- penalty: int32 [1], replicated, may hold values from 1 to 16
- assignment: int32 [512, 256], P(('docs', 'grp')), may hold values from 0 to 255, each once within a row
- targets: bfloat16 [131072, 256], P(('docs', 'grp')), may hold values from -7 to 7
Outputs:
- quality: bfloat16 [131072, 256], P(('docs', 'grp'))
Inputs may be any that keep to these rules, and one draw needn't show every extreme that they name: Each row of assignment names every row of its slab once.
All inputs are finite; a program needn't handle non-finite values. Where the computation divides by a largest or mean magnitude, that divisor is 1e-20 or more.
Results may differ from a plain program's by a relative error of at most 0.0056.
Values sent between devices are 32-bit elements; how exact they have to be, the bound alone decides.
No kernel may reach another device: no remote copies, remote signals or barrier semaphores. Data moves between devices by JAX's collectives and lax.ppermute only.
A program may use at most 64 MiB of HBM per device.

v0:
```python
import math

import jax
import jax.numpy as jnp
from jax import lax
from jax.sharding import PartitionSpec as P


def phase_table(phase_code, width):
    feature_ids = jnp.arange(width, dtype=jnp.int32)
    code_value = phase_code[0]
    index_value = (code_value * 389 + feature_ids * (feature_ids + code_value) * 53) % 4096
    return index_value.astype(jnp.float32) * (2.0 * math.pi / 4096.0)


def on_device(embeddings, projection, phase_code, penalty, assignment, targets):
    width = projection.shape[1]
    phases = phase_table(phase_code, width)
    projected = jnp.dot(embeddings, projection, preferred_element_type=jnp.float32)
    features = jnp.cos(projected + phases).astype(jnp.bfloat16)
    aligned = features[assignment.reshape(-1)]
    gram_part = lax.dot_general(
        features, features, (((0,), (0,)), ((), ())), preferred_element_type=jnp.float32
    )
    cross_part = lax.dot_general(
        aligned, targets, (((0,), (0,)), ((), ())), preferred_element_type=jnp.float32
    )
    packed = jnp.concatenate([gram_part, cross_part], axis=1)
    summed = lax.psum(packed, ("docs", "grp"))
    gram = summed[:, :width]
    cross = summed[:, width:]
    total_rows = embeddings.shape[0] * lax.axis_size("docs") * lax.axis_size("grp")
    ridge_shift = penalty[0].astype(jnp.float32) * jnp.float32(total_rows / 8.0)
    system = gram + ridge_shift * jnp.eye(width, dtype=jnp.float32)
    factor = jnp.linalg.cholesky(system)
    coeffs = jax.scipy.linalg.cho_solve((factor, True), cross).astype(jnp.bfloat16)
    scores = jnp.dot(features, coeffs, preferred_element_type=jnp.float32)
    peak_local = jnp.max(jnp.abs(scores), axis=0)
    column_sum = jnp.sum(scores, axis=0)
    peak = lax.pmax(peak_local, ("docs", "grp"))
    total = lax.psum(column_sum, ("docs", "grp"))
    quality = (scores - total / jnp.float32(total_rows)) / (peak + 1e-06)
    return quality.astype(jnp.bfloat16)


def solution(mesh):
    in_specs = (
        P(("docs", "grp"), None),
        P(),
        P(),
        P(),
        P(("docs", "grp"), None),
        P(("docs", "grp"), None),
    )
    out_specs = P(("docs", "grp"), None)
    return jax.shard_map(
        on_device, mesh=mesh, in_specs=in_specs, out_specs=out_specs, check_vma=False
    )
```

profile of v0, /device:TPU:6, one launch (start us, length us, event | category | flops | bytes accessed | tf_op | source)
XLA Modules:
  0.0 650.9 jit_solution(4927500006929599232)
XLA Ops:
  7.3 0.7 compare_select_fusion
  8.0 3.3 fusion.1
  11.3 0.3 fusion.65
  11.6 1.2 gather_fusion
  13.1 1.3 pad_maximum_fusion
  15.0 280.7 %all-reduce.3.cloned.1.call-done = f32[512,768]{0,1:T(8,128)} async-done(((f32[512,768]{0,1:T(8,128)}), f32[512,768]{0,1:T(8,128)}) %all-reduce.3.cloned.1.call-update) | async-done | bytes 1572880 | tf_op jit(solution)/shard_map/psum | solution.py:29
  295.7 2.3 slice_add_fusion
  298.0 2.6 copy.16
  300.7 1.4 fusion.2
  302.2 1.0 copy-done.2
  303.1 11.7 %cholesky.103 = f32[128,128]{1,0:T(8,128)S(1)} custom-call(f32[128,128]{1,0:T(8,128)S(1)} %cholesky.263), custom_call_target="Cholesky" | custom-call | tf_op jit(solution)/shard_map/jit(cholesky)/cholesky | solution.py:35
  315.0 9.8 %custom-call.34 = f32[1,128,128]{1,2,0:T(8,128)S(1)} custom-call(f32[1,128,128]{2,1,0:T(8,128)S(1)} %get-tuple-element.38), custom_call_target="InvertDiagBlocksLowerTriangular" | custom-call | tf_op jit(solution)/shard_map/jit(cholesky)/cholesky | solution.py:35
  324.8 1.2 fusion.31
  326.2 1.3 convolution_subtract_fusion
  327.4 11.8 %cholesky.215 = f32[128,128]{1,0:T(8,128)S(1)} custom-call(f32[128,128]{1,0:T(8,128)S(1)} %cholesky.267), custom_call_target="Cholesky" | custom-call | tf_op jit(solution)/shard_map/jit(cholesky)/cholesky | solution.py:35
  339.4 9.8 %custom-call.35 = f32[1,128,128]{1,2,0:T(8,128)S(1)} custom-call(f32[1,128,128]{2,1,0:T(8,128)S(1)} %get-tuple-element.36), custom_call_target="InvertDiagBlocksLowerTriangular" | custom-call | tf_op jit(solution)/shard_map/jit(cholesky)/cholesky | solution.py:35
  349.4 0.3 convolution_dynamic-update-slice_fusion
  349.7 1.5 convolution_subtract_fusion.5
  351.2 11.7 %cholesky.236 = f32[128,128]{1,0:T(8,128)S(1)} custom-call(f32[128,128]{1,0:T(8,128)S(1)} %cholesky.272), custom_call_target="Cholesky" | custom-call | tf_op jit(solution)/shard_map/jit(cholesky)/cholesky | solution.py:35
  363.1 9.8 %custom-call.36 = f32[1,128,128]{1,2,0:T(8,128)S(1)} custom-call(f32[1,128,128]{2,1,0:T(8,128)S(1)} %get-tuple-element.34), custom_call_target="InvertDiagBlocksLowerTriangular" | custom-call | tf_op jit(solution)/shard_map/jit(cholesky)/cholesky | solution.py:35
  373.2 1.3 convolution_subtract_fusion.8
  374.6 11.9 %cholesky.253 = f32[128,128]{1,0:T(8,128)S(1)} custom-call(f32[128,128]{1,0:T(8,128)S(1)} %convolution_subtract_fusion.8), custom_call_target="Cholesky" | custom-call | tf_op jit(solution)/shard_map/jit(cholesky)/cholesky | solution.py:35
  386.6 0.7 compare_reduce_fusion.1
  387.3 0.7 compare_reduce_fusion
  388.0 0.7 compare_reduce_fusion.2
  391.3 10.9 %while.1 = (s32[]{:T(128)}, f32[512,512]{0,1:T(8,128)S(1)}, s32[4,2]{0,1:T(2,128)S(1)}, f32[4,128,128]{2,1,0:T(8,128)}, s32[]{:T(128)}) while((s32[]{:T(128)}, f32[512,512]{0,1:T(8,128)S(1)}, s32[4,2]{0,1:T(2,128)S(1)}, f32[4,128,128]{2,1,0:T(8,128)}, s32[]{:T(128)}) %tuple.30), condition=%wide.while_cond, body=%wide.while_body.sunk | while | flops 2 | bytes 393329 | solution.py:36
  391.4 0.6 fusion.85
  392.0 1.3 dynamic-slice.7
  393.4 0.6 bitcast_dynamic-update-slice_fusion.2
  394.1 0.6 fusion.85
  394.7 1.3 dynamic-slice.7
  396.1 0.6 bitcast_dynamic-update-slice_fusion.2
  396.8 0.6 fusion.85
  397.4 1.3 dynamic-slice.7
  398.9 0.6 bitcast_dynamic-update-slice_fusion.2
  399.6 0.6 fusion.85
  400.1 1.3 dynamic-slice.7
  401.6 0.6 bitcast_dynamic-update-slice_fusion.2
  402.2 40.1 %custom-call.37 = f32[4,128,128]{1,2,0:T(8,128)S(1)} custom-call(f32[4,128,128]{2,1,0:T(8,128)} %get-tuple-element.12), custom_call_target="InvertDiagBlocksLowerTriangular" | custom-call | tf_op jit(solution)/shard_map/jit(_cho_solve)/triangular_solve | solution.py:36
  442.3 1.2 fusion.35
  443.6 1.3 convolution_subtract_fusion.7
  445.2 1.5 convolution_subtract_fusion.4
  446.7 0.3 fusion.49
  447.0 1.7 convolution_subtract_fusion.3
  450.4 0.4 convolution_subtract_fusion.1
  451.3 96.2 %pmax.7 = f32[256]{0:T(256)S(1)} all-reduce(f32[256]{0:T(256)S(1)} %get-tuple-element.22), channel_id=1, replica_groups=mesh['docs'=128,'grp'=4] {'docs','grp'}, use_global_device_ids=true, to_apply=%region_12.13 | all-reduce | flops 256 | bytes 2048 | tf_op jit(solution)/shard_map/pmax | solution.py:40
  547.6 95.9 %psum.15 = f32[256]{0:T(256)S(1)} all-reduce(f32[256]{0:T(256)S(1)} %get-tuple-element.21), channel_id=1, replica_groups=mesh['docs'=128,'grp'=4] {'docs','grp'}, use_global_device_ids=true, to_apply=%region_10.11 | all-reduce | flops 256 | bytes 2048 | tf_op jit(solution)/shard_map/psum | solution.py:41
  643.4 0.7 divide_convert_fusion
  (53 shorter events, 4.7 us)
Async XLA Ops:
  6.5 1.5 copy-start
  6.5 289.2 %all-reduce.3.cloned.1.call-start = ((), (), s32[]{:S(2)}) async-start(), calls=%async_computation | async-start | bytes 3145728 | tf_op jit(solution)/shard_map/psum | solution.py:29
  11.6 1.2 copy-start.3
  298.0 2.6 copy-start.1
  302.1 1.0 copy-start.2
Sparse Core Ops, SparseCore 0:
  14.5 281.1 all-reduce.2
where the time goes:
time: 653 us; the launch traced here: 651 us
  waiting for transfers between devices  281 us (43%)
  blocking collectives  192 us (29%)
  other arithmetic  125 us (19%)
  matrix products  18.7 us (3%)
  between operations  17.7 us (3%)
  local copies, waits for them, and re-layouts  16.3 us (2%)
    psum x1, waiting for transfers between devices, on_device(): summed = lax.psum(packed, ('docs', 'grp'))  281 us
    pmax x1, blocking collectives, on_device(): peak = lax.pmax(peak_local, ('docs', 'grp'))  96.2 us
    psum x1, blocking collectives, on_device(): total = lax.psum(column_sum, ('docs', 'grp'))  95.9 us
    another operation x14, other arithmetic, on_device(): factor = jnp.linalg.cholesky(system)  78.8 us
    another operation x3, other arithmetic, on_device(): jax.scipy.linalg.cho_solve((factor, True), cross).astype(jnp.bfloat16)  40.3 us
  transfers between devices with their start and end apart: 1, of which 1 were waited for; matrix products, arithmetic and copies ran while one was open for 0% of the time, Pallas kernels for 0%

commit v1 on v0

--- a/solution.py
+++ b/solution.py
@@ -13,8 +13,49 @@
     return index_value.astype(jnp.float32) * (2.0 * math.pi / 4096.0)
 
 
+def exchange_bits(axis_sizes):
+    bits = []
+    for name, size in axis_sizes:
+        mask = 1
+        while mask < size:
+            bits.append((name, size, mask))
+            mask *= 2
+    return bits
+
+
+def partner(x, name, size, mask):
+    return lax.ppermute(x, name, [(i, i ^ mask) for i in range(size)])
+
+
+def tree_sum(x, bits, halving):
+    for name, size, mask in bits[:halving]:
+        half = x.shape[0] // 2
+        bit = (lax.axis_index(name) // mask) % 2
+        keep = lax.dynamic_slice_in_dim(x, bit * half, half, 0)
+        send = lax.dynamic_slice_in_dim(x, (1 - bit) * half, half, 0)
+        x = keep + partner(send, name, size, mask)
+    for name, size, mask in bits[halving:]:
+        x = x + partner(x, name, size, mask)
+    for name, size, mask in reversed(bits[:halving]):
+        bit = (lax.axis_index(name) // mask) % 2
+        other = partner(x, name, size, mask)
+        x = jnp.where(bit == 0, jnp.concatenate([x, other]), jnp.concatenate([other, x]))
+    return x
+
+
+def peak_and_total(stats, bits):
+    for name, size, mask in bits:
+        other = partner(stats, name, size, mask)
+        stats = jnp.concatenate(
+            [jnp.maximum(stats[:1], other[:1]), stats[1:] + other[1:]], axis=0
+        )
+    return stats
+
+
 def on_device(embeddings, projection, phase_code, penalty, assignment, targets):
     width = projection.shape[1]
+    attrs = targets.shape[1]
+    bits = exchange_bits([("docs", lax.axis_size("docs")), ("grp", lax.axis_size("grp"))])
     phases = phase_table(phase_code, width)
     projected = jnp.dot(embeddings, projection, preferred_element_type=jnp.float32)
     features = jnp.cos(projected + phases).astype(jnp.bfloat16)
@@ -26,7 +67,8 @@
         aligned, targets, (((0,), (0,)), ((), ())), preferred_element_type=jnp.float32
     )
     packed = jnp.concatenate([gram_part, cross_part], axis=1)
-    summed = lax.psum(packed, ("docs", "grp"))
+    flat = packed.reshape(-1, 128)
+    summed = tree_sum(flat, bits, 3).reshape(width, width + attrs)
     gram = summed[:, :width]
     cross = summed[:, width:]
     total_rows = embeddings.shape[0] * lax.axis_size("docs") * lax.axis_size("grp")
@@ -37,8 +79,9 @@
     scores = jnp.dot(features, coeffs, preferred_element_type=jnp.float32)
     peak_local = jnp.max(jnp.abs(scores), axis=0)
     column_sum = jnp.sum(scores, axis=0)
-    peak = lax.pmax(peak_local, ("docs", "grp"))
-    total = lax.psum(column_sum, ("docs", "grp"))
+    stats = peak_and_total(jnp.stack([peak_local, column_sum]), bits)
+    peak = stats[0]
+    total = stats[1]
     quality = (scores - total / jnp.float32(total_rows)) / (peak + 1e-06)
     return quality.astype(jnp.bfloat16)
 

time: 653 us -> 365 us (0.56)
  the two profiles are of different devices: /device:TPU:6 before, /device:TPU:2 now
where the time goes in v1:
time: 365 us; the launch traced here: 360 us
  other arithmetic  127 us (35%)
  waiting for transfers between devices  108 us (30%)
  starting transfers between devices  77.9 us (21%)
  local copies, waits for them, and re-layouts  24.5 us (7%)
  matrix products  17.2 us (5%)
  between operations  5.01 us (1%)
    ppermute x21, waiting for transfers between devices, partner(): return lax.ppermute(x, name, [(i, i ^ mask) for i in range(size)])  108 us
    another operation x14, other arithmetic, on_device(): factor = jnp.linalg.cholesky(system)  78.8 us
    ppermute x21, starting transfers between devices, partner(): return lax.ppermute(x, name, [(i, i ^ mask) for i in range(size)])  77.9 us
    another operation x3, other arithmetic, on_device(): jax.scipy.linalg.cho_solve((factor, True), cross).astype(jnp.bfloat16)  40.3 us
    another operation x20, local copies, waits for them, and re-layouts  10.5 us
    another operation x14, matrix products, on_device(): jax.scipy.linalg.cho_solve((factor, True), cross).astype(jnp.bfloat16)  8.06 us
  transfers between devices with their start and end apart: 21, of which 21 were waited for; matrix products, arithmetic and copies ran while one was open for 0% of the time, Pallas kernels for 0%

profile of v1, /device:TPU:2, one launch (start us, length us, event | category | flops | bytes accessed | tf_op | source)
XLA Modules:
  0.0 360.0 jit_solution(13768581416538232729)
XLA Ops:
  1.5 3.3 fusion.1
  14.8 2.5 collective-permute-done
  19.5 4.3 %collective-permute-start.1 = (f32[768,128]{1,0:T(8,128)S(1)}, f32[768,128]{1,0:T(8,128)S(1)}, u32[]{:S(2)}, u32[]{:S(2)}) collective-permute-start(f32[768,128]{1,0:T(8,128)S(1)} %constant_dynamic-slice_fusion.2), channel_id=1, source_target_pairs={{0,8},{4,12},{8,0},{12,4},{16,24},{20,28},{24,16},{28,20},{32,40},... | collective-permute-start | bytes 1179656 | tf_op jit(solution)/shard_map/ppermute | solution.py:27
  23.9 9.4 %collective-permute-done.1 = f32[768,128]{1,0:T(8,128)S(1)} collective-permute-done((f32[768,128]{1,0:T(8,128)S(1)}, f32[768,128]{1,0:T(8,128)S(1)}, u32[]{:S(2)}, u32[]{:S(2)}) %collective-permute-start.1) | collective-permute-done | bytes 393248 | tf_op jit(solution)/shard_map/ppermute | solution.py:27
  34.3 6.1 %collective-permute-start.2 = (f32[384,128]{1,0:T(8,128)S(1)}, f32[384,128]{1,0:T(8,128)S(1)}, u32[]{:S(2)}, u32[]{:S(2)}) collective-permute-start(f32[384,128]{1,0:T(8,128)S(1)} %constant_dynamic-slice_fusion.1), channel_id=1, source_target_pairs={{0,16},{4,20},{8,24},{12,28},{16,0},{20,4},{24,8},{28,12},{32,48},... | collective-permute-start | bytes 589832 | tf_op jit(solution)/shard_map/ppermute | solution.py:27
  40.4 8.9 %collective-permute-done.2 = f32[384,128]{1,0:T(8,128)S(1)} collective-permute-done((f32[384,128]{1,0:T(8,128)S(1)}, f32[384,128]{1,0:T(8,128)S(1)}, u32[]{:S(2)}, u32[]{:S(2)}) %collective-permute-start.2) | collective-permute-done | bytes 196640 | tf_op jit(solution)/shard_map/ppermute | solution.py:27
  49.3 8.4 %collective-permute-start.3 = (f32[384,128]{1,0:T(8,128)S(1)}, f32[384,128]{1,0:T(8,128)S(1)}, u32[]{:S(2)}, u32[]{:S(2)}) collective-permute-start(f32[384,128]{1,0:T(8,128)S(1)} %dynamic-slice_add_fusion.2), channel_id=1, source_target_pairs={{0,32},{4,36},{8,40},{12,44},{16,48},{20,52},{24,56},{28,60},{32,0... | collective-permute-start | bytes 589832 | tf_op jit(solution)/shard_map/ppermute | solution.py:27
  57.7 7.0 %collective-permute-done.3 = f32[384,128]{1,0:T(8,128)S(1)} collective-permute-done((f32[384,128]{1,0:T(8,128)S(1)}, f32[384,128]{1,0:T(8,128)S(1)}, u32[]{:S(2)}, u32[]{:S(2)}) %collective-permute-start.3) | collective-permute-done | bytes 196640 | tf_op jit(solution)/shard_map/ppermute | solution.py:27
  64.8 3.5 collective-permute-start.4
  68.3 4.1 %collective-permute-done.4 = f32[384,128]{1,0:T(8,128)S(1)} collective-permute-done((f32[384,128]{1,0:T(8,128)S(1)}, f32[384,128]{1,0:T(8,128)S(1)}, u32[]{:S(2)}, u32[]{:S(2)}) %collective-permute-start.4) | collective-permute-done | bytes 196640 | tf_op jit(solution)/shard_map/ppermute | solution.py:27
  72.4 4.5 %collective-permute-start.5 = (f32[384,128]{1,0:T(8,128)S(1)}, f32[384,128]{1,0:T(8,128)S(1)}, u32[]{:S(2)}, u32[]{:S(2)}) collective-permute-start(f32[384,128]{1,0:T(8,128)S(1)} %add.215), channel_id=1, source_target_pairs={{0,128},{4,132},{8,136},{12,140},{16,144},{20,148},{24,152},{28,15... | collective-permute-start | bytes 589832 | tf_op jit(solution)/shard_map/ppermute | solution.py:27
  76.9 6.5 %collective-permute-done.5 = f32[384,128]{1,0:T(8,128)S(1)} collective-permute-done((f32[384,128]{1,0:T(8,128)S(1)}, f32[384,128]{1,0:T(8,128)S(1)}, u32[]{:S(2)}, u32[]{:S(2)}) %collective-permute-start.5) | collective-permute-done | bytes 196640 | tf_op jit(solution)/shard_map/ppermute | solution.py:27
  83.4 7.8 %collective-permute-start.6 = (f32[384,128]{1,0:T(8,128)S(1)}, f32[384,128]{1,0:T(8,128)S(1)}, u32[]{:S(2)}, u32[]{:S(2)}) collective-permute-start(f32[384,128]{1,0:T(8,128)S(1)} %add.216), channel_id=1, source_target_pairs={{0,256},{4,260},{8,264},{12,268},{16,272},{20,276},{24,280},{28,28... | collective-permute-start | bytes 589832 | tf_op jit(solution)/shard_map/ppermute | solution.py:27
  91.2 5.9 %collective-permute-done.6 = f32[384,128]{1,0:T(8,128)S(1)} collective-permute-done((f32[384,128]{1,0:T(8,128)S(1)}, f32[384,128]{1,0:T(8,128)S(1)}, u32[]{:S(2)}, u32[]{:S(2)}) %collective-permute-start.6) | collective-permute-done | bytes 196640 | tf_op jit(solution)/shard_map/ppermute | solution.py:27
  97.2 9.4 %collective-permute-start.7 = (f32[384,128]{1,0:T(8,128)S(1)}, f32[384,128]{1,0:T(8,128)S(1)}, u32[]{:S(2)}, u32[]{:S(2)}) collective-permute-start(f32[384,128]{1,0:T(8,128)S(1)} %add.217), channel_id=1, source_target_pairs={{0,1},{1,0},{2,3},{3,2},{4,5},{5,4},{6,7},{7,6},{8,9},{9,8},{10,11... | collective-permute-start | bytes 589832 | tf_op jit(solution)/shard_map/ppermute | solution.py:27
  106.6 3.9 %collective-permute-done.7 = f32[384,128]{1,0:T(8,128)S(1)} collective-permute-done((f32[384,128]{1,0:T(8,128)S(1)}, f32[384,128]{1,0:T(8,128)S(1)}, u32[]{:S(2)}, u32[]{:S(2)}) %collective-permute-start.7) | collective-permute-done | bytes 196640 | tf_op jit(solution)/shard_map/ppermute | solution.py:27
  110.5 1.9 collective-permute-start.8
  112.5 7.1 %collective-permute-done.8 = f32[384,128]{1,0:T(8,128)S(1)} collective-permute-done((f32[384,128]{1,0:T(8,128)S(1)}, f32[384,128]{1,0:T(8,128)S(1)}, u32[]{:S(2)}, u32[]{:S(2)}) %collective-permute-start.8) | collective-permute-done | bytes 196640 | tf_op jit(solution)/shard_map/ppermute | solution.py:27
  119.6 1.9 collective-permute-start.9
  121.6 8.2 %collective-permute-done.9 = f32[384,128]{1,0:T(8,128)S(1)} collective-permute-done((f32[384,128]{1,0:T(8,128)S(1)}, f32[384,128]{1,0:T(8,128)S(1)}, u32[]{:S(2)}, u32[]{:S(2)}) %collective-permute-start.9) | collective-permute-done | bytes 196640 | tf_op jit(solution)/shard_map/ppermute | solution.py:27
  129.8 1.9 collective-permute-start.10
  131.7 9.2 %collective-permute-done.10 = f32[768,128]{1,0:T(8,128)S(1)} collective-permute-done((f32[768,128]{1,0:T(8,128)S(1)}, f32[768,128]{1,0:T(8,128)S(1)}, u32[]{:S(2)}, u32[]{:S(2)}) %collective-permute-start.10) | collective-permute-done | bytes 393248 | tf_op jit(solution)/shard_map/ppermute | solution.py:27
  141.0 1.9 collective-permute-start.11
  146.5 2.0 select_n.121
  155.3 11.7 %cholesky.103 = f32[128,128]{1,0:T(8,128)S(1)} custom-call(f32[128,128]{1,0:T(8,128)S(1)} %cholesky.263), custom_call_target="Cholesky" | custom-call | tf_op jit(solution)/shard_map/jit(cholesky)/cholesky | solution.py:77
  167.2 9.8 %custom-call.34 = f32[1,128,128]{1,2,0:T(8,128)S(1)} custom-call(f32[1,128,128]{2,1,0:T(8,128)S(1)} %get-tuple-element.38), custom_call_target="InvertDiagBlocksLowerTriangular" | custom-call | tf_op jit(solution)/shard_map/jit(cholesky)/cholesky | solution.py:77
  177.8 11.7 %cholesky.215 = f32[128,128]{1,0:T(8,128)S(1)} custom-call(f32[128,128]{1,0:T(8,128)S(1)} %cholesky.267), custom_call_target="Cholesky" | custom-call | tf_op jit(solution)/shard_map/jit(cholesky)/cholesky | solution.py:77
  189.7 10.0 %custom-call.35 = f32[1,128,128]{1,2,0:T(8,128)S(1)} custom-call(f32[1,128,128]{2,1,0:T(8,128)S(1)} %get-tuple-element.36), custom_call_target="InvertDiagBlocksLowerTriangular" | custom-call | tf_op jit(solution)/shard_map/jit(cholesky)/cholesky | solution.py:77
  201.6 11.7 %cholesky.236 = f32[128,128]{1,0:T(8,128)S(1)} custom-call(f32[128,128]{1,0:T(8,128)S(1)} %cholesky.272), custom_call_target="Cholesky" | custom-call | tf_op jit(solution)/shard_map/jit(cholesky)/cholesky | solution.py:77
  213.5 9.8 %custom-call.36 = f32[1,128,128]{1,2,0:T(8,128)S(1)} custom-call(f32[1,128,128]{2,1,0:T(8,128)S(1)} %get-tuple-element.34), custom_call_target="InvertDiagBlocksLowerTriangular" | custom-call | tf_op jit(solution)/shard_map/jit(cholesky)/cholesky | solution.py:77
  225.0 11.9 %cholesky.253 = f32[128,128]{1,0:T(8,128)S(1)} custom-call(f32[128,128]{1,0:T(8,128)S(1)} %convolution_subtract_fusion.5), custom_call_target="Cholesky" | custom-call | tf_op jit(solution)/shard_map/jit(cholesky)/cholesky | solution.py:77
  241.8 10.6 %while.1 = (s32[]{:T(128)}, f32[512,512]{0,1:T(8,128)S(1)}, s32[4,2]{0,1:T(2,128)S(1)}, f32[4,128,128]{2,1,0:T(8,128)}, s32[]{:T(128)}) while((s32[]{:T(128)}, f32[512,512]{0,1:T(8,128)S(1)}, s32[4,2]{0,1:T(2,128)S(1)}, f32[4,128,128]{2,1,0:T(8,128)}, s32[]{:T(128)}) %tuple.39), condition=%wide.while_cond, body=%wide.while_body.sunk | while | flops 2 | bytes 393329 | solution.py:78
  252.4 40.1 %custom-call.37 = f32[4,128,128]{1,2,0:T(8,128)S(1)} custom-call(f32[4,128,128]{2,1,0:T(8,128)} %get-tuple-element.12), custom_call_target="InvertDiagBlocksLowerTriangular" | custom-call | tf_op jit(solution)/shard_map/jit(_cho_solve)/triangular_solve | solution.py:78
  300.9 2.0 collective-permute-start.12
  304.0 2.2 collective-permute-start.13
  306.2 3.3 collective-permute-done.13
  309.5 3.0 collective-permute-start.14
  312.5 3.4 collective-permute-done.14
  315.9 3.7 %collective-permute-start.15 = (f32[2,256]{1,0:T(2,128)S(1)}, f32[2,256]{1,0:T(2,128)S(1)}, u32[]{:S(2)}, u32[]{:S(2)}) collective-permute-start(f32[2,256]{1,0:T(2,128)S(1)} %pad_maximum_fusion.4), channel_id=1, source_target_pairs={{0,32},{4,36},{8,40},{12,44},{16,48},{20,52},{24,56},{28,60},{32,0... | collective-permute-start | bytes 6152 | tf_op jit(solution)/shard_map/ppermute | solution.py:27
  319.6 5.7 %collective-permute-done.15 = f32[2,256]{1,0:T(2,128)S(1)} collective-permute-done((f32[2,256]{1,0:T(2,128)S(1)}, f32[2,256]{1,0:T(2,128)S(1)}, u32[]{:S(2)}, u32[]{:S(2)}) %collective-permute-start.15) | collective-permute-done | bytes 2080 | tf_op jit(solution)/shard_map/ppermute | solution.py:27
  325.3 1.9 collective-permute-start.16
  327.2 3.6 collective-permute-done.16
  330.8 1.9 collective-permute-start.17
  332.7 4.4 %collective-permute-done.17 = f32[2,256]{1,0:T(2,128)S(1)} collective-permute-done((f32[2,256]{1,0:T(2,128)S(1)}, f32[2,256]{1,0:T(2,128)S(1)}, u32[]{:S(2)}, u32[]{:S(2)}) %collective-permute-start.17) | collective-permute-done | bytes 2080 | tf_op jit(solution)/shard_map/ppermute | solution.py:27
  337.2 5.8 %collective-permute-start.18 = (f32[2,256]{1,0:T(2,128)S(1)}, f32[2,256]{1,0:T(2,128)S(1)}, u32[]{:S(2)}, u32[]{:S(2)}) collective-permute-start(f32[2,256]{1,0:T(2,128)S(1)} %pad_maximum_fusion.7), channel_id=1, source_target_pairs={{0,256},{4,260},{8,264},{12,268},{16,272},{20,276},{24,280},{28,28... | collective-permute-start | bytes 6152 | tf_op jit(solution)/shard_map/ppermute | solution.py:27
  343.0 3.5 collective-permute-done.18
  348.5 3.6 collective-permute-done.19
  354.0 5.1 %collective-permute-done.20 = f32[2,256]{1,0:T(2,128)S(1)} collective-permute-done((f32[2,256]{1,0:T(2,128)S(1)}, f32[2,256]{1,0:T(2,128)S(1)}, u32[]{:S(2)}, u32[]{:S(2)}) %collective-permute-start.20) | collective-permute-done | bytes 2080 | tf_op jit(solution)/shard_map/ppermute | solution.py:27
  (128 shorter events, 55.4 us)
Async XLA Ops:
  0.0 1.5 copy-start
  6.1 1.2 copy-start.4
  12.9 4.5 %collective-permute-start = (f32[1536,128]{1,0:T(8,128)}, f32[1536,128]{1,0:T(8,128)}, u32[]{:S(2)}, u32[]{:S(2)}) collective-permute-start(f32[1536,128]{1,0:T(8,128)} %constant_dynamic-slice_fusion.3), channel_id=1, source_target_pairs={{0,4},{4,0},{8,12},{12,8},{16,20},{20,16},{24,28},{28,24},{32,36},... | collective-permute-start | bytes 2359304 | tf_op jit(solution)/shard_map/ppermute | solution.py:27
  18.6 0.9 copy-start.2
  19.5 13.7 %collective-permute-start.1 = (f32[768,128]{1,0:T(8,128)S(1)}, f32[768,128]{1,0:T(8,128)S(1)}, u32[]{:S(2)}, u32[]{:S(2)}) collective-permute-start(f32[768,128]{1,0:T(8,128)S(1)} %constant_dynamic-slice_fusion.2), channel_id=1, source_target_pairs={{0,8},{4,12},{8,0},{12,4},{16,24},{20,28},{24,16},{28,20},{32,40},... | collective-permute-start | bytes 1179656 | tf_op jit(solution)/shard_map/ppermute | solution.py:27
  34.3 15.0 %collective-permute-start.2 = (f32[384,128]{1,0:T(8,128)S(1)}, f32[384,128]{1,0:T(8,128)S(1)}, u32[]{:S(2)}, u32[]{:S(2)}) collective-permute-start(f32[384,128]{1,0:T(8,128)S(1)} %constant_dynamic-slice_fusion.1), channel_id=1, source_target_pairs={{0,16},{4,20},{8,24},{12,28},{16,0},{20,4},{24,8},{28,12},{32,48},... | collective-permute-start | bytes 589832 | tf_op jit(solution)/shard_map/ppermute | solution.py:27
  49.3 15.5 %collective-permute-start.3 = (f32[384,128]{1,0:T(8,128)S(1)}, f32[384,128]{1,0:T(8,128)S(1)}, u32[]{:S(2)}, u32[]{:S(2)}) collective-permute-start(f32[384,128]{1,0:T(8,128)S(1)} %dynamic-slice_add_fusion.2), channel_id=1, source_target_pairs={{0,32},{4,36},{8,40},{12,44},{16,48},{20,52},{24,56},{28,60},{32,0... | collective-permute-start | bytes 589832 | tf_op jit(solution)/shard_map/ppermute | solution.py:27
  64.8 7.6 %collective-permute-start.4 = (f32[384,128]{1,0:T(8,128)S(1)}, f32[384,128]{1,0:T(8,128)S(1)}, u32[]{:S(2)}, u32[]{:S(2)}) collective-permute-start(f32[384,128]{1,0:T(8,128)S(1)} %add.214), channel_id=1, source_target_pairs={{0,64},{4,68},{8,72},{12,76},{16,80},{20,84},{24,88},{28,92},{32,9... | collective-permute-start | bytes 589832 | tf_op jit(solution)/shard_map/ppermute | solution.py:27
  72.4 11.0 %collective-permute-start.5 = (f32[384,128]{1,0:T(8,128)S(1)}, f32[384,128]{1,0:T(8,128)S(1)}, u32[]{:S(2)}, u32[]{:S(2)}) collective-permute-start(f32[384,128]{1,0:T(8,128)S(1)} %add.215), channel_id=1, source_target_pairs={{0,128},{4,132},{8,136},{12,140},{16,144},{20,148},{24,152},{28,15... | collective-permute-start | bytes 589832 | tf_op jit(solution)/shard_map/ppermute | solution.py:27
  83.4 13.7 %collective-permute-start.6 = (f32[384,128]{1,0:T(8,128)S(1)}, f32[384,128]{1,0:T(8,128)S(1)}, u32[]{:S(2)}, u32[]{:S(2)}) collective-permute-start(f32[384,128]{1,0:T(8,128)S(1)} %add.216), channel_id=1, source_target_pairs={{0,256},{4,260},{8,264},{12,268},{16,272},{20,276},{24,280},{28,28... | collective-permute-start | bytes 589832 | tf_op jit(solution)/shard_map/ppermute | solution.py:27
  97.2 13.3 %collective-permute-start.7 = (f32[384,128]{1,0:T(8,128)S(1)}, f32[384,128]{1,0:T(8,128)S(1)}, u32[]{:S(2)}, u32[]{:S(2)}) collective-permute-start(f32[384,128]{1,0:T(8,128)S(1)} %add.217), channel_id=1, source_target_pairs={{0,1},{1,0},{2,3},{3,2},{4,5},{5,4},{6,7},{7,6},{8,9},{9,8},{10,11... | collective-permute-start | bytes 589832 | tf_op jit(solution)/shard_map/ppermute | solution.py:27
  110.5 9.1 %collective-permute-start.8 = (f32[384,128]{1,0:T(8,128)S(1)}, f32[384,128]{1,0:T(8,128)S(1)}, u32[]{:S(2)}, u32[]{:S(2)}) collective-permute-start(f32[384,128]{1,0:T(8,128)S(1)} %add.218), channel_id=1, source_target_pairs={{0,2},{1,3},{2,0},{3,1},{4,6},{5,7},{6,4},{7,5},{8,10},{9,11},{10,... | collective-permute-start | bytes 589832 | tf_op jit(solution)/shard_map/ppermute | solution.py:27
  119.6 10.1 %collective-permute-start.9 = (f32[384,128]{1,0:T(8,128)S(1)}, f32[384,128]{1,0:T(8,128)S(1)}, u32[]{:S(2)}, u32[]{:S(2)}) collective-permute-start(f32[384,128]{1,0:T(8,128)S(1)} %add.219), channel_id=1, source_target_pairs={{0,16},{4,20},{8,24},{12,28},{16,0},{20,4},{24,8},{28,12},{32,48},... | collective-permute-start | bytes 589832 | tf_op jit(solution)/shard_map/ppermute | solution.py:27
  129.8 11.1 %collective-permute-start.10 = (f32[768,128]{1,0:T(8,128)S(1)}, f32[768,128]{1,0:T(8,128)S(1)}, u32[]{:S(2)}, u32[]{:S(2)}) collective-permute-start(f32[768,128]{1,0:T(8,128)S(1)} %maximum_select_fusion.2), channel_id=1, source_target_pairs={{0,8},{4,12},{8,0},{12,4},{16,24},{20,28},{24,16},{28,20},{32,40},... | collective-permute-start | bytes 1179656 | tf_op jit(solution)/shard_map/ppermute | solution.py:27
  141.0 4.2 %collective-permute-start.11 = (f32[1536,128]{1,0:T(8,128)S(1)}, f32[1536,128]{1,0:T(8,128)S(1)}, u32[]{:S(2)}, u32[]{:S(2)}) collective-permute-start(f32[1536,128]{1,0:T(8,128)S(1)} %maximum_select_fusion.1), channel_id=1, source_target_pairs={{0,4},{4,0},{8,12},{12,8},{16,20},{20,16},{24,28},{28,24},{32,36},... | collective-permute-start | bytes 2359304 | tf_op jit(solution)/shard_map/ppermute | solution.py:27
  148.5 1.2 copy-start.1
  155.3 34.4 %copy-start.3 = (f32[512,512]{1,0:T(8,128)}, f32[512,512]{1,0:T(8,128)S(1)}, u32[]{:S(2)}) copy-start(f32[512,512]{1,0:T(8,128)S(1)} %fusion.2) | copy-start | bytes 3145732
  300.9 3.1 collective-permute-start.12
  304.0 5.5 %collective-permute-start.13 = (f32[2,256]{1,0:T(2,128)S(1)}, f32[2,256]{1,0:T(2,128)S(1)}, u32[]{:S(2)}, u32[]{:S(2)}) collective-permute-start(f32[2,256]{1,0:T(2,128)S(1)} %pad_maximum_fusion.2), channel_id=1, source_target_pairs={{0,8},{4,12},{8,0},{12,4},{16,24},{20,28},{24,16},{28,20},{32,40},... | collective-permute-start | bytes 6152 | tf_op jit(solution)/shard_map/ppermute | solution.py:27
  309.5 6.4 %collective-permute-start.14 = (f32[2,256]{1,0:T(2,128)S(1)}, f32[2,256]{1,0:T(2,128)S(1)}, u32[]{:S(2)}, u32[]{:S(2)}) collective-permute-start(f32[2,256]{1,0:T(2,128)S(1)} %pad_maximum_fusion.3), channel_id=1, source_target_pairs={{0,16},{4,20},{8,24},{12,28},{16,0},{20,4},{24,8},{28,12},{32,48},... | collective-permute-start | bytes 6152 | tf_op jit(solution)/shard_map/ppermute | solution.py:27
  315.9 9.4 %collective-permute-start.15 = (f32[2,256]{1,0:T(2,128)S(1)}, f32[2,256]{1,0:T(2,128)S(1)}, u32[]{:S(2)}, u32[]{:S(2)}) collective-permute-start(f32[2,256]{1,0:T(2,128)S(1)} %pad_maximum_fusion.4), channel_id=1, source_target_pairs={{0,32},{4,36},{8,40},{12,44},{16,48},{20,52},{24,56},{28,60},{32,0... | collective-permute-start | bytes 6152 | tf_op jit(solution)/shard_map/ppermute | solution.py:27
  325.3 5.5 %collective-permute-start.16 = (f32[2,256]{1,0:T(2,128)S(1)}, f32[2,256]{1,0:T(2,128)S(1)}, u32[]{:S(2)}, u32[]{:S(2)}) collective-permute-start(f32[2,256]{1,0:T(2,128)S(1)} %pad_maximum_fusion.5), channel_id=1, source_target_pairs={{0,64},{4,68},{8,72},{12,76},{16,80},{20,84},{24,88},{28,92},{32,9... | collective-permute-start | bytes 6152 | tf_op jit(solution)/shard_map/ppermute | solution.py:27
  330.8 6.4 %collective-permute-start.17 = (f32[2,256]{1,0:T(2,128)S(1)}, f32[2,256]{1,0:T(2,128)S(1)}, u32[]{:S(2)}, u32[]{:S(2)}) collective-permute-start(f32[2,256]{1,0:T(2,128)S(1)} %pad_maximum_fusion.6), channel_id=1, source_target_pairs={{0,128},{4,132},{8,136},{12,140},{16,144},{20,148},{24,152},{28,15... | collective-permute-start | bytes 6152 | tf_op jit(solution)/shard_map/ppermute | solution.py:27
  337.2 9.4 %collective-permute-start.18 = (f32[2,256]{1,0:T(2,128)S(1)}, f32[2,256]{1,0:T(2,128)S(1)}, u32[]{:S(2)}, u32[]{:S(2)}) collective-permute-start(f32[2,256]{1,0:T(2,128)S(1)} %pad_maximum_fusion.7), channel_id=1, source_target_pairs={{0,256},{4,260},{8,264},{12,268},{16,272},{20,276},{24,280},{28,28... | collective-permute-start | bytes 6152 | tf_op jit(solution)/shard_map/ppermute | solution.py:27
  346.6 5.5 %collective-permute-start.19 = (f32[2,256]{1,0:T(2,128)S(1)}, f32[2,256]{1,0:T(2,128)S(1)}, u32[]{:S(2)}, u32[]{:S(2)}) collective-permute-start(f32[2,256]{1,0:T(2,128)S(1)} %pad_maximum_fusion.8), channel_id=1, source_target_pairs={{0,1},{1,0},{2,3},{3,2},{4,5},{5,4},{6,7},{7,6},{8,9},{9,8},{10,11... | collective-permute-start | bytes 6152 | tf_op jit(solution)/shard_map/ppermute | solution.py:27
  352.1 7.0 %collective-permute-start.20 = (f32[2,256]{1,0:T(2,128)S(1)}, f32[2,256]{1,0:T(2,128)S(1)}, u32[]{:S(2)}, u32[]{:S(2)}) collective-permute-start(f32[2,256]{1,0:T(2,128)S(1)} %pad_maximum_fusion.9), channel_id=1, source_target_pairs={{0,2},{1,3},{2,0},{3,1},{4,6},{5,7},{6,4},{7,5},{8,10},{9,11},{10,... | collective-permute-start | bytes 6152 | tf_op jit(solution)/shard_map/ppermute | solution.py:27

commit v2 on v1

--- a/solution.py
+++ b/solution.py
@@ -66,15 +66,28 @@
     cross_part = lax.dot_general(
         aligned, targets, (((0,), (0,)), ((), ())), preferred_element_type=jnp.float32
     )
-    packed = jnp.concatenate([gram_part, cross_part], axis=1)
-    flat = packed.reshape(-1, 128)
-    summed = tree_sum(flat, bits, 3).reshape(width, width + attrs)
-    gram = summed[:, :width]
-    cross = summed[:, width:]
+    block = 128
+    nb = width // block
+    lower_blocks = [
+        gram_part[i * block:(i + 1) * block, j * block:(j + 1) * block]
+        for i in range(nb)
+        for j in range(i + 1)
+    ]
+    gram_flat = jnp.concatenate(lower_blocks, axis=0).reshape(-1, 128)
+    gram_sum = tree_sum(gram_flat, bits, 3).reshape(len(lower_blocks), block, block)
+    cross = tree_sum(cross_part.reshape(-1, 128), bits, 3).reshape(width, attrs)
+    block_of = {}
+    for n, (i, j) in enumerate((i, j) for i in range(nb) for j in range(i + 1)):
+        block_of[(i, j)] = gram_sum[n]
+        block_of[(j, i)] = gram_sum[n].T
+    gram = jnp.concatenate(
+        [jnp.concatenate([block_of[(i, j)] for j in range(nb)], axis=1) for i in range(nb)],
+        axis=0,
+    )
     total_rows = embeddings.shape[0] * lax.axis_size("docs") * lax.axis_size("grp")
     ridge_shift = penalty[0].astype(jnp.float32) * jnp.float32(total_rows / 8.0)
     system = gram + ridge_shift * jnp.eye(width, dtype=jnp.float32)
-    factor = jnp.linalg.cholesky(system)
+    factor = lax.linalg.cholesky(system, symmetrize_input=False)
     coeffs = jax.scipy.linalg.cho_solve((factor, True), cross).astype(jnp.bfloat16)
     scores = jnp.dot(features, coeffs, preferred_element_type=jnp.float32)
     peak_local = jnp.max(jnp.abs(scores), axis=0)

time: 365 us -> 343 us (0.940)
  the two profiles are of different devices: /device:TPU:2 before, /device:TPU:6 now
where the time goes in v2:
time: 343 us; the launch traced here: 337 us
  other arithmetic  126 us (37%)
  starting transfers between devices  112 us (33%)
  waiting for transfers between devices  61.2 us (18%)
  local copies, waits for them, and re-layouts  20.3 us (6%)
  matrix products  12.1 us (4%)
  between operations  5.22 us (2%)
    ppermute x33, starting transfers between devices, partner(): return lax.ppermute(x, name, [(i, i ^ mask) for i in range(size)])  112 us
    another operation x14, other arithmetic, on_device(): factor = lax.linalg.cholesky(system, symmetrize_input=False)  83.1 us
    ppermute x33, waiting for transfers between devices, partner(): return lax.ppermute(x, name, [(i, i ^ mask) for i in range(size)])  61.2 us
    another operation x3, other arithmetic, on_device(): jax.scipy.linalg.cho_solve((factor, True), cross).astype(jnp.bfloat16)  40.3 us
    another operation x12, local copies, waits for them, and re-layouts  10.5 us
  transfers between devices with their start and end apart: 33, of which 23 were waited for; matrix products, arithmetic and copies ran while one was open for 2% of the time, Pallas kernels for 0%

profile of v2, /device:TPU:6, one launch (start us, length us, event | category | flops | bytes accessed | tf_op | source)
XLA Modules:
  0.0 337.1 jit_solution(7364113096395977666)
XLA Ops:
  1.5 3.3 fusion.1
  9.4 2.4 collective-permute-start
  13.0 4.3 %collective-permute-start.13 = (f32[256,128]{1,0:T(8,128)S(1)}, f32[256,128]{1,0:T(8,128)S(1)}, u32[]{:S(2)}, u32[]{:S(2)}) collective-permute-start(f32[256,128]{1,0:T(8,128)S(1)} %constant_dynamic-slice_fusion.2), channel_id=1, source_target_pairs={{0,8},{4,12},{8,0},{12,4},{16,24},{20,28},{24,16},{28,20},{32,40},... | collective-permute-start | bytes 393224 | tf_op jit(solution)/shard_map/ppermute | solution.py:27
  21.0 4.9 %collective-permute-done.1 = f32[320,128]{0,1:T(8,128)S(1)} collective-permute-done((f32[320,128]{0,1:T(8,128)S(1)}, f32[320,128]{0,1:T(8,128)S(1)}, u32[]{:S(2)}, u32[]{:S(2)}) %collective-permute-start.1) | collective-permute-done | bytes 163872 | tf_op jit(solution)/shard_map/ppermute | solution.py:27
  26.1 6.1 %collective-permute-start.2 = (f32[160,128]{0,1:T(8,128)S(1)}, f32[160,128]{0,1:T(8,128)S(1)}, u32[]{:S(2)}, u32[]{:S(2)}) collective-permute-start(f32[160,128]{0,1:T(8,128)S(1)} %constant_dynamic-slice_fusion.4), channel_id=1, source_target_pairs={{0,16},{4,20},{8,24},{12,28},{16,0},{20,4},{24,8},{28,12},{32,48},... | collective-permute-start | bytes 245768 | tf_op jit(solution)/shard_map/ppermute | solution.py:27
  34.2 4.8 %collective-permute-done.2 = f32[160,128]{0,1:T(8,128)S(1)} collective-permute-done((f32[160,128]{0,1:T(8,128)S(1)}, f32[160,128]{0,1:T(8,128)S(1)}, u32[]{:S(2)}, u32[]{:S(2)}) %collective-permute-start.2) | collective-permute-done | bytes 81952 | tf_op jit(solution)/shard_map/ppermute | solution.py:27
  39.0 9.2 %collective-permute-start.3 = (f32[160,128]{0,1:T(8,128)S(1)}, f32[160,128]{0,1:T(8,128)S(1)}, u32[]{:S(2)}, u32[]{:S(2)}) collective-permute-start(f32[160,128]{0,1:T(8,128)S(1)} %dynamic-slice_add_fusion.4), channel_id=1, source_target_pairs={{0,32},{4,36},{8,40},{12,44},{16,48},{20,52},{24,56},{28,60},{32,0... | collective-permute-start | bytes 245768 | tf_op jit(solution)/shard_map/ppermute | solution.py:27
  52.2 3.5 %collective-permute-start.4 = (f32[160,128]{0,1:T(8,128)S(1)}, f32[160,128]{0,1:T(8,128)S(1)}, u32[]{:S(2)}, u32[]{:S(2)}) collective-permute-start(f32[160,128]{0,1:T(8,128)S(1)} %add.252), channel_id=1, source_target_pairs={{0,64},{4,68},{8,72},{12,76},{16,80},{20,84},{24,88},{28,92},{32,9... | collective-permute-start | bytes 245768 | tf_op jit(solution)/shard_map/ppermute | solution.py:27
  55.7 2.6 collective-permute-done.15
  58.3 3.5 %collective-permute-start.16 = (f32[128,128]{1,0:T(8,128)S(1)}, f32[128,128]{1,0:T(8,128)S(1)}, u32[]{:S(2)}, u32[]{:S(2)}) collective-permute-start(f32[128,128]{1,0:T(8,128)S(1)} %add.270), channel_id=1, source_target_pairs={{0,64},{4,68},{8,72},{12,76},{16,80},{20,84},{24,88},{28,92},{32,9... | collective-permute-start | bytes 196616 | tf_op jit(solution)/shard_map/ppermute | solution.py:27
  61.9 4.5 %collective-permute-start.5 = (f32[160,128]{0,1:T(8,128)S(1)}, f32[160,128]{0,1:T(8,128)S(1)}, u32[]{:S(2)}, u32[]{:S(2)}) collective-permute-start(f32[160,128]{0,1:T(8,128)S(1)} %add.253), channel_id=1, source_target_pairs={{0,128},{4,132},{8,136},{12,140},{16,144},{20,148},{24,152},{28,15... | collective-permute-start | bytes 245768 | tf_op jit(solution)/shard_map/ppermute | solution.py:27
  66.4 2.6 collective-permute-start.17
  69.0 5.0 %collective-permute-done.17 = f32[128,128]{1,0:T(8,128)S(1)} collective-permute-done((f32[128,128]{1,0:T(8,128)S(1)}, f32[128,128]{1,0:T(8,128)S(1)}, u32[]{:S(2)}, u32[]{:S(2)}) %collective-permute-start.17) | collective-permute-done | bytes 65568 | tf_op jit(solution)/shard_map/ppermute | solution.py:27
  74.1 6.1 %collective-permute-start.18 = (f32[128,128]{1,0:T(8,128)S(1)}, f32[128,128]{1,0:T(8,128)S(1)}, u32[]{:S(2)}, u32[]{:S(2)}) collective-permute-start(f32[128,128]{1,0:T(8,128)S(1)} %add.272), channel_id=1, source_target_pairs={{0,256},{4,260},{8,264},{12,268},{16,272},{20,276},{24,280},{28,28... | collective-permute-start | bytes 196616 | tf_op jit(solution)/shard_map/ppermute | solution.py:27
  80.2 3.7 %collective-permute-start.6 = (f32[160,128]{0,1:T(8,128)S(1)}, f32[160,128]{0,1:T(8,128)S(1)}, u32[]{:S(2)}, u32[]{:S(2)}) collective-permute-start(f32[160,128]{0,1:T(8,128)S(1)} %add.254), channel_id=1, source_target_pairs={{0,256},{4,260},{8,264},{12,268},{16,272},{20,276},{24,280},{28,28... | collective-permute-start | bytes 245768 | tf_op jit(solution)/shard_map/ppermute | solution.py:27
  83.9 3.0 collective-permute-done.18
  86.9 2.7 collective-permute-start.19
  91.6 2.7 collective-permute-start.7
  94.3 2.9 collective-permute-start.20
  98.5 3.3 collective-permute-start.8
  104.4 2.5 collective-permute-done.8
  108.8 2.4 collective-permute-done.21
  111.2 3.8 %collective-permute-start.22 = (f32[256,128]{1,0:T(8,128)S(1)}, f32[256,128]{1,0:T(8,128)S(1)}, u32[]{:S(2)}, u32[]{:S(2)}) collective-permute-start(f32[256,128]{1,0:T(8,128)S(1)} %maximum_select_fusion.5), channel_id=1, source_target_pairs={{0,8},{4,12},{8,0},{12,4},{16,24},{20,28},{24,16},{28,20},{32,40},... | collective-permute-start | bytes 393224 | tf_op jit(solution)/shard_map/ppermute | solution.py:27
  115.8 3.2 collective-permute-start.10
  123.5 2.4 collective-permute-start.11
  129.8 11.7 %cholesky.103 = f32[128,128]{1,0:T(8,128)S(1)} custom-call(f32[128,128]{1,0:T(8,128)S(1)} %cholesky.263), custom_call_target="Cholesky" | custom-call | tf_op jit(solution)/shard_map/cholesky | solution.py:90
  141.7 9.8 %custom-call.27 = f32[1,128,128]{1,2,0:T(8,128)S(1)} custom-call(f32[1,128,128]{2,1,0:T(8,128)S(1)} %get-tuple-element.52), custom_call_target="InvertDiagBlocksLowerTriangular" | custom-call | tf_op jit(solution)/shard_map/cholesky | solution.py:90
  152.8 11.7 %cholesky.215 = f32[128,128]{1,0:T(8,128)S(1)} custom-call(f32[128,128]{1,0:T(8,128)S(1)} %cholesky.267), custom_call_target="Cholesky" | custom-call | tf_op jit(solution)/shard_map/cholesky | solution.py:90
  164.6 10.0 %custom-call.28 = f32[1,128,128]{1,2,0:T(8,128)S(1)} custom-call(f32[1,128,128]{2,1,0:T(8,128)S(1)} %get-tuple-element.49), custom_call_target="InvertDiagBlocksLowerTriangular" | custom-call | tf_op jit(solution)/shard_map/cholesky | solution.py:90
  176.7 13.2 %cholesky.236 = f32[128,128]{1,0:T(8,128)} custom-call(f32[128,128]{1,0:T(8,128)} %cholesky.272), custom_call_target="Cholesky" | custom-call | tf_op jit(solution)/shard_map/cholesky | solution.py:90
  192.1 11.3 %custom-call.29 = f32[1,128,128]{1,2,0:T(8,128)} custom-call(f32[1,128,128]{2,1,0:T(8,128)} %get-tuple-element.46), custom_call_target="InvertDiagBlocksLowerTriangular" | custom-call | tf_op jit(solution)/shard_map/cholesky | solution.py:90
  204.8 11.9 %cholesky.253 = f32[128,128]{1,0:T(8,128)S(1)} custom-call(f32[128,128]{1,0:T(8,128)S(1)} %convolution_subtract_fusion.5), custom_call_target="Cholesky" | custom-call | tf_op jit(solution)/shard_map/cholesky | solution.py:90
  220.6 10.5 %while.1 = (s32[]{:T(128)}, f32[512,512]{1,0:T(8,128)S(1)}, s32[4,2]{0,1:T(2,128)S(1)}, f32[4,128,128]{2,1,0:T(8,128)}, s32[]{:T(128)}) while((s32[]{:T(128)}, f32[512,512]{1,0:T(8,128)S(1)}, s32[4,2]{0,1:T(2,128)S(1)}, f32[4,128,128]{2,1,0:T(8,128)}, s32[]{:T(128)}) %tuple.57), condition=%wide.while_cond, body=%wide.while_body.sunk | while | flops 2 | bytes 132705 | solution.py:91
  231.2 40.1 %custom-call.30 = f32[4,128,128]{1,2,0:T(8,128)S(1)} custom-call(f32[4,128,128]{2,1,0:T(8,128)} %get-tuple-element.12), custom_call_target="InvertDiagBlocksLowerTriangular" | custom-call | tf_op jit(solution)/shard_map/jit(_cho_solve)/triangular_solve | solution.py:91
  277.9 2.4 collective-permute-start.24
  281.1 3.2 collective-permute-start.25
  286.6 3.3 collective-permute-start.26
  289.9 3.1 collective-permute-done.26
  293.0 7.0 %collective-permute-start.27 = (f32[2,256]{1,0:T(2,128)S(1)}, f32[2,256]{1,0:T(2,128)S(1)}, u32[]{:S(2)}, u32[]{:S(2)}) collective-permute-start(f32[2,256]{1,0:T(2,128)S(1)} %pad_maximum_fusion.4), channel_id=1, source_target_pairs={{0,32},{4,36},{8,40},{12,44},{16,48},{20,52},{24,56},{28,60},{32,0... | collective-permute-start | bytes 6152 | tf_op jit(solution)/shard_map/ppermute | solution.py:27
  304.3 3.6 %collective-permute-done.28 = f32[2,256]{1,0:T(2,128)S(1)} collective-permute-done((f32[2,256]{1,0:T(2,128)S(1)}, f32[2,256]{1,0:T(2,128)S(1)}, u32[]{:S(2)}, u32[]{:S(2)}) %collective-permute-start.28) | collective-permute-done | bytes 2080 | tf_op jit(solution)/shard_map/ppermute | solution.py:27
  307.9 2.8 collective-permute-start.29
  310.7 3.6 %collective-permute-done.29 = f32[2,256]{1,0:T(2,128)S(1)} collective-permute-done((f32[2,256]{1,0:T(2,128)S(1)}, f32[2,256]{1,0:T(2,128)S(1)}, u32[]{:S(2)}, u32[]{:S(2)}) %collective-permute-start.29) | collective-permute-done | bytes 2080 | tf_op jit(solution)/shard_map/ppermute | solution.py:27
  314.3 4.5 %collective-permute-start.30 = (f32[2,256]{1,0:T(2,128)S(1)}, f32[2,256]{1,0:T(2,128)S(1)}, u32[]{:S(2)}, u32[]{:S(2)}) collective-permute-start(f32[2,256]{1,0:T(2,128)S(1)} %pad_maximum_fusion.7), channel_id=1, source_target_pairs={{0,256},{4,260},{8,264},{12,268},{16,272},{20,276},{24,280},{28,28... | collective-permute-start | bytes 6152 | tf_op jit(solution)/shard_map/ppermute | solution.py:27
  318.8 4.9 %collective-permute-done.30 = f32[2,256]{1,0:T(2,128)S(1)} collective-permute-done((f32[2,256]{1,0:T(2,128)S(1)}, f32[2,256]{1,0:T(2,128)S(1)}, u32[]{:S(2)}, u32[]{:S(2)}) %collective-permute-start.30) | collective-permute-done | bytes 2080 | tf_op jit(solution)/shard_map/ppermute | solution.py:27
  323.7 2.8 collective-permute-start.31
  326.5 2.7 collective-permute-done.31
  329.2 3.5 %collective-permute-start.32 = (f32[2,256]{1,0:T(2,128)S(1)}, f32[2,256]{1,0:T(2,128)S(1)}, u32[]{:S(2)}, u32[]{:S(2)}) collective-permute-start(f32[2,256]{1,0:T(2,128)S(1)} %pad_maximum_fusion.9), channel_id=1, source_target_pairs={{0,2},{1,3},{2,0},{3,1},{4,6},{5,7},{6,4},{7,5},{8,10},{9,11},{10,... | collective-permute-start | bytes 6152 | tf_op jit(solution)/shard_map/ppermute | solution.py:27
  332.7 3.4 %collective-permute-done.32 = f32[2,256]{1,0:T(2,128)S(1)} collective-permute-done((f32[2,256]{1,0:T(2,128)S(1)}, f32[2,256]{1,0:T(2,128)S(1)}, u32[]{:S(2)}, u32[]{:S(2)}) %collective-permute-start.32) | collective-permute-done | bytes 2080 | tf_op jit(solution)/shard_map/ppermute | solution.py:27
  (172 shorter events, 66.2 us)
Async XLA Ops:
  0.0 1.5 copy-start
  0.7 0.7 copy-start.7
  4.7 1.2 copy-start.6
  6.9 5.0 %collective-permute-start.12 = (f32[512,128]{1,0:T(8,128)}, f32[512,128]{1,0:T(8,128)}, u32[]{:S(2)}, u32[]{:S(2)}) collective-permute-start(f32[512,128]{1,0:T(8,128)} %constant_dynamic-slice_fusion.3), channel_id=1, source_target_pairs={{0,4},{4,0},{8,12},{12,8},{16,20},{20,16},{24,28},{28,24},{32,36},... | collective-permute-start | bytes 786440 | tf_op jit(solution)/shard_map/ppermute | solution.py:27
  9.4 7.8 %collective-permute-start = (f32[640,128]{0,1:T(8,128)S(1)}, f32[640,128]{0,1:T(8,128)S(1)}, u32[]{:S(2)}, u32[]{:S(2)}) collective-permute-start(f32[640,128]{0,1:T(8,128)S(1)} %constant_dynamic-slice_fusion.6), channel_id=1, source_target_pairs={{0,4},{4,0},{8,12},{12,8},{16,20},{20,16},{24,28},{28,24},{32,36},... | collective-permute-start | bytes 983048 | tf_op jit(solution)/shard_map/ppermute | solution.py:27
  13.0 8.0 %collective-permute-start.13 = (f32[256,128]{1,0:T(8,128)S(1)}, f32[256,128]{1,0:T(8,128)S(1)}, u32[]{:S(2)}, u32[]{:S(2)}) collective-permute-start(f32[256,128]{1,0:T(8,128)S(1)} %constant_dynamic-slice_fusion.2), channel_id=1, source_target_pairs={{0,8},{4,12},{8,0},{12,4},{16,24},{20,28},{24,16},{28,20},{32,40},... | collective-permute-start | bytes 393224 | tf_op jit(solution)/shard_map/ppermute | solution.py:27
  17.5 8.4 %collective-permute-start.1 = (f32[320,128]{0,1:T(8,128)S(1)}, f32[320,128]{0,1:T(8,128)S(1)}, u32[]{:S(2)}, u32[]{:S(2)}) collective-permute-start(f32[320,128]{0,1:T(8,128)S(1)} %constant_dynamic-slice_fusion.5), channel_id=1, source_target_pairs={{0,8},{4,12},{8,0},{12,4},{16,24},{20,28},{24,16},{28,20},{32,40},... | collective-permute-start | bytes 491528 | tf_op jit(solution)/shard_map/ppermute | solution.py:27
  26.1 12.8 %collective-permute-start.2 = (f32[160,128]{0,1:T(8,128)S(1)}, f32[160,128]{0,1:T(8,128)S(1)}, u32[]{:S(2)}, u32[]{:S(2)}) collective-permute-start(f32[160,128]{0,1:T(8,128)S(1)} %constant_dynamic-slice_fusion.4), channel_id=1, source_target_pairs={{0,16},{4,20},{8,24},{12,28},{16,0},{20,4},{24,8},{28,12},{32,48},... | collective-permute-start | bytes 245768 | tf_op jit(solution)/shard_map/ppermute | solution.py:27
  32.3 16.0 %collective-permute-start.14 = (f32[128,128]{1,0:T(8,128)S(1)}, f32[128,128]{1,0:T(8,128)S(1)}, u32[]{:S(2)}, u32[]{:S(2)}) collective-permute-start(f32[128,128]{1,0:T(8,128)S(1)} %constant_dynamic-slice_fusion.1), channel_id=1, source_target_pairs={{0,16},{4,20},{8,24},{12,28},{16,0},{20,4},{24,8},{28,12},{32,48},... | collective-permute-start | bytes 196616 | tf_op jit(solution)/shard_map/ppermute | solution.py:27
  39.0 13.2 %collective-permute-start.3 = (f32[160,128]{0,1:T(8,128)S(1)}, f32[160,128]{0,1:T(8,128)S(1)}, u32[]{:S(2)}, u32[]{:S(2)}) collective-permute-start(f32[160,128]{0,1:T(8,128)S(1)} %dynamic-slice_add_fusion.4), channel_id=1, source_target_pairs={{0,32},{4,36},{8,40},{12,44},{16,48},{20,52},{24,56},{28,60},{32,0... | collective-permute-start | bytes 245768 | tf_op jit(solution)/shard_map/ppermute | solution.py:27
  48.3 10.1 %collective-permute-start.15 = (f32[128,128]{1,0:T(8,128)S(1)}, f32[128,128]{1,0:T(8,128)S(1)}, u32[]{:S(2)}, u32[]{:S(2)}) collective-permute-start(f32[128,128]{1,0:T(8,128)S(1)} %dynamic-slice_add_fusion.5), channel_id=1, source_target_pairs={{0,32},{4,36},{8,40},{12,44},{16,48},{20,52},{24,56},{28,60},{32,0... | collective-permute-start | bytes 196616 | tf_op jit(solution)/shard_map/ppermute | solution.py:27
  52.2 9.6 %collective-permute-start.4 = (f32[160,128]{0,1:T(8,128)S(1)}, f32[160,128]{0,1:T(8,128)S(1)}, u32[]{:S(2)}, u32[]{:S(2)}) collective-permute-start(f32[160,128]{0,1:T(8,128)S(1)} %add.252), channel_id=1, source_target_pairs={{0,64},{4,68},{8,72},{12,76},{16,80},{20,84},{24,88},{28,92},{32,9... | collective-permute-start | bytes 245768 | tf_op jit(solution)/shard_map/ppermute | solution.py:27
  58.3 8.0 %collective-permute-start.16 = (f32[128,128]{1,0:T(8,128)S(1)}, f32[128,128]{1,0:T(8,128)S(1)}, u32[]{:S(2)}, u32[]{:S(2)}) collective-permute-start(f32[128,128]{1,0:T(8,128)S(1)} %add.270), channel_id=1, source_target_pairs={{0,64},{4,68},{8,72},{12,76},{16,80},{20,84},{24,88},{28,92},{32,9... | collective-permute-start | bytes 196616 | tf_op jit(solution)/shard_map/ppermute | solution.py:27
  61.9 18.3 %collective-permute-start.5 = (f32[160,128]{0,1:T(8,128)S(1)}, f32[160,128]{0,1:T(8,128)S(1)}, u32[]{:S(2)}, u32[]{:S(2)}) collective-permute-start(f32[160,128]{0,1:T(8,128)S(1)} %add.253), channel_id=1, source_target_pairs={{0,128},{4,132},{8,136},{12,140},{16,144},{20,148},{24,152},{28,15... | collective-permute-start | bytes 245768 | tf_op jit(solution)/shard_map/ppermute | solution.py:27
  66.4 7.6 %collective-permute-start.17 = (f32[128,128]{1,0:T(8,128)S(1)}, f32[128,128]{1,0:T(8,128)S(1)}, u32[]{:S(2)}, u32[]{:S(2)}) collective-permute-start(f32[128,128]{1,0:T(8,128)S(1)} %add.271), channel_id=1, source_target_pairs={{0,128},{4,132},{8,136},{12,140},{16,144},{20,148},{24,152},{28,15... | collective-permute-start | bytes 196616 | tf_op jit(solution)/shard_map/ppermute | solution.py:27
  74.1 12.8 %collective-permute-start.18 = (f32[128,128]{1,0:T(8,128)S(1)}, f32[128,128]{1,0:T(8,128)S(1)}, u32[]{:S(2)}, u32[]{:S(2)}) collective-permute-start(f32[128,128]{1,0:T(8,128)S(1)} %add.272), channel_id=1, source_target_pairs={{0,256},{4,260},{8,264},{12,268},{16,272},{20,276},{24,280},{28,28... | collective-permute-start | bytes 196616 | tf_op jit(solution)/shard_map/ppermute | solution.py:27
  80.2 11.4 %collective-permute-start.6 = (f32[160,128]{0,1:T(8,128)S(1)}, f32[160,128]{0,1:T(8,128)S(1)}, u32[]{:S(2)}, u32[]{:S(2)}) collective-permute-start(f32[160,128]{0,1:T(8,128)S(1)} %add.254), channel_id=1, source_target_pairs={{0,256},{4,260},{8,264},{12,268},{16,272},{20,276},{24,280},{28,28... | collective-permute-start | bytes 245768 | tf_op jit(solution)/shard_map/ppermute | solution.py:27
  86.9 7.4 %collective-permute-start.19 = (f32[128,128]{1,0:T(8,128)S(1)}, f32[128,128]{1,0:T(8,128)S(1)}, u32[]{:S(2)}, u32[]{:S(2)}) collective-permute-start(f32[128,128]{1,0:T(8,128)S(1)} %add.273), channel_id=1, source_target_pairs={{0,1},{1,0},{2,3},{3,2},{4,5},{5,4},{6,7},{7,6},{8,9},{9,8},{10,11... | collective-permute-start | bytes 196616 | tf_op jit(solution)/shard_map/ppermute | solution.py:27
  91.6 6.9 %collective-permute-start.7 = (f32[160,128]{0,1:T(8,128)S(1)}, f32[160,128]{0,1:T(8,128)S(1)}, u32[]{:S(2)}, u32[]{:S(2)}) collective-permute-start(f32[160,128]{0,1:T(8,128)S(1)} %add.255), channel_id=1, source_target_pairs={{0,1},{1,0},{2,3},{3,2},{4,5},{5,4},{6,7},{7,6},{8,9},{9,8},{10,11... | collective-permute-start | bytes 245768 | tf_op jit(solution)/shard_map/ppermute | solution.py:27
  94.3 7.7 %collective-permute-start.20 = (f32[128,128]{1,0:T(8,128)S(1)}, f32[128,128]{1,0:T(8,128)S(1)}, u32[]{:S(2)}, u32[]{:S(2)}) collective-permute-start(f32[128,128]{1,0:T(8,128)S(1)} %add.274), channel_id=1, source_target_pairs={{0,2},{1,3},{2,0},{3,1},{4,6},{5,7},{6,4},{7,5},{8,10},{9,11},{10,... | collective-permute-start | bytes 196616 | tf_op jit(solution)/shard_map/ppermute | solution.py:27
  98.5 8.4 %collective-permute-start.8 = (f32[160,128]{0,1:T(8,128)S(1)}, f32[160,128]{0,1:T(8,128)S(1)}, u32[]{:S(2)}, u32[]{:S(2)}) collective-permute-start(f32[160,128]{0,1:T(8,128)S(1)} %add.256), channel_id=1, source_target_pairs={{0,2},{1,3},{2,0},{3,1},{4,6},{5,7},{6,4},{7,5},{8,10},{9,11},{10,... | collective-permute-start | bytes 245768 | tf_op jit(solution)/shard_map/ppermute | solution.py:27
  102.0 9.2 %collective-permute-start.21 = (f32[128,128]{1,0:T(8,128)S(1)}, f32[128,128]{1,0:T(8,128)S(1)}, u32[]{:S(2)}, u32[]{:S(2)}) collective-permute-start(f32[128,128]{1,0:T(8,128)S(1)} %add.275), channel_id=1, source_target_pairs={{0,16},{4,20},{8,24},{12,28},{16,0},{20,4},{24,8},{28,12},{32,48},... | collective-permute-start | bytes 196616 | tf_op jit(solution)/shard_map/ppermute | solution.py:27
  106.9 8.8 %collective-permute-start.9 = (f32[160,128]{0,1:T(8,128)S(1)}, f32[160,128]{0,1:T(8,128)S(1)}, u32[]{:S(2)}, u32[]{:S(2)}) collective-permute-start(f32[160,128]{0,1:T(8,128)S(1)} %add.257), channel_id=1, source_target_pairs={{0,16},{4,20},{8,24},{12,28},{16,0},{20,4},{24,8},{28,12},{32,48},... | collective-permute-start | bytes 245768 | tf_op jit(solution)/shard_map/ppermute | solution.py:27
  111.2 7.8 %collective-permute-start.22 = (f32[256,128]{1,0:T(8,128)S(1)}, f32[256,128]{1,0:T(8,128)S(1)}, u32[]{:S(2)}, u32[]{:S(2)}) collective-permute-start(f32[256,128]{1,0:T(8,128)S(1)} %maximum_select_fusion.5), channel_id=1, source_target_pairs={{0,8},{4,12},{8,0},{12,4},{16,24},{20,28},{24,16},{28,20},{32,40},... | collective-permute-start | bytes 393224 | tf_op jit(solution)/shard_map/ppermute | solution.py:27
  115.8 7.6 %collective-permute-start.10 = (f32[320,128]{0,1:T(8,128)S(1)}, f32[320,128]{0,1:T(8,128)S(1)}, u32[]{:S(2)}, u32[]{:S(2)}) collective-permute-start(f32[320,128]{0,1:T(8,128)S(1)} %maximum_select_fusion.4), channel_id=1, source_target_pairs={{0,8},{4,12},{8,0},{12,4},{16,24},{20,28},{24,16},{28,20},{32,40},... | collective-permute-start | bytes 491528 | tf_op jit(solution)/shard_map/ppermute | solution.py:27
  119.0 6.9 %collective-permute-start.23 = (f32[512,128]{1,0:T(8,128)S(1)}, f32[512,128]{1,0:T(8,128)S(1)}, u32[]{:S(2)}, u32[]{:S(2)}) collective-permute-start(f32[512,128]{1,0:T(8,128)S(1)} %maximum_select_fusion.3), channel_id=1, source_target_pairs={{0,4},{4,0},{8,12},{12,8},{16,20},{20,16},{24,28},{28,24},{32,36},... | collective-permute-start | bytes 786440 | tf_op jit(solution)/shard_map/ppermute | solution.py:27
  123.5 5.3 %collective-permute-start.11 = (f32[640,128]{0,1:T(8,128)S(1)}, f32[640,128]{0,1:T(8,128)S(1)}, u32[]{:S(2)}, u32[]{:S(2)}) collective-permute-start(f32[640,128]{0,1:T(8,128)S(1)} %maximum_select_fusion.2), channel_id=1, source_target_pairs={{0,4},{4,0},{8,12},{12,8},{16,20},{20,16},{24,28},{28,24},{32,36},... | collective-permute-start | bytes 983048 | tf_op jit(solution)/shard_map/ppermute | solution.py:27
  152.1 0.7 copy-start.1
  220.6 50.7 %copy-start.5 = (f32[128,256]{1,0:T(8,128)S(1)}, f32[128,256]{1,0:T(8,128)}, u32[]{:S(2)}) copy-start(f32[128,256]{1,0:T(8,128)} %triangular_solve.136) | copy-start | bytes 393220
  271.6 0.9 copy-start.4
  272.9 0.9 copy-start.3
  274.1 0.9 copy-start.2
  277.9 3.2 collective-permute-start.24
  281.1 5.5 %collective-permute-start.25 = (f32[2,256]{1,0:T(2,128)S(1)}, f32[2,256]{1,0:T(2,128)S(1)}, u32[]{:S(2)}, u32[]{:S(2)}) collective-permute-start(f32[2,256]{1,0:T(2,128)S(1)} %pad_maximum_fusion.2), channel_id=1, source_target_pairs={{0,8},{4,12},{8,0},{12,4},{16,24},{20,28},{24,16},{28,20},{32,40},... | collective-permute-start | bytes 6152 | tf_op jit(solution)/shard_map/ppermute | solution.py:27
  286.6 6.4 %collective-permute-start.26 = (f32[2,256]{1,0:T(2,128)S(1)}, f32[2,256]{1,0:T(2,128)S(1)}, u32[]{:S(2)}, u32[]{:S(2)}) collective-permute-start(f32[2,256]{1,0:T(2,128)S(1)} %pad_maximum_fusion.3), channel_id=1, source_target_pairs={{0,16},{4,20},{8,24},{12,28},{16,0},{20,4},{24,8},{28,12},{32,48},... | collective-permute-start | bytes 6152 | tf_op jit(solution)/shard_map/ppermute | solution.py:27
  293.0 9.4 %collective-permute-start.27 = (f32[2,256]{1,0:T(2,128)S(1)}, f32[2,256]{1,0:T(2,128)S(1)}, u32[]{:S(2)}, u32[]{:S(2)}) collective-permute-start(f32[2,256]{1,0:T(2,128)S(1)} %pad_maximum_fusion.4), channel_id=1, source_target_pairs={{0,32},{4,36},{8,40},{12,44},{16,48},{20,52},{24,56},{28,60},{32,0... | collective-permute-start | bytes 6152 | tf_op jit(solution)/shard_map/ppermute | solution.py:27
  302.4 5.5 %collective-permute-start.28 = (f32[2,256]{1,0:T(2,128)S(1)}, f32[2,256]{1,0:T(2,128)S(1)}, u32[]{:S(2)}, u32[]{:S(2)}) collective-permute-start(f32[2,256]{1,0:T(2,128)S(1)} %pad_maximum_fusion.5), channel_id=1, source_target_pairs={{0,64},{4,68},{8,72},{12,76},{16,80},{20,84},{24,88},{28,92},{32,9... | collective-permute-start | bytes 6152 | tf_op jit(solution)/shard_map/ppermute | solution.py:27
  307.9 6.4 %collective-permute-start.29 = (f32[2,256]{1,0:T(2,128)S(1)}, f32[2,256]{1,0:T(2,128)S(1)}, u32[]{:S(2)}, u32[]{:S(2)}) collective-permute-start(f32[2,256]{1,0:T(2,128)S(1)} %pad_maximum_fusion.6), channel_id=1, source_target_pairs={{0,128},{4,132},{8,136},{12,140},{16,144},{20,148},{24,152},{28,15... | collective-permute-start | bytes 6152 | tf_op jit(solution)/shard_map/ppermute | solution.py:27
  314.3 9.4 %collective-permute-start.30 = (f32[2,256]{1,0:T(2,128)S(1)}, f32[2,256]{1,0:T(2,128)S(1)}, u32[]{:S(2)}, u32[]{:S(2)}) collective-permute-start(f32[2,256]{1,0:T(2,128)S(1)} %pad_maximum_fusion.7), channel_id=1, source_target_pairs={{0,256},{4,260},{8,264},{12,268},{16,272},{20,276},{24,280},{28,28... | collective-permute-start | bytes 6152 | tf_op jit(solution)/shard_map/ppermute | solution.py:27
  323.7 5.5 %collective-permute-start.31 = (f32[2,256]{1,0:T(2,128)S(1)}, f32[2,256]{1,0:T(2,128)S(1)}, u32[]{:S(2)}, u32[]{:S(2)}) collective-permute-start(f32[2,256]{1,0:T(2,128)S(1)} %pad_maximum_fusion.8), channel_id=1, source_target_pairs={{0,1},{1,0},{2,3},{3,2},{4,5},{5,4},{6,7},{7,6},{8,9},{9,8},{10,11... | collective-permute-start | bytes 6152 | tf_op jit(solution)/shard_map/ppermute | solution.py:27
  329.2 7.0 %collective-permute-start.32 = (f32[2,256]{1,0:T(2,128)S(1)}, f32[2,256]{1,0:T(2,128)S(1)}, u32[]{:S(2)}, u32[]{:S(2)}) collective-permute-start(f32[2,256]{1,0:T(2,128)S(1)} %pad_maximum_fusion.9), channel_id=1, source_target_pairs={{0,2},{1,3},{2,0},{3,1},{4,6},{5,7},{6,4},{7,5},{8,10},{9,11},{10,... | collective-permute-start | bytes 6152 | tf_op jit(solution)/shard_map/ppermute | solution.py:27

commit v3 on v2

--- a/solution.py
+++ b/solution.py
@@ -75,7 +75,8 @@
     ]
     gram_flat = jnp.concatenate(lower_blocks, axis=0).reshape(-1, 128)
     gram_sum = tree_sum(gram_flat, bits, 3).reshape(len(lower_blocks), block, block)
-    cross = tree_sum(cross_part.reshape(-1, 128), bits, 3).reshape(width, attrs)
+    cross_bits = bits[:1] + bits[4:7] + bits[1:4] + bits[7:]
+    cross = tree_sum(cross_part.reshape(-1, 128), cross_bits, 3).reshape(width, attrs)
     block_of = {}
     for n, (i, j) in enumerate((i, j) for i in range(nb) for j in range(i + 1)):
         block_of[(i, j)] = gram_sum[n]

time: 343 us -> 340 us (level)
  the two profiles are of different devices: /device:TPU:6 before, /device:TPU:12 now
where the time goes in v3:
time: 340 us; the launch traced here: 334 us
  other arithmetic  126 us (37%)
  starting transfers between devices  112 us (33%)
  waiting for transfers between devices  58.5 us (17%)
  local copies, waits for them, and re-layouts  20.3 us (6%)
  matrix products  12.1 us (4%)
  between operations  5.31 us (2%)
    ppermute x33, starting transfers between devices, partner(): return lax.ppermute(x, name, [(i, i ^ mask) for i in range(size)])  112 us
    another operation x14, other arithmetic, on_device(): factor = lax.linalg.cholesky(system, symmetrize_input=False)  83.1 us
    ppermute x33, waiting for transfers between devices, partner(): return lax.ppermute(x, name, [(i, i ^ mask) for i in range(size)])  58.5 us
    another operation x3, other arithmetic, on_device(): jax.scipy.linalg.cho_solve((factor, True), cross).astype(jnp.bfloat16)  40.3 us
    another operation x12, local copies, waits for them, and re-layouts  10.5 us
  transfers between devices with their start and end apart: 33, of which 21 were waited for; matrix products, arithmetic and copies ran while one was open for 2% of the time, Pallas kernels for 0%

profile of v3, /device:TPU:12, one launch (start us, length us, event | category | flops | bytes accessed | tf_op | source)
XLA Modules:
  0.0 334.5 jit_solution(6596393941000339755)
XLA Ops:
  1.5 3.3 fusion.1
  9.4 2.4 collective-permute-start
  13.0 2.4 collective-permute-start.13
  15.6 4.3 %collective-permute-start.1 = (f32[320,128]{0,1:T(8,128)S(1)}, f32[320,128]{0,1:T(8,128)S(1)}, u32[]{:S(2)}, u32[]{:S(2)}) collective-permute-start(f32[320,128]{0,1:T(8,128)S(1)} %constant_dynamic-slice_fusion.5), channel_id=1, source_target_pairs={{0,8},{4,12},{8,0},{12,4},{16,24},{20,28},{24,16},{28,20},{32,40},... | collective-permute-start | bytes 491528 | tf_op jit(solution)/shard_map/ppermute | solution.py:27
  20.4 4.3 %collective-permute-done.1 = f32[320,128]{0,1:T(8,128)S(1)} collective-permute-done((f32[320,128]{0,1:T(8,128)S(1)}, f32[320,128]{0,1:T(8,128)S(1)}, u32[]{:S(2)}, u32[]{:S(2)}) %collective-permute-start.1) | collective-permute-done | bytes 163872 | tf_op jit(solution)/shard_map/ppermute | solution.py:27
  24.9 6.1 %collective-permute-start.2 = (f32[160,128]{0,1:T(8,128)S(1)}, f32[160,128]{0,1:T(8,128)S(1)}, u32[]{:S(2)}, u32[]{:S(2)}) collective-permute-start(f32[160,128]{0,1:T(8,128)S(1)} %constant_dynamic-slice_fusion.4), channel_id=1, source_target_pairs={{0,16},{4,20},{8,24},{12,28},{16,0},{20,4},{24,8},{28,12},{32,48},... | collective-permute-start | bytes 245768 | tf_op jit(solution)/shard_map/ppermute | solution.py:27
  31.0 4.5 %collective-permute-start.14 = (f32[128,128]{1,0:T(8,128)S(1)}, f32[128,128]{1,0:T(8,128)S(1)}, u32[]{:S(2)}, u32[]{:S(2)}) collective-permute-start(f32[128,128]{1,0:T(8,128)S(1)} %constant_dynamic-slice_fusion.1), channel_id=1, source_target_pairs={{0,128},{4,132},{8,136},{12,140},{16,144},{20,148},{24,152},{28,15... | collective-permute-start | bytes 196616 | tf_op jit(solution)/shard_map/ppermute | solution.py:27
  36.7 8.4 %collective-permute-start.3 = (f32[160,128]{0,1:T(8,128)S(1)}, f32[160,128]{0,1:T(8,128)S(1)}, u32[]{:S(2)}, u32[]{:S(2)}) collective-permute-start(f32[160,128]{0,1:T(8,128)S(1)} %dynamic-slice_add_fusion.4), channel_id=1, source_target_pairs={{0,32},{4,36},{8,40},{12,44},{16,48},{20,52},{24,56},{28,60},{32,0... | collective-permute-start | bytes 245768 | tf_op jit(solution)/shard_map/ppermute | solution.py:27
  45.2 7.7 %collective-permute-start.15 = (f32[128,128]{1,0:T(8,128)S(1)}, f32[128,128]{1,0:T(8,128)S(1)}, u32[]{:S(2)}, u32[]{:S(2)}) collective-permute-start(f32[128,128]{1,0:T(8,128)S(1)} %dynamic-slice_add_fusion.5), channel_id=1, source_target_pairs={{0,256},{4,260},{8,264},{12,268},{16,272},{20,276},{24,280},{28,28... | collective-permute-start | bytes 196616 | tf_op jit(solution)/shard_map/ppermute | solution.py:27
  52.9 2.6 collective-permute-start.4
  56.0 2.5 collective-permute-start.16
  59.8 2.7 collective-permute-start.5
  62.6 5.1 %collective-permute-start.17 = (f32[128,128]{1,0:T(8,128)S(1)}, f32[128,128]{1,0:T(8,128)S(1)}, u32[]{:S(2)}, u32[]{:S(2)}) collective-permute-start(f32[128,128]{1,0:T(8,128)S(1)} %add.279), channel_id=1, source_target_pairs={{0,16},{4,20},{8,24},{12,28},{16,0},{20,4},{24,8},{28,12},{32,48},... | collective-permute-start | bytes 196616 | tf_op jit(solution)/shard_map/ppermute | solution.py:27
  69.9 5.1 %collective-permute-start.18 = (f32[128,128]{1,0:T(8,128)S(1)}, f32[128,128]{1,0:T(8,128)S(1)}, u32[]{:S(2)}, u32[]{:S(2)}) collective-permute-start(f32[128,128]{1,0:T(8,128)S(1)} %add.280), channel_id=1, source_target_pairs={{0,32},{4,36},{8,40},{12,44},{16,48},{20,52},{24,56},{28,60},{32,0... | collective-permute-start | bytes 196616 | tf_op jit(solution)/shard_map/ppermute | solution.py:27
  75.1 5.9 %collective-permute-start.6 = (f32[160,128]{0,1:T(8,128)S(1)}, f32[160,128]{0,1:T(8,128)S(1)}, u32[]{:S(2)}, u32[]{:S(2)}) collective-permute-start(f32[160,128]{0,1:T(8,128)S(1)} %add.260), channel_id=1, source_target_pairs={{0,256},{4,260},{8,264},{12,268},{16,272},{20,276},{24,280},{28,28... | collective-permute-start | bytes 245768 | tf_op jit(solution)/shard_map/ppermute | solution.py:27
  81.0 3.1 collective-permute-start.19
  84.1 3.1 collective-permute-done.6
  87.3 3.0 collective-permute-start.7
  90.2 2.6 collective-permute-start.20
  92.9 2.6 collective-permute-done.7
  99.9 4.0 %collective-permute-done.8 = f32[160,128]{0,1:T(8,128)S(1)} collective-permute-done((f32[160,128]{0,1:T(8,128)S(1)}, f32[160,128]{0,1:T(8,128)S(1)}, u32[]{:S(2)}, u32[]{:S(2)}) %collective-permute-start.8) | collective-permute-done | bytes 81952 | tf_op jit(solution)/shard_map/ppermute | solution.py:27
  103.9 4.5 %collective-permute-start.9 = (f32[160,128]{0,1:T(8,128)S(1)}, f32[160,128]{0,1:T(8,128)S(1)}, u32[]{:S(2)}, u32[]{:S(2)}) collective-permute-start(f32[160,128]{0,1:T(8,128)S(1)} %add.263), channel_id=1, source_target_pairs={{0,16},{4,20},{8,24},{12,28},{16,0},{20,4},{24,8},{28,12},{32,48},... | collective-permute-start | bytes 245768 | tf_op jit(solution)/shard_map/ppermute | solution.py:27
  110.4 2.7 collective-permute-done.9
  113.2 2.5 collective-permute-start.10
  118.3 2.5 collective-permute-done.10
  120.9 2.4 collective-permute-start.11
  127.2 11.7 %cholesky.103 = f32[128,128]{1,0:T(8,128)S(1)} custom-call(f32[128,128]{1,0:T(8,128)S(1)} %cholesky.263), custom_call_target="Cholesky" | custom-call | tf_op jit(solution)/shard_map/cholesky | solution.py:91
  139.1 9.8 %custom-call.27 = f32[1,128,128]{1,2,0:T(8,128)S(1)} custom-call(f32[1,128,128]{2,1,0:T(8,128)S(1)} %get-tuple-element.52), custom_call_target="InvertDiagBlocksLowerTriangular" | custom-call | tf_op jit(solution)/shard_map/cholesky | solution.py:91
  150.3 11.7 %cholesky.215 = f32[128,128]{1,0:T(8,128)S(1)} custom-call(f32[128,128]{1,0:T(8,128)S(1)} %cholesky.267), custom_call_target="Cholesky" | custom-call | tf_op jit(solution)/shard_map/cholesky | solution.py:91
  162.0 10.0 %custom-call.28 = f32[1,128,128]{1,2,0:T(8,128)S(1)} custom-call(f32[1,128,128]{2,1,0:T(8,128)S(1)} %get-tuple-element.49), custom_call_target="InvertDiagBlocksLowerTriangular" | custom-call | tf_op jit(solution)/shard_map/cholesky | solution.py:91
  174.2 13.2 %cholesky.236 = f32[128,128]{1,0:T(8,128)} custom-call(f32[128,128]{1,0:T(8,128)} %cholesky.272), custom_call_target="Cholesky" | custom-call | tf_op jit(solution)/shard_map/cholesky | solution.py:91
  189.5 11.3 %custom-call.29 = f32[1,128,128]{1,2,0:T(8,128)} custom-call(f32[1,128,128]{2,1,0:T(8,128)} %get-tuple-element.46), custom_call_target="InvertDiagBlocksLowerTriangular" | custom-call | tf_op jit(solution)/shard_map/cholesky | solution.py:91
  202.2 11.9 %cholesky.253 = f32[128,128]{1,0:T(8,128)S(1)} custom-call(f32[128,128]{1,0:T(8,128)S(1)} %convolution_subtract_fusion.5), custom_call_target="Cholesky" | custom-call | tf_op jit(solution)/shard_map/cholesky | solution.py:91
  218.1 10.5 %while.1 = (s32[]{:T(128)}, f32[512,512]{1,0:T(8,128)S(1)}, s32[4,2]{0,1:T(2,128)S(1)}, f32[4,128,128]{2,1,0:T(8,128)}, s32[]{:T(128)}) while((s32[]{:T(128)}, f32[512,512]{1,0:T(8,128)S(1)}, s32[4,2]{0,1:T(2,128)S(1)}, f32[4,128,128]{2,1,0:T(8,128)}, s32[]{:T(128)}) %tuple.57), condition=%wide.while_cond, body=%wide.while_body.sunk | while | flops 2 | bytes 132705 | solution.py:92
  228.6 40.1 %custom-call.30 = f32[4,128,128]{1,2,0:T(8,128)S(1)} custom-call(f32[4,128,128]{2,1,0:T(8,128)} %get-tuple-element.12), custom_call_target="InvertDiagBlocksLowerTriangular" | custom-call | tf_op jit(solution)/shard_map/jit(_cho_solve)/triangular_solve | solution.py:92
  275.3 2.4 collective-permute-start.24
  278.5 2.4 collective-permute-start.25
  281.0 3.0 collective-permute-done.25
  284.0 3.2 collective-permute-start.26
  287.2 3.2 collective-permute-done.26
  290.4 4.2 %collective-permute-start.27 = (f32[2,256]{1,0:T(2,128)S(1)}, f32[2,256]{1,0:T(2,128)S(1)}, u32[]{:S(2)}, u32[]{:S(2)}) collective-permute-start(f32[2,256]{1,0:T(2,128)S(1)} %pad_maximum_fusion.4), channel_id=1, source_target_pairs={{0,32},{4,36},{8,40},{12,44},{16,48},{20,52},{24,56},{28,60},{32,0... | collective-permute-start | bytes 6152 | tf_op jit(solution)/shard_map/ppermute | solution.py:27
  294.6 5.2 %collective-permute-done.27 = f32[2,256]{1,0:T(2,128)S(1)} collective-permute-done((f32[2,256]{1,0:T(2,128)S(1)}, f32[2,256]{1,0:T(2,128)S(1)}, u32[]{:S(2)}, u32[]{:S(2)}) %collective-permute-start.27) | collective-permute-done | bytes 2080 | tf_op jit(solution)/shard_map/ppermute | solution.py:27
  301.7 3.5 %collective-permute-done.28 = f32[2,256]{1,0:T(2,128)S(1)} collective-permute-done((f32[2,256]{1,0:T(2,128)S(1)}, f32[2,256]{1,0:T(2,128)S(1)}, u32[]{:S(2)}, u32[]{:S(2)}) %collective-permute-start.28) | collective-permute-done | bytes 2080 | tf_op jit(solution)/shard_map/ppermute | solution.py:27
  307.2 4.4 %collective-permute-done.29 = f32[2,256]{1,0:T(2,128)S(1)} collective-permute-done((f32[2,256]{1,0:T(2,128)S(1)}, f32[2,256]{1,0:T(2,128)S(1)}, u32[]{:S(2)}, u32[]{:S(2)}) %collective-permute-start.29) | collective-permute-done | bytes 2080 | tf_op jit(solution)/shard_map/ppermute | solution.py:27
  311.7 4.6 %collective-permute-start.30 = (f32[2,256]{1,0:T(2,128)S(1)}, f32[2,256]{1,0:T(2,128)S(1)}, u32[]{:S(2)}, u32[]{:S(2)}) collective-permute-start(f32[2,256]{1,0:T(2,128)S(1)} %pad_maximum_fusion.7), channel_id=1, source_target_pairs={{0,256},{4,260},{8,264},{12,268},{16,272},{20,276},{24,280},{28,28... | collective-permute-start | bytes 6152 | tf_op jit(solution)/shard_map/ppermute | solution.py:27
  316.3 4.8 %collective-permute-done.30 = f32[2,256]{1,0:T(2,128)S(1)} collective-permute-done((f32[2,256]{1,0:T(2,128)S(1)}, f32[2,256]{1,0:T(2,128)S(1)}, u32[]{:S(2)}, u32[]{:S(2)}) %collective-permute-start.30) | collective-permute-done | bytes 2080 | tf_op jit(solution)/shard_map/ppermute | solution.py:27
  323.2 3.4 %collective-permute-done.31 = f32[2,256]{1,0:T(2,128)S(1)} collective-permute-done((f32[2,256]{1,0:T(2,128)S(1)}, f32[2,256]{1,0:T(2,128)S(1)}, u32[]{:S(2)}, u32[]{:S(2)}) %collective-permute-start.31) | collective-permute-done | bytes 2080 | tf_op jit(solution)/shard_map/ppermute | solution.py:27
  328.5 5.0 %collective-permute-done.32 = f32[2,256]{1,0:T(2,128)S(1)} collective-permute-done((f32[2,256]{1,0:T(2,128)S(1)}, f32[2,256]{1,0:T(2,128)S(1)}, u32[]{:S(2)}, u32[]{:S(2)}) %collective-permute-start.32) | collective-permute-done | bytes 2080 | tf_op jit(solution)/shard_map/ppermute | solution.py:27
  (172 shorter events, 60.0 us)
Async XLA Ops:
  0.0 1.5 copy-start
  0.7 0.7 copy-start.7
  4.7 1.2 copy-start.6
  7.0 5.1 %collective-permute-start.12 = (f32[512,128]{1,0:T(8,128)}, f32[512,128]{1,0:T(8,128)}, u32[]{:S(2)}, u32[]{:S(2)}) collective-permute-start(f32[512,128]{1,0:T(8,128)} %constant_dynamic-slice_fusion.3), channel_id=1, source_target_pairs={{0,4},{4,0},{8,12},{12,8},{16,20},{20,16},{24,28},{28,24},{32,36},... | collective-permute-start | bytes 786440 | tf_op jit(solution)/shard_map/ppermute | solution.py:27
  9.4 6.0 %collective-permute-start = (f32[640,128]{0,1:T(8,128)S(1)}, f32[640,128]{0,1:T(8,128)S(1)}, u32[]{:S(2)}, u32[]{:S(2)}) collective-permute-start(f32[640,128]{0,1:T(8,128)S(1)} %constant_dynamic-slice_fusion.6), channel_id=1, source_target_pairs={{0,4},{4,0},{8,12},{12,8},{16,20},{20,16},{24,28},{28,24},{32,36},... | collective-permute-start | bytes 983048 | tf_op jit(solution)/shard_map/ppermute | solution.py:27
  13.0 7.3 %collective-permute-start.13 = (f32[256,128]{1,0:T(8,128)S(1)}, f32[256,128]{1,0:T(8,128)S(1)}, u32[]{:S(2)}, u32[]{:S(2)}) collective-permute-start(f32[256,128]{1,0:T(8,128)S(1)} %constant_dynamic-slice_fusion.2), channel_id=1, source_target_pairs={{0,64},{4,68},{8,72},{12,76},{16,80},{20,84},{24,88},{28,92},{32,9... | collective-permute-start | bytes 393224 | tf_op jit(solution)/shard_map/ppermute | solution.py:27
  15.6 9.1 %collective-permute-start.1 = (f32[320,128]{0,1:T(8,128)S(1)}, f32[320,128]{0,1:T(8,128)S(1)}, u32[]{:S(2)}, u32[]{:S(2)}) collective-permute-start(f32[320,128]{0,1:T(8,128)S(1)} %constant_dynamic-slice_fusion.5), channel_id=1, source_target_pairs={{0,8},{4,12},{8,0},{12,4},{16,24},{20,28},{24,16},{28,20},{32,40},... | collective-permute-start | bytes 491528 | tf_op jit(solution)/shard_map/ppermute | solution.py:27
  24.9 11.7 %collective-permute-start.2 = (f32[160,128]{0,1:T(8,128)S(1)}, f32[160,128]{0,1:T(8,128)S(1)}, u32[]{:S(2)}, u32[]{:S(2)}) collective-permute-start(f32[160,128]{0,1:T(8,128)S(1)} %constant_dynamic-slice_fusion.4), channel_id=1, source_target_pairs={{0,16},{4,20},{8,24},{12,28},{16,0},{20,4},{24,8},{28,12},{32,48},... | collective-permute-start | bytes 245768 | tf_op jit(solution)/shard_map/ppermute | solution.py:27
  31.0 14.1 %collective-permute-start.14 = (f32[128,128]{1,0:T(8,128)S(1)}, f32[128,128]{1,0:T(8,128)S(1)}, u32[]{:S(2)}, u32[]{:S(2)}) collective-permute-start(f32[128,128]{1,0:T(8,128)S(1)} %constant_dynamic-slice_fusion.1), channel_id=1, source_target_pairs={{0,128},{4,132},{8,136},{12,140},{16,144},{20,148},{24,152},{28,15... | collective-permute-start | bytes 196616 | tf_op jit(solution)/shard_map/ppermute | solution.py:27
  36.7 16.2 %collective-permute-start.3 = (f32[160,128]{0,1:T(8,128)S(1)}, f32[160,128]{0,1:T(8,128)S(1)}, u32[]{:S(2)}, u32[]{:S(2)}) collective-permute-start(f32[160,128]{0,1:T(8,128)S(1)} %dynamic-slice_add_fusion.4), channel_id=1, source_target_pairs={{0,32},{4,36},{8,40},{12,44},{16,48},{20,52},{24,56},{28,60},{32,0... | collective-permute-start | bytes 245768 | tf_op jit(solution)/shard_map/ppermute | solution.py:27
  45.2 10.8 %collective-permute-start.15 = (f32[128,128]{1,0:T(8,128)S(1)}, f32[128,128]{1,0:T(8,128)S(1)}, u32[]{:S(2)}, u32[]{:S(2)}) collective-permute-start(f32[128,128]{1,0:T(8,128)S(1)} %dynamic-slice_add_fusion.5), channel_id=1, source_target_pairs={{0,256},{4,260},{8,264},{12,268},{16,272},{20,276},{24,280},{28,28... | collective-permute-start | bytes 196616 | tf_op jit(solution)/shard_map/ppermute | solution.py:27
  52.9 6.9 %collective-permute-start.4 = (f32[160,128]{0,1:T(8,128)S(1)}, f32[160,128]{0,1:T(8,128)S(1)}, u32[]{:S(2)}, u32[]{:S(2)}) collective-permute-start(f32[160,128]{0,1:T(8,128)S(1)} %add.258), channel_id=1, source_target_pairs={{0,64},{4,68},{8,72},{12,76},{16,80},{20,84},{24,88},{28,92},{32,9... | collective-permute-start | bytes 245768 | tf_op jit(solution)/shard_map/ppermute | solution.py:27
  56.0 6.6 %collective-permute-start.16 = (f32[128,128]{1,0:T(8,128)S(1)}, f32[128,128]{1,0:T(8,128)S(1)}, u32[]{:S(2)}, u32[]{:S(2)}) collective-permute-start(f32[128,128]{1,0:T(8,128)S(1)} %add.278), channel_id=1, source_target_pairs={{0,8},{4,12},{8,0},{12,4},{16,24},{20,28},{24,16},{28,20},{32,40},... | collective-permute-start | bytes 196616 | tf_op jit(solution)/shard_map/ppermute | solution.py:27
  59.8 15.2 %collective-permute-start.5 = (f32[160,128]{0,1:T(8,128)S(1)}, f32[160,128]{0,1:T(8,128)S(1)}, u32[]{:S(2)}, u32[]{:S(2)}) collective-permute-start(f32[160,128]{0,1:T(8,128)S(1)} %add.259), channel_id=1, source_target_pairs={{0,128},{4,132},{8,136},{12,140},{16,144},{20,148},{24,152},{28,15... | collective-permute-start | bytes 245768 | tf_op jit(solution)/shard_map/ppermute | solution.py:27
  62.6 7.4 %collective-permute-start.17 = (f32[128,128]{1,0:T(8,128)S(1)}, f32[128,128]{1,0:T(8,128)S(1)}, u32[]{:S(2)}, u32[]{:S(2)}) collective-permute-start(f32[128,128]{1,0:T(8,128)S(1)} %add.279), channel_id=1, source_target_pairs={{0,16},{4,20},{8,24},{12,28},{16,0},{20,4},{24,8},{28,12},{32,48},... | collective-permute-start | bytes 196616 | tf_op jit(solution)/shard_map/ppermute | solution.py:27
  69.9 11.1 %collective-permute-start.18 = (f32[128,128]{1,0:T(8,128)S(1)}, f32[128,128]{1,0:T(8,128)S(1)}, u32[]{:S(2)}, u32[]{:S(2)}) collective-permute-start(f32[128,128]{1,0:T(8,128)S(1)} %add.280), channel_id=1, source_target_pairs={{0,32},{4,36},{8,40},{12,44},{16,48},{20,52},{24,56},{28,60},{32,0... | collective-permute-start | bytes 196616 | tf_op jit(solution)/shard_map/ppermute | solution.py:27
  75.1 12.2 %collective-permute-start.6 = (f32[160,128]{0,1:T(8,128)S(1)}, f32[160,128]{0,1:T(8,128)S(1)}, u32[]{:S(2)}, u32[]{:S(2)}) collective-permute-start(f32[160,128]{0,1:T(8,128)S(1)} %add.260), channel_id=1, source_target_pairs={{0,256},{4,260},{8,264},{12,268},{16,272},{20,276},{24,280},{28,28... | collective-permute-start | bytes 245768 | tf_op jit(solution)/shard_map/ppermute | solution.py:27
  81.0 9.2 %collective-permute-start.19 = (f32[128,128]{1,0:T(8,128)S(1)}, f32[128,128]{1,0:T(8,128)S(1)}, u32[]{:S(2)}, u32[]{:S(2)}) collective-permute-start(f32[128,128]{1,0:T(8,128)S(1)} %add.281), channel_id=1, source_target_pairs={{0,1},{1,0},{2,3},{3,2},{4,5},{5,4},{6,7},{7,6},{8,9},{9,8},{10,11... | collective-permute-start | bytes 196616 | tf_op jit(solution)/shard_map/ppermute | solution.py:27
  87.3 8.2 %collective-permute-start.7 = (f32[160,128]{0,1:T(8,128)S(1)}, f32[160,128]{0,1:T(8,128)S(1)}, u32[]{:S(2)}, u32[]{:S(2)}) collective-permute-start(f32[160,128]{0,1:T(8,128)S(1)} %add.261), channel_id=1, source_target_pairs={{0,1},{1,0},{2,3},{3,2},{4,5},{5,4},{6,7},{7,6},{8,9},{9,8},{10,11... | collective-permute-start | bytes 245768 | tf_op jit(solution)/shard_map/ppermute | solution.py:27
  90.2 7.7 %collective-permute-start.20 = (f32[128,128]{1,0:T(8,128)S(1)}, f32[128,128]{1,0:T(8,128)S(1)}, u32[]{:S(2)}, u32[]{:S(2)}) collective-permute-start(f32[128,128]{1,0:T(8,128)S(1)} %add.282), channel_id=1, source_target_pairs={{0,2},{1,3},{2,0},{3,1},{4,6},{5,7},{6,4},{7,5},{8,10},{9,11},{10,... | collective-permute-start | bytes 196616 | tf_op jit(solution)/shard_map/ppermute | solution.py:27
  95.5 8.4 %collective-permute-start.8 = (f32[160,128]{0,1:T(8,128)S(1)}, f32[160,128]{0,1:T(8,128)S(1)}, u32[]{:S(2)}, u32[]{:S(2)}) collective-permute-start(f32[160,128]{0,1:T(8,128)S(1)} %add.262), channel_id=1, source_target_pairs={{0,2},{1,3},{2,0},{3,1},{4,6},{5,7},{6,4},{7,5},{8,10},{9,11},{10,... | collective-permute-start | bytes 245768 | tf_op jit(solution)/shard_map/ppermute | solution.py:27
  97.9 10.5 %collective-permute-start.21 = (f32[128,128]{1,0:T(8,128)S(1)}, f32[128,128]{1,0:T(8,128)S(1)}, u32[]{:S(2)}, u32[]{:S(2)}) collective-permute-start(f32[128,128]{1,0:T(8,128)S(1)} %add.283), channel_id=1, source_target_pairs={{0,128},{4,132},{8,136},{12,140},{16,144},{20,148},{24,152},{28,15... | collective-permute-start | bytes 196616 | tf_op jit(solution)/shard_map/ppermute | solution.py:27
  103.9 9.2 %collective-permute-start.9 = (f32[160,128]{0,1:T(8,128)S(1)}, f32[160,128]{0,1:T(8,128)S(1)}, u32[]{:S(2)}, u32[]{:S(2)}) collective-permute-start(f32[160,128]{0,1:T(8,128)S(1)} %add.263), channel_id=1, source_target_pairs={{0,16},{4,20},{8,24},{12,28},{16,0},{20,4},{24,8},{28,12},{32,48},... | collective-permute-start | bytes 245768 | tf_op jit(solution)/shard_map/ppermute | solution.py:27
  108.4 7.2 %collective-permute-start.22 = (f32[256,128]{1,0:T(8,128)S(1)}, f32[256,128]{1,0:T(8,128)S(1)}, u32[]{:S(2)}, u32[]{:S(2)}) collective-permute-start(f32[256,128]{1,0:T(8,128)S(1)} %maximum_select_fusion.5), channel_id=1, source_target_pairs={{0,64},{4,68},{8,72},{12,76},{16,80},{20,84},{24,88},{28,92},{32,9... | collective-permute-start | bytes 393224 | tf_op jit(solution)/shard_map/ppermute | solution.py:27
  113.2 7.6 %collective-permute-start.10 = (f32[320,128]{0,1:T(8,128)S(1)}, f32[320,128]{0,1:T(8,128)S(1)}, u32[]{:S(2)}, u32[]{:S(2)}) collective-permute-start(f32[320,128]{0,1:T(8,128)S(1)} %maximum_select_fusion.4), channel_id=1, source_target_pairs={{0,8},{4,12},{8,0},{12,4},{16,24},{20,28},{24,16},{28,20},{32,40},... | collective-permute-start | bytes 491528 | tf_op jit(solution)/shard_map/ppermute | solution.py:27
  115.7 7.6 %collective-permute-start.23 = (f32[512,128]{1,0:T(8,128)S(1)}, f32[512,128]{1,0:T(8,128)S(1)}, u32[]{:S(2)}, u32[]{:S(2)}) collective-permute-start(f32[512,128]{1,0:T(8,128)S(1)} %maximum_select_fusion.3), channel_id=1, source_target_pairs={{0,4},{4,0},{8,12},{12,8},{16,20},{20,16},{24,28},{28,24},{32,36},... | collective-permute-start | bytes 786440 | tf_op jit(solution)/shard_map/ppermute | solution.py:27
  120.9 5.3 %collective-permute-start.11 = (f32[640,128]{0,1:T(8,128)S(1)}, f32[640,128]{0,1:T(8,128)S(1)}, u32[]{:S(2)}, u32[]{:S(2)}) collective-permute-start(f32[640,128]{0,1:T(8,128)S(1)} %maximum_select_fusion.2), channel_id=1, source_target_pairs={{0,4},{4,0},{8,12},{12,8},{16,20},{20,16},{24,28},{28,24},{32,36},... | collective-permute-start | bytes 983048 | tf_op jit(solution)/shard_map/ppermute | solution.py:27
  149.6 0.7 copy-start.1
  218.1 50.7 %copy-start.5 = (f32[128,256]{1,0:T(8,128)S(1)}, f32[128,256]{1,0:T(8,128)}, u32[]{:S(2)}) copy-start(f32[128,256]{1,0:T(8,128)} %triangular_solve.136) | copy-start | bytes 393220
  269.1 0.9 copy-start.4
  270.3 0.9 copy-start.3
  271.5 0.9 copy-start.2
  275.3 3.2 collective-permute-start.24
  278.5 5.5 %collective-permute-start.25 = (f32[2,256]{1,0:T(2,128)S(1)}, f32[2,256]{1,0:T(2,128)S(1)}, u32[]{:S(2)}, u32[]{:S(2)}) collective-permute-start(f32[2,256]{1,0:T(2,128)S(1)} %pad_maximum_fusion.2), channel_id=1, source_target_pairs={{0,8},{4,12},{8,0},{12,4},{16,24},{20,28},{24,16},{28,20},{32,40},... | collective-permute-start | bytes 6152 | tf_op jit(solution)/shard_map/ppermute | solution.py:27
  284.0 6.4 %collective-permute-start.26 = (f32[2,256]{1,0:T(2,128)S(1)}, f32[2,256]{1,0:T(2,128)S(1)}, u32[]{:S(2)}, u32[]{:S(2)}) collective-permute-start(f32[2,256]{1,0:T(2,128)S(1)} %pad_maximum_fusion.3), channel_id=1, source_target_pairs={{0,16},{4,20},{8,24},{12,28},{16,0},{20,4},{24,8},{28,12},{32,48},... | collective-permute-start | bytes 6152 | tf_op jit(solution)/shard_map/ppermute | solution.py:27
  290.4 9.4 %collective-permute-start.27 = (f32[2,256]{1,0:T(2,128)S(1)}, f32[2,256]{1,0:T(2,128)S(1)}, u32[]{:S(2)}, u32[]{:S(2)}) collective-permute-start(f32[2,256]{1,0:T(2,128)S(1)} %pad_maximum_fusion.4), channel_id=1, source_target_pairs={{0,32},{4,36},{8,40},{12,44},{16,48},{20,52},{24,56},{28,60},{32,0... | collective-permute-start | bytes 6152 | tf_op jit(solution)/shard_map/ppermute | solution.py:27
  299.8 5.5 %collective-permute-start.28 = (f32[2,256]{1,0:T(2,128)S(1)}, f32[2,256]{1,0:T(2,128)S(1)}, u32[]{:S(2)}, u32[]{:S(2)}) collective-permute-start(f32[2,256]{1,0:T(2,128)S(1)} %pad_maximum_fusion.5), channel_id=1, source_target_pairs={{0,64},{4,68},{8,72},{12,76},{16,80},{20,84},{24,88},{28,92},{32,9... | collective-permute-start | bytes 6152 | tf_op jit(solution)/shard_map/ppermute | solution.py:27
  305.3 6.4 %collective-permute-start.29 = (f32[2,256]{1,0:T(2,128)S(1)}, f32[2,256]{1,0:T(2,128)S(1)}, u32[]{:S(2)}, u32[]{:S(2)}) collective-permute-start(f32[2,256]{1,0:T(2,128)S(1)} %pad_maximum_fusion.6), channel_id=1, source_target_pairs={{0,128},{4,132},{8,136},{12,140},{16,144},{20,148},{24,152},{28,15... | collective-permute-start | bytes 6152 | tf_op jit(solution)/shard_map/ppermute | solution.py:27
  311.7 9.4 %collective-permute-start.30 = (f32[2,256]{1,0:T(2,128)S(1)}, f32[2,256]{1,0:T(2,128)S(1)}, u32[]{:S(2)}, u32[]{:S(2)}) collective-permute-start(f32[2,256]{1,0:T(2,128)S(1)} %pad_maximum_fusion.7), channel_id=1, source_target_pairs={{0,256},{4,260},{8,264},{12,268},{16,272},{20,276},{24,280},{28,28... | collective-permute-start | bytes 6152 | tf_op jit(solution)/shard_map/ppermute | solution.py:27
  321.1 5.5 %collective-permute-start.31 = (f32[2,256]{1,0:T(2,128)S(1)}, f32[2,256]{1,0:T(2,128)S(1)}, u32[]{:S(2)}, u32[]{:S(2)}) collective-permute-start(f32[2,256]{1,0:T(2,128)S(1)} %pad_maximum_fusion.8), channel_id=1, source_target_pairs={{0,1},{1,0},{2,3},{3,2},{4,5},{5,4},{6,7},{7,6},{8,9},{9,8},{10,11... | collective-permute-start | bytes 6152 | tf_op jit(solution)/shard_map/ppermute | solution.py:27
  326.6 7.0 %collective-permute-start.32 = (f32[2,256]{1,0:T(2,128)S(1)}, f32[2,256]{1,0:T(2,128)S(1)}, u32[]{:S(2)}, u32[]{:S(2)}) collective-permute-start(f32[2,256]{1,0:T(2,128)S(1)} %pad_maximum_fusion.9), channel_id=1, source_target_pairs={{0,2},{1,3},{2,0},{3,1},{4,6},{5,7},{6,4},{7,5},{8,10},{9,11},{10,... | collective-permute-start | bytes 6152 | tf_op jit(solution)/shard_map/ppermute | solution.py:27

commit v4 on v2

--- a/solution.py
+++ b/solution.py
@@ -74,8 +74,14 @@
         for j in range(i + 1)
     ]
     gram_flat = jnp.concatenate(lower_blocks, axis=0).reshape(-1, 128)
-    gram_sum = tree_sum(gram_flat, bits, 3).reshape(len(lower_blocks), block, block)
-    cross = tree_sum(cross_part.reshape(-1, 128), bits, 3).reshape(width, attrs)
+    cross_flat = cross_part.reshape(-1, 128)
+    chip_bits = bits[1:]
+    orders = [chip_bits[k:] + chip_bits[:k] for k in (0, 3, 6, 5)]
+    pieces = []
+    for n, part in enumerate(jnp.split(gram_flat, 2) + jnp.split(cross_flat, 2)):
+        pieces.append(tree_sum(part, bits[:1] + orders[n], 3))
+    gram_sum = jnp.concatenate(pieces[:2]).reshape(len(lower_blocks), block, block)
+    cross = jnp.concatenate(pieces[2:]).reshape(width, attrs)
     block_of = {}
     for n, (i, j) in enumerate((i, j) for i in range(nb) for j in range(i + 1)):
         block_of[(i, j)] = gram_sum[n]

time: 343 us -> 405 us (1.18)
  the two profiles are of different devices: /device:TPU:6 before, /device:TPU:8 now
where the time goes in v4:
time: 405 us; the launch traced here: 397 us
  starting transfers between devices  197 us (49%)
  other arithmetic  127 us (31%)
  waiting for transfers between devices  32.4 us (8%)
  local copies, waits for them, and re-layouts  22.2 us (5%)
  matrix products  12.1 us (3%)
  between operations  6.26 us (2%)
    ppermute x57, starting transfers between devices, partner(): return lax.ppermute(x, name, [(i, i ^ mask) for i in range(size)])  197 us
    another operation x15, other arithmetic, on_device(): factor = lax.linalg.cholesky(system, symmetrize_input=False)  83.8 us
    another operation x3, other arithmetic, on_device(): jax.scipy.linalg.cho_solve((factor, True), cross).astype(jnp.bfloat16)  40.3 us
    ppermute x57, waiting for transfers between devices, partner(): return lax.ppermute(x, name, [(i, i ^ mask) for i in range(size)])  32.4 us
    another operation x12, local copies, waits for them, and re-layouts  10.8 us
  transfers between devices with their start and end apart: 57, of which 15 were waited for; matrix products, arithmetic and copies ran while one was open for 2% of the time, Pallas kernels for 0%

profile of v4, /device:TPU:8, one launch (start us, length us, event | category | flops | bytes accessed | tf_op | source)
XLA Modules:
  0.0 397.0 jit_solution(5652530019004072260)
XLA Ops:
  1.2 3.2 fusion.1
  19.2 3.4 collective-permute-start.25
  22.6 6.8 %collective-permute-start.37 = (f32[128,128]{1,0:T(8,128)S(1)}, f32[128,128]{1,0:T(8,128)S(1)}, u32[]{:S(2)}, u32[]{:S(2)}) collective-permute-start(f32[128,128]{1,0:T(8,128)S(1)} %constant_dynamic-slice_fusion.2), channel_id=1, source_target_pairs={{0,256},{4,260},{8,264},{12,268},{16,272},{20,276},{24,280},{28,28... | collective-permute-start | bytes 196616 | tf_op jit(solution)/shard_map/ppermute | solution.py:27
  29.5 4.3 %collective-permute-start.1 = (f32[160,128]{1,0:T(8,128)S(1)}, f32[160,128]{1,0:T(8,128)S(1)}, u32[]{:S(2)}, u32[]{:S(2)}) collective-permute-start(f32[160,128]{1,0:T(8,128)S(1)} %constant_dynamic-slice_fusion.11), channel_id=1, source_target_pairs={{0,8},{4,12},{8,0},{12,4},{16,24},{20,28},{24,16},{28,20},{32,40},... | collective-permute-start | bytes 245768 | tf_op jit(solution)/shard_map/ppermute | solution.py:27
  34.1 3.3 collective-permute-start.13
  37.4 4.6 %collective-permute-start.26 = (f32[64,128]{1,0:T(8,128)S(1)}, f32[64,128]{1,0:T(8,128)S(1)}, u32[]{:S(2)}, u32[]{:S(2)}) collective-permute-start(f32[64,128]{1,0:T(8,128)S(1)} %constant_dynamic-slice_fusion.4), channel_id=1, source_target_pairs={{0,2},{1,3},{2,0},{3,1},{4,6},{5,7},{6,4},{7,5},{8,10},{9,11},{10,... | collective-permute-start | bytes 98312 | tf_op jit(solution)/shard_map/ppermute | solution.py:27
  47.9 3.6 collective-permute-start.39
  51.6 6.1 %collective-permute-start.2 = (f32[80,128]{1,0:T(8,128)S(1)}, f32[80,128]{1,0:T(8,128)S(1)}, u32[]{:S(2)}, u32[]{:S(2)}) collective-permute-start(f32[80,128]{1,0:T(8,128)S(1)} %constant_dynamic-slice_fusion.10), channel_id=1, source_target_pairs={{0,16},{4,20},{8,24},{12,28},{16,0},{20,4},{24,8},{28,12},{32,48},... | collective-permute-start | bytes 122888 | tf_op jit(solution)/shard_map/ppermute | solution.py:27
  62.6 3.9 collective-permute-start.40
  66.6 8.8 %collective-permute-start.3 = (f32[80,128]{1,0:T(8,128)S(1)}, f32[80,128]{1,0:T(8,128)S(1)}, u32[]{:S(2)}, u32[]{:S(2)}) collective-permute-start(f32[80,128]{1,0:T(8,128)S(1)} %dynamic-slice_add_fusion.9), channel_id=1, source_target_pairs={{0,32},{4,36},{8,40},{12,44},{16,48},{20,52},{24,56},{28,60},{32,0... | collective-permute-start | bytes 122888 | tf_op jit(solution)/shard_map/ppermute | solution.py:27
  77.4 3.8 collective-permute-start.15
  81.2 4.3 %collective-permute-start.41 = (f32[64,128]{1,0:T(8,128)S(1)}, f32[64,128]{1,0:T(8,128)S(1)}, u32[]{:S(2)}, u32[]{:S(2)}) collective-permute-start(f32[64,128]{1,0:T(8,128)S(1)} %add.411), channel_id=1, source_target_pairs={{0,16},{4,20},{8,24},{12,28},{16,0},{20,4},{24,8},{28,12},{32,48},... | collective-permute-start | bytes 98312 | tf_op jit(solution)/shard_map/ppermute | solution.py:27
  85.6 3.5 collective-permute-start.30
  93.4 7.8 %collective-permute-start.42 = (f32[64,128]{1,0:T(8,128)S(1)}, f32[64,128]{1,0:T(8,128)S(1)}, u32[]{:S(2)}, u32[]{:S(2)}) collective-permute-start(f32[64,128]{1,0:T(8,128)S(1)} %add.412), channel_id=1, source_target_pairs={{0,32},{4,36},{8,40},{12,44},{16,48},{20,52},{24,56},{28,60},{32,0... | collective-permute-start | bytes 98312 | tf_op jit(solution)/shard_map/ppermute | solution.py:27
  103.6 4.5 %collective-permute-start.5 = (f32[80,128]{1,0:T(8,128)S(1)}, f32[80,128]{1,0:T(8,128)S(1)}, u32[]{:S(2)}, u32[]{:S(2)}) collective-permute-start(f32[80,128]{1,0:T(8,128)S(1)} %add.362), channel_id=1, source_target_pairs={{0,128},{4,132},{8,136},{12,140},{16,144},{20,148},{24,152},{28,15... | collective-permute-start | bytes 122888 | tf_op jit(solution)/shard_map/ppermute | solution.py:27
  108.1 4.4 %collective-permute-start.17 = (f32[80,128]{0,1:T(8,128)S(1)}, f32[80,128]{0,1:T(8,128)S(1)}, u32[]{:S(2)}, u32[]{:S(2)}) collective-permute-start(f32[80,128]{0,1:T(8,128)S(1)} %add.377), channel_id=1, source_target_pairs={{0,2},{1,3},{2,0},{3,1},{4,6},{5,7},{6,4},{7,5},{8,10},{9,11},{10,... | collective-permute-start | bytes 122888 | tf_op jit(solution)/shard_map/ppermute | solution.py:27
  112.6 3.5 collective-permute-start.43
  116.1 5.0 %collective-permute-start.32 = (f32[64,128]{1,0:T(8,128)S(1)}, f32[64,128]{1,0:T(8,128)S(1)}, u32[]{:S(2)}, u32[]{:S(2)}) collective-permute-start(f32[64,128]{1,0:T(8,128)S(1)} %add.400), channel_id=1, source_target_pairs={{0,256},{4,260},{8,264},{12,268},{16,272},{20,276},{24,280},{28,28... | collective-permute-start | bytes 98312 | tf_op jit(solution)/shard_map/ppermute | solution.py:27
  121.1 4.0 %collective-permute-start.44 = (f32[64,128]{1,0:T(8,128)S(1)}, f32[64,128]{1,0:T(8,128)S(1)}, u32[]{:S(2)}, u32[]{:S(2)}) collective-permute-start(f32[64,128]{1,0:T(8,128)S(1)} %add.414), channel_id=1, source_target_pairs={{0,128},{4,132},{8,136},{12,140},{16,144},{20,148},{24,152},{28,15... | collective-permute-start | bytes 98312 | tf_op jit(solution)/shard_map/ppermute | solution.py:27
  125.2 3.2 collective-permute-start.6
  130.9 2.9 collective-permute-start.33
  134.6 3.9 collective-permute-start.45
  143.0 3.9 collective-permute-start.34
  146.9 6.6 %collective-permute-start.46 = (f32[128,128]{1,0:T(8,128)S(1)}, f32[128,128]{1,0:T(8,128)S(1)}, u32[]{:S(2)}, u32[]{:S(2)}) collective-permute-start(f32[128,128]{1,0:T(8,128)S(1)} %maximum_select_fusion.11), channel_id=1, source_target_pairs={{0,256},{4,260},{8,264},{12,268},{16,272},{20,276},{24,280},{28,28... | collective-permute-start | bytes 196616 | tf_op jit(solution)/shard_map/ppermute | solution.py:27
  153.6 3.1 collective-permute-start.8
  161.0 4.3 %collective-permute-start.9 = (f32[80,128]{1,0:T(8,128)S(1)}, f32[80,128]{1,0:T(8,128)S(1)}, u32[]{:S(2)}, u32[]{:S(2)}) collective-permute-start(f32[80,128]{1,0:T(8,128)S(1)} %add.366), channel_id=1, source_target_pairs={{0,16},{4,20},{8,24},{12,28},{16,0},{20,4},{24,8},{28,12},{32,48},... | collective-permute-start | bytes 122888 | tf_op jit(solution)/shard_map/ppermute | solution.py:27
  170.2 3.2 collective-permute-start.10
  174.8 4.6 %collective-permute-start.22 = (f32[160,128]{0,1:T(8,128)S(1)}, f32[160,128]{0,1:T(8,128)S(1)}, u32[]{:S(2)}, u32[]{:S(2)}) collective-permute-start(f32[160,128]{0,1:T(8,128)S(1)} %maximum_select_fusion.6), channel_id=1, source_target_pairs={{0,64},{4,68},{8,72},{12,76},{16,80},{20,84},{24,88},{28,92},{32,9... | collective-permute-start | bytes 245768 | tf_op jit(solution)/shard_map/ppermute | solution.py:27
  188.8 11.7 %cholesky.103 = f32[128,128]{1,0:T(8,128)S(1)} custom-call(f32[128,128]{1,0:T(8,128)S(1)} %cholesky.263), custom_call_target="Cholesky" | custom-call | tf_op jit(solution)/shard_map/cholesky | solution.py:96
  200.6 9.8 %custom-call.27 = f32[1,128,128]{1,2,0:T(8,128)S(1)} custom-call(f32[1,128,128]{2,1,0:T(8,128)S(1)} %get-tuple-element.62), custom_call_target="InvertDiagBlocksLowerTriangular" | custom-call | tf_op jit(solution)/shard_map/cholesky | solution.py:96
  211.8 11.7 %cholesky.215 = f32[128,128]{1,0:T(8,128)S(1)} custom-call(f32[128,128]{1,0:T(8,128)S(1)} %cholesky.267), custom_call_target="Cholesky" | custom-call | tf_op jit(solution)/shard_map/cholesky | solution.py:96
  224.8 9.9 %custom-call.28 = f32[1,128,128]{1,2,0:T(8,128)S(1)} custom-call(f32[1,128,128]{2,1,0:T(8,128)S(1)} %get-tuple-element.59), custom_call_target="InvertDiagBlocksLowerTriangular" | custom-call | tf_op jit(solution)/shard_map/cholesky | solution.py:96
  237.0 13.2 %cholesky.236 = f32[128,128]{1,0:T(8,128)} custom-call(f32[128,128]{1,0:T(8,128)} %cholesky.272), custom_call_target="Cholesky" | custom-call | tf_op jit(solution)/shard_map/cholesky | solution.py:96
  252.3 11.3 %custom-call.29 = f32[1,128,128]{1,2,0:T(8,128)} custom-call(f32[1,128,128]{2,1,0:T(8,128)} %get-tuple-element.56), custom_call_target="InvertDiagBlocksLowerTriangular" | custom-call | tf_op jit(solution)/shard_map/cholesky | solution.py:96
  265.0 11.9 %cholesky.253 = f32[128,128]{1,0:T(8,128)S(1)} custom-call(f32[128,128]{1,0:T(8,128)S(1)} %convolution_subtract_fusion.5), custom_call_target="Cholesky" | custom-call | tf_op jit(solution)/shard_map/cholesky | solution.py:96
  280.3 10.9 %while.1 = (s32[]{:T(128)}, f32[512,512]{1,0:T(8,128)S(1)}, s32[4,2]{0,1:T(2,128)S(1)}, f32[4,128,128]{2,1,0:T(8,128)}, s32[]{:T(128)}) while((s32[]{:T(128)}, f32[512,512]{1,0:T(8,128)S(1)}, s32[4,2]{0,1:T(2,128)S(1)}, f32[4,128,128]{2,1,0:T(8,128)}, s32[]{:T(128)}) %tuple.63), condition=%wide.while_cond, body=%wide.while_body.sunk | while | flops 2 | bytes 132705 | solution.py:97
  291.2 40.1 %custom-call.30 = f32[4,128,128]{1,2,0:T(8,128)S(1)} custom-call(f32[4,128,128]{2,1,0:T(8,128)} %get-tuple-element.12), custom_call_target="InvertDiagBlocksLowerTriangular" | custom-call | tf_op jit(solution)/shard_map/jit(_cho_solve)/triangular_solve | solution.py:97
  341.0 3.4 collective-permute-start.49
  346.5 3.3 collective-permute-start.50
  349.8 3.1 collective-permute-done.50
  352.9 7.5 %collective-permute-start.51 = (f32[2,256]{1,0:T(2,128)S(1)}, f32[2,256]{1,0:T(2,128)S(1)}, u32[]{:S(2)}, u32[]{:S(2)}) collective-permute-start(f32[2,256]{1,0:T(2,128)S(1)} %pad_maximum_fusion.6), channel_id=1, source_target_pairs={{0,32},{4,36},{8,40},{12,44},{16,48},{20,52},{24,56},{28,60},{32,0... | collective-permute-start | bytes 6152 | tf_op jit(solution)/shard_map/ppermute | solution.py:27
  364.5 3.3 collective-permute-done.52
  369.7 4.4 %collective-permute-done.53 = f32[2,256]{1,0:T(2,128)S(1)} collective-permute-done((f32[2,256]{1,0:T(2,128)S(1)}, f32[2,256]{1,0:T(2,128)S(1)}, u32[]{:S(2)}, u32[]{:S(2)}) %collective-permute-start.53) | collective-permute-done | bytes 2080 | tf_op jit(solution)/shard_map/ppermute | solution.py:27
  374.2 3.0 collective-permute-start.54
  377.2 6.4 %collective-permute-done.54 = f32[2,256]{1,0:T(2,128)S(1)} collective-permute-done((f32[2,256]{1,0:T(2,128)S(1)}, f32[2,256]{1,0:T(2,128)S(1)}, u32[]{:S(2)}, u32[]{:S(2)}) %collective-permute-start.54) | collective-permute-done | bytes 2080 | tf_op jit(solution)/shard_map/ppermute | solution.py:27
  385.9 3.2 collective-permute-done.55
  389.1 3.9 collective-permute-start.56
  393.0 3.1 collective-permute-done.56
  (258 shorter events, 101.8 us)
Async XLA Ops:
  5.0 24.5 %collective-permute-start = (f32[320,128]{1,0:T(8,128)S(1)}, f32[320,128]{1,0:T(8,128)S(1)}, u32[]{:S(2)}, u32[]{:S(2)}) collective-permute-start(f32[320,128]{1,0:T(8,128)S(1)} %constant_dynamic-slice_fusion.12), channel_id=1, source_target_pairs={{0,4},{4,0},{8,12},{12,8},{16,20},{20,16},{24,28},{28,24},{32,36},... | collective-permute-start | bytes 491528 | tf_op jit(solution)/shard_map/ppermute | solution.py:27
  9.8 8.4 %collective-permute-start.24 = (f32[256,128]{1,0:T(8,128)}, f32[256,128]{1,0:T(8,128)}, u32[]{:S(2)}, u32[]{:S(2)}) collective-permute-start(f32[256,128]{1,0:T(8,128)} %constant_dynamic-slice_fusion.6), channel_id=1, source_target_pairs={{0,4},{4,0},{8,12},{12,8},{16,20},{20,16},{24,28},{28,24},{32,36},... | collective-permute-start | bytes 393224 | tf_op jit(solution)/shard_map/ppermute | solution.py:27
  12.9 20.9 %collective-permute-start.12 = (f32[320,128]{0,1:T(8,128)S(1)}, f32[320,128]{0,1:T(8,128)S(1)}, u32[]{:S(2)}, u32[]{:S(2)}) collective-permute-start(f32[320,128]{0,1:T(8,128)S(1)} %constant_dynamic-slice_fusion.9), channel_id=1, source_target_pairs={{0,4},{4,0},{8,12},{12,8},{16,20},{20,16},{24,28},{28,24},{32,36},... | collective-permute-start | bytes 491528 | tf_op jit(solution)/shard_map/ppermute | solution.py:27
  15.5 7.0 %collective-permute-start.36 = (f32[256,128]{1,0:T(8,128)}, f32[256,128]{1,0:T(8,128)S(1)}, u32[]{:S(2)}, u32[]{:S(2)}) collective-permute-start(f32[256,128]{1,0:T(8,128)} %constant_dynamic-slice_fusion.3), channel_id=1, source_target_pairs={{0,4},{4,0},{8,12},{12,8},{16,20},{20,16},{24,28},{28,24},{32,36},... | collective-permute-start | bytes 393224 | tf_op jit(solution)/shard_map/ppermute | solution.py:27
  19.2 18.2 %collective-permute-start.25 = (f32[128,128]{1,0:T(8,128)S(1)}, f32[128,128]{1,0:T(8,128)S(1)}, u32[]{:S(2)}, u32[]{:S(2)}) collective-permute-start(f32[128,128]{1,0:T(8,128)S(1)} %constant_dynamic-slice_fusion.5), channel_id=1, source_target_pairs={{0,1},{1,0},{2,3},{3,2},{4,5},{5,4},{6,7},{7,6},{8,9},{9,8},{10,11... | collective-permute-start | bytes 196616 | tf_op jit(solution)/shard_map/ppermute | solution.py:27
  22.6 19.4 %collective-permute-start.37 = (f32[128,128]{1,0:T(8,128)S(1)}, f32[128,128]{1,0:T(8,128)S(1)}, u32[]{:S(2)}, u32[]{:S(2)}) collective-permute-start(f32[128,128]{1,0:T(8,128)S(1)} %constant_dynamic-slice_fusion.2), channel_id=1, source_target_pairs={{0,256},{4,260},{8,264},{12,268},{16,272},{20,276},{24,280},{28,28... | collective-permute-start | bytes 196616 | tf_op jit(solution)/shard_map/ppermute | solution.py:27
  29.5 22.0 %collective-permute-start.1 = (f32[160,128]{1,0:T(8,128)S(1)}, f32[160,128]{1,0:T(8,128)S(1)}, u32[]{:S(2)}, u32[]{:S(2)}) collective-permute-start(f32[160,128]{1,0:T(8,128)S(1)} %constant_dynamic-slice_fusion.11), channel_id=1, source_target_pairs={{0,8},{4,12},{8,0},{12,4},{16,24},{20,28},{24,16},{28,20},{32,40},... | collective-permute-start | bytes 245768 | tf_op jit(solution)/shard_map/ppermute | solution.py:27
  34.1 23.6 %collective-permute-start.13 = (f32[160,128]{0,1:T(8,128)S(1)}, f32[160,128]{0,1:T(8,128)S(1)}, u32[]{:S(2)}, u32[]{:S(2)}) collective-permute-start(f32[160,128]{0,1:T(8,128)S(1)} %constant_dynamic-slice_fusion.8), channel_id=1, source_target_pairs={{0,64},{4,68},{8,72},{12,76},{16,80},{20,84},{24,88},{28,92},{32,9... | collective-permute-start | bytes 245768 | tf_op jit(solution)/shard_map/ppermute | solution.py:27
  37.4 7.3 %collective-permute-start.26 = (f32[64,128]{1,0:T(8,128)S(1)}, f32[64,128]{1,0:T(8,128)S(1)}, u32[]{:S(2)}, u32[]{:S(2)}) collective-permute-start(f32[64,128]{1,0:T(8,128)S(1)} %constant_dynamic-slice_fusion.4), channel_id=1, source_target_pairs={{0,2},{1,3},{2,0},{3,1},{4,6},{5,7},{6,4},{7,5},{8,10},{9,11},{10,... | collective-permute-start | bytes 98312 | tf_op jit(solution)/shard_map/ppermute | solution.py:27
  44.7 15.9 %collective-permute-start.27 = (f32[64,128]{1,0:T(8,128)S(1)}, f32[64,128]{1,0:T(8,128)S(1)}, u32[]{:S(2)}, u32[]{:S(2)}) collective-permute-start(f32[64,128]{1,0:T(8,128)S(1)} %dynamic-slice_add_fusion.11), channel_id=1, source_target_pairs={{0,8},{4,12},{8,0},{12,4},{16,24},{20,28},{24,16},{28,20},{32,40},... | collective-permute-start | bytes 98312 | tf_op jit(solution)/shard_map/ppermute | solution.py:27
  47.9 14.7 %collective-permute-start.39 = (f32[64,128]{1,0:T(8,128)S(1)}, f32[64,128]{1,0:T(8,128)S(1)}, u32[]{:S(2)}, u32[]{:S(2)}) collective-permute-start(f32[64,128]{1,0:T(8,128)S(1)} %dynamic-slice_add_fusion.10), channel_id=1, source_target_pairs={{0,2},{1,3},{2,0},{3,1},{4,6},{5,7},{6,4},{7,5},{8,10},{9,11},{10,... | collective-permute-start | bytes 98312 | tf_op jit(solution)/shard_map/ppermute | solution.py:27
  51.6 14.9 %collective-permute-start.2 = (f32[80,128]{1,0:T(8,128)S(1)}, f32[80,128]{1,0:T(8,128)S(1)}, u32[]{:S(2)}, u32[]{:S(2)}) collective-permute-start(f32[80,128]{1,0:T(8,128)S(1)} %constant_dynamic-slice_fusion.10), channel_id=1, source_target_pairs={{0,16},{4,20},{8,24},{12,28},{16,0},{20,4},{24,8},{28,12},{32,48},... | collective-permute-start | bytes 122888 | tf_op jit(solution)/shard_map/ppermute | solution.py:27
  57.9 19.4 %collective-permute-start.14 = (f32[80,128]{0,1:T(8,128)S(1)}, f32[80,128]{0,1:T(8,128)S(1)}, u32[]{:S(2)}, u32[]{:S(2)}) collective-permute-start(f32[80,128]{0,1:T(8,128)S(1)} %constant_dynamic-slice_fusion.7), channel_id=1, source_target_pairs={{0,128},{4,132},{8,136},{12,140},{16,144},{20,148},{24,152},{28,15... | collective-permute-start | bytes 122888 | tf_op jit(solution)/shard_map/ppermute | solution.py:27
  60.7 14.7 %collective-permute-start.28 = (f32[64,128]{1,0:T(8,128)S(1)}, f32[64,128]{1,0:T(8,128)S(1)}, u32[]{:S(2)}, u32[]{:S(2)}) collective-permute-start(f32[64,128]{1,0:T(8,128)S(1)} %add.396), channel_id=1, source_target_pairs={{0,16},{4,20},{8,24},{12,28},{16,0},{20,4},{24,8},{28,12},{32,48},... | collective-permute-start | bytes 98312 | tf_op jit(solution)/shard_map/ppermute | solution.py:27
  62.6 18.6 %collective-permute-start.40 = (f32[64,128]{1,0:T(8,128)S(1)}, f32[64,128]{1,0:T(8,128)S(1)}, u32[]{:S(2)}, u32[]{:S(2)}) collective-permute-start(f32[64,128]{1,0:T(8,128)S(1)} %add.410), channel_id=1, source_target_pairs={{0,8},{4,12},{8,0},{12,4},{16,24},{20,28},{24,16},{28,20},{32,40},... | collective-permute-start | bytes 98312 | tf_op jit(solution)/shard_map/ppermute | solution.py:27
  66.6 22.5 %collective-permute-start.3 = (f32[80,128]{1,0:T(8,128)S(1)}, f32[80,128]{1,0:T(8,128)S(1)}, u32[]{:S(2)}, u32[]{:S(2)}) collective-permute-start(f32[80,128]{1,0:T(8,128)S(1)} %dynamic-slice_add_fusion.9), channel_id=1, source_target_pairs={{0,32},{4,36},{8,40},{12,44},{16,48},{20,52},{24,56},{28,60},{32,0... | collective-permute-start | bytes 122888 | tf_op jit(solution)/shard_map/ppermute | solution.py:27
  75.4 10.2 %collective-permute-start.29 = (f32[64,128]{1,0:T(8,128)S(1)}, f32[64,128]{1,0:T(8,128)S(1)}, u32[]{:S(2)}, u32[]{:S(2)}) collective-permute-start(f32[64,128]{1,0:T(8,128)S(1)} %add.397), channel_id=1, source_target_pairs={{0,32},{4,36},{8,40},{12,44},{16,48},{20,52},{24,56},{28,60},{32,0... | collective-permute-start | bytes 98312 | tf_op jit(solution)/shard_map/ppermute | solution.py:27
  77.4 14.1 %collective-permute-start.15 = (f32[80,128]{0,1:T(8,128)S(1)}, f32[80,128]{0,1:T(8,128)S(1)}, u32[]{:S(2)}, u32[]{:S(2)}) collective-permute-start(f32[80,128]{0,1:T(8,128)S(1)} %dynamic-slice_add_fusion.8), channel_id=1, source_target_pairs={{0,256},{4,260},{8,264},{12,268},{16,272},{20,276},{24,280},{28,28... | collective-permute-start | bytes 122888 | tf_op jit(solution)/shard_map/ppermute | solution.py:27
  81.2 12.2 %collective-permute-start.41 = (f32[64,128]{1,0:T(8,128)S(1)}, f32[64,128]{1,0:T(8,128)S(1)}, u32[]{:S(2)}, u32[]{:S(2)}) collective-permute-start(f32[64,128]{1,0:T(8,128)S(1)} %add.411), channel_id=1, source_target_pairs={{0,16},{4,20},{8,24},{12,28},{16,0},{20,4},{24,8},{28,12},{32,48},... | collective-permute-start | bytes 98312 | tf_op jit(solution)/shard_map/ppermute | solution.py:27
  85.6 15.7 %collective-permute-start.30 = (f32[64,128]{1,0:T(8,128)S(1)}, f32[64,128]{1,0:T(8,128)S(1)}, u32[]{:S(2)}, u32[]{:S(2)}) collective-permute-start(f32[64,128]{1,0:T(8,128)S(1)} %add.398), channel_id=1, source_target_pairs={{0,64},{4,68},{8,72},{12,76},{16,80},{20,84},{24,88},{28,92},{32,9... | collective-permute-start | bytes 98312 | tf_op jit(solution)/shard_map/ppermute | solution.py:27
  89.1 14.5 %collective-permute-start.4 = (f32[80,128]{1,0:T(8,128)S(1)}, f32[80,128]{1,0:T(8,128)S(1)}, u32[]{:S(2)}, u32[]{:S(2)}) collective-permute-start(f32[80,128]{1,0:T(8,128)S(1)} %add.361), channel_id=1, source_target_pairs={{0,64},{4,68},{8,72},{12,76},{16,80},{20,84},{24,88},{28,92},{32,9... | collective-permute-start | bytes 122888 | tf_op jit(solution)/shard_map/ppermute | solution.py:27
  91.5 16.6 %collective-permute-start.16 = (f32[80,128]{0,1:T(8,128)S(1)}, f32[80,128]{0,1:T(8,128)S(1)}, u32[]{:S(2)}, u32[]{:S(2)}) collective-permute-start(f32[80,128]{0,1:T(8,128)S(1)} %add.376), channel_id=1, source_target_pairs={{0,1},{1,0},{2,3},{3,2},{4,5},{5,4},{6,7},{7,6},{8,9},{9,8},{10,11... | collective-permute-start | bytes 122888 | tf_op jit(solution)/shard_map/ppermute | solution.py:27
  93.4 19.1 %collective-permute-start.42 = (f32[64,128]{1,0:T(8,128)S(1)}, f32[64,128]{1,0:T(8,128)S(1)}, u32[]{:S(2)}, u32[]{:S(2)}) collective-permute-start(f32[64,128]{1,0:T(8,128)S(1)} %add.412), channel_id=1, source_target_pairs={{0,32},{4,36},{8,40},{12,44},{16,48},{20,52},{24,56},{28,60},{32,0... | collective-permute-start | bytes 98312 | tf_op jit(solution)/shard_map/ppermute | solution.py:27
  101.3 14.8 %collective-permute-start.31 = (f32[64,128]{1,0:T(8,128)S(1)}, f32[64,128]{1,0:T(8,128)S(1)}, u32[]{:S(2)}, u32[]{:S(2)}) collective-permute-start(f32[64,128]{1,0:T(8,128)S(1)} %add.399), channel_id=1, source_target_pairs={{0,128},{4,132},{8,136},{12,140},{16,144},{20,148},{24,152},{28,15... | collective-permute-start | bytes 98312 | tf_op jit(solution)/shard_map/ppermute | solution.py:27
  103.6 21.6 %collective-permute-start.5 = (f32[80,128]{1,0:T(8,128)S(1)}, f32[80,128]{1,0:T(8,128)S(1)}, u32[]{:S(2)}, u32[]{:S(2)}) collective-permute-start(f32[80,128]{1,0:T(8,128)S(1)} %add.362), channel_id=1, source_target_pairs={{0,128},{4,132},{8,136},{12,140},{16,144},{20,148},{24,152},{28,15... | collective-permute-start | bytes 122888 | tf_op jit(solution)/shard_map/ppermute | solution.py:27
  108.1 20.3 %collective-permute-start.17 = (f32[80,128]{0,1:T(8,128)S(1)}, f32[80,128]{0,1:T(8,128)S(1)}, u32[]{:S(2)}, u32[]{:S(2)}) collective-permute-start(f32[80,128]{0,1:T(8,128)S(1)} %add.377), channel_id=1, source_target_pairs={{0,2},{1,3},{2,0},{3,1},{4,6},{5,7},{6,4},{7,5},{8,10},{9,11},{10,... | collective-permute-start | bytes 122888 | tf_op jit(solution)/shard_map/ppermute | solution.py:27
  112.6 8.6 %collective-permute-start.43 = (f32[64,128]{1,0:T(8,128)S(1)}, f32[64,128]{1,0:T(8,128)S(1)}, u32[]{:S(2)}, u32[]{:S(2)}) collective-permute-start(f32[64,128]{1,0:T(8,128)S(1)} %add.413), channel_id=1, source_target_pairs={{0,64},{4,68},{8,72},{12,76},{16,80},{20,84},{24,88},{28,92},{32,9... | collective-permute-start | bytes 98312 | tf_op jit(solution)/shard_map/ppermute | solution.py:27
  116.1 14.8 %collective-permute-start.32 = (f32[64,128]{1,0:T(8,128)S(1)}, f32[64,128]{1,0:T(8,128)S(1)}, u32[]{:S(2)}, u32[]{:S(2)}) collective-permute-start(f32[64,128]{1,0:T(8,128)S(1)} %add.400), channel_id=1, source_target_pairs={{0,256},{4,260},{8,264},{12,268},{16,272},{20,276},{24,280},{28,28... | collective-permute-start | bytes 98312 | tf_op jit(solution)/shard_map/ppermute | solution.py:27
  121.1 13.4 %collective-permute-start.44 = (f32[64,128]{1,0:T(8,128)S(1)}, f32[64,128]{1,0:T(8,128)S(1)}, u32[]{:S(2)}, u32[]{:S(2)}) collective-permute-start(f32[64,128]{1,0:T(8,128)S(1)} %add.414), channel_id=1, source_target_pairs={{0,128},{4,132},{8,136},{12,140},{16,144},{20,148},{24,152},{28,15... | collective-permute-start | bytes 98312 | tf_op jit(solution)/shard_map/ppermute | solution.py:27
  125.2 13.3 %collective-permute-start.6 = (f32[80,128]{1,0:T(8,128)S(1)}, f32[80,128]{1,0:T(8,128)S(1)}, u32[]{:S(2)}, u32[]{:S(2)}) collective-permute-start(f32[80,128]{1,0:T(8,128)S(1)} %add.363), channel_id=1, source_target_pairs={{0,256},{4,260},{8,264},{12,268},{16,272},{20,276},{24,280},{28,28... | collective-permute-start | bytes 122888 | tf_op jit(solution)/shard_map/ppermute | solution.py:27
  128.4 12.1 %collective-permute-start.18 = (f32[80,128]{0,1:T(8,128)S(1)}, f32[80,128]{0,1:T(8,128)S(1)}, u32[]{:S(2)}, u32[]{:S(2)}) collective-permute-start(f32[80,128]{0,1:T(8,128)S(1)} %add.378), channel_id=1, source_target_pairs={{0,8},{4,12},{8,0},{12,4},{16,24},{20,28},{24,16},{28,20},{32,40},... | collective-permute-start | bytes 122888 | tf_op jit(solution)/shard_map/ppermute | solution.py:27
  130.9 12.1 %collective-permute-start.33 = (f32[64,128]{1,0:T(8,128)S(1)}, f32[64,128]{1,0:T(8,128)S(1)}, u32[]{:S(2)}, u32[]{:S(2)}) collective-permute-start(f32[64,128]{1,0:T(8,128)S(1)} %add.401), channel_id=1, source_target_pairs={{0,2},{1,3},{2,0},{3,1},{4,6},{5,7},{6,4},{7,5},{8,10},{9,11},{10,... | collective-permute-start | bytes 98312 | tf_op jit(solution)/shard_map/ppermute | solution.py:27
  134.6 12.3 %collective-permute-start.45 = (f32[64,128]{1,0:T(8,128)S(1)}, f32[64,128]{1,0:T(8,128)S(1)}, u32[]{:S(2)}, u32[]{:S(2)}) collective-permute-start(f32[64,128]{1,0:T(8,128)S(1)} %add.415), channel_id=1, source_target_pairs={{0,1},{1,0},{2,3},{3,2},{4,5},{5,4},{6,7},{7,6},{8,9},{9,8},{10,11... | collective-permute-start | bytes 98312 | tf_op jit(solution)/shard_map/ppermute | solution.py:27
  138.5 15.0 %collective-permute-start.7 = (f32[80,128]{1,0:T(8,128)S(1)}, f32[80,128]{1,0:T(8,128)S(1)}, u32[]{:S(2)}, u32[]{:S(2)}) collective-permute-start(f32[80,128]{1,0:T(8,128)S(1)} %add.364), channel_id=1, source_target_pairs={{0,1},{1,0},{2,3},{3,2},{4,5},{5,4},{6,7},{7,6},{8,9},{9,8},{10,11... | collective-permute-start | bytes 122888 | tf_op jit(solution)/shard_map/ppermute | solution.py:27
  140.5 16.2 %collective-permute-start.19 = (f32[80,128]{0,1:T(8,128)S(1)}, f32[80,128]{0,1:T(8,128)S(1)}, u32[]{:S(2)}, u32[]{:S(2)}) collective-permute-start(f32[80,128]{0,1:T(8,128)S(1)} %add.379), channel_id=1, source_target_pairs={{0,16},{4,20},{8,24},{12,28},{16,0},{20,4},{24,8},{28,12},{32,48},... | collective-permute-start | bytes 122888 | tf_op jit(solution)/shard_map/ppermute | solution.py:27
  143.0 15.7 %collective-permute-start.34 = (f32[128,128]{1,0:T(8,128)S(1)}, f32[128,128]{1,0:T(8,128)S(1)}, u32[]{:S(2)}, u32[]{:S(2)}) collective-permute-start(f32[128,128]{1,0:T(8,128)S(1)} %maximum_select_fusion.10), channel_id=1, source_target_pairs={{0,1},{1,0},{2,3},{3,2},{4,5},{5,4},{6,7},{7,6},{8,9},{9,8},{10,11... | collective-permute-start | bytes 196616 | tf_op jit(solution)/shard_map/ppermute | solution.py:27
  146.9 18.3 %collective-permute-start.46 = (f32[128,128]{1,0:T(8,128)S(1)}, f32[128,128]{1,0:T(8,128)S(1)}, u32[]{:S(2)}, u32[]{:S(2)}) collective-permute-start(f32[128,128]{1,0:T(8,128)S(1)} %maximum_select_fusion.11), channel_id=1, source_target_pairs={{0,256},{4,260},{8,264},{12,268},{16,272},{20,276},{24,280},{28,28... | collective-permute-start | bytes 196616 | tf_op jit(solution)/shard_map/ppermute | solution.py:27
  153.6 7.4 %collective-permute-start.8 = (f32[80,128]{1,0:T(8,128)S(1)}, f32[80,128]{1,0:T(8,128)S(1)}, u32[]{:S(2)}, u32[]{:S(2)}) collective-permute-start(f32[80,128]{1,0:T(8,128)S(1)} %add.365), channel_id=1, source_target_pairs={{0,2},{1,3},{2,0},{3,1},{4,6},{5,7},{6,4},{7,5},{8,10},{9,11},{10,... | collective-permute-start | bytes 122888 | tf_op jit(solution)/shard_map/ppermute | solution.py:27
  156.8 10.8 %collective-permute-start.20 = (f32[80,128]{0,1:T(8,128)S(1)}, f32[80,128]{0,1:T(8,128)S(1)}, u32[]{:S(2)}, u32[]{:S(2)}) collective-permute-start(f32[80,128]{0,1:T(8,128)S(1)} %add.380), channel_id=1, source_target_pairs={{0,32},{4,36},{8,40},{12,44},{16,48},{20,52},{24,56},{28,60},{32,0... | collective-permute-start | bytes 122888 | tf_op jit(solution)/shard_map/ppermute | solution.py:27
  158.7 20.6 %collective-permute-start.35 = (f32[256,128]{1,0:T(8,128)S(1)}, f32[256,128]{1,0:T(8,128)S(1)}, u32[]{:S(2)}, u32[]{:S(2)}) collective-permute-start(f32[256,128]{1,0:T(8,128)S(1)} %maximum_select_fusion.7), channel_id=1, source_target_pairs={{0,4},{4,0},{8,12},{12,8},{16,20},{20,16},{24,28},{28,24},{32,36},... | collective-permute-start | bytes 393224 | tf_op jit(solution)/shard_map/ppermute | solution.py:27
  161.0 9.2 %collective-permute-start.9 = (f32[80,128]{1,0:T(8,128)S(1)}, f32[80,128]{1,0:T(8,128)S(1)}, u32[]{:S(2)}, u32[]{:S(2)}) collective-permute-start(f32[80,128]{1,0:T(8,128)S(1)} %add.366), channel_id=1, source_target_pairs={{0,16},{4,20},{8,24},{12,28},{16,0},{20,4},{24,8},{28,12},{32,48},... | collective-permute-start | bytes 122888 | tf_op jit(solution)/shard_map/ppermute | solution.py:27
  165.3 14.1 %collective-permute-start.47 = (f32[256,128]{1,0:T(8,128)S(1)}, f32[256,128]{1,0:T(8,128)S(1)}, u32[]{:S(2)}, u32[]{:S(2)}) collective-permute-start(f32[256,128]{1,0:T(8,128)S(1)} %maximum_select_fusion.8), channel_id=1, source_target_pairs={{0,4},{4,0},{8,12},{12,8},{16,20},{20,16},{24,28},{28,24},{32,36},... | collective-permute-start | bytes 393224 | tf_op jit(solution)/shard_map/ppermute | solution.py:27
  167.5 7.1 %collective-permute-start.21 = (f32[80,128]{0,1:T(8,128)S(1)}, f32[80,128]{0,1:T(8,128)S(1)}, u32[]{:S(2)}, u32[]{:S(2)}) collective-permute-start(f32[80,128]{0,1:T(8,128)S(1)} %add.381), channel_id=1, source_target_pairs={{0,128},{4,132},{8,136},{12,140},{16,144},{20,148},{24,152},{28,15... | collective-permute-start | bytes 122888 | tf_op jit(solution)/shard_map/ppermute | solution.py:27
  170.2 9.3 %collective-permute-start.10 = (f32[160,128]{1,0:T(8,128)S(1)}, f32[160,128]{1,0:T(8,128)S(1)}, u32[]{:S(2)}, u32[]{:S(2)}) collective-permute-start(f32[160,128]{1,0:T(8,128)S(1)} %maximum_select_fusion.9), channel_id=1, source_target_pairs={{0,8},{4,12},{8,0},{12,4},{16,24},{20,28},{24,16},{28,20},{32,40},... | collective-permute-start | bytes 245768 | tf_op jit(solution)/shard_map/ppermute | solution.py:27
  174.8 9.4 %collective-permute-start.22 = (f32[160,128]{0,1:T(8,128)S(1)}, f32[160,128]{0,1:T(8,128)S(1)}, u32[]{:S(2)}, u32[]{:S(2)}) collective-permute-start(f32[160,128]{0,1:T(8,128)S(1)} %maximum_select_fusion.6), channel_id=1, source_target_pairs={{0,64},{4,68},{8,72},{12,76},{16,80},{20,84},{24,88},{28,92},{32,9... | collective-permute-start | bytes 245768 | tf_op jit(solution)/shard_map/ppermute | solution.py:27
  179.5 7.7 %collective-permute-start.11 = (f32[320,128]{1,0:T(8,128)S(1)}, f32[320,128]{1,0:T(8,128)S(1)}, u32[]{:S(2)}, u32[]{:S(2)}) collective-permute-start(f32[320,128]{1,0:T(8,128)S(1)} %maximum_select_fusion.5), channel_id=1, source_target_pairs={{0,4},{4,0},{8,12},{12,8},{16,20},{20,16},{24,28},{28,24},{32,36},... | collective-permute-start | bytes 491528 | tf_op jit(solution)/shard_map/ppermute | solution.py:27
  352.9 9.4 %collective-permute-start.51 = (f32[2,256]{1,0:T(2,128)S(1)}, f32[2,256]{1,0:T(2,128)S(1)}, u32[]{:S(2)}, u32[]{:S(2)}) collective-permute-start(f32[2,256]{1,0:T(2,128)S(1)} %pad_maximum_fusion.6), channel_id=1, source_target_pairs={{0,32},{4,36},{8,40},{12,44},{16,48},{20,52},{24,56},{28,60},{32,0... | collective-permute-start | bytes 6152 | tf_op jit(solution)/shard_map/ppermute | solution.py:27
  374.2 9.4 %collective-permute-start.54 = (f32[2,256]{1,0:T(2,128)S(1)}, f32[2,256]{1,0:T(2,128)S(1)}, u32[]{:S(2)}, u32[]{:S(2)}) collective-permute-start(f32[2,256]{1,0:T(2,128)S(1)} %pad_maximum_fusion.9), channel_id=1, source_target_pairs={{0,256},{4,260},{8,264},{12,268},{16,272},{20,276},{24,280},{28,28... | collective-permute-start | bytes 6152 | tf_op jit(solution)/shard_map/ppermute | solution.py:27
  (17 other events, 106.0 us)

commit v5 on v3

--- a/solution.py
+++ b/solution.py
@@ -74,9 +74,9 @@
         for j in range(i + 1)
     ]
     gram_flat = jnp.concatenate(lower_blocks, axis=0).reshape(-1, 128)
-    gram_sum = tree_sum(gram_flat, bits, 3).reshape(len(lower_blocks), block, block)
+    gram_sum = tree_sum(gram_flat, bits, 1).reshape(len(lower_blocks), block, block)
     cross_bits = bits[:1] + bits[4:7] + bits[1:4] + bits[7:]
-    cross = tree_sum(cross_part.reshape(-1, 128), cross_bits, 3).reshape(width, attrs)
+    cross = tree_sum(cross_part.reshape(-1, 128), cross_bits, 1).reshape(width, attrs)
     block_of = {}
     for n, (i, j) in enumerate((i, j) for i in range(nb) for j in range(i + 1)):
         block_of[(i, j)] = gram_sum[n]

time: 340 us -> 370 us (1.088)
  the two profiles are of different devices: /device:TPU:12 before, /device:TPU:6 now
where the time goes in v5:
time: 370 us; the launch traced here: 364 us
  other arithmetic  126 us (34%)
  starting transfers between devices  117 us (32%)
  waiting for transfers between devices  83.3 us (23%)
  local copies, waits for them, and re-layouts  20.9 us (6%)
  matrix products  12.1 us (3%)
  between operations  5.12 us (1%)
    ppermute x29, starting transfers between devices, partner(): return lax.ppermute(x, name, [(i, i ^ mask) for i in range(size)])  117 us
    ppermute x29, waiting for transfers between devices, partner(): return lax.ppermute(x, name, [(i, i ^ mask) for i in range(size)])  83.3 us
    another operation x14, other arithmetic, on_device(): factor = lax.linalg.cholesky(system, symmetrize_input=False)  83.2 us
    another operation x3, other arithmetic, on_device(): jax.scipy.linalg.cho_solve((factor, True), cross).astype(jnp.bfloat16)  40.3 us
    another operation x12, local copies, waits for them, and re-layouts  10.2 us
  transfers between devices with their start and end apart: 29, of which 21 were waited for; matrix products, arithmetic and copies ran while one was open for 2% of the time, Pallas kernels for 0%

profile of v5, /device:TPU:6, one launch (start us, length us, event | category | flops | bytes accessed | tf_op | source)
XLA Modules:
  0.0 364.0 jit_solution(3670655907753358799)
XLA Ops:
  1.2 3.2 fusion.1
  10.6 2.4 collective-permute-start.10
  13.1 4.3 %collective-permute-start.1 = (f32[640,128]{0,1:T(8,128)S(1)}, f32[640,128]{0,1:T(8,128)S(1)}, u32[]{:S(2)}, u32[]{:S(2)}) collective-permute-start(f32[640,128]{0,1:T(8,128)S(1)} %dynamic-slice_add_fusion), channel_id=1, source_target_pairs={{0,8},{4,12},{8,0},{12,4},{16,24},{20,28},{24,16},{28,20},{32,40},... | collective-permute-start | bytes 983048 | tf_op jit(solution)/shard_map/ppermute | solution.py:27
  18.4 3.5 collective-permute-start.11
  21.9 3.4 collective-permute-done.1
  25.3 6.1 %collective-permute-start.2 = (f32[640,128]{0,1:T(8,128)S(1)}, f32[640,128]{0,1:T(8,128)S(1)}, u32[]{:S(2)}, u32[]{:S(2)}) collective-permute-start(f32[640,128]{0,1:T(8,128)S(1)} %add.206), channel_id=1, source_target_pairs={{0,16},{4,20},{8,24},{12,28},{16,0},{20,4},{24,8},{28,12},{32,48},... | collective-permute-start | bytes 983048 | tf_op jit(solution)/shard_map/ppermute | solution.py:27
  31.4 4.5 %collective-permute-start.12 = (f32[512,128]{1,0:T(8,128)S(1)}, f32[512,128]{1,0:T(8,128)S(1)}, u32[]{:S(2)}, u32[]{:S(2)}) collective-permute-start(f32[512,128]{1,0:T(8,128)S(1)} %add.220), channel_id=1, source_target_pairs={{0,128},{4,132},{8,136},{12,140},{16,144},{20,148},{24,152},{28,15... | collective-permute-start | bytes 786440 | tf_op jit(solution)/shard_map/ppermute | solution.py:27
  35.9 9.8 %collective-permute-done.2 = f32[640,128]{0,1:T(8,128)S(1)} collective-permute-done((f32[640,128]{0,1:T(8,128)S(1)}, f32[640,128]{0,1:T(8,128)S(1)}, u32[]{:S(2)}, u32[]{:S(2)}) %collective-permute-start.2) | collective-permute-done | bytes 327712 | tf_op jit(solution)/shard_map/ppermute | solution.py:27
  45.8 8.4 %collective-permute-start.3 = (f32[640,128]{0,1:T(8,128)S(1)}, f32[640,128]{0,1:T(8,128)S(1)}, u32[]{:S(2)}, u32[]{:S(2)}) collective-permute-start(f32[640,128]{0,1:T(8,128)S(1)} %add.207), channel_id=1, source_target_pairs={{0,32},{4,36},{8,40},{12,44},{16,48},{20,52},{24,56},{28,60},{32,0... | collective-permute-start | bytes 983048 | tf_op jit(solution)/shard_map/ppermute | solution.py:27
  54.2 7.7 %collective-permute-start.13 = (f32[512,128]{1,0:T(8,128)S(1)}, f32[512,128]{1,0:T(8,128)S(1)}, u32[]{:S(2)}, u32[]{:S(2)}) collective-permute-start(f32[512,128]{1,0:T(8,128)S(1)} %add.221), channel_id=1, source_target_pairs={{0,256},{4,260},{8,264},{12,268},{16,272},{20,276},{24,280},{28,28... | collective-permute-start | bytes 786440 | tf_op jit(solution)/shard_map/ppermute | solution.py:27
  62.0 6.2 %collective-permute-done.3 = f32[640,128]{0,1:T(8,128)S(1)} collective-permute-done((f32[640,128]{0,1:T(8,128)S(1)}, f32[640,128]{0,1:T(8,128)S(1)}, u32[]{:S(2)}, u32[]{:S(2)}) %collective-permute-start.3) | collective-permute-done | bytes 327712 | tf_op jit(solution)/shard_map/ppermute | solution.py:27
  68.3 3.5 collective-permute-start.4
  71.8 1.9 collective-permute-start.14
  73.7 6.3 %collective-permute-done.14 = f32[512,128]{1,0:T(8,128)S(1)} collective-permute-done((f32[512,128]{1,0:T(8,128)S(1)}, f32[512,128]{1,0:T(8,128)S(1)}, u32[]{:S(2)}, u32[]{:S(2)}) %collective-permute-start.14) | collective-permute-done | bytes 262176 | tf_op jit(solution)/shard_map/ppermute | solution.py:27
  80.3 7.1 %collective-permute-start.5 = (f32[640,128]{0,1:T(8,128)S(1)}, f32[640,128]{0,1:T(8,128)S(1)}, u32[]{:S(2)}, u32[]{:S(2)}) collective-permute-start(f32[640,128]{0,1:T(8,128)S(1)} %add.209), channel_id=1, source_target_pairs={{0,128},{4,132},{8,136},{12,140},{16,144},{20,148},{24,152},{28,15... | collective-permute-start | bytes 983048 | tf_op jit(solution)/shard_map/ppermute | solution.py:27
  87.3 5.0 %collective-permute-start.15 = (f32[512,128]{1,0:T(8,128)S(1)}, f32[512,128]{1,0:T(8,128)S(1)}, u32[]{:S(2)}, u32[]{:S(2)}) collective-permute-start(f32[512,128]{1,0:T(8,128)S(1)} %add.223), channel_id=1, source_target_pairs={{0,16},{4,20},{8,24},{12,28},{16,0},{20,4},{24,8},{28,12},{32,48},... | collective-permute-start | bytes 786440 | tf_op jit(solution)/shard_map/ppermute | solution.py:27
  92.3 11.1 %collective-permute-done.15 = f32[512,128]{1,0:T(8,128)S(1)} collective-permute-done((f32[512,128]{1,0:T(8,128)S(1)}, f32[512,128]{1,0:T(8,128)S(1)}, u32[]{:S(2)}, u32[]{:S(2)}) %collective-permute-start.15) | collective-permute-done | bytes 262176 | tf_op jit(solution)/shard_map/ppermute | solution.py:27
  105.5 4.5 %collective-permute-start.6 = (f32[640,128]{0,1:T(8,128)S(1)}, f32[640,128]{0,1:T(8,128)S(1)}, u32[]{:S(2)}, u32[]{:S(2)}) collective-permute-start(f32[640,128]{0,1:T(8,128)S(1)} %add.210), channel_id=1, source_target_pairs={{0,256},{4,260},{8,264},{12,268},{16,272},{20,276},{24,280},{28,28... | collective-permute-start | bytes 983048 | tf_op jit(solution)/shard_map/ppermute | solution.py:27
  109.9 10.0 %collective-permute-done.16 = f32[512,128]{1,0:T(8,128)S(1)} collective-permute-done((f32[512,128]{1,0:T(8,128)S(1)}, f32[512,128]{1,0:T(8,128)S(1)}, u32[]{:S(2)}, u32[]{:S(2)}) %collective-permute-start.16) | collective-permute-done | bytes 262176 | tf_op jit(solution)/shard_map/ppermute | solution.py:27
  120.0 2.7 collective-permute-start.17
  122.7 2.6 collective-permute-done.6
  125.3 2.8 collective-permute-start.7
  128.4 3.3 collective-permute-start.18
  131.7 6.2 %collective-permute-done.7 = f32[640,128]{0,1:T(8,128)S(1)} collective-permute-done((f32[640,128]{0,1:T(8,128)S(1)}, f32[640,128]{0,1:T(8,128)S(1)}, u32[]{:S(2)}, u32[]{:S(2)}) %collective-permute-start.7) | collective-permute-done | bytes 327712 | tf_op jit(solution)/shard_map/ppermute | solution.py:27
  137.9 3.3 collective-permute-start.8
  145.4 3.0 collective-permute-done.8
  148.4 2.4 collective-permute-start.9
  154.7 11.7 %cholesky.103 = f32[128,128]{1,0:T(8,128)S(1)} custom-call(f32[128,128]{1,0:T(8,128)S(1)} %cholesky.263), custom_call_target="Cholesky" | custom-call | tf_op jit(solution)/shard_map/cholesky | solution.py:91
  166.6 9.8 %custom-call.27 = f32[1,128,128]{1,2,0:T(8,128)S(1)} custom-call(f32[1,128,128]{2,1,0:T(8,128)S(1)} %get-tuple-element.52), custom_call_target="InvertDiagBlocksLowerTriangular" | custom-call | tf_op jit(solution)/shard_map/cholesky | solution.py:91
  177.7 11.7 %cholesky.215 = f32[128,128]{1,0:T(8,128)S(1)} custom-call(f32[128,128]{1,0:T(8,128)S(1)} %cholesky.267), custom_call_target="Cholesky" | custom-call | tf_op jit(solution)/shard_map/cholesky | solution.py:91
  189.5 10.0 %custom-call.28 = f32[1,128,128]{1,2,0:T(8,128)S(1)} custom-call(f32[1,128,128]{2,1,0:T(8,128)S(1)} %get-tuple-element.49), custom_call_target="InvertDiagBlocksLowerTriangular" | custom-call | tf_op jit(solution)/shard_map/cholesky | solution.py:91
  201.6 13.2 %cholesky.236 = f32[128,128]{1,0:T(8,128)} custom-call(f32[128,128]{1,0:T(8,128)} %cholesky.272), custom_call_target="Cholesky" | custom-call | tf_op jit(solution)/shard_map/cholesky | solution.py:91
  217.0 11.3 %custom-call.29 = f32[1,128,128]{1,2,0:T(8,128)} custom-call(f32[1,128,128]{2,1,0:T(8,128)} %get-tuple-element.46), custom_call_target="InvertDiagBlocksLowerTriangular" | custom-call | tf_op jit(solution)/shard_map/cholesky | solution.py:91
  229.7 11.9 %cholesky.253 = f32[128,128]{1,0:T(8,128)S(1)} custom-call(f32[128,128]{1,0:T(8,128)S(1)} %convolution_subtract_fusion.5), custom_call_target="Cholesky" | custom-call | tf_op jit(solution)/shard_map/cholesky | solution.py:91
  245.7 10.2 %while.1 = (s32[]{:T(128)}, f32[512,512]{1,0:T(8,128)S(1)}, s32[4,2]{0,1:T(2,128)S(1)}, f32[4,128,128]{2,1,0:T(8,128)}, s32[]{:T(128)}) while((s32[]{:T(128)}, f32[512,512]{1,0:T(8,128)S(1)}, s32[4,2]{0,1:T(2,128)S(1)}, f32[4,128,128]{2,1,0:T(8,128)}, s32[]{:T(128)}) %tuple.57), condition=%wide.while_cond, body=%wide.while_body.sunk | while | flops 2 | bytes 132705 | solution.py:92
  255.9 40.1 %custom-call.30 = f32[4,128,128]{1,2,0:T(8,128)S(1)} custom-call(f32[4,128,128]{2,1,0:T(8,128)} %get-tuple-element.12), custom_call_target="InvertDiagBlocksLowerTriangular" | custom-call | tf_op jit(solution)/shard_map/jit(_cho_solve)/triangular_solve | solution.py:92
  302.6 2.4 collective-permute-start.20
  305.8 3.5 collective-permute-start.21
  309.3 2.0 collective-permute-done.21
  311.3 4.9 %collective-permute-start.22 = (f32[2,256]{1,0:T(2,128)S(1)}, f32[2,256]{1,0:T(2,128)S(1)}, u32[]{:S(2)}, u32[]{:S(2)}) collective-permute-start(f32[2,256]{1,0:T(2,128)S(1)} %pad_maximum_fusion.3), channel_id=1, source_target_pairs={{0,16},{4,20},{8,24},{12,28},{16,0},{20,4},{24,8},{28,12},{32,48},... | collective-permute-start | bytes 6152 | tf_op jit(solution)/shard_map/ppermute | solution.py:27
  317.8 7.7 %collective-permute-start.23 = (f32[2,256]{1,0:T(2,128)S(1)}, f32[2,256]{1,0:T(2,128)S(1)}, u32[]{:S(2)}, u32[]{:S(2)}) collective-permute-start(f32[2,256]{1,0:T(2,128)S(1)} %pad_maximum_fusion.4), channel_id=1, source_target_pairs={{0,32},{4,36},{8,40},{12,44},{16,48},{20,52},{24,56},{28,60},{32,0... | collective-permute-start | bytes 6152 | tf_op jit(solution)/shard_map/ppermute | solution.py:27
  327.2 3.9 %collective-permute-start.24 = (f32[2,256]{1,0:T(2,128)S(1)}, f32[2,256]{1,0:T(2,128)S(1)}, u32[]{:S(2)}, u32[]{:S(2)}) collective-permute-start(f32[2,256]{1,0:T(2,128)S(1)} %pad_maximum_fusion.5), channel_id=1, source_target_pairs={{0,64},{4,68},{8,72},{12,76},{16,80},{20,84},{24,88},{28,92},{32,9... | collective-permute-start | bytes 6152 | tf_op jit(solution)/shard_map/ppermute | solution.py:27
  332.7 6.9 %collective-permute-start.25 = (f32[2,256]{1,0:T(2,128)S(1)}, f32[2,256]{1,0:T(2,128)S(1)}, u32[]{:S(2)}, u32[]{:S(2)}) collective-permute-start(f32[2,256]{1,0:T(2,128)S(1)} %pad_maximum_fusion.6), channel_id=1, source_target_pairs={{0,128},{4,132},{8,136},{12,140},{16,144},{20,148},{24,152},{28,15... | collective-permute-start | bytes 6152 | tf_op jit(solution)/shard_map/ppermute | solution.py:27
  341.2 3.8 %collective-permute-start.26 = (f32[2,256]{1,0:T(2,128)S(1)}, f32[2,256]{1,0:T(2,128)S(1)}, u32[]{:S(2)}, u32[]{:S(2)}) collective-permute-start(f32[2,256]{1,0:T(2,128)S(1)} %pad_maximum_fusion.7), channel_id=1, source_target_pairs={{0,256},{4,260},{8,264},{12,268},{16,272},{20,276},{24,280},{28,28... | collective-permute-start | bytes 6152 | tf_op jit(solution)/shard_map/ppermute | solution.py:27
  345.0 5.6 %collective-permute-done.26 = f32[2,256]{1,0:T(2,128)S(1)} collective-permute-done((f32[2,256]{1,0:T(2,128)S(1)}, f32[2,256]{1,0:T(2,128)S(1)}, u32[]{:S(2)}, u32[]{:S(2)}) %collective-permute-start.26) | collective-permute-done | bytes 2080 | tf_op jit(solution)/shard_map/ppermute | solution.py:27
  352.5 3.6 collective-permute-done.27
  356.1 2.4 collective-permute-start.28
  358.5 4.6 %collective-permute-done.28 = f32[2,256]{1,0:T(2,128)S(1)} collective-permute-done((f32[2,256]{1,0:T(2,128)S(1)}, f32[2,256]{1,0:T(2,128)S(1)}, u32[]{:S(2)}, u32[]{:S(2)}) %collective-permute-start.28) | collective-permute-done | bytes 2080 | tf_op jit(solution)/shard_map/ppermute | solution.py:27
  (156 shorter events, 52.8 us)
Async XLA Ops:
  0.0 1.2 copy-start
  5.8 7.2 %collective-permute-start = (f32[640,128]{0,1:T(8,128)}, f32[640,128]{0,1:T(8,128)S(1)}, u32[]{:S(2)}, u32[]{:S(2)}) collective-permute-start(f32[640,128]{0,1:T(8,128)} %constant_dynamic-slice_fusion.2), channel_id=1, source_target_pairs={{0,4},{4,0},{8,12},{12,8},{16,20},{20,16},{24,28},{28,24},{32,36},... | collective-permute-start | bytes 983048 | tf_op jit(solution)/shard_map/ppermute | solution.py:27
  7.7 0.7 copy-start.7
  8.4 1.2 copy-start.6
  10.6 6.8 %collective-permute-start.10 = (f32[512,128]{1,0:T(8,128)}, f32[512,128]{1,0:T(8,128)}, u32[]{:S(2)}, u32[]{:S(2)}) collective-permute-start(f32[512,128]{1,0:T(8,128)} %constant_dynamic-slice_fusion.1), channel_id=1, source_target_pairs={{0,4},{4,0},{8,12},{12,8},{16,20},{20,16},{24,28},{28,24},{32,36},... | collective-permute-start | bytes 786440 | tf_op jit(solution)/shard_map/ppermute | solution.py:27
  13.1 12.2 %collective-permute-start.1 = (f32[640,128]{0,1:T(8,128)S(1)}, f32[640,128]{0,1:T(8,128)S(1)}, u32[]{:S(2)}, u32[]{:S(2)}) collective-permute-start(f32[640,128]{0,1:T(8,128)S(1)} %dynamic-slice_add_fusion), channel_id=1, source_target_pairs={{0,8},{4,12},{8,0},{12,4},{16,24},{20,28},{24,16},{28,20},{32,40},... | collective-permute-start | bytes 983048 | tf_op jit(solution)/shard_map/ppermute | solution.py:27
  18.4 13.0 %collective-permute-start.11 = (f32[512,128]{1,0:T(8,128)S(1)}, f32[512,128]{1,0:T(8,128)S(1)}, u32[]{:S(2)}, u32[]{:S(2)}) collective-permute-start(f32[512,128]{1,0:T(8,128)S(1)} %dynamic-slice_add_fusion.1), channel_id=1, source_target_pairs={{0,64},{4,68},{8,72},{12,76},{16,80},{20,84},{24,88},{28,92},{32,9... | collective-permute-start | bytes 786440 | tf_op jit(solution)/shard_map/ppermute | solution.py:27
  25.3 20.5 %collective-permute-start.2 = (f32[640,128]{0,1:T(8,128)S(1)}, f32[640,128]{0,1:T(8,128)S(1)}, u32[]{:S(2)}, u32[]{:S(2)}) collective-permute-start(f32[640,128]{0,1:T(8,128)S(1)} %add.206), channel_id=1, source_target_pairs={{0,16},{4,20},{8,24},{12,28},{16,0},{20,4},{24,8},{28,12},{32,48},... | collective-permute-start | bytes 983048 | tf_op jit(solution)/shard_map/ppermute | solution.py:27
  31.4 22.8 %collective-permute-start.12 = (f32[512,128]{1,0:T(8,128)S(1)}, f32[512,128]{1,0:T(8,128)S(1)}, u32[]{:S(2)}, u32[]{:S(2)}) collective-permute-start(f32[512,128]{1,0:T(8,128)S(1)} %add.220), channel_id=1, source_target_pairs={{0,128},{4,132},{8,136},{12,140},{16,144},{20,148},{24,152},{28,15... | collective-permute-start | bytes 786440 | tf_op jit(solution)/shard_map/ppermute | solution.py:27
  45.8 22.4 %collective-permute-start.3 = (f32[640,128]{0,1:T(8,128)S(1)}, f32[640,128]{0,1:T(8,128)S(1)}, u32[]{:S(2)}, u32[]{:S(2)}) collective-permute-start(f32[640,128]{0,1:T(8,128)S(1)} %add.207), channel_id=1, source_target_pairs={{0,32},{4,36},{8,40},{12,44},{16,48},{20,52},{24,56},{28,60},{32,0... | collective-permute-start | bytes 983048 | tf_op jit(solution)/shard_map/ppermute | solution.py:27
  54.2 17.5 %collective-permute-start.13 = (f32[512,128]{1,0:T(8,128)S(1)}, f32[512,128]{1,0:T(8,128)S(1)}, u32[]{:S(2)}, u32[]{:S(2)}) collective-permute-start(f32[512,128]{1,0:T(8,128)S(1)} %add.221), channel_id=1, source_target_pairs={{0,256},{4,260},{8,264},{12,268},{16,272},{20,276},{24,280},{28,28... | collective-permute-start | bytes 786440 | tf_op jit(solution)/shard_map/ppermute | solution.py:27
  68.3 12.0 %collective-permute-start.4 = (f32[640,128]{0,1:T(8,128)S(1)}, f32[640,128]{0,1:T(8,128)S(1)}, u32[]{:S(2)}, u32[]{:S(2)}) collective-permute-start(f32[640,128]{0,1:T(8,128)S(1)} %add.208), channel_id=1, source_target_pairs={{0,64},{4,68},{8,72},{12,76},{16,80},{20,84},{24,88},{28,92},{32,9... | collective-permute-start | bytes 983048 | tf_op jit(solution)/shard_map/ppermute | solution.py:27
  71.8 8.3 %collective-permute-start.14 = (f32[512,128]{1,0:T(8,128)S(1)}, f32[512,128]{1,0:T(8,128)S(1)}, u32[]{:S(2)}, u32[]{:S(2)}) collective-permute-start(f32[512,128]{1,0:T(8,128)S(1)} %add.222), channel_id=1, source_target_pairs={{0,8},{4,12},{8,0},{12,4},{16,24},{20,28},{24,16},{28,20},{32,40},... | collective-permute-start | bytes 786440 | tf_op jit(solution)/shard_map/ppermute | solution.py:27
  80.3 25.2 %collective-permute-start.5 = (f32[640,128]{0,1:T(8,128)S(1)}, f32[640,128]{0,1:T(8,128)S(1)}, u32[]{:S(2)}, u32[]{:S(2)}) collective-permute-start(f32[640,128]{0,1:T(8,128)S(1)} %add.209), channel_id=1, source_target_pairs={{0,128},{4,132},{8,136},{12,140},{16,144},{20,148},{24,152},{28,15... | collective-permute-start | bytes 983048 | tf_op jit(solution)/shard_map/ppermute | solution.py:27
  87.3 16.1 %collective-permute-start.15 = (f32[512,128]{1,0:T(8,128)S(1)}, f32[512,128]{1,0:T(8,128)S(1)}, u32[]{:S(2)}, u32[]{:S(2)}) collective-permute-start(f32[512,128]{1,0:T(8,128)S(1)} %add.223), channel_id=1, source_target_pairs={{0,16},{4,20},{8,24},{12,28},{16,0},{20,4},{24,8},{28,12},{32,48},... | collective-permute-start | bytes 786440 | tf_op jit(solution)/shard_map/ppermute | solution.py:27
  103.5 16.5 %collective-permute-start.16 = (f32[512,128]{1,0:T(8,128)S(1)}, f32[512,128]{1,0:T(8,128)S(1)}, u32[]{:S(2)}, u32[]{:S(2)}) collective-permute-start(f32[512,128]{1,0:T(8,128)S(1)} %add.224), channel_id=1, source_target_pairs={{0,32},{4,36},{8,40},{12,44},{16,48},{20,52},{24,56},{28,60},{32,0... | collective-permute-start | bytes 786440 | tf_op jit(solution)/shard_map/ppermute | solution.py:27
  105.5 19.8 %collective-permute-start.6 = (f32[640,128]{0,1:T(8,128)S(1)}, f32[640,128]{0,1:T(8,128)S(1)}, u32[]{:S(2)}, u32[]{:S(2)}) collective-permute-start(f32[640,128]{0,1:T(8,128)S(1)} %add.210), channel_id=1, source_target_pairs={{0,256},{4,260},{8,264},{12,268},{16,272},{20,276},{24,280},{28,28... | collective-permute-start | bytes 983048 | tf_op jit(solution)/shard_map/ppermute | solution.py:27
  120.0 8.4 %collective-permute-start.17 = (f32[512,128]{1,0:T(8,128)S(1)}, f32[512,128]{1,0:T(8,128)S(1)}, u32[]{:S(2)}, u32[]{:S(2)}) collective-permute-start(f32[512,128]{1,0:T(8,128)S(1)} %add.225), channel_id=1, source_target_pairs={{0,1},{1,0},{2,3},{3,2},{4,5},{5,4},{6,7},{7,6},{8,9},{9,8},{10,11... | collective-permute-start | bytes 786440 | tf_op jit(solution)/shard_map/ppermute | solution.py:27
  125.3 12.5 %collective-permute-start.7 = (f32[640,128]{0,1:T(8,128)S(1)}, f32[640,128]{0,1:T(8,128)S(1)}, u32[]{:S(2)}, u32[]{:S(2)}) collective-permute-start(f32[640,128]{0,1:T(8,128)S(1)} %add.211), channel_id=1, source_target_pairs={{0,1},{1,0},{2,3},{3,2},{4,5},{5,4},{6,7},{7,6},{8,9},{9,8},{10,11... | collective-permute-start | bytes 983048 | tf_op jit(solution)/shard_map/ppermute | solution.py:27
  128.4 14.3 %collective-permute-start.18 = (f32[512,128]{1,0:T(8,128)S(1)}, f32[512,128]{1,0:T(8,128)S(1)}, u32[]{:S(2)}, u32[]{:S(2)}) collective-permute-start(f32[512,128]{1,0:T(8,128)S(1)} %add.226), channel_id=1, source_target_pairs={{0,2},{1,3},{2,0},{3,1},{4,6},{5,7},{6,4},{7,5},{8,10},{9,11},{10,... | collective-permute-start | bytes 786440 | tf_op jit(solution)/shard_map/ppermute | solution.py:27
  137.9 10.5 %collective-permute-start.8 = (f32[640,128]{0,1:T(8,128)S(1)}, f32[640,128]{0,1:T(8,128)S(1)}, u32[]{:S(2)}, u32[]{:S(2)}) collective-permute-start(f32[640,128]{0,1:T(8,128)S(1)} %add.212), channel_id=1, source_target_pairs={{0,2},{1,3},{2,0},{3,1},{4,6},{5,7},{6,4},{7,5},{8,10},{9,11},{10,... | collective-permute-start | bytes 983048 | tf_op jit(solution)/shard_map/ppermute | solution.py:27
  142.8 8.1 %collective-permute-start.19 = (f32[512,128]{1,0:T(8,128)S(1)}, f32[512,128]{1,0:T(8,128)S(1)}, u32[]{:S(2)}, u32[]{:S(2)}) collective-permute-start(f32[512,128]{1,0:T(8,128)S(1)} %add.227), channel_id=1, source_target_pairs={{0,4},{4,0},{8,12},{12,8},{16,20},{20,16},{24,28},{28,24},{32,36},... | collective-permute-start | bytes 786440 | tf_op jit(solution)/shard_map/ppermute | solution.py:27
  148.4 5.3 %collective-permute-start.9 = (f32[640,128]{0,1:T(8,128)S(1)}, f32[640,128]{0,1:T(8,128)S(1)}, u32[]{:S(2)}, u32[]{:S(2)}) collective-permute-start(f32[640,128]{0,1:T(8,128)S(1)} %add.213), channel_id=1, source_target_pairs={{0,4},{4,0},{8,12},{12,8},{16,20},{20,16},{24,28},{28,24},{32,36},... | collective-permute-start | bytes 983048 | tf_op jit(solution)/shard_map/ppermute | solution.py:27
  177.1 0.7 copy-start.1
  245.7 50.3 %copy-start.5 = (f32[128,256]{1,0:T(8,128)S(1)}, f32[128,256]{1,0:T(8,128)}, u32[]{:S(2)}) copy-start(f32[128,256]{1,0:T(8,128)} %triangular_solve.136) | copy-start | bytes 393220
  296.4 0.9 copy-start.4
  297.6 0.9 copy-start.3
  298.8 0.9 copy-start.2
  302.6 3.2 collective-permute-start.20
  305.8 5.5 %collective-permute-start.21 = (f32[2,256]{1,0:T(2,128)S(1)}, f32[2,256]{1,0:T(2,128)S(1)}, u32[]{:S(2)}, u32[]{:S(2)}) collective-permute-start(f32[2,256]{1,0:T(2,128)S(1)} %pad_maximum_fusion.2), channel_id=1, source_target_pairs={{0,8},{4,12},{8,0},{12,4},{16,24},{20,28},{24,16},{28,20},{32,40},... | collective-permute-start | bytes 6152 | tf_op jit(solution)/shard_map/ppermute | solution.py:27
  311.3 6.4 %collective-permute-start.22 = (f32[2,256]{1,0:T(2,128)S(1)}, f32[2,256]{1,0:T(2,128)S(1)}, u32[]{:S(2)}, u32[]{:S(2)}) collective-permute-start(f32[2,256]{1,0:T(2,128)S(1)} %pad_maximum_fusion.3), channel_id=1, source_target_pairs={{0,16},{4,20},{8,24},{12,28},{16,0},{20,4},{24,8},{28,12},{32,48},... | collective-permute-start | bytes 6152 | tf_op jit(solution)/shard_map/ppermute | solution.py:27
  317.8 9.4 %collective-permute-start.23 = (f32[2,256]{1,0:T(2,128)S(1)}, f32[2,256]{1,0:T(2,128)S(1)}, u32[]{:S(2)}, u32[]{:S(2)}) collective-permute-start(f32[2,256]{1,0:T(2,128)S(1)} %pad_maximum_fusion.4), channel_id=1, source_target_pairs={{0,32},{4,36},{8,40},{12,44},{16,48},{20,52},{24,56},{28,60},{32,0... | collective-permute-start | bytes 6152 | tf_op jit(solution)/shard_map/ppermute | solution.py:27
  327.2 5.5 %collective-permute-start.24 = (f32[2,256]{1,0:T(2,128)S(1)}, f32[2,256]{1,0:T(2,128)S(1)}, u32[]{:S(2)}, u32[]{:S(2)}) collective-permute-start(f32[2,256]{1,0:T(2,128)S(1)} %pad_maximum_fusion.5), channel_id=1, source_target_pairs={{0,64},{4,68},{8,72},{12,76},{16,80},{20,84},{24,88},{28,92},{32,9... | collective-permute-start | bytes 6152 | tf_op jit(solution)/shard_map/ppermute | solution.py:27
  332.7 8.5 %collective-permute-start.25 = (f32[2,256]{1,0:T(2,128)S(1)}, f32[2,256]{1,0:T(2,128)S(1)}, u32[]{:S(2)}, u32[]{:S(2)}) collective-permute-start(f32[2,256]{1,0:T(2,128)S(1)} %pad_maximum_fusion.6), channel_id=1, source_target_pairs={{0,128},{4,132},{8,136},{12,140},{16,144},{20,148},{24,152},{28,15... | collective-permute-start | bytes 6152 | tf_op jit(solution)/shard_map/ppermute | solution.py:27
  341.2 9.4 %collective-permute-start.26 = (f32[2,256]{1,0:T(2,128)S(1)}, f32[2,256]{1,0:T(2,128)S(1)}, u32[]{:S(2)}, u32[]{:S(2)}) collective-permute-start(f32[2,256]{1,0:T(2,128)S(1)} %pad_maximum_fusion.7), channel_id=1, source_target_pairs={{0,256},{4,260},{8,264},{12,268},{16,272},{20,276},{24,280},{28,28... | collective-permute-start | bytes 6152 | tf_op jit(solution)/shard_map/ppermute | solution.py:27
  350.6 5.5 %collective-permute-start.27 = (f32[2,256]{1,0:T(2,128)S(1)}, f32[2,256]{1,0:T(2,128)S(1)}, u32[]{:S(2)}, u32[]{:S(2)}) collective-permute-start(f32[2,256]{1,0:T(2,128)S(1)} %pad_maximum_fusion.8), channel_id=1, source_target_pairs={{0,1},{1,0},{2,3},{3,2},{4,5},{5,4},{6,7},{7,6},{8,9},{9,8},{10,11... | collective-permute-start | bytes 6152 | tf_op jit(solution)/shard_map/ppermute | solution.py:27
  356.1 7.0 %collective-permute-start.28 = (f32[2,256]{1,0:T(2,128)S(1)}, f32[2,256]{1,0:T(2,128)S(1)}, u32[]{:S(2)}, u32[]{:S(2)}) collective-permute-start(f32[2,256]{1,0:T(2,128)S(1)} %pad_maximum_fusion.9), channel_id=1, source_target_pairs={{0,2},{1,3},{2,0},{3,1},{4,6},{5,7},{6,4},{7,5},{8,10},{9,11},{10,... | collective-permute-start | bytes 6152 | tf_op jit(solution)/shard_map/ppermute | solution.py:27

commit v6 on v3

--- a/solution.py
+++ b/solution.py
@@ -52,6 +52,50 @@
     return stats
 
 
+HIGHEST = lax.Precision.HIGHEST
+
+
+def diagonal_block_inverses(factor, block):
+    count = factor.shape[0] // block
+    diag = jnp.stack(
+        [factor[k * block:(k + 1) * block, k * block:(k + 1) * block] for k in range(count)]
+    )
+    pivots = jnp.diagonal(diag, axis1=1, axis2=2)
+    eye = jnp.eye(block, dtype=factor.dtype)
+    power = eye - diag / pivots[:, :, None]
+    product = eye + power
+    reach = 2
+    while reach < block:
+        power = jnp.einsum("kij,kjl->kil", power, power, precision=HIGHEST)
+        product = jnp.einsum("kij,kjl->kil", product, eye + power, precision=HIGHEST)
+        reach *= 2
+    return product / pivots[:, None, :]
+
+
+def cholesky_solve(factor, rhs, block):
+    count = factor.shape[0] // block
+    inverses = diagonal_block_inverses(factor, block)
+    forward = []
+    for k in range(count):
+        rows = slice(k * block, (k + 1) * block)
+        residual = rhs[rows]
+        if k:
+            residual = residual - jnp.dot(
+                factor[rows, :k * block], jnp.concatenate(forward), precision=HIGHEST
+            )
+        forward.append(jnp.dot(inverses[k], residual, precision=HIGHEST))
+    backward = [None] * count
+    for k in reversed(range(count)):
+        residual = forward[k]
+        if k < count - 1:
+            below = factor[(k + 1) * block:, k * block:(k + 1) * block]
+            residual = residual - jnp.dot(
+                below.T, jnp.concatenate(backward[k + 1:]), precision=HIGHEST
+            )
+        backward[k] = jnp.dot(inverses[k].T, residual, precision=HIGHEST)
+    return jnp.concatenate(backward)
+
+
 def on_device(embeddings, projection, phase_code, penalty, assignment, targets):
     width = projection.shape[1]
     attrs = targets.shape[1]
@@ -89,7 +133,7 @@
     ridge_shift = penalty[0].astype(jnp.float32) * jnp.float32(total_rows / 8.0)
     system = gram + ridge_shift * jnp.eye(width, dtype=jnp.float32)
     factor = lax.linalg.cholesky(system, symmetrize_input=False)
-    coeffs = jax.scipy.linalg.cho_solve((factor, True), cross).astype(jnp.bfloat16)
+    coeffs = cholesky_solve(factor, cross, 64).astype(jnp.bfloat16)
     scores = jnp.dot(features, coeffs, preferred_element_type=jnp.float32)
     peak_local = jnp.max(jnp.abs(scores), axis=0)
     column_sum = jnp.sum(scores, axis=0)

time: 340 us -> 321 us (0.944)
  the two profiles are of different devices: /device:TPU:12 before, /device:TPU:16 now
where the time goes in v6:
time: 321 us; the launch traced here: 315 us
  starting transfers between devices  109 us (34%)
  other arithmetic  92.6 us (29%)
  waiting for transfers between devices  70.3 us (22%)
  matrix products  21.9 us (7%)
  local copies, waits for them, and re-layouts  15.8 us (5%)
  between operations  5.87 us (2%)
    ppermute x33, starting transfers between devices, partner(): return lax.ppermute(x, name, [(i, i ^ mask) for i in range(size)])  109 us
    another operation x14, other arithmetic, on_device(): factor = lax.linalg.cholesky(system, symmetrize_input=False)  88.9 us
    ppermute x33, waiting for transfers between devices, partner(): return lax.ppermute(x, name, [(i, i ^ mask) for i in range(size)])  70.3 us
  transfers between devices with their start and end apart: 33, of which 19 were waited for; matrix products, arithmetic and copies ran while one was open for 2% of the time, Pallas kernels for 0%

profile of v6, /device:TPU:16, one launch (start us, length us, event | category | flops | bytes accessed | tf_op | source)
XLA Modules:
  0.0 315.3 jit_solution(3656459654660340103)
XLA Ops:
  1.5 3.3 %fusion.1 = bf16[256,512]{1,0:T(8,128)(2,1)S(1)} fusion(bf16[256,1024]{1,0:T(8,128)(2,1)} %param.6, bf16[1024,512]{1,0:T(8,128)(2,1)S(1)} %copy-done, f32[512]{0:T(512)S(1)} %fusion.104), kind=kOutput, calls=%fused_computation.4 | convolution fusion | flops 268697600 | bytes 1837056 | tf_op jit(solution)/shard_map/dot_general | solution.py:104
  9.5 2.4 collective-permute-start
  13.1 3.5 %collective-permute-start.13 = (f32[256,128]{1,0:T(8,128)S(1)}, f32[256,128]{1,0:T(8,128)S(1)}, u32[]{:S(2)}, u32[]{:S(2)}) collective-permute-start(f32[256,128]{1,0:T(8,128)S(1)} %constant_dynamic-slice_fusion.1), channel_id=1, source_target_pairs={{0,64},{4,68},{8,72},{12,76},{16,80},{20,84},{24,88},{28,92},{32,9... | collective-permute-start | bytes 393224 | tf_op jit(solution)/shard_map/ppermute | solution.py:27
  16.7 4.3 %collective-permute-start.1 = (f32[320,128]{0,1:T(8,128)S(1)}, f32[320,128]{0,1:T(8,128)S(1)}, u32[]{:S(2)}, u32[]{:S(2)}) collective-permute-start(f32[320,128]{0,1:T(8,128)S(1)} %constant_dynamic-slice_fusion.4), channel_id=1, source_target_pairs={{0,8},{4,12},{8,0},{12,4},{16,24},{20,28},{24,16},{28,20},{32,40},... | collective-permute-start | bytes 491528 | tf_op jit(solution)/shard_map/ppermute | solution.py:27
  21.1 6.9 %collective-permute-start.14 = (f32[128,128]{1,0:T(8,128)S(1)}, f32[128,128]{1,0:T(8,128)S(1)}, u32[]{:S(2)}, u32[]{:S(2)}) collective-permute-start(f32[128,128]{1,0:T(8,128)S(1)} %constant_dynamic-slice_fusion), channel_id=1, source_target_pairs={{0,128},{4,132},{8,136},{12,140},{16,144},{20,148},{24,152},{28,15... | collective-permute-start | bytes 196616 | tf_op jit(solution)/shard_map/ppermute | solution.py:27
  28.3 3.8 %collective-permute-start.2 = (f32[160,128]{0,1:T(8,128)S(1)}, f32[160,128]{0,1:T(8,128)S(1)}, u32[]{:S(2)}, u32[]{:S(2)}) collective-permute-start(f32[160,128]{0,1:T(8,128)S(1)} %constant_dynamic-slice_fusion.3), channel_id=1, source_target_pairs={{0,16},{4,20},{8,24},{12,28},{16,0},{20,4},{24,8},{28,12},{32,48},... | collective-permute-start | bytes 245768 | tf_op jit(solution)/shard_map/ppermute | solution.py:27
  32.2 5.0 %collective-permute-start.15 = (f32[128,128]{1,0:T(8,128)S(1)}, f32[128,128]{1,0:T(8,128)S(1)}, u32[]{:S(2)}, u32[]{:S(2)}) collective-permute-start(f32[128,128]{1,0:T(8,128)S(1)} %dynamic-slice_add_fusion.5), channel_id=1, source_target_pairs={{0,256},{4,260},{8,264},{12,268},{16,272},{20,276},{24,280},{28,28... | collective-permute-start | bytes 196616 | tf_op jit(solution)/shard_map/ppermute | solution.py:27
  37.2 5.0 %collective-permute-done.15 = f32[128,128]{1,0:T(8,128)S(1)} collective-permute-done((f32[128,128]{1,0:T(8,128)S(1)}, f32[128,128]{1,0:T(8,128)S(1)}, u32[]{:S(2)}, u32[]{:S(2)}) %collective-permute-start.15) | collective-permute-done | bytes 65568 | tf_op jit(solution)/shard_map/ppermute | solution.py:27
  42.3 4.1 %collective-permute-start.16 = (f32[128,128]{1,0:T(8,128)S(1)}, f32[128,128]{1,0:T(8,128)S(1)}, u32[]{:S(2)}, u32[]{:S(2)}) collective-permute-start(f32[128,128]{1,0:T(8,128)S(1)} %add.333), channel_id=1, source_target_pairs={{0,8},{4,12},{8,0},{12,4},{16,24},{20,28},{24,16},{28,20},{32,40},... | collective-permute-start | bytes 196616 | tf_op jit(solution)/shard_map/ppermute | solution.py:27
  46.5 8.2 %collective-permute-start.3 = (f32[160,128]{0,1:T(8,128)S(1)}, f32[160,128]{0,1:T(8,128)S(1)}, u32[]{:S(2)}, u32[]{:S(2)}) collective-permute-start(f32[160,128]{0,1:T(8,128)S(1)} %dynamic-slice_add_fusion.4), channel_id=1, source_target_pairs={{0,32},{4,36},{8,40},{12,44},{16,48},{20,52},{24,56},{28,60},{32,0... | collective-permute-start | bytes 245768 | tf_op jit(solution)/shard_map/ppermute | solution.py:27
  54.8 2.6 collective-permute-start.17
  57.4 5.2 %collective-permute-done.17 = f32[128,128]{1,0:T(8,128)S(1)} collective-permute-done((f32[128,128]{1,0:T(8,128)S(1)}, f32[128,128]{1,0:T(8,128)S(1)}, u32[]{:S(2)}, u32[]{:S(2)}) %collective-permute-start.17) | collective-permute-done | bytes 65568 | tf_op jit(solution)/shard_map/ppermute | solution.py:27
  62.5 4.6 %collective-permute-start.18 = (f32[128,128]{1,0:T(8,128)S(1)}, f32[128,128]{1,0:T(8,128)S(1)}, u32[]{:S(2)}, u32[]{:S(2)}) collective-permute-start(f32[128,128]{1,0:T(8,128)S(1)} %add.335), channel_id=1, source_target_pairs={{0,32},{4,36},{8,40},{12,44},{16,48},{20,52},{24,56},{28,60},{32,0... | collective-permute-start | bytes 196616 | tf_op jit(solution)/shard_map/ppermute | solution.py:27
  69.1 3.9 %collective-permute-done.18 = f32[128,128]{1,0:T(8,128)S(1)} collective-permute-done((f32[128,128]{1,0:T(8,128)S(1)}, f32[128,128]{1,0:T(8,128)S(1)}, u32[]{:S(2)}, u32[]{:S(2)}) %collective-permute-start.18) | collective-permute-done | bytes 65568 | tf_op jit(solution)/shard_map/ppermute | solution.py:27
  73.0 3.4 %collective-permute-start.19 = (f32[128,128]{1,0:T(8,128)S(1)}, f32[128,128]{1,0:T(8,128)S(1)}, u32[]{:S(2)}, u32[]{:S(2)}) collective-permute-start(f32[128,128]{1,0:T(8,128)S(1)} %add.336), channel_id=1, source_target_pairs={{0,1},{1,0},{2,3},{3,2},{4,5},{5,4},{6,7},{7,6},{8,9},{9,8},{10,11... | collective-permute-start | bytes 196616 | tf_op jit(solution)/shard_map/ppermute | solution.py:27
  76.4 2.1 collective-permute-start.5
  79.2 4.9 %collective-permute-start.20 = (f32[128,128]{1,0:T(8,128)S(1)}, f32[128,128]{1,0:T(8,128)S(1)}, u32[]{:S(2)}, u32[]{:S(2)}) collective-permute-start(f32[128,128]{1,0:T(8,128)S(1)} %add.337), channel_id=1, source_target_pairs={{0,2},{1,3},{2,0},{3,1},{4,6},{5,7},{6,4},{7,5},{8,10},{9,11},{10,... | collective-permute-start | bytes 196616 | tf_op jit(solution)/shard_map/ppermute | solution.py:27
  84.2 5.2 %collective-permute-start.6 = (f32[160,128]{0,1:T(8,128)S(1)}, f32[160,128]{0,1:T(8,128)S(1)}, u32[]{:S(2)}, u32[]{:S(2)}) collective-permute-start(f32[160,128]{0,1:T(8,128)S(1)} %add.309), channel_id=1, source_target_pairs={{0,256},{4,260},{8,264},{12,268},{16,272},{20,276},{24,280},{28,28... | collective-permute-start | bytes 245768 | tf_op jit(solution)/shard_map/ppermute | solution.py:27
  89.4 3.4 %collective-permute-start.21 = (f32[128,128]{1,0:T(8,128)S(1)}, f32[128,128]{1,0:T(8,128)S(1)}, u32[]{:S(2)}, u32[]{:S(2)}) collective-permute-start(f32[128,128]{1,0:T(8,128)S(1)} %add.338), channel_id=1, source_target_pairs={{0,128},{4,132},{8,136},{12,140},{16,144},{20,148},{24,152},{28,15... | collective-permute-start | bytes 196616 | tf_op jit(solution)/shard_map/ppermute | solution.py:27
  92.8 4.1 %collective-permute-done.6 = f32[160,128]{0,1:T(8,128)S(1)} collective-permute-done((f32[160,128]{0,1:T(8,128)S(1)}, f32[160,128]{0,1:T(8,128)S(1)}, u32[]{:S(2)}, u32[]{:S(2)}) %collective-permute-start.6) | collective-permute-done | bytes 81952 | tf_op jit(solution)/shard_map/ppermute | solution.py:27
  96.9 2.5 collective-permute-start.7
  101.4 3.4 %collective-permute-done.7 = f32[160,128]{0,1:T(8,128)S(1)} collective-permute-done((f32[160,128]{0,1:T(8,128)S(1)}, f32[160,128]{0,1:T(8,128)S(1)}, u32[]{:S(2)}, u32[]{:S(2)}) %collective-permute-start.7) | collective-permute-done | bytes 81952 | tf_op jit(solution)/shard_map/ppermute | solution.py:27
  104.9 3.1 collective-permute-start.8
  108.1 5.2 %collective-permute-done.8 = f32[160,128]{0,1:T(8,128)S(1)} collective-permute-done((f32[160,128]{0,1:T(8,128)S(1)}, f32[160,128]{0,1:T(8,128)S(1)}, u32[]{:S(2)}, u32[]{:S(2)}) %collective-permute-start.8) | collective-permute-done | bytes 81952 | tf_op jit(solution)/shard_map/ppermute | solution.py:27
  117.2 4.6 %collective-permute-done.9 = f32[160,128]{0,1:T(8,128)S(1)} collective-permute-done((f32[160,128]{0,1:T(8,128)S(1)}, f32[160,128]{0,1:T(8,128)S(1)}, u32[]{:S(2)}, u32[]{:S(2)}) %collective-permute-start.9) | collective-permute-done | bytes 81952 | tf_op jit(solution)/shard_map/ppermute | solution.py:27
  124.5 4.9 %collective-permute-done.10 = f32[320,128]{0,1:T(8,128)S(1)} collective-permute-done((f32[320,128]{0,1:T(8,128)S(1)}, f32[320,128]{0,1:T(8,128)S(1)}, u32[]{:S(2)}, u32[]{:S(2)}) %collective-permute-start.10) | collective-permute-done | bytes 163872 | tf_op jit(solution)/shard_map/ppermute | solution.py:27
  129.7 2.4 collective-permute-start.11
  137.7 11.7 %cholesky.103 = f32[128,128]{1,0:T(8,128)S(1)} custom-call(f32[128,128]{1,0:T(8,128)S(1)} %cholesky.263), custom_call_target="Cholesky" | custom-call | tf_op jit(solution)/shard_map/cholesky | solution.py:135
  150.0 10.4 %custom-call.20 = f32[1,128,128]{1,2,0:T(8,128)} custom-call(f32[1,128,128]{2,1,0:T(8,128)S(1)} %get-tuple-element.55), custom_call_target="InvertDiagBlocksLowerTriangular" | custom-call | tf_op jit(solution)/shard_map/cholesky | solution.py:135
  164.2 13.2 %cholesky.215 = f32[128,128]{1,0:T(8,128)} custom-call(f32[128,128]{1,0:T(8,128)} %cholesky.267), custom_call_target="Cholesky" | custom-call | tf_op jit(solution)/shard_map/cholesky | solution.py:135
  178.9 11.4 %custom-call.21 = f32[1,128,128]{1,2,0:T(8,128)} custom-call(f32[1,128,128]{2,1,0:T(8,128)} %get-tuple-element.52), custom_call_target="InvertDiagBlocksLowerTriangular" | custom-call | tf_op jit(solution)/shard_map/cholesky | solution.py:135
  193.1 13.2 %cholesky.236 = f32[128,128]{1,0:T(8,128)} custom-call(f32[128,128]{1,0:T(8,128)} %cholesky.272), custom_call_target="Cholesky" | custom-call | tf_op jit(solution)/shard_map/cholesky | solution.py:135
  208.4 11.3 %custom-call.22 = f32[1,128,128]{1,2,0:T(8,128)} custom-call(f32[1,128,128]{2,1,0:T(8,128)} %get-tuple-element.49), custom_call_target="InvertDiagBlocksLowerTriangular" | custom-call | tf_op jit(solution)/shard_map/cholesky | solution.py:135
  221.8 12.7 %cholesky.253 = f32[128,128]{1,0:T(8,128)S(1)} custom-call(f32[128,128]{1,0:T(8,128)} %convolution_subtract_fusion.8), custom_call_target="Cholesky" | custom-call | tf_op jit(solution)/shard_map/cholesky | solution.py:135
  238.9 2.0 copy.42
  256.1 2.4 collective-permute-start.24
  259.3 1.9 collective-permute-start.25
  261.3 3.5 %collective-permute-done.25 = f32[2,256]{1,0:T(2,128)S(1)} collective-permute-done((f32[2,256]{1,0:T(2,128)S(1)}, f32[2,256]{1,0:T(2,128)S(1)}, u32[]{:S(2)}, u32[]{:S(2)}) %collective-permute-start.25) | collective-permute-done | bytes 2080 | tf_op jit(solution)/shard_map/ppermute | solution.py:27
  266.8 4.4 %collective-permute-done.26 = f32[2,256]{1,0:T(2,128)S(1)} collective-permute-done((f32[2,256]{1,0:T(2,128)S(1)}, f32[2,256]{1,0:T(2,128)S(1)}, u32[]{:S(2)}, u32[]{:S(2)}) %collective-permute-start.26) | collective-permute-done | bytes 2080 | tf_op jit(solution)/shard_map/ppermute | solution.py:27
  271.2 4.3 %collective-permute-start.27 = (f32[2,256]{1,0:T(2,128)S(1)}, f32[2,256]{1,0:T(2,128)S(1)}, u32[]{:S(2)}, u32[]{:S(2)}) collective-permute-start(f32[2,256]{1,0:T(2,128)S(1)} %pad_maximum_fusion.4), channel_id=1, source_target_pairs={{0,32},{4,36},{8,40},{12,44},{16,48},{20,52},{24,56},{28,60},{32,0... | collective-permute-start | bytes 6152 | tf_op jit(solution)/shard_map/ppermute | solution.py:27
  275.5 5.1 %collective-permute-done.27 = f32[2,256]{1,0:T(2,128)S(1)} collective-permute-done((f32[2,256]{1,0:T(2,128)S(1)}, f32[2,256]{1,0:T(2,128)S(1)}, u32[]{:S(2)}, u32[]{:S(2)}) %collective-permute-start.27) | collective-permute-done | bytes 2080 | tf_op jit(solution)/shard_map/ppermute | solution.py:27
  282.5 3.6 %collective-permute-done.28 = f32[2,256]{1,0:T(2,128)S(1)} collective-permute-done((f32[2,256]{1,0:T(2,128)S(1)}, f32[2,256]{1,0:T(2,128)S(1)}, u32[]{:S(2)}, u32[]{:S(2)}) %collective-permute-start.28) | collective-permute-done | bytes 2080 | tf_op jit(solution)/shard_map/ppermute | solution.py:27
  288.0 4.4 %collective-permute-done.29 = f32[2,256]{1,0:T(2,128)S(1)} collective-permute-done((f32[2,256]{1,0:T(2,128)S(1)}, f32[2,256]{1,0:T(2,128)S(1)}, u32[]{:S(2)}, u32[]{:S(2)}) %collective-permute-start.29) | collective-permute-done | bytes 2080 | tf_op jit(solution)/shard_map/ppermute | solution.py:27
  292.5 4.8 %collective-permute-start.30 = (f32[2,256]{1,0:T(2,128)S(1)}, f32[2,256]{1,0:T(2,128)S(1)}, u32[]{:S(2)}, u32[]{:S(2)}) collective-permute-start(f32[2,256]{1,0:T(2,128)S(1)} %pad_maximum_fusion.7), channel_id=1, source_target_pairs={{0,256},{4,260},{8,264},{12,268},{16,272},{20,276},{24,280},{28,28... | collective-permute-start | bytes 6152 | tf_op jit(solution)/shard_map/ppermute | solution.py:27
  297.4 4.5 %collective-permute-done.30 = f32[2,256]{1,0:T(2,128)S(1)} collective-permute-done((f32[2,256]{1,0:T(2,128)S(1)}, f32[2,256]{1,0:T(2,128)S(1)}, u32[]{:S(2)}, u32[]{:S(2)}) %collective-permute-start.30) | collective-permute-done | bytes 2080 | tf_op jit(solution)/shard_map/ppermute | solution.py:27
  303.8 3.6 %collective-permute-done.31 = f32[2,256]{1,0:T(2,128)S(1)} collective-permute-done((f32[2,256]{1,0:T(2,128)S(1)}, f32[2,256]{1,0:T(2,128)S(1)}, u32[]{:S(2)}, u32[]{:S(2)}) %collective-permute-start.31) | collective-permute-done | bytes 2080 | tf_op jit(solution)/shard_map/ppermute | solution.py:27
  307.4 3.8 %collective-permute-start.32 = (f32[2,256]{1,0:T(2,128)S(1)}, f32[2,256]{1,0:T(2,128)S(1)}, u32[]{:S(2)}, u32[]{:S(2)}) collective-permute-start(f32[2,256]{1,0:T(2,128)S(1)} %pad_maximum_fusion.9), channel_id=1, source_target_pairs={{0,2},{1,3},{2,0},{3,1},{4,6},{5,7},{6,4},{7,5},{8,10},{9,11},{10,... | collective-permute-start | bytes 6152 | tf_op jit(solution)/shard_map/ppermute | solution.py:27
  311.2 3.2 %collective-permute-done.32 = f32[2,256]{1,0:T(2,128)S(1)} collective-permute-done((f32[2,256]{1,0:T(2,128)S(1)}, f32[2,256]{1,0:T(2,128)S(1)}, u32[]{:S(2)}, u32[]{:S(2)}) %collective-permute-start.32) | collective-permute-done | bytes 2080 | tf_op jit(solution)/shard_map/ppermute | solution.py:27
  (228 shorter events, 61.7 us)
Async XLA Ops:
  0.0 1.5 copy-start
  1.5 4.5 %copy-start.11 = (bf16[256,256]{1,0:T(8,128)(2,1)S(1)}, bf16[256,256]{1,0:T(8,128)(2,1)}, u32[]{:S(2)}) copy-start(bf16[256,256]{1,0:T(8,128)(2,1)} %param.11) | copy-start | bytes 393220
  7.0 5.1 %collective-permute-start.12 = (f32[512,128]{1,0:T(8,128)}, f32[512,128]{1,0:T(8,128)}, u32[]{:S(2)}, u32[]{:S(2)}) collective-permute-start(f32[512,128]{1,0:T(8,128)} %constant_dynamic-slice_fusion.2), channel_id=1, source_target_pairs={{0,4},{4,0},{8,12},{12,8},{16,20},{20,16},{24,28},{28,24},{32,36},... | collective-permute-start | bytes 786440 | tf_op jit(solution)/shard_map/ppermute | solution.py:27
  9.5 7.1 %collective-permute-start = (f32[640,128]{0,1:T(8,128)S(1)}, f32[640,128]{0,1:T(8,128)S(1)}, u32[]{:S(2)}, u32[]{:S(2)}) collective-permute-start(f32[640,128]{0,1:T(8,128)S(1)} %constant_dynamic-slice_fusion.5), channel_id=1, source_target_pairs={{0,4},{4,0},{8,12},{12,8},{16,20},{20,16},{24,28},{28,24},{32,36},... | collective-permute-start | bytes 983048 | tf_op jit(solution)/shard_map/ppermute | solution.py:27
  13.1 8.0 %collective-permute-start.13 = (f32[256,128]{1,0:T(8,128)S(1)}, f32[256,128]{1,0:T(8,128)S(1)}, u32[]{:S(2)}, u32[]{:S(2)}) collective-permute-start(f32[256,128]{1,0:T(8,128)S(1)} %constant_dynamic-slice_fusion.1), channel_id=1, source_target_pairs={{0,64},{4,68},{8,72},{12,76},{16,80},{20,84},{24,88},{28,92},{32,9... | collective-permute-start | bytes 393224 | tf_op jit(solution)/shard_map/ppermute | solution.py:27
  16.7 11.3 %collective-permute-start.1 = (f32[320,128]{0,1:T(8,128)S(1)}, f32[320,128]{0,1:T(8,128)S(1)}, u32[]{:S(2)}, u32[]{:S(2)}) collective-permute-start(f32[320,128]{0,1:T(8,128)S(1)} %constant_dynamic-slice_fusion.4), channel_id=1, source_target_pairs={{0,8},{4,12},{8,0},{12,4},{16,24},{20,28},{24,16},{28,20},{32,40},... | collective-permute-start | bytes 491528 | tf_op jit(solution)/shard_map/ppermute | solution.py:27
  21.1 11.1 %collective-permute-start.14 = (f32[128,128]{1,0:T(8,128)S(1)}, f32[128,128]{1,0:T(8,128)S(1)}, u32[]{:S(2)}, u32[]{:S(2)}) collective-permute-start(f32[128,128]{1,0:T(8,128)S(1)} %constant_dynamic-slice_fusion), channel_id=1, source_target_pairs={{0,128},{4,132},{8,136},{12,140},{16,144},{20,148},{24,152},{28,15... | collective-permute-start | bytes 196616 | tf_op jit(solution)/shard_map/ppermute | solution.py:27
  28.3 18.1 %collective-permute-start.2 = (f32[160,128]{0,1:T(8,128)S(1)}, f32[160,128]{0,1:T(8,128)S(1)}, u32[]{:S(2)}, u32[]{:S(2)}) collective-permute-start(f32[160,128]{0,1:T(8,128)S(1)} %constant_dynamic-slice_fusion.3), channel_id=1, source_target_pairs={{0,16},{4,20},{8,24},{12,28},{16,0},{20,4},{24,8},{28,12},{32,48},... | collective-permute-start | bytes 245768 | tf_op jit(solution)/shard_map/ppermute | solution.py:27
  32.2 10.1 %collective-permute-start.15 = (f32[128,128]{1,0:T(8,128)S(1)}, f32[128,128]{1,0:T(8,128)S(1)}, u32[]{:S(2)}, u32[]{:S(2)}) collective-permute-start(f32[128,128]{1,0:T(8,128)S(1)} %dynamic-slice_add_fusion.5), channel_id=1, source_target_pairs={{0,256},{4,260},{8,264},{12,268},{16,272},{20,276},{24,280},{28,28... | collective-permute-start | bytes 196616 | tf_op jit(solution)/shard_map/ppermute | solution.py:27
  42.3 12.5 %collective-permute-start.16 = (f32[128,128]{1,0:T(8,128)S(1)}, f32[128,128]{1,0:T(8,128)S(1)}, u32[]{:S(2)}, u32[]{:S(2)}) collective-permute-start(f32[128,128]{1,0:T(8,128)S(1)} %add.333), channel_id=1, source_target_pairs={{0,8},{4,12},{8,0},{12,4},{16,24},{20,28},{24,16},{28,20},{32,40},... | collective-permute-start | bytes 196616 | tf_op jit(solution)/shard_map/ppermute | solution.py:27
  46.5 20.6 %collective-permute-start.3 = (f32[160,128]{0,1:T(8,128)S(1)}, f32[160,128]{0,1:T(8,128)S(1)}, u32[]{:S(2)}, u32[]{:S(2)}) collective-permute-start(f32[160,128]{0,1:T(8,128)S(1)} %dynamic-slice_add_fusion.4), channel_id=1, source_target_pairs={{0,32},{4,36},{8,40},{12,44},{16,48},{20,52},{24,56},{28,60},{32,0... | collective-permute-start | bytes 245768 | tf_op jit(solution)/shard_map/ppermute | solution.py:27
  54.8 7.7 %collective-permute-start.17 = (f32[128,128]{1,0:T(8,128)S(1)}, f32[128,128]{1,0:T(8,128)S(1)}, u32[]{:S(2)}, u32[]{:S(2)}) collective-permute-start(f32[128,128]{1,0:T(8,128)S(1)} %add.334), channel_id=1, source_target_pairs={{0,16},{4,20},{8,24},{12,28},{16,0},{20,4},{24,8},{28,12},{32,48},... | collective-permute-start | bytes 196616 | tf_op jit(solution)/shard_map/ppermute | solution.py:27
  62.5 10.5 %collective-permute-start.18 = (f32[128,128]{1,0:T(8,128)S(1)}, f32[128,128]{1,0:T(8,128)S(1)}, u32[]{:S(2)}, u32[]{:S(2)}) collective-permute-start(f32[128,128]{1,0:T(8,128)S(1)} %add.335), channel_id=1, source_target_pairs={{0,32},{4,36},{8,40},{12,44},{16,48},{20,52},{24,56},{28,60},{32,0... | collective-permute-start | bytes 196616 | tf_op jit(solution)/shard_map/ppermute | solution.py:27
  67.2 9.2 %collective-permute-start.4 = (f32[160,128]{0,1:T(8,128)S(1)}, f32[160,128]{0,1:T(8,128)S(1)}, u32[]{:S(2)}, u32[]{:S(2)}) collective-permute-start(f32[160,128]{0,1:T(8,128)S(1)} %add.307), channel_id=1, source_target_pairs={{0,64},{4,68},{8,72},{12,76},{16,80},{20,84},{24,88},{28,92},{32,9... | collective-permute-start | bytes 245768 | tf_op jit(solution)/shard_map/ppermute | solution.py:27
  73.0 6.2 %collective-permute-start.19 = (f32[128,128]{1,0:T(8,128)S(1)}, f32[128,128]{1,0:T(8,128)S(1)}, u32[]{:S(2)}, u32[]{:S(2)}) collective-permute-start(f32[128,128]{1,0:T(8,128)S(1)} %add.336), channel_id=1, source_target_pairs={{0,1},{1,0},{2,3},{3,2},{4,5},{5,4},{6,7},{7,6},{8,9},{9,8},{10,11... | collective-permute-start | bytes 196616 | tf_op jit(solution)/shard_map/ppermute | solution.py:27
  76.4 7.8 %collective-permute-start.5 = (f32[160,128]{0,1:T(8,128)S(1)}, f32[160,128]{0,1:T(8,128)S(1)}, u32[]{:S(2)}, u32[]{:S(2)}) collective-permute-start(f32[160,128]{0,1:T(8,128)S(1)} %add.308), channel_id=1, source_target_pairs={{0,128},{4,132},{8,136},{12,140},{16,144},{20,148},{24,152},{28,15... | collective-permute-start | bytes 245768 | tf_op jit(solution)/shard_map/ppermute | solution.py:27
  79.2 10.2 %collective-permute-start.20 = (f32[128,128]{1,0:T(8,128)S(1)}, f32[128,128]{1,0:T(8,128)S(1)}, u32[]{:S(2)}, u32[]{:S(2)}) collective-permute-start(f32[128,128]{1,0:T(8,128)S(1)} %add.337), channel_id=1, source_target_pairs={{0,2},{1,3},{2,0},{3,1},{4,6},{5,7},{6,4},{7,5},{8,10},{9,11},{10,... | collective-permute-start | bytes 196616 | tf_op jit(solution)/shard_map/ppermute | solution.py:27
  84.2 12.7 %collective-permute-start.6 = (f32[160,128]{0,1:T(8,128)S(1)}, f32[160,128]{0,1:T(8,128)S(1)}, u32[]{:S(2)}, u32[]{:S(2)}) collective-permute-start(f32[160,128]{0,1:T(8,128)S(1)} %add.309), channel_id=1, source_target_pairs={{0,256},{4,260},{8,264},{12,268},{16,272},{20,276},{24,280},{28,28... | collective-permute-start | bytes 245768 | tf_op jit(solution)/shard_map/ppermute | solution.py:27
  89.4 10.1 %collective-permute-start.21 = (f32[128,128]{1,0:T(8,128)S(1)}, f32[128,128]{1,0:T(8,128)S(1)}, u32[]{:S(2)}, u32[]{:S(2)}) collective-permute-start(f32[128,128]{1,0:T(8,128)S(1)} %add.338), channel_id=1, source_target_pairs={{0,128},{4,132},{8,136},{12,140},{16,144},{20,148},{24,152},{28,15... | collective-permute-start | bytes 196616 | tf_op jit(solution)/shard_map/ppermute | solution.py:27
  96.9 8.0 %collective-permute-start.7 = (f32[160,128]{0,1:T(8,128)S(1)}, f32[160,128]{0,1:T(8,128)S(1)}, u32[]{:S(2)}, u32[]{:S(2)}) collective-permute-start(f32[160,128]{0,1:T(8,128)S(1)} %add.310), channel_id=1, source_target_pairs={{0,1},{1,0},{2,3},{3,2},{4,5},{5,4},{6,7},{7,6},{8,9},{9,8},{10,11... | collective-permute-start | bytes 245768 | tf_op jit(solution)/shard_map/ppermute | solution.py:27
  99.5 15.7 %collective-permute-start.22 = (f32[256,128]{1,0:T(8,128)S(1)}, f32[256,128]{1,0:T(8,128)S(1)}, u32[]{:S(2)}, u32[]{:S(2)}) collective-permute-start(f32[256,128]{1,0:T(8,128)S(1)} %maximum_select_fusion.5), channel_id=1, source_target_pairs={{0,64},{4,68},{8,72},{12,76},{16,80},{20,84},{24,88},{28,92},{32,9... | collective-permute-start | bytes 393224 | tf_op jit(solution)/shard_map/ppermute | solution.py:27
  104.9 8.4 %collective-permute-start.8 = (f32[160,128]{0,1:T(8,128)S(1)}, f32[160,128]{0,1:T(8,128)S(1)}, u32[]{:S(2)}, u32[]{:S(2)}) collective-permute-start(f32[160,128]{0,1:T(8,128)S(1)} %add.311), channel_id=1, source_target_pairs={{0,2},{1,3},{2,0},{3,1},{4,6},{5,7},{6,4},{7,5},{8,10},{9,11},{10,... | collective-permute-start | bytes 245768 | tf_op jit(solution)/shard_map/ppermute | solution.py:27
  113.3 8.5 %collective-permute-start.9 = (f32[160,128]{0,1:T(8,128)S(1)}, f32[160,128]{0,1:T(8,128)S(1)}, u32[]{:S(2)}, u32[]{:S(2)}) collective-permute-start(f32[160,128]{0,1:T(8,128)S(1)} %add.312), channel_id=1, source_target_pairs={{0,16},{4,20},{8,24},{12,28},{16,0},{20,4},{24,8},{28,12},{32,48},... | collective-permute-start | bytes 245768 | tf_op jit(solution)/shard_map/ppermute | solution.py:27
  115.3 16.8 %collective-permute-start.23 = (f32[512,128]{1,0:T(8,128)S(1)}, f32[512,128]{1,0:T(8,128)S(1)}, u32[]{:S(2)}, u32[]{:S(2)}) collective-permute-start(f32[512,128]{1,0:T(8,128)S(1)} %maximum_select_fusion.3), channel_id=1, source_target_pairs={{0,4},{4,0},{8,12},{12,8},{16,20},{20,16},{24,28},{28,24},{32,36},... | collective-permute-start | bytes 786440 | tf_op jit(solution)/shard_map/ppermute | solution.py:27
  121.9 7.6 %collective-permute-start.10 = (f32[320,128]{0,1:T(8,128)S(1)}, f32[320,128]{0,1:T(8,128)S(1)}, u32[]{:S(2)}, u32[]{:S(2)}) collective-permute-start(f32[320,128]{0,1:T(8,128)S(1)} %maximum_select_fusion.4), channel_id=1, source_target_pairs={{0,8},{4,12},{8,0},{12,4},{16,24},{20,28},{24,16},{28,20},{32,40},... | collective-permute-start | bytes 491528 | tf_op jit(solution)/shard_map/ppermute | solution.py:27
  129.7 7.0 %collective-permute-start.11 = (f32[640,128]{0,1:T(8,128)S(1)}, f32[640,128]{0,1:T(8,128)S(1)}, u32[]{:S(2)}, u32[]{:S(2)}) collective-permute-start(f32[640,128]{0,1:T(8,128)S(1)} %maximum_select_fusion.2), channel_id=1, source_target_pairs={{0,4},{4,0},{8,12},{12,8},{16,20},{20,16},{24,28},{28,24},{32,36},... | collective-permute-start | bytes 983048 | tf_op jit(solution)/shard_map/ppermute | solution.py:27
  149.4 0.6 copy-start.3
  162.9 0.7 copy-start.1
  191.8 0.7 copy-start.2
  244.7 2.0 copy-start.10
  245.1 2.1 copy-start.9
  245.1 2.5 copy-start.8
  245.5 2.5 copy-start.7
  245.9 2.6 copy-start.6
  246.7 2.3 copy-start.5
  247.1 2.5 copy-start.4
  256.1 3.2 %collective-permute-start.24 = (f32[2,256]{1,0:T(2,128)S(1)}, f32[2,256]{1,0:T(2,128)S(1)}, u32[]{:S(2)}, u32[]{:S(2)}) collective-permute-start(f32[2,256]{1,0:T(2,128)S(1)} %pad_maximum_fusion.1), channel_id=1, source_target_pairs={{0,4},{4,0},{8,12},{12,8},{16,20},{20,16},{24,28},{28,24},{32,36},... | collective-permute-start | bytes 6152 | tf_op jit(solution)/shard_map/ppermute | solution.py:27
  259.3 5.5 %collective-permute-start.25 = (f32[2,256]{1,0:T(2,128)S(1)}, f32[2,256]{1,0:T(2,128)S(1)}, u32[]{:S(2)}, u32[]{:S(2)}) collective-permute-start(f32[2,256]{1,0:T(2,128)S(1)} %pad_maximum_fusion.2), channel_id=1, source_target_pairs={{0,8},{4,12},{8,0},{12,4},{16,24},{20,28},{24,16},{28,20},{32,40},... | collective-permute-start | bytes 6152 | tf_op jit(solution)/shard_map/ppermute | solution.py:27
  264.8 6.4 %collective-permute-start.26 = (f32[2,256]{1,0:T(2,128)S(1)}, f32[2,256]{1,0:T(2,128)S(1)}, u32[]{:S(2)}, u32[]{:S(2)}) collective-permute-start(f32[2,256]{1,0:T(2,128)S(1)} %pad_maximum_fusion.3), channel_id=1, source_target_pairs={{0,16},{4,20},{8,24},{12,28},{16,0},{20,4},{24,8},{28,12},{32,48},... | collective-permute-start | bytes 6152 | tf_op jit(solution)/shard_map/ppermute | solution.py:27
  271.2 9.4 %collective-permute-start.27 = (f32[2,256]{1,0:T(2,128)S(1)}, f32[2,256]{1,0:T(2,128)S(1)}, u32[]{:S(2)}, u32[]{:S(2)}) collective-permute-start(f32[2,256]{1,0:T(2,128)S(1)} %pad_maximum_fusion.4), channel_id=1, source_target_pairs={{0,32},{4,36},{8,40},{12,44},{16,48},{20,52},{24,56},{28,60},{32,0... | collective-permute-start | bytes 6152 | tf_op jit(solution)/shard_map/ppermute | solution.py:27
  280.6 5.5 %collective-permute-start.28 = (f32[2,256]{1,0:T(2,128)S(1)}, f32[2,256]{1,0:T(2,128)S(1)}, u32[]{:S(2)}, u32[]{:S(2)}) collective-permute-start(f32[2,256]{1,0:T(2,128)S(1)} %pad_maximum_fusion.5), channel_id=1, source_target_pairs={{0,64},{4,68},{8,72},{12,76},{16,80},{20,84},{24,88},{28,92},{32,9... | collective-permute-start | bytes 6152 | tf_op jit(solution)/shard_map/ppermute | solution.py:27
  286.1 6.4 %collective-permute-start.29 = (f32[2,256]{1,0:T(2,128)S(1)}, f32[2,256]{1,0:T(2,128)S(1)}, u32[]{:S(2)}, u32[]{:S(2)}) collective-permute-start(f32[2,256]{1,0:T(2,128)S(1)} %pad_maximum_fusion.6), channel_id=1, source_target_pairs={{0,128},{4,132},{8,136},{12,140},{16,144},{20,148},{24,152},{28,15... | collective-permute-start | bytes 6152 | tf_op jit(solution)/shard_map/ppermute | solution.py:27
  292.5 9.4 %collective-permute-start.30 = (f32[2,256]{1,0:T(2,128)S(1)}, f32[2,256]{1,0:T(2,128)S(1)}, u32[]{:S(2)}, u32[]{:S(2)}) collective-permute-start(f32[2,256]{1,0:T(2,128)S(1)} %pad_maximum_fusion.7), channel_id=1, source_target_pairs={{0,256},{4,260},{8,264},{12,268},{16,272},{20,276},{24,280},{28,28... | collective-permute-start | bytes 6152 | tf_op jit(solution)/shard_map/ppermute | solution.py:27
  301.9 5.5 %collective-permute-start.31 = (f32[2,256]{1,0:T(2,128)S(1)}, f32[2,256]{1,0:T(2,128)S(1)}, u32[]{:S(2)}, u32[]{:S(2)}) collective-permute-start(f32[2,256]{1,0:T(2,128)S(1)} %pad_maximum_fusion.8), channel_id=1, source_target_pairs={{0,1},{1,0},{2,3},{3,2},{4,5},{5,4},{6,7},{7,6},{8,9},{9,8},{10,11... | collective-permute-start | bytes 6152 | tf_op jit(solution)/shard_map/ppermute | solution.py:27
  307.4 7.0 %collective-permute-start.32 = (f32[2,256]{1,0:T(2,128)S(1)}, f32[2,256]{1,0:T(2,128)S(1)}, u32[]{:S(2)}, u32[]{:S(2)}) collective-permute-start(f32[2,256]{1,0:T(2,128)S(1)} %pad_maximum_fusion.9), channel_id=1, source_target_pairs={{0,2},{1,3},{2,0},{3,1},{4,6},{5,7},{6,4},{7,5},{8,10},{9,11},{10,... | collective-permute-start | bytes 6152 | tf_op jit(solution)/shard_map/ppermute | solution.py:27

commit v7 on v6

--- a/solution.py
+++ b/solution.py
@@ -55,26 +55,41 @@
 HIGHEST = lax.Precision.HIGHEST
 
 
-def diagonal_block_inverses(factor, block):
-    count = factor.shape[0] // block
-    diag = jnp.stack(
-        [factor[k * block:(k + 1) * block, k * block:(k + 1) * block] for k in range(count)]
-    )
-    pivots = jnp.diagonal(diag, axis1=1, axis2=2)
-    eye = jnp.eye(block, dtype=factor.dtype)
-    power = eye - diag / pivots[:, :, None]
+def triangular_inverse(lower):
+    size = lower.shape[0]
+    pivots = jnp.diagonal(lower)
+    eye = jnp.eye(size, dtype=lower.dtype)
+    power = eye - lower / pivots[:, None]
     product = eye + power
     reach = 2
-    while reach < block:
-        power = jnp.einsum("kij,kjl->kil", power, power, precision=HIGHEST)
-        product = jnp.einsum("kij,kjl->kil", product, eye + power, precision=HIGHEST)
+    while reach < size:
+        power = jnp.dot(power, power, precision=HIGHEST)
+        product = jnp.dot(product, eye + power, precision=HIGHEST)
         reach *= 2
-    return product / pivots[:, None, :]
+    return product / pivots[None, :]
 
 
-def cholesky_solve(factor, rhs, block):
+def blocked_cholesky(system, block):
+    count = system.shape[0] // block
+    trailing = system
+    columns = []
+    inverses = []
+    for k in range(count):
+        head = lax.linalg.cholesky(trailing[:block, :block], symmetrize_input=False)
+        inverse = triangular_inverse(head)
+        inverses.append(inverse)
+        above = [jnp.zeros((k * block, block), system.dtype)] if k else []
+        if k < count - 1:
+            panel = jnp.dot(trailing[block:, :block], inverse.T, precision=HIGHEST)
+            trailing = trailing[block:, block:] - jnp.dot(panel, panel.T, precision=HIGHEST)
+            columns.append(jnp.concatenate(above + [head, panel]))
+        else:
+            columns.append(jnp.concatenate(above + [head]))
+    return jnp.concatenate(columns, axis=1), inverses
+
+
+def cholesky_solve(factor, inverses, rhs, block):
     count = factor.shape[0] // block
-    inverses = diagonal_block_inverses(factor, block)
     forward = []
     for k in range(count):
         rows = slice(k * block, (k + 1) * block)
@@ -132,8 +147,8 @@
     total_rows = embeddings.shape[0] * lax.axis_size("docs") * lax.axis_size("grp")
     ridge_shift = penalty[0].astype(jnp.float32) * jnp.float32(total_rows / 8.0)
     system = gram + ridge_shift * jnp.eye(width, dtype=jnp.float32)
-    factor = lax.linalg.cholesky(system, symmetrize_input=False)
-    coeffs = cholesky_solve(factor, cross, 64).astype(jnp.bfloat16)
+    factor, inverses = blocked_cholesky(system, block)
+    coeffs = cholesky_solve(factor, inverses, cross, block).astype(jnp.bfloat16)
     scores = jnp.dot(features, coeffs, preferred_element_type=jnp.float32)
     peak_local = jnp.max(jnp.abs(scores), axis=0)
     column_sum = jnp.sum(scores, axis=0)

time: 321 us -> 266 us (0.83)
  the two profiles are of different devices: /device:TPU:16 before, /device:TPU:6 now
where the time goes in v7:
time: 266 us; the launch traced here: 263 us
  starting transfers between devices  129 us (48%)
  other arithmetic  56 us (21%)
  waiting for transfers between devices  39.8 us (15%)
  matrix products  21.1 us (8%)
  local copies, waits for them, and re-layouts  14 us (5%)
  between operations  3.04 us (1%)
    ppermute x33, starting transfers between devices, partner(): return lax.ppermute(x, name, [(i, i ^ mask) for i in range(size)])  129 us
    another operation x12, other arithmetic, blocked_cholesky(): head = lax.linalg.cholesky(trailing[:block, :block], symmetrize_input=False)  49.8 us
    ppermute x33, waiting for transfers between devices, partner(): return lax.ppermute(x, name, [(i, i ^ mask) for i in range(size)])  39.8 us
    gather x4, local copies, waits for them, and re-layouts, triangular_inverse(): pivots = jnp.diagonal(lower)  5.46 us
  transfers between devices with their start and end apart: 33, of which 21 were waited for; matrix products, arithmetic and copies ran while one was open for 2% of the time, Pallas kernels for 0%

profile of v7, /device:TPU:6, one launch (start us, length us, event | category | flops | bytes accessed | tf_op | source)
XLA Modules:
  0.0 262.9 jit_solution(8644752045075833194)
XLA Ops:
  1.5 3.3 %fusion.1 = bf16[256,512]{1,0:T(8,128)(2,1)S(1)} fusion(bf16[256,1024]{1,0:T(8,128)(2,1)} %param.7, bf16[1024,512]{1,0:T(8,128)(2,1)S(1)} %copy-done, f32[512]{0:T(512)S(1)} %fusion.79), kind=kOutput, calls=%fused_computation.8 | convolution fusion | flops 268697600 | bytes 1837056 | tf_op jit(solution)/shard_map/dot_general | solution.py:119
  7.0 1.9 collective-permute-start.12
  9.5 2.4 collective-permute-start
  13.0 3.5 %collective-permute-start.13 = (f32[256,128]{1,0:T(8,128)S(1)}, f32[256,128]{1,0:T(8,128)S(1)}, u32[]{:S(2)}, u32[]{:S(2)}) collective-permute-start(f32[256,128]{1,0:T(8,128)S(1)} %constant_dynamic-slice_fusion.1), channel_id=1, source_target_pairs={{0,64},{4,68},{8,72},{12,76},{16,80},{20,84},{24,88},{28,92},{32,9... | collective-permute-start | bytes 393224 | tf_op jit(solution)/shard_map/ppermute | solution.py:27
  16.7 4.3 %collective-permute-start.1 = (f32[320,128]{0,1:T(8,128)S(1)}, f32[320,128]{0,1:T(8,128)S(1)}, u32[]{:S(2)}, u32[]{:S(2)}) collective-permute-start(f32[320,128]{0,1:T(8,128)S(1)} %constant_dynamic-slice_fusion.4), channel_id=1, source_target_pairs={{0,8},{4,12},{8,0},{12,4},{16,24},{20,28},{24,16},{28,20},{32,40},... | collective-permute-start | bytes 491528 | tf_op jit(solution)/shard_map/ppermute | solution.py:27
  21.1 4.7 %collective-permute-done.1 = f32[320,128]{0,1:T(8,128)S(1)} collective-permute-done((f32[320,128]{0,1:T(8,128)S(1)}, f32[320,128]{0,1:T(8,128)S(1)}, u32[]{:S(2)}, u32[]{:S(2)}) %collective-permute-start.1) | collective-permute-done | bytes 163872 | tf_op jit(solution)/shard_map/ppermute | solution.py:27
  26.0 6.1 %collective-permute-start.2 = (f32[160,128]{0,1:T(8,128)S(1)}, f32[160,128]{0,1:T(8,128)S(1)}, u32[]{:S(2)}, u32[]{:S(2)}) collective-permute-start(f32[160,128]{0,1:T(8,128)S(1)} %constant_dynamic-slice_fusion.3), channel_id=1, source_target_pairs={{0,16},{4,20},{8,24},{12,28},{16,0},{20,4},{24,8},{28,12},{32,48},... | collective-permute-start | bytes 245768 | tf_op jit(solution)/shard_map/ppermute | solution.py:27
  32.2 4.5 %collective-permute-start.14 = (f32[128,128]{1,0:T(8,128)S(1)}, f32[128,128]{1,0:T(8,128)S(1)}, u32[]{:S(2)}, u32[]{:S(2)}) collective-permute-start(f32[128,128]{1,0:T(8,128)S(1)} %constant_dynamic-slice_fusion), channel_id=1, source_target_pairs={{0,128},{4,132},{8,136},{12,140},{16,144},{20,148},{24,152},{28,15... | collective-permute-start | bytes 196616 | tf_op jit(solution)/shard_map/ppermute | solution.py:27
  37.9 8.4 %collective-permute-start.3 = (f32[160,128]{0,1:T(8,128)S(1)}, f32[160,128]{0,1:T(8,128)S(1)}, u32[]{:S(2)}, u32[]{:S(2)}) collective-permute-start(f32[160,128]{0,1:T(8,128)S(1)} %dynamic-slice_add_fusion.4), channel_id=1, source_target_pairs={{0,32},{4,36},{8,40},{12,44},{16,48},{20,52},{24,56},{28,60},{32,0... | collective-permute-start | bytes 245768 | tf_op jit(solution)/shard_map/ppermute | solution.py:27
  46.3 6.8 %collective-permute-start.15 = (f32[128,128]{1,0:T(8,128)S(1)}, f32[128,128]{1,0:T(8,128)S(1)}, u32[]{:S(2)}, u32[]{:S(2)}) collective-permute-start(f32[128,128]{1,0:T(8,128)S(1)} %dynamic-slice_add_fusion.5), channel_id=1, source_target_pairs={{0,256},{4,260},{8,264},{12,268},{16,272},{20,276},{24,280},{28,28... | collective-permute-start | bytes 196616 | tf_op jit(solution)/shard_map/ppermute | solution.py:27
  53.2 3.3 %collective-permute-start.4 = (f32[160,128]{0,1:T(8,128)S(1)}, f32[160,128]{0,1:T(8,128)S(1)}, u32[]{:S(2)}, u32[]{:S(2)}) collective-permute-start(f32[160,128]{0,1:T(8,128)S(1)} %add.322), channel_id=1, source_target_pairs={{0,64},{4,68},{8,72},{12,76},{16,80},{20,84},{24,88},{28,92},{32,9... | collective-permute-start | bytes 245768 | tf_op jit(solution)/shard_map/ppermute | solution.py:27
  56.6 2.3 collective-permute-start.16
  60.3 4.2 %collective-permute-start.5 = (f32[160,128]{0,1:T(8,128)S(1)}, f32[160,128]{0,1:T(8,128)S(1)}, u32[]{:S(2)}, u32[]{:S(2)}) collective-permute-start(f32[160,128]{0,1:T(8,128)S(1)} %add.323), channel_id=1, source_target_pairs={{0,128},{4,132},{8,136},{12,140},{16,144},{20,148},{24,152},{28,15... | collective-permute-start | bytes 245768 | tf_op jit(solution)/shard_map/ppermute | solution.py:27
  64.5 5.4 %collective-permute-start.17 = (f32[128,128]{1,0:T(8,128)S(1)}, f32[128,128]{1,0:T(8,128)S(1)}, u32[]{:S(2)}, u32[]{:S(2)}) collective-permute-start(f32[128,128]{1,0:T(8,128)S(1)} %add.350), channel_id=1, source_target_pairs={{0,16},{4,20},{8,24},{12,28},{16,0},{20,4},{24,8},{28,12},{32,48},... | collective-permute-start | bytes 196616 | tf_op jit(solution)/shard_map/ppermute | solution.py:27
  69.9 2.9 %collective-permute-done.17 = f32[128,128]{1,0:T(8,128)S(1)} collective-permute-done((f32[128,128]{1,0:T(8,128)S(1)}, f32[128,128]{1,0:T(8,128)S(1)}, u32[]{:S(2)}, u32[]{:S(2)}) %collective-permute-start.17) | collective-permute-done | bytes 65568 | tf_op jit(solution)/shard_map/ppermute | solution.py:27
  72.9 3.8 %collective-permute-start.18 = (f32[128,128]{1,0:T(8,128)S(1)}, f32[128,128]{1,0:T(8,128)S(1)}, u32[]{:S(2)}, u32[]{:S(2)}) collective-permute-start(f32[128,128]{1,0:T(8,128)S(1)} %add.351), channel_id=1, source_target_pairs={{0,32},{4,36},{8,40},{12,44},{16,48},{20,52},{24,56},{28,60},{32,0... | collective-permute-start | bytes 196616 | tf_op jit(solution)/shard_map/ppermute | solution.py:27
  76.7 4.4 %collective-permute-start.6 = (f32[160,128]{0,1:T(8,128)S(1)}, f32[160,128]{0,1:T(8,128)S(1)}, u32[]{:S(2)}, u32[]{:S(2)}) collective-permute-start(f32[160,128]{0,1:T(8,128)S(1)} %add.324), channel_id=1, source_target_pairs={{0,256},{4,260},{8,264},{12,268},{16,272},{20,276},{24,280},{28,28... | collective-permute-start | bytes 245768 | tf_op jit(solution)/shard_map/ppermute | solution.py:27
  81.1 1.9 collective-permute-done.18
  83.0 2.7 %collective-permute-start.19 = (f32[128,128]{1,0:T(8,128)S(1)}, f32[128,128]{1,0:T(8,128)S(1)}, u32[]{:S(2)}, u32[]{:S(2)}) collective-permute-start(f32[128,128]{1,0:T(8,128)S(1)} %add.352), channel_id=1, source_target_pairs={{0,1},{1,0},{2,3},{3,2},{4,5},{5,4},{6,7},{7,6},{8,9},{9,8},{10,11... | collective-permute-start | bytes 196616 | tf_op jit(solution)/shard_map/ppermute | solution.py:27
  87.5 2.3 collective-permute-start.7
  89.8 3.2 %collective-permute-start.20 = (f32[128,128]{1,0:T(8,128)S(1)}, f32[128,128]{1,0:T(8,128)S(1)}, u32[]{:S(2)}, u32[]{:S(2)}) collective-permute-start(f32[128,128]{1,0:T(8,128)S(1)} %add.353), channel_id=1, source_target_pairs={{0,2},{1,3},{2,0},{3,1},{4,6},{5,7},{6,4},{7,5},{8,10},{9,11},{10,... | collective-permute-start | bytes 196616 | tf_op jit(solution)/shard_map/ppermute | solution.py:27
  92.9 2.0 collective-permute-done.7
  95.0 2.2 collective-permute-start.8
  97.5 3.3 %collective-permute-start.21 = (f32[128,128]{1,0:T(8,128)S(1)}, f32[128,128]{1,0:T(8,128)S(1)}, u32[]{:S(2)}, u32[]{:S(2)}) collective-permute-start(f32[128,128]{1,0:T(8,128)S(1)} %add.354), channel_id=1, source_target_pairs={{0,128},{4,132},{8,136},{12,140},{16,144},{20,148},{24,152},{28,15... | collective-permute-start | bytes 196616 | tf_op jit(solution)/shard_map/ppermute | solution.py:27
  100.8 2.6 collective-permute-done.8
  103.3 4.0 %collective-permute-start.9 = (f32[160,128]{0,1:T(8,128)S(1)}, f32[160,128]{0,1:T(8,128)S(1)}, u32[]{:S(2)}, u32[]{:S(2)}) collective-permute-start(f32[160,128]{0,1:T(8,128)S(1)} %add.327), channel_id=1, source_target_pairs={{0,16},{4,20},{8,24},{12,28},{16,0},{20,4},{24,8},{28,12},{32,48},... | collective-permute-start | bytes 245768 | tf_op jit(solution)/shard_map/ppermute | solution.py:27
  107.4 4.1 %collective-permute-start.22 = (f32[256,128]{1,0:T(8,128)S(1)}, f32[256,128]{1,0:T(8,128)S(1)}, u32[]{:S(2)}, u32[]{:S(2)}) collective-permute-start(f32[256,128]{1,0:T(8,128)S(1)} %maximum_select_fusion.5), channel_id=1, source_target_pairs={{0,64},{4,68},{8,72},{12,76},{16,80},{20,84},{24,88},{28,92},{32,9... | collective-permute-start | bytes 393224 | tf_op jit(solution)/shard_map/ppermute | solution.py:27
  111.8 3.4 %collective-permute-start.10 = (f32[320,128]{0,1:T(8,128)S(1)}, f32[320,128]{0,1:T(8,128)S(1)}, u32[]{:S(2)}, u32[]{:S(2)}) collective-permute-start(f32[320,128]{0,1:T(8,128)S(1)} %maximum_select_fusion.4), channel_id=1, source_target_pairs={{0,8},{4,12},{8,0},{12,4},{16,24},{20,28},{24,16},{28,20},{32,40},... | collective-permute-start | bytes 491528 | tf_op jit(solution)/shard_map/ppermute | solution.py:27
  115.2 1.9 collective-permute-start.23
  119.5 2.1 collective-permute-start.11
  126.3 11.7 %custom-call.14 = f32[128,128]{1,0:T(8,128)S(1)} custom-call(f32[128,128]{1,0:T(8,128)S(1)} %slice.279), custom_call_target="Cholesky" | custom-call | tf_op jit(solution)/shard_map/cholesky/custom-call.1 | solution.py:78
  144.3 11.7 %custom-call.15 = f32[128,128]{1,0:T(8,128)S(1)} custom-call(f32[128,128]{1,0:T(8,128)S(1)} %slice.283), custom_call_target="Cholesky" | custom-call | tf_op jit(solution)/shard_map/cholesky/custom-call.1 | solution.py:78
  162.2 11.7 %custom-call.16 = f32[128,128]{1,0:T(8,128)S(1)} custom-call(f32[128,128]{1,0:T(8,128)S(1)} %slice.288), custom_call_target="Cholesky" | custom-call | tf_op jit(solution)/shard_map/cholesky/custom-call.1 | solution.py:78
  179.8 11.7 %custom-call.17 = f32[128,128]{1,0:T(8,128)S(1)} custom-call(f32[128,128]{1,0:T(8,128)S(1)} %convolution_subtract_fusion.5), custom_call_target="Cholesky" | custom-call | tf_op jit(solution)/shard_map/cholesky/custom-call.1 | solution.py:78
  203.9 2.4 collective-permute-start.24
  207.1 3.4 %collective-permute-start.25 = (f32[2,256]{1,0:T(2,128)S(1)}, f32[2,256]{1,0:T(2,128)S(1)}, u32[]{:S(2)}, u32[]{:S(2)}) collective-permute-start(f32[2,256]{1,0:T(2,128)S(1)} %pad_maximum_fusion.15), channel_id=1, source_target_pairs={{0,8},{4,12},{8,0},{12,4},{16,24},{20,28},{24,16},{28,20},{32,40},... | collective-permute-start | bytes 6152 | tf_op jit(solution)/shard_map/ppermute | solution.py:27
  210.6 2.1 collective-permute-done.25
  212.6 3.8 %collective-permute-start.26 = (f32[2,256]{1,0:T(2,128)S(1)}, f32[2,256]{1,0:T(2,128)S(1)}, u32[]{:S(2)}, u32[]{:S(2)}) collective-permute-start(f32[2,256]{1,0:T(2,128)S(1)} %pad_maximum_fusion.16), channel_id=1, source_target_pairs={{0,16},{4,20},{8,24},{12,28},{16,0},{20,4},{24,8},{28,12},{32,48},... | collective-permute-start | bytes 6152 | tf_op jit(solution)/shard_map/ppermute | solution.py:27
  216.4 2.6 collective-permute-done.26
  219.0 7.9 %collective-permute-start.27 = (f32[2,256]{1,0:T(2,128)S(1)}, f32[2,256]{1,0:T(2,128)S(1)}, u32[]{:S(2)}, u32[]{:S(2)}) collective-permute-start(f32[2,256]{1,0:T(2,128)S(1)} %pad_maximum_fusion.17), channel_id=1, source_target_pairs={{0,32},{4,36},{8,40},{12,44},{16,48},{20,52},{24,56},{28,60},{32,0... | collective-permute-start | bytes 6152 | tf_op jit(solution)/shard_map/ppermute | solution.py:27
  228.5 3.8 %collective-permute-start.28 = (f32[2,256]{1,0:T(2,128)S(1)}, f32[2,256]{1,0:T(2,128)S(1)}, u32[]{:S(2)}, u32[]{:S(2)}) collective-permute-start(f32[2,256]{1,0:T(2,128)S(1)} %pad_maximum_fusion.18), channel_id=1, source_target_pairs={{0,64},{4,68},{8,72},{12,76},{16,80},{20,84},{24,88},{28,92},{32,9... | collective-permute-start | bytes 6152 | tf_op jit(solution)/shard_map/ppermute | solution.py:27
  234.0 3.9 %collective-permute-start.29 = (f32[2,256]{1,0:T(2,128)S(1)}, f32[2,256]{1,0:T(2,128)S(1)}, u32[]{:S(2)}, u32[]{:S(2)}) collective-permute-start(f32[2,256]{1,0:T(2,128)S(1)} %pad_maximum_fusion.19), channel_id=1, source_target_pairs={{0,128},{4,132},{8,136},{12,140},{16,144},{20,148},{24,152},{28,15... | collective-permute-start | bytes 6152 | tf_op jit(solution)/shard_map/ppermute | solution.py:27
  237.9 2.5 collective-permute-done.29
  240.4 6.5 %collective-permute-start.30 = (f32[2,256]{1,0:T(2,128)S(1)}, f32[2,256]{1,0:T(2,128)S(1)}, u32[]{:S(2)}, u32[]{:S(2)}) collective-permute-start(f32[2,256]{1,0:T(2,128)S(1)} %pad_maximum_fusion.20), channel_id=1, source_target_pairs={{0,256},{4,260},{8,264},{12,268},{16,272},{20,276},{24,280},{28,28... | collective-permute-start | bytes 6152 | tf_op jit(solution)/shard_map/ppermute | solution.py:27
  246.9 2.9 %collective-permute-done.30 = f32[2,256]{1,0:T(2,128)S(1)} collective-permute-done((f32[2,256]{1,0:T(2,128)S(1)}, f32[2,256]{1,0:T(2,128)S(1)}, u32[]{:S(2)}, u32[]{:S(2)}) %collective-permute-start.30) | collective-permute-done | bytes 2080 | tf_op jit(solution)/shard_map/ppermute | solution.py:27
  249.8 3.7 %collective-permute-start.31 = (f32[2,256]{1,0:T(2,128)S(1)}, f32[2,256]{1,0:T(2,128)S(1)}, u32[]{:S(2)}, u32[]{:S(2)}) collective-permute-start(f32[2,256]{1,0:T(2,128)S(1)} %pad_maximum_fusion.21), channel_id=1, source_target_pairs={{0,1},{1,0},{2,3},{3,2},{4,5},{5,4},{6,7},{7,6},{8,9},{9,8},{10,11... | collective-permute-start | bytes 6152 | tf_op jit(solution)/shard_map/ppermute | solution.py:27
  255.3 3.2 %collective-permute-start.32 = (f32[2,256]{1,0:T(2,128)S(1)}, f32[2,256]{1,0:T(2,128)S(1)}, u32[]{:S(2)}, u32[]{:S(2)}) collective-permute-start(f32[2,256]{1,0:T(2,128)S(1)} %pad_maximum_fusion.22), channel_id=1, source_target_pairs={{0,2},{1,3},{2,0},{3,1},{4,6},{5,7},{6,4},{7,5},{8,10},{9,11},{10,... | collective-permute-start | bytes 6152 | tf_op jit(solution)/shard_map/ppermute | solution.py:27
  258.5 3.8 %collective-permute-done.32 = f32[2,256]{1,0:T(2,128)S(1)} collective-permute-done((f32[2,256]{1,0:T(2,128)S(1)}, f32[2,256]{1,0:T(2,128)S(1)}, u32[]{:S(2)}, u32[]{:S(2)}) %collective-permute-start.32) | collective-permute-done | bytes 2080 | tf_op jit(solution)/shard_map/ppermute | solution.py:27
  (206 shorter events, 52.8 us)
Async XLA Ops:
  0.0 1.5 copy-start
  0.7 0.7 copy-start.5
  4.7 1.2 copy-start.4
  7.0 5.1 %collective-permute-start.12 = (f32[512,128]{1,0:T(8,128)}, f32[512,128]{1,0:T(8,128)}, u32[]{:S(2)}, u32[]{:S(2)}) collective-permute-start(f32[512,128]{1,0:T(8,128)} %constant_dynamic-slice_fusion.2), channel_id=1, source_target_pairs={{0,4},{4,0},{8,12},{12,8},{16,20},{20,16},{24,28},{28,24},{32,36},... | collective-permute-start | bytes 786440 | tf_op jit(solution)/shard_map/ppermute | solution.py:27
  9.5 7.1 %collective-permute-start = (f32[640,128]{0,1:T(8,128)S(1)}, f32[640,128]{0,1:T(8,128)S(1)}, u32[]{:S(2)}, u32[]{:S(2)}) collective-permute-start(f32[640,128]{0,1:T(8,128)S(1)} %constant_dynamic-slice_fusion.5), channel_id=1, source_target_pairs={{0,4},{4,0},{8,12},{12,8},{16,20},{20,16},{24,28},{28,24},{32,36},... | collective-permute-start | bytes 983048 | tf_op jit(solution)/shard_map/ppermute | solution.py:27
  13.0 8.0 %collective-permute-start.13 = (f32[256,128]{1,0:T(8,128)S(1)}, f32[256,128]{1,0:T(8,128)S(1)}, u32[]{:S(2)}, u32[]{:S(2)}) collective-permute-start(f32[256,128]{1,0:T(8,128)S(1)} %constant_dynamic-slice_fusion.1), channel_id=1, source_target_pairs={{0,64},{4,68},{8,72},{12,76},{16,80},{20,84},{24,88},{28,92},{32,9... | collective-permute-start | bytes 393224 | tf_op jit(solution)/shard_map/ppermute | solution.py:27
  16.7 9.1 %collective-permute-start.1 = (f32[320,128]{0,1:T(8,128)S(1)}, f32[320,128]{0,1:T(8,128)S(1)}, u32[]{:S(2)}, u32[]{:S(2)}) collective-permute-start(f32[320,128]{0,1:T(8,128)S(1)} %constant_dynamic-slice_fusion.4), channel_id=1, source_target_pairs={{0,8},{4,12},{8,0},{12,4},{16,24},{20,28},{24,16},{28,20},{32,40},... | collective-permute-start | bytes 491528 | tf_op jit(solution)/shard_map/ppermute | solution.py:27
  26.0 11.7 %collective-permute-start.2 = (f32[160,128]{0,1:T(8,128)S(1)}, f32[160,128]{0,1:T(8,128)S(1)}, u32[]{:S(2)}, u32[]{:S(2)}) collective-permute-start(f32[160,128]{0,1:T(8,128)S(1)} %constant_dynamic-slice_fusion.3), channel_id=1, source_target_pairs={{0,16},{4,20},{8,24},{12,28},{16,0},{20,4},{24,8},{28,12},{32,48},... | collective-permute-start | bytes 245768 | tf_op jit(solution)/shard_map/ppermute | solution.py:27
  32.2 14.1 %collective-permute-start.14 = (f32[128,128]{1,0:T(8,128)S(1)}, f32[128,128]{1,0:T(8,128)S(1)}, u32[]{:S(2)}, u32[]{:S(2)}) collective-permute-start(f32[128,128]{1,0:T(8,128)S(1)} %constant_dynamic-slice_fusion), channel_id=1, source_target_pairs={{0,128},{4,132},{8,136},{12,140},{16,144},{20,148},{24,152},{28,15... | collective-permute-start | bytes 196616 | tf_op jit(solution)/shard_map/ppermute | solution.py:27
  37.9 15.3 %collective-permute-start.3 = (f32[160,128]{0,1:T(8,128)S(1)}, f32[160,128]{0,1:T(8,128)S(1)}, u32[]{:S(2)}, u32[]{:S(2)}) collective-permute-start(f32[160,128]{0,1:T(8,128)S(1)} %dynamic-slice_add_fusion.4), channel_id=1, source_target_pairs={{0,32},{4,36},{8,40},{12,44},{16,48},{20,52},{24,56},{28,60},{32,0... | collective-permute-start | bytes 245768 | tf_op jit(solution)/shard_map/ppermute | solution.py:27
  46.3 10.2 %collective-permute-start.15 = (f32[128,128]{1,0:T(8,128)S(1)}, f32[128,128]{1,0:T(8,128)S(1)}, u32[]{:S(2)}, u32[]{:S(2)}) collective-permute-start(f32[128,128]{1,0:T(8,128)S(1)} %dynamic-slice_add_fusion.5), channel_id=1, source_target_pairs={{0,256},{4,260},{8,264},{12,268},{16,272},{20,276},{24,280},{28,28... | collective-permute-start | bytes 196616 | tf_op jit(solution)/shard_map/ppermute | solution.py:27
  53.2 7.0 %collective-permute-start.4 = (f32[160,128]{0,1:T(8,128)S(1)}, f32[160,128]{0,1:T(8,128)S(1)}, u32[]{:S(2)}, u32[]{:S(2)}) collective-permute-start(f32[160,128]{0,1:T(8,128)S(1)} %add.322), channel_id=1, source_target_pairs={{0,64},{4,68},{8,72},{12,76},{16,80},{20,84},{24,88},{28,92},{32,9... | collective-permute-start | bytes 245768 | tf_op jit(solution)/shard_map/ppermute | solution.py:27
  56.6 7.9 %collective-permute-start.16 = (f32[128,128]{1,0:T(8,128)S(1)}, f32[128,128]{1,0:T(8,128)S(1)}, u32[]{:S(2)}, u32[]{:S(2)}) collective-permute-start(f32[128,128]{1,0:T(8,128)S(1)} %add.349), channel_id=1, source_target_pairs={{0,8},{4,12},{8,0},{12,4},{16,24},{20,28},{24,16},{28,20},{32,40},... | collective-permute-start | bytes 196616 | tf_op jit(solution)/shard_map/ppermute | solution.py:27
  60.3 16.4 %collective-permute-start.5 = (f32[160,128]{0,1:T(8,128)S(1)}, f32[160,128]{0,1:T(8,128)S(1)}, u32[]{:S(2)}, u32[]{:S(2)}) collective-permute-start(f32[160,128]{0,1:T(8,128)S(1)} %add.323), channel_id=1, source_target_pairs={{0,128},{4,132},{8,136},{12,140},{16,144},{20,148},{24,152},{28,15... | collective-permute-start | bytes 245768 | tf_op jit(solution)/shard_map/ppermute | solution.py:27
  64.5 8.3 %collective-permute-start.17 = (f32[128,128]{1,0:T(8,128)S(1)}, f32[128,128]{1,0:T(8,128)S(1)}, u32[]{:S(2)}, u32[]{:S(2)}) collective-permute-start(f32[128,128]{1,0:T(8,128)S(1)} %add.350), channel_id=1, source_target_pairs={{0,16},{4,20},{8,24},{12,28},{16,0},{20,4},{24,8},{28,12},{32,48},... | collective-permute-start | bytes 196616 | tf_op jit(solution)/shard_map/ppermute | solution.py:27
  72.9 10.1 %collective-permute-start.18 = (f32[128,128]{1,0:T(8,128)S(1)}, f32[128,128]{1,0:T(8,128)S(1)}, u32[]{:S(2)}, u32[]{:S(2)}) collective-permute-start(f32[128,128]{1,0:T(8,128)S(1)} %add.351), channel_id=1, source_target_pairs={{0,32},{4,36},{8,40},{12,44},{16,48},{20,52},{24,56},{28,60},{32,0... | collective-permute-start | bytes 196616 | tf_op jit(solution)/shard_map/ppermute | solution.py:27
  76.7 10.8 %collective-permute-start.6 = (f32[160,128]{0,1:T(8,128)S(1)}, f32[160,128]{0,1:T(8,128)S(1)}, u32[]{:S(2)}, u32[]{:S(2)}) collective-permute-start(f32[160,128]{0,1:T(8,128)S(1)} %add.324), channel_id=1, source_target_pairs={{0,256},{4,260},{8,264},{12,268},{16,272},{20,276},{24,280},{28,28... | collective-permute-start | bytes 245768 | tf_op jit(solution)/shard_map/ppermute | solution.py:27
  83.0 6.7 %collective-permute-start.19 = (f32[128,128]{1,0:T(8,128)S(1)}, f32[128,128]{1,0:T(8,128)S(1)}, u32[]{:S(2)}, u32[]{:S(2)}) collective-permute-start(f32[128,128]{1,0:T(8,128)S(1)} %add.352), channel_id=1, source_target_pairs={{0,1},{1,0},{2,3},{3,2},{4,5},{5,4},{6,7},{7,6},{8,9},{9,8},{10,11... | collective-permute-start | bytes 196616 | tf_op jit(solution)/shard_map/ppermute | solution.py:27
  87.5 7.5 %collective-permute-start.7 = (f32[160,128]{0,1:T(8,128)S(1)}, f32[160,128]{0,1:T(8,128)S(1)}, u32[]{:S(2)}, u32[]{:S(2)}) collective-permute-start(f32[160,128]{0,1:T(8,128)S(1)} %add.325), channel_id=1, source_target_pairs={{0,1},{1,0},{2,3},{3,2},{4,5},{5,4},{6,7},{7,6},{8,9},{9,8},{10,11... | collective-permute-start | bytes 245768 | tf_op jit(solution)/shard_map/ppermute | solution.py:27
  89.8 7.7 %collective-permute-start.20 = (f32[128,128]{1,0:T(8,128)S(1)}, f32[128,128]{1,0:T(8,128)S(1)}, u32[]{:S(2)}, u32[]{:S(2)}) collective-permute-start(f32[128,128]{1,0:T(8,128)S(1)} %add.353), channel_id=1, source_target_pairs={{0,2},{1,3},{2,0},{3,1},{4,6},{5,7},{6,4},{7,5},{8,10},{9,11},{10,... | collective-permute-start | bytes 196616 | tf_op jit(solution)/shard_map/ppermute | solution.py:27
  95.0 8.4 %collective-permute-start.8 = (f32[160,128]{0,1:T(8,128)S(1)}, f32[160,128]{0,1:T(8,128)S(1)}, u32[]{:S(2)}, u32[]{:S(2)}) collective-permute-start(f32[160,128]{0,1:T(8,128)S(1)} %add.326), channel_id=1, source_target_pairs={{0,2},{1,3},{2,0},{3,1},{4,6},{5,7},{6,4},{7,5},{8,10},{9,11},{10,... | collective-permute-start | bytes 245768 | tf_op jit(solution)/shard_map/ppermute | solution.py:27
  97.5 9.9 %collective-permute-start.21 = (f32[128,128]{1,0:T(8,128)S(1)}, f32[128,128]{1,0:T(8,128)S(1)}, u32[]{:S(2)}, u32[]{:S(2)}) collective-permute-start(f32[128,128]{1,0:T(8,128)S(1)} %add.354), channel_id=1, source_target_pairs={{0,128},{4,132},{8,136},{12,140},{16,144},{20,148},{24,152},{28,15... | collective-permute-start | bytes 196616 | tf_op jit(solution)/shard_map/ppermute | solution.py:27
  103.3 8.3 %collective-permute-start.9 = (f32[160,128]{0,1:T(8,128)S(1)}, f32[160,128]{0,1:T(8,128)S(1)}, u32[]{:S(2)}, u32[]{:S(2)}) collective-permute-start(f32[160,128]{0,1:T(8,128)S(1)} %add.327), channel_id=1, source_target_pairs={{0,16},{4,20},{8,24},{12,28},{16,0},{20,4},{24,8},{28,12},{32,48},... | collective-permute-start | bytes 245768 | tf_op jit(solution)/shard_map/ppermute | solution.py:27
  107.4 7.8 %collective-permute-start.22 = (f32[256,128]{1,0:T(8,128)S(1)}, f32[256,128]{1,0:T(8,128)S(1)}, u32[]{:S(2)}, u32[]{:S(2)}) collective-permute-start(f32[256,128]{1,0:T(8,128)S(1)} %maximum_select_fusion.5), channel_id=1, source_target_pairs={{0,64},{4,68},{8,72},{12,76},{16,80},{20,84},{24,88},{28,92},{32,9... | collective-permute-start | bytes 393224 | tf_op jit(solution)/shard_map/ppermute | solution.py:27
  111.8 7.6 %collective-permute-start.10 = (f32[320,128]{0,1:T(8,128)S(1)}, f32[320,128]{0,1:T(8,128)S(1)}, u32[]{:S(2)}, u32[]{:S(2)}) collective-permute-start(f32[320,128]{0,1:T(8,128)S(1)} %maximum_select_fusion.4), channel_id=1, source_target_pairs={{0,8},{4,12},{8,0},{12,4},{16,24},{20,28},{24,16},{28,20},{32,40},... | collective-permute-start | bytes 491528 | tf_op jit(solution)/shard_map/ppermute | solution.py:27
  115.2 6.4 %collective-permute-start.23 = (f32[512,128]{1,0:T(8,128)S(1)}, f32[512,128]{1,0:T(8,128)S(1)}, u32[]{:S(2)}, u32[]{:S(2)}) collective-permute-start(f32[512,128]{1,0:T(8,128)S(1)} %maximum_select_fusion.3), channel_id=1, source_target_pairs={{0,4},{4,0},{8,12},{12,8},{16,20},{20,16},{24,28},{28,24},{32,36},... | collective-permute-start | bytes 786440 | tf_op jit(solution)/shard_map/ppermute | solution.py:27
  119.5 4.3 %collective-permute-start.11 = (f32[640,128]{0,1:T(8,128)S(1)}, f32[640,128]{0,1:T(8,128)S(1)}, u32[]{:S(2)}, u32[]{:S(2)}) collective-permute-start(f32[640,128]{0,1:T(8,128)S(1)} %maximum_select_fusion.2), channel_id=1, source_target_pairs={{0,4},{4,0},{8,12},{12,8},{16,20},{20,16},{24,28},{28,24},{32,36},... | collective-permute-start | bytes 983048 | tf_op jit(solution)/shard_map/ppermute | solution.py:27
  196.7 0.9 copy-start.3
  198.1 0.9 copy-start.2
  199.3 0.9 copy-start.1
  203.9 3.2 %collective-permute-start.24 = (f32[2,256]{1,0:T(2,128)S(1)}, f32[2,256]{1,0:T(2,128)S(1)}, u32[]{:S(2)}, u32[]{:S(2)}) collective-permute-start(f32[2,256]{1,0:T(2,128)S(1)} %pad_maximum_fusion.14), channel_id=1, source_target_pairs={{0,4},{4,0},{8,12},{12,8},{16,20},{20,16},{24,28},{28,24},{32,36},... | collective-permute-start | bytes 6152 | tf_op jit(solution)/shard_map/ppermute | solution.py:27
  207.1 5.5 %collective-permute-start.25 = (f32[2,256]{1,0:T(2,128)S(1)}, f32[2,256]{1,0:T(2,128)S(1)}, u32[]{:S(2)}, u32[]{:S(2)}) collective-permute-start(f32[2,256]{1,0:T(2,128)S(1)} %pad_maximum_fusion.15), channel_id=1, source_target_pairs={{0,8},{4,12},{8,0},{12,4},{16,24},{20,28},{24,16},{28,20},{32,40},... | collective-permute-start | bytes 6152 | tf_op jit(solution)/shard_map/ppermute | solution.py:27
  212.6 6.4 %collective-permute-start.26 = (f32[2,256]{1,0:T(2,128)S(1)}, f32[2,256]{1,0:T(2,128)S(1)}, u32[]{:S(2)}, u32[]{:S(2)}) collective-permute-start(f32[2,256]{1,0:T(2,128)S(1)} %pad_maximum_fusion.16), channel_id=1, source_target_pairs={{0,16},{4,20},{8,24},{12,28},{16,0},{20,4},{24,8},{28,12},{32,48},... | collective-permute-start | bytes 6152 | tf_op jit(solution)/shard_map/ppermute | solution.py:27
  219.0 9.4 %collective-permute-start.27 = (f32[2,256]{1,0:T(2,128)S(1)}, f32[2,256]{1,0:T(2,128)S(1)}, u32[]{:S(2)}, u32[]{:S(2)}) collective-permute-start(f32[2,256]{1,0:T(2,128)S(1)} %pad_maximum_fusion.17), channel_id=1, source_target_pairs={{0,32},{4,36},{8,40},{12,44},{16,48},{20,52},{24,56},{28,60},{32,0... | collective-permute-start | bytes 6152 | tf_op jit(solution)/shard_map/ppermute | solution.py:27
  228.5 5.5 %collective-permute-start.28 = (f32[2,256]{1,0:T(2,128)S(1)}, f32[2,256]{1,0:T(2,128)S(1)}, u32[]{:S(2)}, u32[]{:S(2)}) collective-permute-start(f32[2,256]{1,0:T(2,128)S(1)} %pad_maximum_fusion.18), channel_id=1, source_target_pairs={{0,64},{4,68},{8,72},{12,76},{16,80},{20,84},{24,88},{28,92},{32,9... | collective-permute-start | bytes 6152 | tf_op jit(solution)/shard_map/ppermute | solution.py:27
  234.0 6.4 %collective-permute-start.29 = (f32[2,256]{1,0:T(2,128)S(1)}, f32[2,256]{1,0:T(2,128)S(1)}, u32[]{:S(2)}, u32[]{:S(2)}) collective-permute-start(f32[2,256]{1,0:T(2,128)S(1)} %pad_maximum_fusion.19), channel_id=1, source_target_pairs={{0,128},{4,132},{8,136},{12,140},{16,144},{20,148},{24,152},{28,15... | collective-permute-start | bytes 6152 | tf_op jit(solution)/shard_map/ppermute | solution.py:27
  240.4 9.4 %collective-permute-start.30 = (f32[2,256]{1,0:T(2,128)S(1)}, f32[2,256]{1,0:T(2,128)S(1)}, u32[]{:S(2)}, u32[]{:S(2)}) collective-permute-start(f32[2,256]{1,0:T(2,128)S(1)} %pad_maximum_fusion.20), channel_id=1, source_target_pairs={{0,256},{4,260},{8,264},{12,268},{16,272},{20,276},{24,280},{28,28... | collective-permute-start | bytes 6152 | tf_op jit(solution)/shard_map/ppermute | solution.py:27
  249.8 5.5 %collective-permute-start.31 = (f32[2,256]{1,0:T(2,128)S(1)}, f32[2,256]{1,0:T(2,128)S(1)}, u32[]{:S(2)}, u32[]{:S(2)}) collective-permute-start(f32[2,256]{1,0:T(2,128)S(1)} %pad_maximum_fusion.21), channel_id=1, source_target_pairs={{0,1},{1,0},{2,3},{3,2},{4,5},{5,4},{6,7},{7,6},{8,9},{9,8},{10,11... | collective-permute-start | bytes 6152 | tf_op jit(solution)/shard_map/ppermute | solution.py:27
  255.3 7.0 %collective-permute-start.32 = (f32[2,256]{1,0:T(2,128)S(1)}, f32[2,256]{1,0:T(2,128)S(1)}, u32[]{:S(2)}, u32[]{:S(2)}) collective-permute-start(f32[2,256]{1,0:T(2,128)S(1)} %pad_maximum_fusion.22), channel_id=1, source_target_pairs={{0,2},{1,3},{2,0},{3,1},{4,6},{5,7},{6,4},{7,5},{8,10},{9,11},{10,... | collective-permute-start | bytes 6152 | tf_op jit(solution)/shard_map/ppermute | solution.py:27

commit v8 on v7

--- a/solution.py
+++ b/solution.py
@@ -57,8 +57,8 @@
 
 def triangular_inverse(lower):
     size = lower.shape[0]
-    pivots = jnp.diagonal(lower)
     eye = jnp.eye(size, dtype=lower.dtype)
+    pivots = jnp.sum(lower * eye, axis=1)
     power = eye - lower / pivots[:, None]
     product = eye + power
     reach = 2

time: 266 us -> 262 us (0.985)
  local copies, waits for them, and re-layouts: 14 us -> 9.21 us
    gather x4 -> x0, local copies, waits for them, and re-layouts: 5.46 us -> none  [triangular_inverse(): pivots = jnp.diagonal(lower)]
    reduce_sum x0 -> x4, other arithmetic: none -> 2.92 us  [triangular_inverse(): pivots = jnp.sum(lower * eye, axis=1)]
  transfers between devices with their start and end apart: 33 -> 33, of which waited for: 21 -> 20; matrix products, arithmetic and copies ran while one was open for 2% -> 1% of each run, Pallas kernels for 0% -> 0%
where the time goes in v8:
time: 262 us; the launch traced here: 260 us
  starting transfers between devices  129 us (49%)
  other arithmetic  56.4 us (22%)
  waiting for transfers between devices  40.2 us (15%)
  matrix products  22.8 us (9%)
  local copies, waits for them, and re-layouts  9.21 us (4%)
  between operations  2.97 us (1%)
    ppermute x33, starting transfers between devices, partner(): return lax.ppermute(x, name, [(i, i ^ mask) for i in range(size)])  129 us
    another operation x12, other arithmetic, blocked_cholesky(): head = lax.linalg.cholesky(trailing[:block, :block], symmetrize_input=False)  49.7 us
    ppermute x33, waiting for transfers between devices, partner(): return lax.ppermute(x, name, [(i, i ^ mask) for i in range(size)])  40.2 us
    dot_general x24, matrix products, triangular_inverse(): product = jnp.dot(product, eye + power, precision=HIGHEST)  6.05 us
    dot_general x24, matrix products, triangular_inverse(): power = jnp.dot(power, power, precision=HIGHEST)  5.86 us
  transfers between devices with their start and end apart: 33, of which 20 were waited for; matrix products, arithmetic and copies ran while one was open for 1% of the time, Pallas kernels for 0%

profile of v8, /device:TPU:6, one launch (start us, length us, event | category | flops | bytes accessed | tf_op | source)
XLA Modules:
  0.0 260.5 jit_solution(604955775612842401)
XLA Ops:
  1.5 3.3 %fusion.1 = bf16[256,512]{1,0:T(8,128)(2,1)S(1)} fusion(bf16[256,1024]{1,0:T(8,128)(2,1)} %param.7, bf16[1024,512]{1,0:T(8,128)(2,1)S(1)} %copy-done, f32[512]{0:T(512)S(1)} %fusion.78), kind=kOutput, calls=%fused_computation.4 | convolution fusion | flops 268697600 | bytes 1837056 | tf_op jit(solution)/shard_map/dot_general | solution.py:119
  7.0 1.9 collective-permute-start.12
  9.4 2.4 collective-permute-start
  13.0 3.5 %collective-permute-start.13 = (f32[256,128]{1,0:T(8,128)S(1)}, f32[256,128]{1,0:T(8,128)S(1)}, u32[]{:S(2)}, u32[]{:S(2)}) collective-permute-start(f32[256,128]{1,0:T(8,128)S(1)} %constant_dynamic-slice_fusion.1), channel_id=1, source_target_pairs={{0,64},{4,68},{8,72},{12,76},{16,80},{20,84},{24,88},{28,92},{32,9... | collective-permute-start | bytes 393224 | tf_op jit(solution)/shard_map/ppermute | solution.py:27
  16.7 4.3 %collective-permute-start.1 = (f32[320,128]{0,1:T(8,128)S(1)}, f32[320,128]{0,1:T(8,128)S(1)}, u32[]{:S(2)}, u32[]{:S(2)}) collective-permute-start(f32[320,128]{0,1:T(8,128)S(1)} %constant_dynamic-slice_fusion.4), channel_id=1, source_target_pairs={{0,8},{4,12},{8,0},{12,4},{16,24},{20,28},{24,16},{28,20},{32,40},... | collective-permute-start | bytes 491528 | tf_op jit(solution)/shard_map/ppermute | solution.py:27
  21.1 4.7 %collective-permute-done.1 = f32[320,128]{0,1:T(8,128)S(1)} collective-permute-done((f32[320,128]{0,1:T(8,128)S(1)}, f32[320,128]{0,1:T(8,128)S(1)}, u32[]{:S(2)}, u32[]{:S(2)}) %collective-permute-start.1) | collective-permute-done | bytes 163872 | tf_op jit(solution)/shard_map/ppermute | solution.py:27
  26.0 6.1 %collective-permute-start.2 = (f32[160,128]{0,1:T(8,128)S(1)}, f32[160,128]{0,1:T(8,128)S(1)}, u32[]{:S(2)}, u32[]{:S(2)}) collective-permute-start(f32[160,128]{0,1:T(8,128)S(1)} %constant_dynamic-slice_fusion.3), channel_id=1, source_target_pairs={{0,16},{4,20},{8,24},{12,28},{16,0},{20,4},{24,8},{28,12},{32,48},... | collective-permute-start | bytes 245768 | tf_op jit(solution)/shard_map/ppermute | solution.py:27
  32.2 4.5 %collective-permute-start.14 = (f32[128,128]{1,0:T(8,128)S(1)}, f32[128,128]{1,0:T(8,128)S(1)}, u32[]{:S(2)}, u32[]{:S(2)}) collective-permute-start(f32[128,128]{1,0:T(8,128)S(1)} %constant_dynamic-slice_fusion), channel_id=1, source_target_pairs={{0,128},{4,132},{8,136},{12,140},{16,144},{20,148},{24,152},{28,15... | collective-permute-start | bytes 196616 | tf_op jit(solution)/shard_map/ppermute | solution.py:27
  37.9 8.4 %collective-permute-start.3 = (f32[160,128]{0,1:T(8,128)S(1)}, f32[160,128]{0,1:T(8,128)S(1)}, u32[]{:S(2)}, u32[]{:S(2)}) collective-permute-start(f32[160,128]{0,1:T(8,128)S(1)} %dynamic-slice_add_fusion.4), channel_id=1, source_target_pairs={{0,32},{4,36},{8,40},{12,44},{16,48},{20,52},{24,56},{28,60},{32,0... | collective-permute-start | bytes 245768 | tf_op jit(solution)/shard_map/ppermute | solution.py:27
  46.3 6.8 %collective-permute-start.15 = (f32[128,128]{1,0:T(8,128)S(1)}, f32[128,128]{1,0:T(8,128)S(1)}, u32[]{:S(2)}, u32[]{:S(2)}) collective-permute-start(f32[128,128]{1,0:T(8,128)S(1)} %dynamic-slice_add_fusion.5), channel_id=1, source_target_pairs={{0,256},{4,260},{8,264},{12,268},{16,272},{20,276},{24,280},{28,28... | collective-permute-start | bytes 196616 | tf_op jit(solution)/shard_map/ppermute | solution.py:27
  53.2 3.3 %collective-permute-start.4 = (f32[160,128]{0,1:T(8,128)S(1)}, f32[160,128]{0,1:T(8,128)S(1)}, u32[]{:S(2)}, u32[]{:S(2)}) collective-permute-start(f32[160,128]{0,1:T(8,128)S(1)} %add.312), channel_id=1, source_target_pairs={{0,64},{4,68},{8,72},{12,76},{16,80},{20,84},{24,88},{28,92},{32,9... | collective-permute-start | bytes 245768 | tf_op jit(solution)/shard_map/ppermute | solution.py:27
  56.6 2.3 collective-permute-start.16
  60.3 4.2 %collective-permute-start.5 = (f32[160,128]{0,1:T(8,128)S(1)}, f32[160,128]{0,1:T(8,128)S(1)}, u32[]{:S(2)}, u32[]{:S(2)}) collective-permute-start(f32[160,128]{0,1:T(8,128)S(1)} %add.313), channel_id=1, source_target_pairs={{0,128},{4,132},{8,136},{12,140},{16,144},{20,148},{24,152},{28,15... | collective-permute-start | bytes 245768 | tf_op jit(solution)/shard_map/ppermute | solution.py:27
  64.5 5.4 %collective-permute-start.17 = (f32[128,128]{1,0:T(8,128)S(1)}, f32[128,128]{1,0:T(8,128)S(1)}, u32[]{:S(2)}, u32[]{:S(2)}) collective-permute-start(f32[128,128]{1,0:T(8,128)S(1)} %add.340), channel_id=1, source_target_pairs={{0,16},{4,20},{8,24},{12,28},{16,0},{20,4},{24,8},{28,12},{32,48},... | collective-permute-start | bytes 196616 | tf_op jit(solution)/shard_map/ppermute | solution.py:27
  69.9 2.9 %collective-permute-done.17 = f32[128,128]{1,0:T(8,128)S(1)} collective-permute-done((f32[128,128]{1,0:T(8,128)S(1)}, f32[128,128]{1,0:T(8,128)S(1)}, u32[]{:S(2)}, u32[]{:S(2)}) %collective-permute-start.17) | collective-permute-done | bytes 65568 | tf_op jit(solution)/shard_map/ppermute | solution.py:27
  72.9 3.8 %collective-permute-start.18 = (f32[128,128]{1,0:T(8,128)S(1)}, f32[128,128]{1,0:T(8,128)S(1)}, u32[]{:S(2)}, u32[]{:S(2)}) collective-permute-start(f32[128,128]{1,0:T(8,128)S(1)} %add.341), channel_id=1, source_target_pairs={{0,32},{4,36},{8,40},{12,44},{16,48},{20,52},{24,56},{28,60},{32,0... | collective-permute-start | bytes 196616 | tf_op jit(solution)/shard_map/ppermute | solution.py:27
  76.7 4.4 %collective-permute-start.6 = (f32[160,128]{0,1:T(8,128)S(1)}, f32[160,128]{0,1:T(8,128)S(1)}, u32[]{:S(2)}, u32[]{:S(2)}) collective-permute-start(f32[160,128]{0,1:T(8,128)S(1)} %add.314), channel_id=1, source_target_pairs={{0,256},{4,260},{8,264},{12,268},{16,272},{20,276},{24,280},{28,28... | collective-permute-start | bytes 245768 | tf_op jit(solution)/shard_map/ppermute | solution.py:27
  83.0 3.2 %collective-permute-start.19 = (f32[128,128]{1,0:T(8,128)S(1)}, f32[128,128]{1,0:T(8,128)S(1)}, u32[]{:S(2)}, u32[]{:S(2)}) collective-permute-start(f32[128,128]{1,0:T(8,128)S(1)} %add.342), channel_id=1, source_target_pairs={{0,1},{1,0},{2,3},{3,2},{4,5},{5,4},{6,7},{7,6},{8,9},{9,8},{10,11... | collective-permute-start | bytes 196616 | tf_op jit(solution)/shard_map/ppermute | solution.py:27
  87.5 1.9 collective-permute-start.7
  89.4 3.5 %collective-permute-start.20 = (f32[128,128]{1,0:T(8,128)S(1)}, f32[128,128]{1,0:T(8,128)S(1)}, u32[]{:S(2)}, u32[]{:S(2)}) collective-permute-start(f32[128,128]{1,0:T(8,128)S(1)} %add.343), channel_id=1, source_target_pairs={{0,2},{1,3},{2,0},{3,1},{4,6},{5,7},{6,4},{7,5},{8,10},{9,11},{10,... | collective-permute-start | bytes 196616 | tf_op jit(solution)/shard_map/ppermute | solution.py:27
  92.9 2.0 collective-permute-done.7
  94.9 2.5 collective-permute-start.8
  97.4 3.3 %collective-permute-start.21 = (f32[128,128]{1,0:T(8,128)S(1)}, f32[128,128]{1,0:T(8,128)S(1)}, u32[]{:S(2)}, u32[]{:S(2)}) collective-permute-start(f32[128,128]{1,0:T(8,128)S(1)} %add.344), channel_id=1, source_target_pairs={{0,128},{4,132},{8,136},{12,140},{16,144},{20,148},{24,152},{28,15... | collective-permute-start | bytes 196616 | tf_op jit(solution)/shard_map/ppermute | solution.py:27
  100.8 2.5 collective-permute-done.8
  103.3 4.0 %collective-permute-start.9 = (f32[160,128]{0,1:T(8,128)S(1)}, f32[160,128]{0,1:T(8,128)S(1)}, u32[]{:S(2)}, u32[]{:S(2)}) collective-permute-start(f32[160,128]{0,1:T(8,128)S(1)} %add.317), channel_id=1, source_target_pairs={{0,16},{4,20},{8,24},{12,28},{16,0},{20,4},{24,8},{28,12},{32,48},... | collective-permute-start | bytes 245768 | tf_op jit(solution)/shard_map/ppermute | solution.py:27
  107.4 4.1 %collective-permute-start.22 = (f32[256,128]{1,0:T(8,128)S(1)}, f32[256,128]{1,0:T(8,128)S(1)}, u32[]{:S(2)}, u32[]{:S(2)}) collective-permute-start(f32[256,128]{1,0:T(8,128)S(1)} %maximum_select_fusion.5), channel_id=1, source_target_pairs={{0,64},{4,68},{8,72},{12,76},{16,80},{20,84},{24,88},{28,92},{32,9... | collective-permute-start | bytes 393224 | tf_op jit(solution)/shard_map/ppermute | solution.py:27
  111.7 3.4 %collective-permute-start.10 = (f32[320,128]{0,1:T(8,128)S(1)}, f32[320,128]{0,1:T(8,128)S(1)}, u32[]{:S(2)}, u32[]{:S(2)}) collective-permute-start(f32[320,128]{0,1:T(8,128)S(1)} %maximum_select_fusion.4), channel_id=1, source_target_pairs={{0,8},{4,12},{8,0},{12,4},{16,24},{20,28},{24,16},{28,20},{32,40},... | collective-permute-start | bytes 491528 | tf_op jit(solution)/shard_map/ppermute | solution.py:27
  115.2 1.9 collective-permute-start.23
  119.5 2.1 collective-permute-start.11
  127.7 11.7 %custom-call.6 = f32[128,128]{1,0:T(8,128)S(1)} custom-call(f32[128,128]{1,0:T(8,128)S(1)} %slice.271), custom_call_target="Cholesky" | custom-call | tf_op jit(solution)/shard_map/cholesky/custom-call.1 | solution.py:78
  144.5 11.7 %custom-call.7 = f32[128,128]{1,0:T(8,128)S(1)} custom-call(f32[128,128]{1,0:T(8,128)S(1)} %slice.275), custom_call_target="Cholesky" | custom-call | tf_op jit(solution)/shard_map/cholesky/custom-call.1 | solution.py:78
  161.3 11.7 %custom-call.8 = f32[128,128]{1,0:T(8,128)S(1)} custom-call(f32[128,128]{1,0:T(8,128)S(1)} %slice.280), custom_call_target="Cholesky" | custom-call | tf_op jit(solution)/shard_map/cholesky/custom-call.1 | solution.py:78
  177.7 11.7 %custom-call.9 = f32[128,128]{1,0:T(8,128)S(1)} custom-call(f32[128,128]{1,0:T(8,128)S(1)} %convolution_subtract_fusion.5), custom_call_target="Cholesky" | custom-call | tf_op jit(solution)/shard_map/cholesky/custom-call.1 | solution.py:78
  201.2 2.4 collective-permute-start.24
  204.5 3.4 %collective-permute-start.25 = (f32[2,256]{1,0:T(2,128)S(1)}, f32[2,256]{1,0:T(2,128)S(1)}, u32[]{:S(2)}, u32[]{:S(2)}) collective-permute-start(f32[2,256]{1,0:T(2,128)S(1)} %pad_maximum_fusion.15), channel_id=1, source_target_pairs={{0,8},{4,12},{8,0},{12,4},{16,24},{20,28},{24,16},{28,20},{32,40},... | collective-permute-start | bytes 6152 | tf_op jit(solution)/shard_map/ppermute | solution.py:27
  207.9 2.0 collective-permute-done.25
  210.0 3.8 %collective-permute-start.26 = (f32[2,256]{1,0:T(2,128)S(1)}, f32[2,256]{1,0:T(2,128)S(1)}, u32[]{:S(2)}, u32[]{:S(2)}) collective-permute-start(f32[2,256]{1,0:T(2,128)S(1)} %pad_maximum_fusion.16), channel_id=1, source_target_pairs={{0,16},{4,20},{8,24},{12,28},{16,0},{20,4},{24,8},{28,12},{32,48},... | collective-permute-start | bytes 6152 | tf_op jit(solution)/shard_map/ppermute | solution.py:27
  213.8 2.6 collective-permute-done.26
  216.4 8.1 %collective-permute-start.27 = (f32[2,256]{1,0:T(2,128)S(1)}, f32[2,256]{1,0:T(2,128)S(1)}, u32[]{:S(2)}, u32[]{:S(2)}) collective-permute-start(f32[2,256]{1,0:T(2,128)S(1)} %pad_maximum_fusion.17), channel_id=1, source_target_pairs={{0,32},{4,36},{8,40},{12,44},{16,48},{20,52},{24,56},{28,60},{32,0... | collective-permute-start | bytes 6152 | tf_op jit(solution)/shard_map/ppermute | solution.py:27
  226.0 3.6 %collective-permute-start.28 = (f32[2,256]{1,0:T(2,128)S(1)}, f32[2,256]{1,0:T(2,128)S(1)}, u32[]{:S(2)}, u32[]{:S(2)}) collective-permute-start(f32[2,256]{1,0:T(2,128)S(1)} %pad_maximum_fusion.18), channel_id=1, source_target_pairs={{0,64},{4,68},{8,72},{12,76},{16,80},{20,84},{24,88},{28,92},{32,9... | collective-permute-start | bytes 6152 | tf_op jit(solution)/shard_map/ppermute | solution.py:27
  231.5 3.7 %collective-permute-start.29 = (f32[2,256]{1,0:T(2,128)S(1)}, f32[2,256]{1,0:T(2,128)S(1)}, u32[]{:S(2)}, u32[]{:S(2)}) collective-permute-start(f32[2,256]{1,0:T(2,128)S(1)} %pad_maximum_fusion.19), channel_id=1, source_target_pairs={{0,128},{4,132},{8,136},{12,140},{16,144},{20,148},{24,152},{28,15... | collective-permute-start | bytes 6152 | tf_op jit(solution)/shard_map/ppermute | solution.py:27
  235.3 2.7 %collective-permute-done.29 = f32[2,256]{1,0:T(2,128)S(1)} collective-permute-done((f32[2,256]{1,0:T(2,128)S(1)}, f32[2,256]{1,0:T(2,128)S(1)}, u32[]{:S(2)}, u32[]{:S(2)}) %collective-permute-start.29) | collective-permute-done | bytes 2080 | tf_op jit(solution)/shard_map/ppermute | solution.py:27
  237.9 6.3 %collective-permute-start.30 = (f32[2,256]{1,0:T(2,128)S(1)}, f32[2,256]{1,0:T(2,128)S(1)}, u32[]{:S(2)}, u32[]{:S(2)}) collective-permute-start(f32[2,256]{1,0:T(2,128)S(1)} %pad_maximum_fusion.20), channel_id=1, source_target_pairs={{0,256},{4,260},{8,264},{12,268},{16,272},{20,276},{24,280},{28,28... | collective-permute-start | bytes 6152 | tf_op jit(solution)/shard_map/ppermute | solution.py:27
  244.2 3.1 %collective-permute-done.30 = f32[2,256]{1,0:T(2,128)S(1)} collective-permute-done((f32[2,256]{1,0:T(2,128)S(1)}, f32[2,256]{1,0:T(2,128)S(1)}, u32[]{:S(2)}, u32[]{:S(2)}) %collective-permute-start.30) | collective-permute-done | bytes 2080 | tf_op jit(solution)/shard_map/ppermute | solution.py:27
  247.3 3.2 %collective-permute-start.31 = (f32[2,256]{1,0:T(2,128)S(1)}, f32[2,256]{1,0:T(2,128)S(1)}, u32[]{:S(2)}, u32[]{:S(2)}) collective-permute-start(f32[2,256]{1,0:T(2,128)S(1)} %pad_maximum_fusion.21), channel_id=1, source_target_pairs={{0,1},{1,0},{2,3},{3,2},{4,5},{5,4},{6,7},{7,6},{8,9},{9,8},{10,11... | collective-permute-start | bytes 6152 | tf_op jit(solution)/shard_map/ppermute | solution.py:27
  250.5 2.3 collective-permute-done.31
  252.8 3.1 %collective-permute-start.32 = (f32[2,256]{1,0:T(2,128)S(1)}, f32[2,256]{1,0:T(2,128)S(1)}, u32[]{:S(2)}, u32[]{:S(2)}) collective-permute-start(f32[2,256]{1,0:T(2,128)S(1)} %pad_maximum_fusion.22), channel_id=1, source_target_pairs={{0,2},{1,3},{2,0},{3,1},{4,6},{5,7},{6,4},{7,5},{8,10},{9,11},{10,... | collective-permute-start | bytes 6152 | tf_op jit(solution)/shard_map/ppermute | solution.py:27
  255.9 3.9 %collective-permute-done.32 = f32[2,256]{1,0:T(2,128)S(1)} collective-permute-done((f32[2,256]{1,0:T(2,128)S(1)}, f32[2,256]{1,0:T(2,128)S(1)}, u32[]{:S(2)}, u32[]{:S(2)}) %collective-permute-start.32) | collective-permute-done | bytes 2080 | tf_op jit(solution)/shard_map/ppermute | solution.py:27
  (199 shorter events, 49.9 us)
Async XLA Ops:
  0.0 1.5 copy-start
  0.7 0.7 copy-start.4
  4.7 1.2 copy-start.3
  7.0 5.1 %collective-permute-start.12 = (f32[512,128]{1,0:T(8,128)}, f32[512,128]{1,0:T(8,128)}, u32[]{:S(2)}, u32[]{:S(2)}) collective-permute-start(f32[512,128]{1,0:T(8,128)} %constant_dynamic-slice_fusion.2), channel_id=1, source_target_pairs={{0,4},{4,0},{8,12},{12,8},{16,20},{20,16},{24,28},{28,24},{32,36},... | collective-permute-start | bytes 786440 | tf_op jit(solution)/shard_map/ppermute | solution.py:27
  9.4 7.1 %collective-permute-start = (f32[640,128]{0,1:T(8,128)S(1)}, f32[640,128]{0,1:T(8,128)S(1)}, u32[]{:S(2)}, u32[]{:S(2)}) collective-permute-start(f32[640,128]{0,1:T(8,128)S(1)} %constant_dynamic-slice_fusion.5), channel_id=1, source_target_pairs={{0,4},{4,0},{8,12},{12,8},{16,20},{20,16},{24,28},{28,24},{32,36},... | collective-permute-start | bytes 983048 | tf_op jit(solution)/shard_map/ppermute | solution.py:27
  13.0 8.0 %collective-permute-start.13 = (f32[256,128]{1,0:T(8,128)S(1)}, f32[256,128]{1,0:T(8,128)S(1)}, u32[]{:S(2)}, u32[]{:S(2)}) collective-permute-start(f32[256,128]{1,0:T(8,128)S(1)} %constant_dynamic-slice_fusion.1), channel_id=1, source_target_pairs={{0,64},{4,68},{8,72},{12,76},{16,80},{20,84},{24,88},{28,92},{32,9... | collective-permute-start | bytes 393224 | tf_op jit(solution)/shard_map/ppermute | solution.py:27
  16.7 9.1 %collective-permute-start.1 = (f32[320,128]{0,1:T(8,128)S(1)}, f32[320,128]{0,1:T(8,128)S(1)}, u32[]{:S(2)}, u32[]{:S(2)}) collective-permute-start(f32[320,128]{0,1:T(8,128)S(1)} %constant_dynamic-slice_fusion.4), channel_id=1, source_target_pairs={{0,8},{4,12},{8,0},{12,4},{16,24},{20,28},{24,16},{28,20},{32,40},... | collective-permute-start | bytes 491528 | tf_op jit(solution)/shard_map/ppermute | solution.py:27
  26.0 11.7 %collective-permute-start.2 = (f32[160,128]{0,1:T(8,128)S(1)}, f32[160,128]{0,1:T(8,128)S(1)}, u32[]{:S(2)}, u32[]{:S(2)}) collective-permute-start(f32[160,128]{0,1:T(8,128)S(1)} %constant_dynamic-slice_fusion.3), channel_id=1, source_target_pairs={{0,16},{4,20},{8,24},{12,28},{16,0},{20,4},{24,8},{28,12},{32,48},... | collective-permute-start | bytes 245768 | tf_op jit(solution)/shard_map/ppermute | solution.py:27
  32.2 14.1 %collective-permute-start.14 = (f32[128,128]{1,0:T(8,128)S(1)}, f32[128,128]{1,0:T(8,128)S(1)}, u32[]{:S(2)}, u32[]{:S(2)}) collective-permute-start(f32[128,128]{1,0:T(8,128)S(1)} %constant_dynamic-slice_fusion), channel_id=1, source_target_pairs={{0,128},{4,132},{8,136},{12,140},{16,144},{20,148},{24,152},{28,15... | collective-permute-start | bytes 196616 | tf_op jit(solution)/shard_map/ppermute | solution.py:27
  37.9 15.3 %collective-permute-start.3 = (f32[160,128]{0,1:T(8,128)S(1)}, f32[160,128]{0,1:T(8,128)S(1)}, u32[]{:S(2)}, u32[]{:S(2)}) collective-permute-start(f32[160,128]{0,1:T(8,128)S(1)} %dynamic-slice_add_fusion.4), channel_id=1, source_target_pairs={{0,32},{4,36},{8,40},{12,44},{16,48},{20,52},{24,56},{28,60},{32,0... | collective-permute-start | bytes 245768 | tf_op jit(solution)/shard_map/ppermute | solution.py:27
  46.3 10.3 %collective-permute-start.15 = (f32[128,128]{1,0:T(8,128)S(1)}, f32[128,128]{1,0:T(8,128)S(1)}, u32[]{:S(2)}, u32[]{:S(2)}) collective-permute-start(f32[128,128]{1,0:T(8,128)S(1)} %dynamic-slice_add_fusion.5), channel_id=1, source_target_pairs={{0,256},{4,260},{8,264},{12,268},{16,272},{20,276},{24,280},{28,28... | collective-permute-start | bytes 196616 | tf_op jit(solution)/shard_map/ppermute | solution.py:27
  53.2 7.0 %collective-permute-start.4 = (f32[160,128]{0,1:T(8,128)S(1)}, f32[160,128]{0,1:T(8,128)S(1)}, u32[]{:S(2)}, u32[]{:S(2)}) collective-permute-start(f32[160,128]{0,1:T(8,128)S(1)} %add.312), channel_id=1, source_target_pairs={{0,64},{4,68},{8,72},{12,76},{16,80},{20,84},{24,88},{28,92},{32,9... | collective-permute-start | bytes 245768 | tf_op jit(solution)/shard_map/ppermute | solution.py:27
  56.6 7.9 %collective-permute-start.16 = (f32[128,128]{1,0:T(8,128)S(1)}, f32[128,128]{1,0:T(8,128)S(1)}, u32[]{:S(2)}, u32[]{:S(2)}) collective-permute-start(f32[128,128]{1,0:T(8,128)S(1)} %add.339), channel_id=1, source_target_pairs={{0,8},{4,12},{8,0},{12,4},{16,24},{20,28},{24,16},{28,20},{32,40},... | collective-permute-start | bytes 196616 | tf_op jit(solution)/shard_map/ppermute | solution.py:27
  60.3 16.4 %collective-permute-start.5 = (f32[160,128]{0,1:T(8,128)S(1)}, f32[160,128]{0,1:T(8,128)S(1)}, u32[]{:S(2)}, u32[]{:S(2)}) collective-permute-start(f32[160,128]{0,1:T(8,128)S(1)} %add.313), channel_id=1, source_target_pairs={{0,128},{4,132},{8,136},{12,140},{16,144},{20,148},{24,152},{28,15... | collective-permute-start | bytes 245768 | tf_op jit(solution)/shard_map/ppermute | solution.py:27
  64.5 8.3 %collective-permute-start.17 = (f32[128,128]{1,0:T(8,128)S(1)}, f32[128,128]{1,0:T(8,128)S(1)}, u32[]{:S(2)}, u32[]{:S(2)}) collective-permute-start(f32[128,128]{1,0:T(8,128)S(1)} %add.340), channel_id=1, source_target_pairs={{0,16},{4,20},{8,24},{12,28},{16,0},{20,4},{24,8},{28,12},{32,48},... | collective-permute-start | bytes 196616 | tf_op jit(solution)/shard_map/ppermute | solution.py:27
  72.9 10.1 %collective-permute-start.18 = (f32[128,128]{1,0:T(8,128)S(1)}, f32[128,128]{1,0:T(8,128)S(1)}, u32[]{:S(2)}, u32[]{:S(2)}) collective-permute-start(f32[128,128]{1,0:T(8,128)S(1)} %add.341), channel_id=1, source_target_pairs={{0,32},{4,36},{8,40},{12,44},{16,48},{20,52},{24,56},{28,60},{32,0... | collective-permute-start | bytes 196616 | tf_op jit(solution)/shard_map/ppermute | solution.py:27
  76.7 10.8 %collective-permute-start.6 = (f32[160,128]{0,1:T(8,128)S(1)}, f32[160,128]{0,1:T(8,128)S(1)}, u32[]{:S(2)}, u32[]{:S(2)}) collective-permute-start(f32[160,128]{0,1:T(8,128)S(1)} %add.314), channel_id=1, source_target_pairs={{0,256},{4,260},{8,264},{12,268},{16,272},{20,276},{24,280},{28,28... | collective-permute-start | bytes 245768 | tf_op jit(solution)/shard_map/ppermute | solution.py:27
  83.0 6.4 %collective-permute-start.19 = (f32[128,128]{1,0:T(8,128)S(1)}, f32[128,128]{1,0:T(8,128)S(1)}, u32[]{:S(2)}, u32[]{:S(2)}) collective-permute-start(f32[128,128]{1,0:T(8,128)S(1)} %add.342), channel_id=1, source_target_pairs={{0,1},{1,0},{2,3},{3,2},{4,5},{5,4},{6,7},{7,6},{8,9},{9,8},{10,11... | collective-permute-start | bytes 196616 | tf_op jit(solution)/shard_map/ppermute | solution.py:27
  87.5 7.5 %collective-permute-start.7 = (f32[160,128]{0,1:T(8,128)S(1)}, f32[160,128]{0,1:T(8,128)S(1)}, u32[]{:S(2)}, u32[]{:S(2)}) collective-permute-start(f32[160,128]{0,1:T(8,128)S(1)} %add.315), channel_id=1, source_target_pairs={{0,1},{1,0},{2,3},{3,2},{4,5},{5,4},{6,7},{7,6},{8,9},{9,8},{10,11... | collective-permute-start | bytes 245768 | tf_op jit(solution)/shard_map/ppermute | solution.py:27
  89.4 8.0 %collective-permute-start.20 = (f32[128,128]{1,0:T(8,128)S(1)}, f32[128,128]{1,0:T(8,128)S(1)}, u32[]{:S(2)}, u32[]{:S(2)}) collective-permute-start(f32[128,128]{1,0:T(8,128)S(1)} %add.343), channel_id=1, source_target_pairs={{0,2},{1,3},{2,0},{3,1},{4,6},{5,7},{6,4},{7,5},{8,10},{9,11},{10,... | collective-permute-start | bytes 196616 | tf_op jit(solution)/shard_map/ppermute | solution.py:27
  94.9 8.4 %collective-permute-start.8 = (f32[160,128]{0,1:T(8,128)S(1)}, f32[160,128]{0,1:T(8,128)S(1)}, u32[]{:S(2)}, u32[]{:S(2)}) collective-permute-start(f32[160,128]{0,1:T(8,128)S(1)} %add.316), channel_id=1, source_target_pairs={{0,2},{1,3},{2,0},{3,1},{4,6},{5,7},{6,4},{7,5},{8,10},{9,11},{10,... | collective-permute-start | bytes 245768 | tf_op jit(solution)/shard_map/ppermute | solution.py:27
  97.4 9.9 %collective-permute-start.21 = (f32[128,128]{1,0:T(8,128)S(1)}, f32[128,128]{1,0:T(8,128)S(1)}, u32[]{:S(2)}, u32[]{:S(2)}) collective-permute-start(f32[128,128]{1,0:T(8,128)S(1)} %add.344), channel_id=1, source_target_pairs={{0,128},{4,132},{8,136},{12,140},{16,144},{20,148},{24,152},{28,15... | collective-permute-start | bytes 196616 | tf_op jit(solution)/shard_map/ppermute | solution.py:27
  103.3 8.3 %collective-permute-start.9 = (f32[160,128]{0,1:T(8,128)S(1)}, f32[160,128]{0,1:T(8,128)S(1)}, u32[]{:S(2)}, u32[]{:S(2)}) collective-permute-start(f32[160,128]{0,1:T(8,128)S(1)} %add.317), channel_id=1, source_target_pairs={{0,16},{4,20},{8,24},{12,28},{16,0},{20,4},{24,8},{28,12},{32,48},... | collective-permute-start | bytes 245768 | tf_op jit(solution)/shard_map/ppermute | solution.py:27
  107.4 7.8 %collective-permute-start.22 = (f32[256,128]{1,0:T(8,128)S(1)}, f32[256,128]{1,0:T(8,128)S(1)}, u32[]{:S(2)}, u32[]{:S(2)}) collective-permute-start(f32[256,128]{1,0:T(8,128)S(1)} %maximum_select_fusion.5), channel_id=1, source_target_pairs={{0,64},{4,68},{8,72},{12,76},{16,80},{20,84},{24,88},{28,92},{32,9... | collective-permute-start | bytes 393224 | tf_op jit(solution)/shard_map/ppermute | solution.py:27
  111.7 7.6 %collective-permute-start.10 = (f32[320,128]{0,1:T(8,128)S(1)}, f32[320,128]{0,1:T(8,128)S(1)}, u32[]{:S(2)}, u32[]{:S(2)}) collective-permute-start(f32[320,128]{0,1:T(8,128)S(1)} %maximum_select_fusion.4), channel_id=1, source_target_pairs={{0,8},{4,12},{8,0},{12,4},{16,24},{20,28},{24,16},{28,20},{32,40},... | collective-permute-start | bytes 491528 | tf_op jit(solution)/shard_map/ppermute | solution.py:27
  115.2 6.4 %collective-permute-start.23 = (f32[512,128]{1,0:T(8,128)S(1)}, f32[512,128]{1,0:T(8,128)S(1)}, u32[]{:S(2)}, u32[]{:S(2)}) collective-permute-start(f32[512,128]{1,0:T(8,128)S(1)} %maximum_select_fusion.3), channel_id=1, source_target_pairs={{0,4},{4,0},{8,12},{12,8},{16,20},{20,16},{24,28},{28,24},{32,36},... | collective-permute-start | bytes 786440 | tf_op jit(solution)/shard_map/ppermute | solution.py:27
  119.5 3.7 %collective-permute-start.11 = (f32[640,128]{0,1:T(8,128)S(1)}, f32[640,128]{0,1:T(8,128)S(1)}, u32[]{:S(2)}, u32[]{:S(2)}) collective-permute-start(f32[640,128]{0,1:T(8,128)S(1)} %maximum_select_fusion.2), channel_id=1, source_target_pairs={{0,4},{4,0},{8,12},{12,8},{16,20},{20,16},{24,28},{28,24},{32,36},... | collective-permute-start | bytes 983048 | tf_op jit(solution)/shard_map/ppermute | solution.py:27
  194.4 0.9 copy-start.2
  195.8 0.9 copy-start.1
  201.2 3.2 %collective-permute-start.24 = (f32[2,256]{1,0:T(2,128)S(1)}, f32[2,256]{1,0:T(2,128)S(1)}, u32[]{:S(2)}, u32[]{:S(2)}) collective-permute-start(f32[2,256]{1,0:T(2,128)S(1)} %pad_maximum_fusion.14), channel_id=1, source_target_pairs={{0,4},{4,0},{8,12},{12,8},{16,20},{20,16},{24,28},{28,24},{32,36},... | collective-permute-start | bytes 6152 | tf_op jit(solution)/shard_map/ppermute | solution.py:27
  204.5 5.5 %collective-permute-start.25 = (f32[2,256]{1,0:T(2,128)S(1)}, f32[2,256]{1,0:T(2,128)S(1)}, u32[]{:S(2)}, u32[]{:S(2)}) collective-permute-start(f32[2,256]{1,0:T(2,128)S(1)} %pad_maximum_fusion.15), channel_id=1, source_target_pairs={{0,8},{4,12},{8,0},{12,4},{16,24},{20,28},{24,16},{28,20},{32,40},... | collective-permute-start | bytes 6152 | tf_op jit(solution)/shard_map/ppermute | solution.py:27
  210.0 6.4 %collective-permute-start.26 = (f32[2,256]{1,0:T(2,128)S(1)}, f32[2,256]{1,0:T(2,128)S(1)}, u32[]{:S(2)}, u32[]{:S(2)}) collective-permute-start(f32[2,256]{1,0:T(2,128)S(1)} %pad_maximum_fusion.16), channel_id=1, source_target_pairs={{0,16},{4,20},{8,24},{12,28},{16,0},{20,4},{24,8},{28,12},{32,48},... | collective-permute-start | bytes 6152 | tf_op jit(solution)/shard_map/ppermute | solution.py:27
  216.4 9.7 %collective-permute-start.27 = (f32[2,256]{1,0:T(2,128)S(1)}, f32[2,256]{1,0:T(2,128)S(1)}, u32[]{:S(2)}, u32[]{:S(2)}) collective-permute-start(f32[2,256]{1,0:T(2,128)S(1)} %pad_maximum_fusion.17), channel_id=1, source_target_pairs={{0,32},{4,36},{8,40},{12,44},{16,48},{20,52},{24,56},{28,60},{32,0... | collective-permute-start | bytes 6152 | tf_op jit(solution)/shard_map/ppermute | solution.py:27
  226.0 5.5 %collective-permute-start.28 = (f32[2,256]{1,0:T(2,128)S(1)}, f32[2,256]{1,0:T(2,128)S(1)}, u32[]{:S(2)}, u32[]{:S(2)}) collective-permute-start(f32[2,256]{1,0:T(2,128)S(1)} %pad_maximum_fusion.18), channel_id=1, source_target_pairs={{0,64},{4,68},{8,72},{12,76},{16,80},{20,84},{24,88},{28,92},{32,9... | collective-permute-start | bytes 6152 | tf_op jit(solution)/shard_map/ppermute | solution.py:27
  231.5 6.4 %collective-permute-start.29 = (f32[2,256]{1,0:T(2,128)S(1)}, f32[2,256]{1,0:T(2,128)S(1)}, u32[]{:S(2)}, u32[]{:S(2)}) collective-permute-start(f32[2,256]{1,0:T(2,128)S(1)} %pad_maximum_fusion.19), channel_id=1, source_target_pairs={{0,128},{4,132},{8,136},{12,140},{16,144},{20,148},{24,152},{28,15... | collective-permute-start | bytes 6152 | tf_op jit(solution)/shard_map/ppermute | solution.py:27
  237.9 9.4 %collective-permute-start.30 = (f32[2,256]{1,0:T(2,128)S(1)}, f32[2,256]{1,0:T(2,128)S(1)}, u32[]{:S(2)}, u32[]{:S(2)}) collective-permute-start(f32[2,256]{1,0:T(2,128)S(1)} %pad_maximum_fusion.20), channel_id=1, source_target_pairs={{0,256},{4,260},{8,264},{12,268},{16,272},{20,276},{24,280},{28,28... | collective-permute-start | bytes 6152 | tf_op jit(solution)/shard_map/ppermute | solution.py:27
  247.3 5.5 %collective-permute-start.31 = (f32[2,256]{1,0:T(2,128)S(1)}, f32[2,256]{1,0:T(2,128)S(1)}, u32[]{:S(2)}, u32[]{:S(2)}) collective-permute-start(f32[2,256]{1,0:T(2,128)S(1)} %pad_maximum_fusion.21), channel_id=1, source_target_pairs={{0,1},{1,0},{2,3},{3,2},{4,5},{5,4},{6,7},{7,6},{8,9},{9,8},{10,11... | collective-permute-start | bytes 6152 | tf_op jit(solution)/shard_map/ppermute | solution.py:27
  252.8 7.0 %collective-permute-start.32 = (f32[2,256]{1,0:T(2,128)S(1)}, f32[2,256]{1,0:T(2,128)S(1)}, u32[]{:S(2)}, u32[]{:S(2)}) collective-permute-start(f32[2,256]{1,0:T(2,128)S(1)} %pad_maximum_fusion.22), channel_id=1, source_target_pairs={{0,2},{1,3},{2,0},{3,1},{4,6},{5,7},{6,4},{7,5},{8,10},{9,11},{10,... | collective-permute-start | bytes 6152 | tf_op jit(solution)/shard_map/ppermute | solution.py:27

commit v9 on v8

--- a/solution.py
+++ b/solution.py
@@ -152,7 +152,7 @@
     scores = jnp.dot(features, coeffs, preferred_element_type=jnp.float32)
     peak_local = jnp.max(jnp.abs(scores), axis=0)
     column_sum = jnp.sum(scores, axis=0)
-    stats = peak_and_total(jnp.stack([peak_local, column_sum]), bits)
+    stats = peak_and_total(jnp.stack([peak_local, column_sum]), bits[::-1])
     peak = stats[0]
     total = stats[1]
     quality = (scores - total / jnp.float32(total_rows)) / (peak + 1e-06)

time: 262 us -> 263 us (level)
  no operation moved by 1% of the time
where the time goes in v9:
time: 263 us; the launch traced here: 260 us
  starting transfers between devices  128 us (49%)
  other arithmetic  56.4 us (21%)
  waiting for transfers between devices  40.9 us (16%)
  matrix products  22.8 us (9%)
  local copies, waits for them, and re-layouts  9.21 us (4%)
  between operations  2.97 us (1%)
    ppermute x33, starting transfers between devices, partner(): return lax.ppermute(x, name, [(i, i ^ mask) for i in range(size)])  128 us
    another operation x12, other arithmetic, blocked_cholesky(): head = lax.linalg.cholesky(trailing[:block, :block], symmetrize_input=False)  49.7 us
    ppermute x33, waiting for transfers between devices, partner(): return lax.ppermute(x, name, [(i, i ^ mask) for i in range(size)])  40.9 us
    dot_general x24, matrix products, triangular_inverse(): product = jnp.dot(product, eye + power, precision=HIGHEST)  6.05 us
    dot_general x24, matrix products, triangular_inverse(): power = jnp.dot(power, power, precision=HIGHEST)  5.86 us
  transfers between devices with their start and end apart: 33, of which 20 were waited for; matrix products, arithmetic and copies ran while one was open for 1% of the time, Pallas kernels for 0%

profile of v9, /device:TPU:6, one launch (start us, length us, event | category | flops | bytes accessed | tf_op | source)
XLA Modules:
  0.0 260.3 jit_solution(9802727754946737284)
XLA Ops:
  1.5 3.3 %fusion.1 = bf16[256,512]{1,0:T(8,128)(2,1)S(1)} fusion(bf16[256,1024]{1,0:T(8,128)(2,1)} %param.7, bf16[1024,512]{1,0:T(8,128)(2,1)S(1)} %copy-done, f32[512]{0:T(512)S(1)} %fusion.78), kind=kOutput, calls=%fused_computation.4 | convolution fusion | flops 268697600 | bytes 1837056 | tf_op jit(solution)/shard_map/dot_general | solution.py:119
  7.0 1.9 collective-permute-start.12
  9.4 2.4 collective-permute-start
  13.0 3.5 %collective-permute-start.13 = (f32[256,128]{1,0:T(8,128)S(1)}, f32[256,128]{1,0:T(8,128)S(1)}, u32[]{:S(2)}, u32[]{:S(2)}) collective-permute-start(f32[256,128]{1,0:T(8,128)S(1)} %constant_dynamic-slice_fusion.1), channel_id=1, source_target_pairs={{0,64},{4,68},{8,72},{12,76},{16,80},{20,84},{24,88},{28,92},{32,9... | collective-permute-start | bytes 393224 | tf_op jit(solution)/shard_map/ppermute | solution.py:27
  16.7 4.3 %collective-permute-start.1 = (f32[320,128]{0,1:T(8,128)S(1)}, f32[320,128]{0,1:T(8,128)S(1)}, u32[]{:S(2)}, u32[]{:S(2)}) collective-permute-start(f32[320,128]{0,1:T(8,128)S(1)} %constant_dynamic-slice_fusion.4), channel_id=1, source_target_pairs={{0,8},{4,12},{8,0},{12,4},{16,24},{20,28},{24,16},{28,20},{32,40},... | collective-permute-start | bytes 491528 | tf_op jit(solution)/shard_map/ppermute | solution.py:27
  21.1 4.7 %collective-permute-done.1 = f32[320,128]{0,1:T(8,128)S(1)} collective-permute-done((f32[320,128]{0,1:T(8,128)S(1)}, f32[320,128]{0,1:T(8,128)S(1)}, u32[]{:S(2)}, u32[]{:S(2)}) %collective-permute-start.1) | collective-permute-done | bytes 163872 | tf_op jit(solution)/shard_map/ppermute | solution.py:27
  26.0 6.1 %collective-permute-start.2 = (f32[160,128]{0,1:T(8,128)S(1)}, f32[160,128]{0,1:T(8,128)S(1)}, u32[]{:S(2)}, u32[]{:S(2)}) collective-permute-start(f32[160,128]{0,1:T(8,128)S(1)} %constant_dynamic-slice_fusion.3), channel_id=1, source_target_pairs={{0,16},{4,20},{8,24},{12,28},{16,0},{20,4},{24,8},{28,12},{32,48},... | collective-permute-start | bytes 245768 | tf_op jit(solution)/shard_map/ppermute | solution.py:27
  32.2 4.5 %collective-permute-start.14 = (f32[128,128]{1,0:T(8,128)S(1)}, f32[128,128]{1,0:T(8,128)S(1)}, u32[]{:S(2)}, u32[]{:S(2)}) collective-permute-start(f32[128,128]{1,0:T(8,128)S(1)} %constant_dynamic-slice_fusion), channel_id=1, source_target_pairs={{0,128},{4,132},{8,136},{12,140},{16,144},{20,148},{24,152},{28,15... | collective-permute-start | bytes 196616 | tf_op jit(solution)/shard_map/ppermute | solution.py:27
  37.9 8.4 %collective-permute-start.3 = (f32[160,128]{0,1:T(8,128)S(1)}, f32[160,128]{0,1:T(8,128)S(1)}, u32[]{:S(2)}, u32[]{:S(2)}) collective-permute-start(f32[160,128]{0,1:T(8,128)S(1)} %dynamic-slice_add_fusion.4), channel_id=1, source_target_pairs={{0,32},{4,36},{8,40},{12,44},{16,48},{20,52},{24,56},{28,60},{32,0... | collective-permute-start | bytes 245768 | tf_op jit(solution)/shard_map/ppermute | solution.py:27
  46.3 6.8 %collective-permute-start.15 = (f32[128,128]{1,0:T(8,128)S(1)}, f32[128,128]{1,0:T(8,128)S(1)}, u32[]{:S(2)}, u32[]{:S(2)}) collective-permute-start(f32[128,128]{1,0:T(8,128)S(1)} %dynamic-slice_add_fusion.5), channel_id=1, source_target_pairs={{0,256},{4,260},{8,264},{12,268},{16,272},{20,276},{24,280},{28,28... | collective-permute-start | bytes 196616 | tf_op jit(solution)/shard_map/ppermute | solution.py:27
  53.2 3.3 %collective-permute-start.4 = (f32[160,128]{0,1:T(8,128)S(1)}, f32[160,128]{0,1:T(8,128)S(1)}, u32[]{:S(2)}, u32[]{:S(2)}) collective-permute-start(f32[160,128]{0,1:T(8,128)S(1)} %add.312), channel_id=1, source_target_pairs={{0,64},{4,68},{8,72},{12,76},{16,80},{20,84},{24,88},{28,92},{32,9... | collective-permute-start | bytes 245768 | tf_op jit(solution)/shard_map/ppermute | solution.py:27
  56.6 2.3 collective-permute-start.16
  60.3 4.2 %collective-permute-start.5 = (f32[160,128]{0,1:T(8,128)S(1)}, f32[160,128]{0,1:T(8,128)S(1)}, u32[]{:S(2)}, u32[]{:S(2)}) collective-permute-start(f32[160,128]{0,1:T(8,128)S(1)} %add.313), channel_id=1, source_target_pairs={{0,128},{4,132},{8,136},{12,140},{16,144},{20,148},{24,152},{28,15... | collective-permute-start | bytes 245768 | tf_op jit(solution)/shard_map/ppermute | solution.py:27
  64.5 5.4 %collective-permute-start.17 = (f32[128,128]{1,0:T(8,128)S(1)}, f32[128,128]{1,0:T(8,128)S(1)}, u32[]{:S(2)}, u32[]{:S(2)}) collective-permute-start(f32[128,128]{1,0:T(8,128)S(1)} %add.340), channel_id=1, source_target_pairs={{0,16},{4,20},{8,24},{12,28},{16,0},{20,4},{24,8},{28,12},{32,48},... | collective-permute-start | bytes 196616 | tf_op jit(solution)/shard_map/ppermute | solution.py:27
  69.9 2.9 %collective-permute-done.17 = f32[128,128]{1,0:T(8,128)S(1)} collective-permute-done((f32[128,128]{1,0:T(8,128)S(1)}, f32[128,128]{1,0:T(8,128)S(1)}, u32[]{:S(2)}, u32[]{:S(2)}) %collective-permute-start.17) | collective-permute-done | bytes 65568 | tf_op jit(solution)/shard_map/ppermute | solution.py:27
  72.9 3.8 %collective-permute-start.18 = (f32[128,128]{1,0:T(8,128)S(1)}, f32[128,128]{1,0:T(8,128)S(1)}, u32[]{:S(2)}, u32[]{:S(2)}) collective-permute-start(f32[128,128]{1,0:T(8,128)S(1)} %add.341), channel_id=1, source_target_pairs={{0,32},{4,36},{8,40},{12,44},{16,48},{20,52},{24,56},{28,60},{32,0... | collective-permute-start | bytes 196616 | tf_op jit(solution)/shard_map/ppermute | solution.py:27
  76.7 4.4 %collective-permute-start.6 = (f32[160,128]{0,1:T(8,128)S(1)}, f32[160,128]{0,1:T(8,128)S(1)}, u32[]{:S(2)}, u32[]{:S(2)}) collective-permute-start(f32[160,128]{0,1:T(8,128)S(1)} %add.314), channel_id=1, source_target_pairs={{0,256},{4,260},{8,264},{12,268},{16,272},{20,276},{24,280},{28,28... | collective-permute-start | bytes 245768 | tf_op jit(solution)/shard_map/ppermute | solution.py:27
  83.0 3.2 %collective-permute-start.19 = (f32[128,128]{1,0:T(8,128)S(1)}, f32[128,128]{1,0:T(8,128)S(1)}, u32[]{:S(2)}, u32[]{:S(2)}) collective-permute-start(f32[128,128]{1,0:T(8,128)S(1)} %add.342), channel_id=1, source_target_pairs={{0,1},{1,0},{2,3},{3,2},{4,5},{5,4},{6,7},{7,6},{8,9},{9,8},{10,11... | collective-permute-start | bytes 196616 | tf_op jit(solution)/shard_map/ppermute | solution.py:27
  87.5 1.9 collective-permute-start.7
  89.4 3.5 %collective-permute-start.20 = (f32[128,128]{1,0:T(8,128)S(1)}, f32[128,128]{1,0:T(8,128)S(1)}, u32[]{:S(2)}, u32[]{:S(2)}) collective-permute-start(f32[128,128]{1,0:T(8,128)S(1)} %add.343), channel_id=1, source_target_pairs={{0,2},{1,3},{2,0},{3,1},{4,6},{5,7},{6,4},{7,5},{8,10},{9,11},{10,... | collective-permute-start | bytes 196616 | tf_op jit(solution)/shard_map/ppermute | solution.py:27
  92.9 2.0 collective-permute-done.7
  94.9 2.5 collective-permute-start.8
  97.4 3.3 %collective-permute-start.21 = (f32[128,128]{1,0:T(8,128)S(1)}, f32[128,128]{1,0:T(8,128)S(1)}, u32[]{:S(2)}, u32[]{:S(2)}) collective-permute-start(f32[128,128]{1,0:T(8,128)S(1)} %add.344), channel_id=1, source_target_pairs={{0,128},{4,132},{8,136},{12,140},{16,144},{20,148},{24,152},{28,15... | collective-permute-start | bytes 196616 | tf_op jit(solution)/shard_map/ppermute | solution.py:27
  100.8 2.5 collective-permute-done.8
  103.3 4.0 %collective-permute-start.9 = (f32[160,128]{0,1:T(8,128)S(1)}, f32[160,128]{0,1:T(8,128)S(1)}, u32[]{:S(2)}, u32[]{:S(2)}) collective-permute-start(f32[160,128]{0,1:T(8,128)S(1)} %add.317), channel_id=1, source_target_pairs={{0,16},{4,20},{8,24},{12,28},{16,0},{20,4},{24,8},{28,12},{32,48},... | collective-permute-start | bytes 245768 | tf_op jit(solution)/shard_map/ppermute | solution.py:27
  107.4 4.1 %collective-permute-start.22 = (f32[256,128]{1,0:T(8,128)S(1)}, f32[256,128]{1,0:T(8,128)S(1)}, u32[]{:S(2)}, u32[]{:S(2)}) collective-permute-start(f32[256,128]{1,0:T(8,128)S(1)} %maximum_select_fusion.5), channel_id=1, source_target_pairs={{0,64},{4,68},{8,72},{12,76},{16,80},{20,84},{24,88},{28,92},{32,9... | collective-permute-start | bytes 393224 | tf_op jit(solution)/shard_map/ppermute | solution.py:27
  111.7 3.4 %collective-permute-start.10 = (f32[320,128]{0,1:T(8,128)S(1)}, f32[320,128]{0,1:T(8,128)S(1)}, u32[]{:S(2)}, u32[]{:S(2)}) collective-permute-start(f32[320,128]{0,1:T(8,128)S(1)} %maximum_select_fusion.4), channel_id=1, source_target_pairs={{0,8},{4,12},{8,0},{12,4},{16,24},{20,28},{24,16},{28,20},{32,40},... | collective-permute-start | bytes 491528 | tf_op jit(solution)/shard_map/ppermute | solution.py:27
  115.2 1.9 collective-permute-start.23
  119.5 2.1 collective-permute-start.11
  127.7 11.7 %custom-call.6 = f32[128,128]{1,0:T(8,128)S(1)} custom-call(f32[128,128]{1,0:T(8,128)S(1)} %slice.271), custom_call_target="Cholesky" | custom-call | tf_op jit(solution)/shard_map/cholesky/custom-call.1 | solution.py:78
  144.5 11.7 %custom-call.7 = f32[128,128]{1,0:T(8,128)S(1)} custom-call(f32[128,128]{1,0:T(8,128)S(1)} %slice.275), custom_call_target="Cholesky" | custom-call | tf_op jit(solution)/shard_map/cholesky/custom-call.1 | solution.py:78
  161.3 11.7 %custom-call.8 = f32[128,128]{1,0:T(8,128)S(1)} custom-call(f32[128,128]{1,0:T(8,128)S(1)} %slice.280), custom_call_target="Cholesky" | custom-call | tf_op jit(solution)/shard_map/cholesky/custom-call.1 | solution.py:78
  177.7 11.7 %custom-call.9 = f32[128,128]{1,0:T(8,128)S(1)} custom-call(f32[128,128]{1,0:T(8,128)S(1)} %convolution_subtract_fusion.5), custom_call_target="Cholesky" | custom-call | tf_op jit(solution)/shard_map/cholesky/custom-call.1 | solution.py:78
  201.2 2.9 %collective-permute-start.24 = (f32[2,256]{1,0:T(2,128)S(1)}, f32[2,256]{1,0:T(2,128)S(1)}, u32[]{:S(2)}, u32[]{:S(2)}) collective-permute-start(f32[2,256]{1,0:T(2,128)S(1)} %pad_maximum_fusion.14), channel_id=1, source_target_pairs={{0,2},{1,3},{2,0},{3,1},{4,6},{5,7},{6,4},{7,5},{8,10},{9,11},{10,... | collective-permute-start | bytes 6152 | tf_op jit(solution)/shard_map/ppermute | solution.py:27
  204.1 4.1 %collective-permute-done.24 = f32[2,256]{1,0:T(2,128)S(1)} collective-permute-done((f32[2,256]{1,0:T(2,128)S(1)}, f32[2,256]{1,0:T(2,128)S(1)}, u32[]{:S(2)}, u32[]{:S(2)}) %collective-permute-start.24) | collective-permute-done | bytes 2080 | tf_op jit(solution)/shard_map/ppermute | solution.py:27
  208.3 3.4 %collective-permute-start.25 = (f32[2,256]{1,0:T(2,128)S(1)}, f32[2,256]{1,0:T(2,128)S(1)}, u32[]{:S(2)}, u32[]{:S(2)}) collective-permute-start(f32[2,256]{1,0:T(2,128)S(1)} %pad_maximum_fusion.15), channel_id=1, source_target_pairs={{0,1},{1,0},{2,3},{3,2},{4,5},{5,4},{6,7},{7,6},{8,9},{9,8},{10,11... | collective-permute-start | bytes 6152 | tf_op jit(solution)/shard_map/ppermute | solution.py:27
  211.7 2.0 collective-permute-done.25
  213.7 6.5 %collective-permute-start.26 = (f32[2,256]{1,0:T(2,128)S(1)}, f32[2,256]{1,0:T(2,128)S(1)}, u32[]{:S(2)}, u32[]{:S(2)}) collective-permute-start(f32[2,256]{1,0:T(2,128)S(1)} %pad_maximum_fusion.16), channel_id=1, source_target_pairs={{0,256},{4,260},{8,264},{12,268},{16,272},{20,276},{24,280},{28,28... | collective-permute-start | bytes 6152 | tf_op jit(solution)/shard_map/ppermute | solution.py:27
  220.2 2.9 %collective-permute-done.26 = f32[2,256]{1,0:T(2,128)S(1)} collective-permute-done((f32[2,256]{1,0:T(2,128)S(1)}, f32[2,256]{1,0:T(2,128)S(1)}, u32[]{:S(2)}, u32[]{:S(2)}) %collective-permute-start.26) | collective-permute-done | bytes 2080 | tf_op jit(solution)/shard_map/ppermute | solution.py:27
  223.1 2.5 collective-permute-start.27
  225.6 3.9 %collective-permute-done.27 = f32[2,256]{1,0:T(2,128)S(1)} collective-permute-done((f32[2,256]{1,0:T(2,128)S(1)}, f32[2,256]{1,0:T(2,128)S(1)}, u32[]{:S(2)}, u32[]{:S(2)}) %collective-permute-start.27) | collective-permute-done | bytes 2080 | tf_op jit(solution)/shard_map/ppermute | solution.py:27
  229.5 3.9 %collective-permute-start.28 = (f32[2,256]{1,0:T(2,128)S(1)}, f32[2,256]{1,0:T(2,128)S(1)}, u32[]{:S(2)}, u32[]{:S(2)}) collective-permute-start(f32[2,256]{1,0:T(2,128)S(1)} %pad_maximum_fusion.18), channel_id=1, source_target_pairs={{0,64},{4,68},{8,72},{12,76},{16,80},{20,84},{24,88},{28,92},{32,9... | collective-permute-start | bytes 6152 | tf_op jit(solution)/shard_map/ppermute | solution.py:27
  235.0 8.1 %collective-permute-start.29 = (f32[2,256]{1,0:T(2,128)S(1)}, f32[2,256]{1,0:T(2,128)S(1)}, u32[]{:S(2)}, u32[]{:S(2)}) collective-permute-start(f32[2,256]{1,0:T(2,128)S(1)} %pad_maximum_fusion.19), channel_id=1, source_target_pairs={{0,32},{4,36},{8,40},{12,44},{16,48},{20,52},{24,56},{28,60},{32,0... | collective-permute-start | bytes 6152 | tf_op jit(solution)/shard_map/ppermute | solution.py:27
  244.7 4.2 %collective-permute-start.30 = (f32[2,256]{1,0:T(2,128)S(1)}, f32[2,256]{1,0:T(2,128)S(1)}, u32[]{:S(2)}, u32[]{:S(2)}) collective-permute-start(f32[2,256]{1,0:T(2,128)S(1)} %pad_maximum_fusion.20), channel_id=1, source_target_pairs={{0,16},{4,20},{8,24},{12,28},{16,0},{20,4},{24,8},{28,12},{32,48},... | collective-permute-start | bytes 6152 | tf_op jit(solution)/shard_map/ppermute | solution.py:27
  249.0 2.1 collective-permute-done.30
  251.1 3.4 %collective-permute-start.31 = (f32[2,256]{1,0:T(2,128)S(1)}, f32[2,256]{1,0:T(2,128)S(1)}, u32[]{:S(2)}, u32[]{:S(2)}) collective-permute-start(f32[2,256]{1,0:T(2,128)S(1)} %pad_maximum_fusion.21), channel_id=1, source_target_pairs={{0,8},{4,12},{8,0},{12,4},{16,24},{20,28},{24,16},{28,20},{32,40},... | collective-permute-start | bytes 6152 | tf_op jit(solution)/shard_map/ppermute | solution.py:27
  254.5 2.1 collective-permute-done.31
  256.6 1.9 collective-permute-start.32
  (199 shorter events, 49.9 us)
Async XLA Ops:
  0.0 1.5 copy-start
  0.7 0.7 copy-start.4
  4.7 1.2 copy-start.3
  7.0 5.1 %collective-permute-start.12 = (f32[512,128]{1,0:T(8,128)}, f32[512,128]{1,0:T(8,128)}, u32[]{:S(2)}, u32[]{:S(2)}) collective-permute-start(f32[512,128]{1,0:T(8,128)} %constant_dynamic-slice_fusion.2), channel_id=1, source_target_pairs={{0,4},{4,0},{8,12},{12,8},{16,20},{20,16},{24,28},{28,24},{32,36},... | collective-permute-start | bytes 786440 | tf_op jit(solution)/shard_map/ppermute | solution.py:27
  9.4 7.1 %collective-permute-start = (f32[640,128]{0,1:T(8,128)S(1)}, f32[640,128]{0,1:T(8,128)S(1)}, u32[]{:S(2)}, u32[]{:S(2)}) collective-permute-start(f32[640,128]{0,1:T(8,128)S(1)} %constant_dynamic-slice_fusion.5), channel_id=1, source_target_pairs={{0,4},{4,0},{8,12},{12,8},{16,20},{20,16},{24,28},{28,24},{32,36},... | collective-permute-start | bytes 983048 | tf_op jit(solution)/shard_map/ppermute | solution.py:27
  13.0 8.0 %collective-permute-start.13 = (f32[256,128]{1,0:T(8,128)S(1)}, f32[256,128]{1,0:T(8,128)S(1)}, u32[]{:S(2)}, u32[]{:S(2)}) collective-permute-start(f32[256,128]{1,0:T(8,128)S(1)} %constant_dynamic-slice_fusion.1), channel_id=1, source_target_pairs={{0,64},{4,68},{8,72},{12,76},{16,80},{20,84},{24,88},{28,92},{32,9... | collective-permute-start | bytes 393224 | tf_op jit(solution)/shard_map/ppermute | solution.py:27
  16.7 9.1 %collective-permute-start.1 = (f32[320,128]{0,1:T(8,128)S(1)}, f32[320,128]{0,1:T(8,128)S(1)}, u32[]{:S(2)}, u32[]{:S(2)}) collective-permute-start(f32[320,128]{0,1:T(8,128)S(1)} %constant_dynamic-slice_fusion.4), channel_id=1, source_target_pairs={{0,8},{4,12},{8,0},{12,4},{16,24},{20,28},{24,16},{28,20},{32,40},... | collective-permute-start | bytes 491528 | tf_op jit(solution)/shard_map/ppermute | solution.py:27
  26.0 11.7 %collective-permute-start.2 = (f32[160,128]{0,1:T(8,128)S(1)}, f32[160,128]{0,1:T(8,128)S(1)}, u32[]{:S(2)}, u32[]{:S(2)}) collective-permute-start(f32[160,128]{0,1:T(8,128)S(1)} %constant_dynamic-slice_fusion.3), channel_id=1, source_target_pairs={{0,16},{4,20},{8,24},{12,28},{16,0},{20,4},{24,8},{28,12},{32,48},... | collective-permute-start | bytes 245768 | tf_op jit(solution)/shard_map/ppermute | solution.py:27
  32.2 14.1 %collective-permute-start.14 = (f32[128,128]{1,0:T(8,128)S(1)}, f32[128,128]{1,0:T(8,128)S(1)}, u32[]{:S(2)}, u32[]{:S(2)}) collective-permute-start(f32[128,128]{1,0:T(8,128)S(1)} %constant_dynamic-slice_fusion), channel_id=1, source_target_pairs={{0,128},{4,132},{8,136},{12,140},{16,144},{20,148},{24,152},{28,15... | collective-permute-start | bytes 196616 | tf_op jit(solution)/shard_map/ppermute | solution.py:27
  37.9 15.3 %collective-permute-start.3 = (f32[160,128]{0,1:T(8,128)S(1)}, f32[160,128]{0,1:T(8,128)S(1)}, u32[]{:S(2)}, u32[]{:S(2)}) collective-permute-start(f32[160,128]{0,1:T(8,128)S(1)} %dynamic-slice_add_fusion.4), channel_id=1, source_target_pairs={{0,32},{4,36},{8,40},{12,44},{16,48},{20,52},{24,56},{28,60},{32,0... | collective-permute-start | bytes 245768 | tf_op jit(solution)/shard_map/ppermute | solution.py:27
  46.3 10.3 %collective-permute-start.15 = (f32[128,128]{1,0:T(8,128)S(1)}, f32[128,128]{1,0:T(8,128)S(1)}, u32[]{:S(2)}, u32[]{:S(2)}) collective-permute-start(f32[128,128]{1,0:T(8,128)S(1)} %dynamic-slice_add_fusion.5), channel_id=1, source_target_pairs={{0,256},{4,260},{8,264},{12,268},{16,272},{20,276},{24,280},{28,28... | collective-permute-start | bytes 196616 | tf_op jit(solution)/shard_map/ppermute | solution.py:27
  53.2 7.0 %collective-permute-start.4 = (f32[160,128]{0,1:T(8,128)S(1)}, f32[160,128]{0,1:T(8,128)S(1)}, u32[]{:S(2)}, u32[]{:S(2)}) collective-permute-start(f32[160,128]{0,1:T(8,128)S(1)} %add.312), channel_id=1, source_target_pairs={{0,64},{4,68},{8,72},{12,76},{16,80},{20,84},{24,88},{28,92},{32,9... | collective-permute-start | bytes 245768 | tf_op jit(solution)/shard_map/ppermute | solution.py:27
  56.6 7.9 %collective-permute-start.16 = (f32[128,128]{1,0:T(8,128)S(1)}, f32[128,128]{1,0:T(8,128)S(1)}, u32[]{:S(2)}, u32[]{:S(2)}) collective-permute-start(f32[128,128]{1,0:T(8,128)S(1)} %add.339), channel_id=1, source_target_pairs={{0,8},{4,12},{8,0},{12,4},{16,24},{20,28},{24,16},{28,20},{32,40},... | collective-permute-start | bytes 196616 | tf_op jit(solution)/shard_map/ppermute | solution.py:27
  60.3 16.4 %collective-permute-start.5 = (f32[160,128]{0,1:T(8,128)S(1)}, f32[160,128]{0,1:T(8,128)S(1)}, u32[]{:S(2)}, u32[]{:S(2)}) collective-permute-start(f32[160,128]{0,1:T(8,128)S(1)} %add.313), channel_id=1, source_target_pairs={{0,128},{4,132},{8,136},{12,140},{16,144},{20,148},{24,152},{28,15... | collective-permute-start | bytes 245768 | tf_op jit(solution)/shard_map/ppermute | solution.py:27
  64.5 8.3 %collective-permute-start.17 = (f32[128,128]{1,0:T(8,128)S(1)}, f32[128,128]{1,0:T(8,128)S(1)}, u32[]{:S(2)}, u32[]{:S(2)}) collective-permute-start(f32[128,128]{1,0:T(8,128)S(1)} %add.340), channel_id=1, source_target_pairs={{0,16},{4,20},{8,24},{12,28},{16,0},{20,4},{24,8},{28,12},{32,48},... | collective-permute-start | bytes 196616 | tf_op jit(solution)/shard_map/ppermute | solution.py:27
  72.9 10.1 %collective-permute-start.18 = (f32[128,128]{1,0:T(8,128)S(1)}, f32[128,128]{1,0:T(8,128)S(1)}, u32[]{:S(2)}, u32[]{:S(2)}) collective-permute-start(f32[128,128]{1,0:T(8,128)S(1)} %add.341), channel_id=1, source_target_pairs={{0,32},{4,36},{8,40},{12,44},{16,48},{20,52},{24,56},{28,60},{32,0... | collective-permute-start | bytes 196616 | tf_op jit(solution)/shard_map/ppermute | solution.py:27
  76.7 10.8 %collective-permute-start.6 = (f32[160,128]{0,1:T(8,128)S(1)}, f32[160,128]{0,1:T(8,128)S(1)}, u32[]{:S(2)}, u32[]{:S(2)}) collective-permute-start(f32[160,128]{0,1:T(8,128)S(1)} %add.314), channel_id=1, source_target_pairs={{0,256},{4,260},{8,264},{12,268},{16,272},{20,276},{24,280},{28,28... | collective-permute-start | bytes 245768 | tf_op jit(solution)/shard_map/ppermute | solution.py:27
  83.0 6.4 %collective-permute-start.19 = (f32[128,128]{1,0:T(8,128)S(1)}, f32[128,128]{1,0:T(8,128)S(1)}, u32[]{:S(2)}, u32[]{:S(2)}) collective-permute-start(f32[128,128]{1,0:T(8,128)S(1)} %add.342), channel_id=1, source_target_pairs={{0,1},{1,0},{2,3},{3,2},{4,5},{5,4},{6,7},{7,6},{8,9},{9,8},{10,11... | collective-permute-start | bytes 196616 | tf_op jit(solution)/shard_map/ppermute | solution.py:27
  87.5 7.5 %collective-permute-start.7 = (f32[160,128]{0,1:T(8,128)S(1)}, f32[160,128]{0,1:T(8,128)S(1)}, u32[]{:S(2)}, u32[]{:S(2)}) collective-permute-start(f32[160,128]{0,1:T(8,128)S(1)} %add.315), channel_id=1, source_target_pairs={{0,1},{1,0},{2,3},{3,2},{4,5},{5,4},{6,7},{7,6},{8,9},{9,8},{10,11... | collective-permute-start | bytes 245768 | tf_op jit(solution)/shard_map/ppermute | solution.py:27
  89.4 8.0 %collective-permute-start.20 = (f32[128,128]{1,0:T(8,128)S(1)}, f32[128,128]{1,0:T(8,128)S(1)}, u32[]{:S(2)}, u32[]{:S(2)}) collective-permute-start(f32[128,128]{1,0:T(8,128)S(1)} %add.343), channel_id=1, source_target_pairs={{0,2},{1,3},{2,0},{3,1},{4,6},{5,7},{6,4},{7,5},{8,10},{9,11},{10,... | collective-permute-start | bytes 196616 | tf_op jit(solution)/shard_map/ppermute | solution.py:27
  94.9 8.4 %collective-permute-start.8 = (f32[160,128]{0,1:T(8,128)S(1)}, f32[160,128]{0,1:T(8,128)S(1)}, u32[]{:S(2)}, u32[]{:S(2)}) collective-permute-start(f32[160,128]{0,1:T(8,128)S(1)} %add.316), channel_id=1, source_target_pairs={{0,2},{1,3},{2,0},{3,1},{4,6},{5,7},{6,4},{7,5},{8,10},{9,11},{10,... | collective-permute-start | bytes 245768 | tf_op jit(solution)/shard_map/ppermute | solution.py:27
  97.4 9.9 %collective-permute-start.21 = (f32[128,128]{1,0:T(8,128)S(1)}, f32[128,128]{1,0:T(8,128)S(1)}, u32[]{:S(2)}, u32[]{:S(2)}) collective-permute-start(f32[128,128]{1,0:T(8,128)S(1)} %add.344), channel_id=1, source_target_pairs={{0,128},{4,132},{8,136},{12,140},{16,144},{20,148},{24,152},{28,15... | collective-permute-start | bytes 196616 | tf_op jit(solution)/shard_map/ppermute | solution.py:27
  103.3 8.3 %collective-permute-start.9 = (f32[160,128]{0,1:T(8,128)S(1)}, f32[160,128]{0,1:T(8,128)S(1)}, u32[]{:S(2)}, u32[]{:S(2)}) collective-permute-start(f32[160,128]{0,1:T(8,128)S(1)} %add.317), channel_id=1, source_target_pairs={{0,16},{4,20},{8,24},{12,28},{16,0},{20,4},{24,8},{28,12},{32,48},... | collective-permute-start | bytes 245768 | tf_op jit(solution)/shard_map/ppermute | solution.py:27
  107.4 7.8 %collective-permute-start.22 = (f32[256,128]{1,0:T(8,128)S(1)}, f32[256,128]{1,0:T(8,128)S(1)}, u32[]{:S(2)}, u32[]{:S(2)}) collective-permute-start(f32[256,128]{1,0:T(8,128)S(1)} %maximum_select_fusion.5), channel_id=1, source_target_pairs={{0,64},{4,68},{8,72},{12,76},{16,80},{20,84},{24,88},{28,92},{32,9... | collective-permute-start | bytes 393224 | tf_op jit(solution)/shard_map/ppermute | solution.py:27
  111.7 7.6 %collective-permute-start.10 = (f32[320,128]{0,1:T(8,128)S(1)}, f32[320,128]{0,1:T(8,128)S(1)}, u32[]{:S(2)}, u32[]{:S(2)}) collective-permute-start(f32[320,128]{0,1:T(8,128)S(1)} %maximum_select_fusion.4), channel_id=1, source_target_pairs={{0,8},{4,12},{8,0},{12,4},{16,24},{20,28},{24,16},{28,20},{32,40},... | collective-permute-start | bytes 491528 | tf_op jit(solution)/shard_map/ppermute | solution.py:27
  115.2 6.4 %collective-permute-start.23 = (f32[512,128]{1,0:T(8,128)S(1)}, f32[512,128]{1,0:T(8,128)S(1)}, u32[]{:S(2)}, u32[]{:S(2)}) collective-permute-start(f32[512,128]{1,0:T(8,128)S(1)} %maximum_select_fusion.3), channel_id=1, source_target_pairs={{0,4},{4,0},{8,12},{12,8},{16,20},{20,16},{24,28},{28,24},{32,36},... | collective-permute-start | bytes 786440 | tf_op jit(solution)/shard_map/ppermute | solution.py:27
  119.5 3.7 %collective-permute-start.11 = (f32[640,128]{0,1:T(8,128)S(1)}, f32[640,128]{0,1:T(8,128)S(1)}, u32[]{:S(2)}, u32[]{:S(2)}) collective-permute-start(f32[640,128]{0,1:T(8,128)S(1)} %maximum_select_fusion.2), channel_id=1, source_target_pairs={{0,4},{4,0},{8,12},{12,8},{16,20},{20,16},{24,28},{28,24},{32,36},... | collective-permute-start | bytes 983048 | tf_op jit(solution)/shard_map/ppermute | solution.py:27
  194.4 0.9 copy-start.2
  195.8 0.9 copy-start.1
  201.2 7.0 %collective-permute-start.24 = (f32[2,256]{1,0:T(2,128)S(1)}, f32[2,256]{1,0:T(2,128)S(1)}, u32[]{:S(2)}, u32[]{:S(2)}) collective-permute-start(f32[2,256]{1,0:T(2,128)S(1)} %pad_maximum_fusion.14), channel_id=1, source_target_pairs={{0,2},{1,3},{2,0},{3,1},{4,6},{5,7},{6,4},{7,5},{8,10},{9,11},{10,... | collective-permute-start | bytes 6152 | tf_op jit(solution)/shard_map/ppermute | solution.py:27
  208.3 5.5 %collective-permute-start.25 = (f32[2,256]{1,0:T(2,128)S(1)}, f32[2,256]{1,0:T(2,128)S(1)}, u32[]{:S(2)}, u32[]{:S(2)}) collective-permute-start(f32[2,256]{1,0:T(2,128)S(1)} %pad_maximum_fusion.15), channel_id=1, source_target_pairs={{0,1},{1,0},{2,3},{3,2},{4,5},{5,4},{6,7},{7,6},{8,9},{9,8},{10,11... | collective-permute-start | bytes 6152 | tf_op jit(solution)/shard_map/ppermute | solution.py:27
  213.7 9.4 %collective-permute-start.26 = (f32[2,256]{1,0:T(2,128)S(1)}, f32[2,256]{1,0:T(2,128)S(1)}, u32[]{:S(2)}, u32[]{:S(2)}) collective-permute-start(f32[2,256]{1,0:T(2,128)S(1)} %pad_maximum_fusion.16), channel_id=1, source_target_pairs={{0,256},{4,260},{8,264},{12,268},{16,272},{20,276},{24,280},{28,28... | collective-permute-start | bytes 6152 | tf_op jit(solution)/shard_map/ppermute | solution.py:27
  223.1 6.4 %collective-permute-start.27 = (f32[2,256]{1,0:T(2,128)S(1)}, f32[2,256]{1,0:T(2,128)S(1)}, u32[]{:S(2)}, u32[]{:S(2)}) collective-permute-start(f32[2,256]{1,0:T(2,128)S(1)} %pad_maximum_fusion.17), channel_id=1, source_target_pairs={{0,128},{4,132},{8,136},{12,140},{16,144},{20,148},{24,152},{28,15... | collective-permute-start | bytes 6152 | tf_op jit(solution)/shard_map/ppermute | solution.py:27
  229.5 5.5 %collective-permute-start.28 = (f32[2,256]{1,0:T(2,128)S(1)}, f32[2,256]{1,0:T(2,128)S(1)}, u32[]{:S(2)}, u32[]{:S(2)}) collective-permute-start(f32[2,256]{1,0:T(2,128)S(1)} %pad_maximum_fusion.18), channel_id=1, source_target_pairs={{0,64},{4,68},{8,72},{12,76},{16,80},{20,84},{24,88},{28,92},{32,9... | collective-permute-start | bytes 6152 | tf_op jit(solution)/shard_map/ppermute | solution.py:27
  235.0 9.6 %collective-permute-start.29 = (f32[2,256]{1,0:T(2,128)S(1)}, f32[2,256]{1,0:T(2,128)S(1)}, u32[]{:S(2)}, u32[]{:S(2)}) collective-permute-start(f32[2,256]{1,0:T(2,128)S(1)} %pad_maximum_fusion.19), channel_id=1, source_target_pairs={{0,32},{4,36},{8,40},{12,44},{16,48},{20,52},{24,56},{28,60},{32,0... | collective-permute-start | bytes 6152 | tf_op jit(solution)/shard_map/ppermute | solution.py:27
  244.7 6.4 %collective-permute-start.30 = (f32[2,256]{1,0:T(2,128)S(1)}, f32[2,256]{1,0:T(2,128)S(1)}, u32[]{:S(2)}, u32[]{:S(2)}) collective-permute-start(f32[2,256]{1,0:T(2,128)S(1)} %pad_maximum_fusion.20), channel_id=1, source_target_pairs={{0,16},{4,20},{8,24},{12,28},{16,0},{20,4},{24,8},{28,12},{32,48},... | collective-permute-start | bytes 6152 | tf_op jit(solution)/shard_map/ppermute | solution.py:27
  251.1 5.5 %collective-permute-start.31 = (f32[2,256]{1,0:T(2,128)S(1)}, f32[2,256]{1,0:T(2,128)S(1)}, u32[]{:S(2)}, u32[]{:S(2)}) collective-permute-start(f32[2,256]{1,0:T(2,128)S(1)} %pad_maximum_fusion.21), channel_id=1, source_target_pairs={{0,8},{4,12},{8,0},{12,4},{16,24},{20,28},{24,16},{28,20},{32,40},... | collective-permute-start | bytes 6152 | tf_op jit(solution)/shard_map/ppermute | solution.py:27
  256.6 3.0 %collective-permute-start.32 = (f32[2,256]{1,0:T(2,128)S(1)}, f32[2,256]{1,0:T(2,128)S(1)}, u32[]{:S(2)}, u32[]{:S(2)}) collective-permute-start(f32[2,256]{1,0:T(2,128)S(1)} %pad_maximum_fusion.22), channel_id=1, source_target_pairs={{0,4},{4,0},{8,12},{12,8},{16,20},{20,16},{24,28},{28,24},{32,36},... | collective-permute-start | bytes 6152 | tf_op jit(solution)/shard_map/ppermute | solution.py:27

commit v10 on v8

--- a/solution.py
+++ b/solution.py
@@ -134,7 +134,7 @@
     ]
     gram_flat = jnp.concatenate(lower_blocks, axis=0).reshape(-1, 128)
     gram_sum = tree_sum(gram_flat, bits, 3).reshape(len(lower_blocks), block, block)
-    cross_bits = bits[:1] + bits[4:7] + bits[1:4] + bits[7:]
+    cross_bits = bits[:1] + bits[7:] + bits[4:7] + bits[1:4]
     cross = tree_sum(cross_part.reshape(-1, 128), cross_bits, 3).reshape(width, attrs)
     block_of = {}
     for n, (i, j) in enumerate((i, j) for i in range(nb) for j in range(i + 1)):

time: 262 us -> 266 us (1.015)
  waiting for transfers between devices: 40.2 us -> 47 us
  starting transfers between devices: 129 us -> 126 us
    ppermute x33, waiting for transfers between devices: 40.2 us -> 47 us  [partner(): return lax.ppermute(x, name, [(i, i ^ mask) for i in range(size)])]
    ppermute x33, starting transfers between devices: 129 us -> 126 us  [partner(): return lax.ppermute(x, name, [(i, i ^ mask) for i in range(size)])]
  transfers between devices with their start and end apart: 33 -> 33, of which waited for: 20 -> 19; matrix products, arithmetic and copies ran while one was open for 1% -> 1% of each run, Pallas kernels for 0% -> 0%
where the time goes in v10:
time: 266 us; the launch traced here: 264 us
  starting transfers between devices  126 us (47%)
  other arithmetic  56.4 us (21%)
  waiting for transfers between devices  47 us (18%)
  matrix products  22.8 us (9%)
  local copies, waits for them, and re-layouts  9.21 us (3%)
  between operations  2.97 us (1%)
    ppermute x33, starting transfers between devices, partner(): return lax.ppermute(x, name, [(i, i ^ mask) for i in range(size)])  126 us
    another operation x12, other arithmetic, blocked_cholesky(): head = lax.linalg.cholesky(trailing[:block, :block], symmetrize_input=False)  49.7 us
    ppermute x33, waiting for transfers between devices, partner(): return lax.ppermute(x, name, [(i, i ^ mask) for i in range(size)])  47 us
    dot_general x24, matrix products, triangular_inverse(): product = jnp.dot(product, eye + power, precision=HIGHEST)  6.05 us
    dot_general x24, matrix products, triangular_inverse(): power = jnp.dot(power, power, precision=HIGHEST)  5.85 us
  transfers between devices with their start and end apart: 33, of which 19 were waited for; matrix products, arithmetic and copies ran while one was open for 1% of the time, Pallas kernels for 0%

profile of v10, /device:TPU:6, one launch (start us, length us, event | category | flops | bytes accessed | tf_op | source)
XLA Modules:
  0.0 264.1 jit_solution(16321966470911329884)
XLA Ops:
  1.5 3.3 %fusion.1 = bf16[256,512]{1,0:T(8,128)(2,1)S(1)} fusion(bf16[256,1024]{1,0:T(8,128)(2,1)} %param.7, bf16[1024,512]{1,0:T(8,128)(2,1)S(1)} %copy-done, f32[512]{0:T(512)S(1)} %fusion.78), kind=kOutput, calls=%fused_computation.4 | convolution fusion | flops 268697600 | bytes 1837056 | tf_op jit(solution)/shard_map/dot_general | solution.py:119
  9.4 2.4 collective-permute-start
  13.0 2.7 %collective-permute-start.13 = (f32[256,128]{1,0:T(8,128)S(1)}, f32[256,128]{1,0:T(8,128)S(1)}, u32[]{:S(2)}, u32[]{:S(2)}) collective-permute-start(f32[256,128]{1,0:T(8,128)S(1)} %constant_dynamic-slice_fusion.1), channel_id=1, source_target_pairs={{0,1},{1,0},{2,3},{3,2},{4,5},{5,4},{6,7},{7,6},{8,9},{9,8},{10,11... | collective-permute-start | bytes 393224 | tf_op jit(solution)/shard_map/ppermute | solution.py:27
  16.0 4.3 %collective-permute-start.1 = (f32[320,128]{0,1:T(8,128)S(1)}, f32[320,128]{0,1:T(8,128)S(1)}, u32[]{:S(2)}, u32[]{:S(2)}) collective-permute-start(f32[320,128]{0,1:T(8,128)S(1)} %constant_dynamic-slice_fusion.4), channel_id=1, source_target_pairs={{0,8},{4,12},{8,0},{12,4},{16,24},{20,28},{24,16},{28,20},{32,40},... | collective-permute-start | bytes 491528 | tf_op jit(solution)/shard_map/ppermute | solution.py:27
  20.4 4.7 %collective-permute-done.1 = f32[320,128]{0,1:T(8,128)S(1)} collective-permute-done((f32[320,128]{0,1:T(8,128)S(1)}, f32[320,128]{0,1:T(8,128)S(1)}, u32[]{:S(2)}, u32[]{:S(2)}) %collective-permute-start.1) | collective-permute-done | bytes 163872 | tf_op jit(solution)/shard_map/ppermute | solution.py:27
  25.3 6.1 %collective-permute-start.2 = (f32[160,128]{0,1:T(8,128)S(1)}, f32[160,128]{0,1:T(8,128)S(1)}, u32[]{:S(2)}, u32[]{:S(2)}) collective-permute-start(f32[160,128]{0,1:T(8,128)S(1)} %constant_dynamic-slice_fusion.3), channel_id=1, source_target_pairs={{0,16},{4,20},{8,24},{12,28},{16,0},{20,4},{24,8},{28,12},{32,48},... | collective-permute-start | bytes 245768 | tf_op jit(solution)/shard_map/ppermute | solution.py:27
  31.4 3.6 %collective-permute-start.14 = (f32[128,128]{1,0:T(8,128)S(1)}, f32[128,128]{1,0:T(8,128)S(1)}, u32[]{:S(2)}, u32[]{:S(2)}) collective-permute-start(f32[128,128]{1,0:T(8,128)S(1)} %constant_dynamic-slice_fusion), channel_id=1, source_target_pairs={{0,2},{1,3},{2,0},{3,1},{4,6},{5,7},{6,4},{7,5},{8,10},{9,11},{10,... | collective-permute-start | bytes 196616 | tf_op jit(solution)/shard_map/ppermute | solution.py:27
  35.0 2.0 collective-permute-done.2
  37.1 8.4 %collective-permute-start.3 = (f32[160,128]{0,1:T(8,128)S(1)}, f32[160,128]{0,1:T(8,128)S(1)}, u32[]{:S(2)}, u32[]{:S(2)}) collective-permute-start(f32[160,128]{0,1:T(8,128)S(1)} %dynamic-slice_add_fusion.4), channel_id=1, source_target_pairs={{0,32},{4,36},{8,40},{12,44},{16,48},{20,52},{24,56},{28,60},{32,0... | collective-permute-start | bytes 245768 | tf_op jit(solution)/shard_map/ppermute | solution.py:27
  45.6 3.5 %collective-permute-start.15 = (f32[128,128]{1,0:T(8,128)S(1)}, f32[128,128]{1,0:T(8,128)S(1)}, u32[]{:S(2)}, u32[]{:S(2)}) collective-permute-start(f32[128,128]{1,0:T(8,128)S(1)} %dynamic-slice_add_fusion.5), channel_id=1, source_target_pairs={{0,64},{4,68},{8,72},{12,76},{16,80},{20,84},{24,88},{28,92},{32,9... | collective-permute-start | bytes 196616 | tf_op jit(solution)/shard_map/ppermute | solution.py:27
  49.9 3.5 %collective-permute-start.4 = (f32[160,128]{0,1:T(8,128)S(1)}, f32[160,128]{0,1:T(8,128)S(1)}, u32[]{:S(2)}, u32[]{:S(2)}) collective-permute-start(f32[160,128]{0,1:T(8,128)S(1)} %add.312), channel_id=1, source_target_pairs={{0,64},{4,68},{8,72},{12,76},{16,80},{20,84},{24,88},{28,92},{32,9... | collective-permute-start | bytes 245768 | tf_op jit(solution)/shard_map/ppermute | solution.py:27
  53.4 4.5 %collective-permute-start.16 = (f32[128,128]{1,0:T(8,128)S(1)}, f32[128,128]{1,0:T(8,128)S(1)}, u32[]{:S(2)}, u32[]{:S(2)}) collective-permute-start(f32[128,128]{1,0:T(8,128)S(1)} %add.339), channel_id=1, source_target_pairs={{0,128},{4,132},{8,136},{12,140},{16,144},{20,148},{24,152},{28,15... | collective-permute-start | bytes 196616 | tf_op jit(solution)/shard_map/ppermute | solution.py:27
  57.9 3.3 %collective-permute-start.5 = (f32[160,128]{0,1:T(8,128)S(1)}, f32[160,128]{0,1:T(8,128)S(1)}, u32[]{:S(2)}, u32[]{:S(2)}) collective-permute-start(f32[160,128]{0,1:T(8,128)S(1)} %add.313), channel_id=1, source_target_pairs={{0,128},{4,132},{8,136},{12,140},{16,144},{20,148},{24,152},{28,15... | collective-permute-start | bytes 245768 | tf_op jit(solution)/shard_map/ppermute | solution.py:27
  63.1 7.0 %collective-permute-start.17 = (f32[128,128]{1,0:T(8,128)S(1)}, f32[128,128]{1,0:T(8,128)S(1)}, u32[]{:S(2)}, u32[]{:S(2)}) collective-permute-start(f32[128,128]{1,0:T(8,128)S(1)} %add.340), channel_id=1, source_target_pairs={{0,256},{4,260},{8,264},{12,268},{16,272},{20,276},{24,280},{28,28... | collective-permute-start | bytes 196616 | tf_op jit(solution)/shard_map/ppermute | solution.py:27
  70.2 3.0 %collective-permute-done.17 = f32[128,128]{1,0:T(8,128)S(1)} collective-permute-done((f32[128,128]{1,0:T(8,128)S(1)}, f32[128,128]{1,0:T(8,128)S(1)}, u32[]{:S(2)}, u32[]{:S(2)}) %collective-permute-start.17) | collective-permute-done | bytes 65568 | tf_op jit(solution)/shard_map/ppermute | solution.py:27
  73.2 1.9 collective-permute-start.18
  75.2 7.0 %collective-permute-start.6 = (f32[160,128]{0,1:T(8,128)S(1)}, f32[160,128]{0,1:T(8,128)S(1)}, u32[]{:S(2)}, u32[]{:S(2)}) collective-permute-start(f32[160,128]{0,1:T(8,128)S(1)} %add.314), channel_id=1, source_target_pairs={{0,256},{4,260},{8,264},{12,268},{16,272},{20,276},{24,280},{28,28... | collective-permute-start | bytes 245768 | tf_op jit(solution)/shard_map/ppermute | solution.py:27
  82.3 5.9 %collective-permute-start.19 = (f32[128,128]{1,0:T(8,128)S(1)}, f32[128,128]{1,0:T(8,128)S(1)}, u32[]{:S(2)}, u32[]{:S(2)}) collective-permute-start(f32[128,128]{1,0:T(8,128)S(1)} %add.342), channel_id=1, source_target_pairs={{0,16},{4,20},{8,24},{12,28},{16,0},{20,4},{24,8},{28,12},{32,48},... | collective-permute-start | bytes 196616 | tf_op jit(solution)/shard_map/ppermute | solution.py:27
  88.2 3.1 %collective-permute-start.7 = (f32[160,128]{0,1:T(8,128)S(1)}, f32[160,128]{0,1:T(8,128)S(1)}, u32[]{:S(2)}, u32[]{:S(2)}) collective-permute-start(f32[160,128]{0,1:T(8,128)S(1)} %add.315), channel_id=1, source_target_pairs={{0,1},{1,0},{2,3},{3,2},{4,5},{5,4},{6,7},{7,6},{8,9},{9,8},{10,11... | collective-permute-start | bytes 245768 | tf_op jit(solution)/shard_map/ppermute | solution.py:27
  91.4 6.3 %collective-permute-start.20 = (f32[128,128]{1,0:T(8,128)S(1)}, f32[128,128]{1,0:T(8,128)S(1)}, u32[]{:S(2)}, u32[]{:S(2)}) collective-permute-start(f32[128,128]{1,0:T(8,128)S(1)} %add.343), channel_id=1, source_target_pairs={{0,32},{4,36},{8,40},{12,44},{16,48},{20,52},{24,56},{28,60},{32,0... | collective-permute-start | bytes 196616 | tf_op jit(solution)/shard_map/ppermute | solution.py:27
  97.8 3.6 %collective-permute-start.8 = (f32[160,128]{0,1:T(8,128)S(1)}, f32[160,128]{0,1:T(8,128)S(1)}, u32[]{:S(2)}, u32[]{:S(2)}) collective-permute-start(f32[160,128]{0,1:T(8,128)S(1)} %add.316), channel_id=1, source_target_pairs={{0,2},{1,3},{2,0},{3,1},{4,6},{5,7},{6,4},{7,5},{8,10},{9,11},{10,... | collective-permute-start | bytes 245768 | tf_op jit(solution)/shard_map/ppermute | solution.py:27
  101.5 3.6 %collective-permute-start.21 = (f32[128,128]{1,0:T(8,128)S(1)}, f32[128,128]{1,0:T(8,128)S(1)}, u32[]{:S(2)}, u32[]{:S(2)}) collective-permute-start(f32[128,128]{1,0:T(8,128)S(1)} %add.344), channel_id=1, source_target_pairs={{0,2},{1,3},{2,0},{3,1},{4,6},{5,7},{6,4},{7,5},{8,10},{9,11},{10,... | collective-permute-start | bytes 196616 | tf_op jit(solution)/shard_map/ppermute | solution.py:27
  106.3 3.6 %collective-permute-start.9 = (f32[160,128]{0,1:T(8,128)S(1)}, f32[160,128]{0,1:T(8,128)S(1)}, u32[]{:S(2)}, u32[]{:S(2)}) collective-permute-start(f32[160,128]{0,1:T(8,128)S(1)} %add.317), channel_id=1, source_target_pairs={{0,16},{4,20},{8,24},{12,28},{16,0},{20,4},{24,8},{28,12},{32,48},... | collective-permute-start | bytes 245768 | tf_op jit(solution)/shard_map/ppermute | solution.py:27
  109.9 3.5 %collective-permute-start.22 = (f32[256,128]{1,0:T(8,128)S(1)}, f32[256,128]{1,0:T(8,128)S(1)}, u32[]{:S(2)}, u32[]{:S(2)}) collective-permute-start(f32[256,128]{1,0:T(8,128)S(1)} %maximum_select_fusion.5), channel_id=1, source_target_pairs={{0,1},{1,0},{2,3},{3,2},{4,5},{5,4},{6,7},{7,6},{8,9},{9,8},{10,11... | collective-permute-start | bytes 393224 | tf_op jit(solution)/shard_map/ppermute | solution.py:27
  113.4 2.0 collective-permute-done.9
  115.6 1.9 collective-permute-start.10
  120.1 3.0 %collective-permute-done.10 = f32[320,128]{0,1:T(8,128)S(1)} collective-permute-done((f32[320,128]{0,1:T(8,128)S(1)}, f32[320,128]{0,1:T(8,128)S(1)}, u32[]{:S(2)}, u32[]{:S(2)}) %collective-permute-start.10) | collective-permute-done | bytes 163872 | tf_op jit(solution)/shard_map/ppermute | solution.py:27
  123.3 2.1 collective-permute-start.11
  131.5 11.7 %custom-call.6 = f32[128,128]{1,0:T(8,128)S(1)} custom-call(f32[128,128]{1,0:T(8,128)S(1)} %slice.271), custom_call_target="Cholesky" | custom-call | tf_op jit(solution)/shard_map/cholesky/custom-call.1 | solution.py:78
  148.4 11.7 %custom-call.7 = f32[128,128]{1,0:T(8,128)S(1)} custom-call(f32[128,128]{1,0:T(8,128)S(1)} %slice.275), custom_call_target="Cholesky" | custom-call | tf_op jit(solution)/shard_map/cholesky/custom-call.1 | solution.py:78
  165.1 11.7 %custom-call.8 = f32[128,128]{1,0:T(8,128)S(1)} custom-call(f32[128,128]{1,0:T(8,128)S(1)} %slice.280), custom_call_target="Cholesky" | custom-call | tf_op jit(solution)/shard_map/cholesky/custom-call.1 | solution.py:78
  181.5 11.7 %custom-call.9 = f32[128,128]{1,0:T(8,128)S(1)} custom-call(f32[128,128]{1,0:T(8,128)S(1)} %convolution_subtract_fusion.5), custom_call_target="Cholesky" | custom-call | tf_op jit(solution)/shard_map/cholesky/custom-call.1 | solution.py:78
  205.1 2.4 collective-permute-start.24
  210.3 3.6 %collective-permute-done.25 = f32[2,256]{1,0:T(2,128)S(1)} collective-permute-done((f32[2,256]{1,0:T(2,128)S(1)}, f32[2,256]{1,0:T(2,128)S(1)}, u32[]{:S(2)}, u32[]{:S(2)}) %collective-permute-start.25) | collective-permute-done | bytes 2080 | tf_op jit(solution)/shard_map/ppermute | solution.py:27
  213.8 2.6 collective-permute-start.26
  216.5 3.7 %collective-permute-done.26 = f32[2,256]{1,0:T(2,128)S(1)} collective-permute-done((f32[2,256]{1,0:T(2,128)S(1)}, f32[2,256]{1,0:T(2,128)S(1)}, u32[]{:S(2)}, u32[]{:S(2)}) %collective-permute-start.26) | collective-permute-done | bytes 2080 | tf_op jit(solution)/shard_map/ppermute | solution.py:27
  220.2 5.2 %collective-permute-start.27 = (f32[2,256]{1,0:T(2,128)S(1)}, f32[2,256]{1,0:T(2,128)S(1)}, u32[]{:S(2)}, u32[]{:S(2)}) collective-permute-start(f32[2,256]{1,0:T(2,128)S(1)} %pad_maximum_fusion.17), channel_id=1, source_target_pairs={{0,32},{4,36},{8,40},{12,44},{16,48},{20,52},{24,56},{28,60},{32,0... | collective-permute-start | bytes 6152 | tf_op jit(solution)/shard_map/ppermute | solution.py:27
  225.4 4.2 %collective-permute-done.27 = f32[2,256]{1,0:T(2,128)S(1)} collective-permute-done((f32[2,256]{1,0:T(2,128)S(1)}, f32[2,256]{1,0:T(2,128)S(1)}, u32[]{:S(2)}, u32[]{:S(2)}) %collective-permute-start.27) | collective-permute-done | bytes 2080 | tf_op jit(solution)/shard_map/ppermute | solution.py:27
  229.6 2.4 collective-permute-start.28
  232.0 3.1 %collective-permute-done.28 = f32[2,256]{1,0:T(2,128)S(1)} collective-permute-done((f32[2,256]{1,0:T(2,128)S(1)}, f32[2,256]{1,0:T(2,128)S(1)}, u32[]{:S(2)}, u32[]{:S(2)}) %collective-permute-start.28) | collective-permute-done | bytes 2080 | tf_op jit(solution)/shard_map/ppermute | solution.py:27
  235.1 2.4 collective-permute-start.29
  237.6 3.9 %collective-permute-done.29 = f32[2,256]{1,0:T(2,128)S(1)} collective-permute-done((f32[2,256]{1,0:T(2,128)S(1)}, f32[2,256]{1,0:T(2,128)S(1)}, u32[]{:S(2)}, u32[]{:S(2)}) %collective-permute-start.29) | collective-permute-done | bytes 2080 | tf_op jit(solution)/shard_map/ppermute | solution.py:27
  241.5 7.1 %collective-permute-start.30 = (f32[2,256]{1,0:T(2,128)S(1)}, f32[2,256]{1,0:T(2,128)S(1)}, u32[]{:S(2)}, u32[]{:S(2)}) collective-permute-start(f32[2,256]{1,0:T(2,128)S(1)} %pad_maximum_fusion.20), channel_id=1, source_target_pairs={{0,256},{4,260},{8,264},{12,268},{16,272},{20,276},{24,280},{28,28... | collective-permute-start | bytes 6152 | tf_op jit(solution)/shard_map/ppermute | solution.py:27
  248.6 2.3 collective-permute-done.30
  250.9 2.0 collective-permute-start.31
  253.0 3.4 %collective-permute-done.31 = f32[2,256]{1,0:T(2,128)S(1)} collective-permute-done((f32[2,256]{1,0:T(2,128)S(1)}, f32[2,256]{1,0:T(2,128)S(1)}, u32[]{:S(2)}, u32[]{:S(2)}) %collective-permute-start.31) | collective-permute-done | bytes 2080 | tf_op jit(solution)/shard_map/ppermute | solution.py:27
  256.4 3.8 %collective-permute-start.32 = (f32[2,256]{1,0:T(2,128)S(1)}, f32[2,256]{1,0:T(2,128)S(1)}, u32[]{:S(2)}, u32[]{:S(2)}) collective-permute-start(f32[2,256]{1,0:T(2,128)S(1)} %pad_maximum_fusion.22), channel_id=1, source_target_pairs={{0,2},{1,3},{2,0},{3,1},{4,6},{5,7},{6,4},{7,5},{8,10},{9,11},{10,... | collective-permute-start | bytes 6152 | tf_op jit(solution)/shard_map/ppermute | solution.py:27
  260.2 3.2 %collective-permute-done.32 = f32[2,256]{1,0:T(2,128)S(1)} collective-permute-done((f32[2,256]{1,0:T(2,128)S(1)}, f32[2,256]{1,0:T(2,128)S(1)}, u32[]{:S(2)}, u32[]{:S(2)}) %collective-permute-start.32) | collective-permute-done | bytes 2080 | tf_op jit(solution)/shard_map/ppermute | solution.py:27
  (199 shorter events, 48.9 us)
Async XLA Ops:
  0.0 1.5 copy-start
  0.7 0.7 copy-start.4
  4.7 1.2 copy-start.3
  7.0 5.0 %collective-permute-start.12 = (f32[512,128]{1,0:T(8,128)}, f32[512,128]{1,0:T(8,128)}, u32[]{:S(2)}, u32[]{:S(2)}) collective-permute-start(f32[512,128]{1,0:T(8,128)} %constant_dynamic-slice_fusion.2), channel_id=1, source_target_pairs={{0,4},{4,0},{8,12},{12,8},{16,20},{20,16},{24,28},{28,24},{32,36},... | collective-permute-start | bytes 786440 | tf_op jit(solution)/shard_map/ppermute | solution.py:27
  9.4 6.3 %collective-permute-start = (f32[640,128]{0,1:T(8,128)S(1)}, f32[640,128]{0,1:T(8,128)S(1)}, u32[]{:S(2)}, u32[]{:S(2)}) collective-permute-start(f32[640,128]{0,1:T(8,128)S(1)} %constant_dynamic-slice_fusion.5), channel_id=1, source_target_pairs={{0,4},{4,0},{8,12},{12,8},{16,20},{20,16},{24,28},{28,24},{32,36},... | collective-permute-start | bytes 983048 | tf_op jit(solution)/shard_map/ppermute | solution.py:27
  13.0 7.3 %collective-permute-start.13 = (f32[256,128]{1,0:T(8,128)S(1)}, f32[256,128]{1,0:T(8,128)S(1)}, u32[]{:S(2)}, u32[]{:S(2)}) collective-permute-start(f32[256,128]{1,0:T(8,128)S(1)} %constant_dynamic-slice_fusion.1), channel_id=1, source_target_pairs={{0,1},{1,0},{2,3},{3,2},{4,5},{5,4},{6,7},{7,6},{8,9},{9,8},{10,11... | collective-permute-start | bytes 393224 | tf_op jit(solution)/shard_map/ppermute | solution.py:27
  16.0 9.1 %collective-permute-start.1 = (f32[320,128]{0,1:T(8,128)S(1)}, f32[320,128]{0,1:T(8,128)S(1)}, u32[]{:S(2)}, u32[]{:S(2)}) collective-permute-start(f32[320,128]{0,1:T(8,128)S(1)} %constant_dynamic-slice_fusion.4), channel_id=1, source_target_pairs={{0,8},{4,12},{8,0},{12,4},{16,24},{20,28},{24,16},{28,20},{32,40},... | collective-permute-start | bytes 491528 | tf_op jit(solution)/shard_map/ppermute | solution.py:27
  25.3 11.7 %collective-permute-start.2 = (f32[160,128]{0,1:T(8,128)S(1)}, f32[160,128]{0,1:T(8,128)S(1)}, u32[]{:S(2)}, u32[]{:S(2)}) collective-permute-start(f32[160,128]{0,1:T(8,128)S(1)} %constant_dynamic-slice_fusion.3), channel_id=1, source_target_pairs={{0,16},{4,20},{8,24},{12,28},{16,0},{20,4},{24,8},{28,12},{32,48},... | collective-permute-start | bytes 245768 | tf_op jit(solution)/shard_map/ppermute | solution.py:27
  31.4 14.1 %collective-permute-start.14 = (f32[128,128]{1,0:T(8,128)S(1)}, f32[128,128]{1,0:T(8,128)S(1)}, u32[]{:S(2)}, u32[]{:S(2)}) collective-permute-start(f32[128,128]{1,0:T(8,128)S(1)} %constant_dynamic-slice_fusion), channel_id=1, source_target_pairs={{0,2},{1,3},{2,0},{3,1},{4,6},{5,7},{6,4},{7,5},{8,10},{9,11},{10,... | collective-permute-start | bytes 196616 | tf_op jit(solution)/shard_map/ppermute | solution.py:27
  37.1 12.7 %collective-permute-start.3 = (f32[160,128]{0,1:T(8,128)S(1)}, f32[160,128]{0,1:T(8,128)S(1)}, u32[]{:S(2)}, u32[]{:S(2)}) collective-permute-start(f32[160,128]{0,1:T(8,128)S(1)} %dynamic-slice_add_fusion.4), channel_id=1, source_target_pairs={{0,32},{4,36},{8,40},{12,44},{16,48},{20,52},{24,56},{28,60},{32,0... | collective-permute-start | bytes 245768 | tf_op jit(solution)/shard_map/ppermute | solution.py:27
  45.6 7.8 %collective-permute-start.15 = (f32[128,128]{1,0:T(8,128)S(1)}, f32[128,128]{1,0:T(8,128)S(1)}, u32[]{:S(2)}, u32[]{:S(2)}) collective-permute-start(f32[128,128]{1,0:T(8,128)S(1)} %dynamic-slice_add_fusion.5), channel_id=1, source_target_pairs={{0,64},{4,68},{8,72},{12,76},{16,80},{20,84},{24,88},{28,92},{32,9... | collective-permute-start | bytes 196616 | tf_op jit(solution)/shard_map/ppermute | solution.py:27
  49.9 8.0 %collective-permute-start.4 = (f32[160,128]{0,1:T(8,128)S(1)}, f32[160,128]{0,1:T(8,128)S(1)}, u32[]{:S(2)}, u32[]{:S(2)}) collective-permute-start(f32[160,128]{0,1:T(8,128)S(1)} %add.312), channel_id=1, source_target_pairs={{0,64},{4,68},{8,72},{12,76},{16,80},{20,84},{24,88},{28,92},{32,9... | collective-permute-start | bytes 245768 | tf_op jit(solution)/shard_map/ppermute | solution.py:27
  53.4 9.7 %collective-permute-start.16 = (f32[128,128]{1,0:T(8,128)S(1)}, f32[128,128]{1,0:T(8,128)S(1)}, u32[]{:S(2)}, u32[]{:S(2)}) collective-permute-start(f32[128,128]{1,0:T(8,128)S(1)} %add.339), channel_id=1, source_target_pairs={{0,128},{4,132},{8,136},{12,140},{16,144},{20,148},{24,152},{28,15... | collective-permute-start | bytes 196616 | tf_op jit(solution)/shard_map/ppermute | solution.py:27
  57.9 17.2 %collective-permute-start.5 = (f32[160,128]{0,1:T(8,128)S(1)}, f32[160,128]{0,1:T(8,128)S(1)}, u32[]{:S(2)}, u32[]{:S(2)}) collective-permute-start(f32[160,128]{0,1:T(8,128)S(1)} %add.313), channel_id=1, source_target_pairs={{0,128},{4,132},{8,136},{12,140},{16,144},{20,148},{24,152},{28,15... | collective-permute-start | bytes 245768 | tf_op jit(solution)/shard_map/ppermute | solution.py:27
  63.1 10.1 %collective-permute-start.17 = (f32[128,128]{1,0:T(8,128)S(1)}, f32[128,128]{1,0:T(8,128)S(1)}, u32[]{:S(2)}, u32[]{:S(2)}) collective-permute-start(f32[128,128]{1,0:T(8,128)S(1)} %add.340), channel_id=1, source_target_pairs={{0,256},{4,260},{8,264},{12,268},{16,272},{20,276},{24,280},{28,28... | collective-permute-start | bytes 196616 | tf_op jit(solution)/shard_map/ppermute | solution.py:27
  73.2 9.0 %collective-permute-start.18 = (f32[128,128]{1,0:T(8,128)S(1)}, f32[128,128]{1,0:T(8,128)S(1)}, u32[]{:S(2)}, u32[]{:S(2)}) collective-permute-start(f32[128,128]{1,0:T(8,128)S(1)} %add.341), channel_id=1, source_target_pairs={{0,8},{4,12},{8,0},{12,4},{16,24},{20,28},{24,16},{28,20},{32,40},... | collective-permute-start | bytes 196616 | tf_op jit(solution)/shard_map/ppermute | solution.py:27
  75.2 13.0 %collective-permute-start.6 = (f32[160,128]{0,1:T(8,128)S(1)}, f32[160,128]{0,1:T(8,128)S(1)}, u32[]{:S(2)}, u32[]{:S(2)}) collective-permute-start(f32[160,128]{0,1:T(8,128)S(1)} %add.314), channel_id=1, source_target_pairs={{0,256},{4,260},{8,264},{12,268},{16,272},{20,276},{24,280},{28,28... | collective-permute-start | bytes 245768 | tf_op jit(solution)/shard_map/ppermute | solution.py:27
  82.3 9.1 %collective-permute-start.19 = (f32[128,128]{1,0:T(8,128)S(1)}, f32[128,128]{1,0:T(8,128)S(1)}, u32[]{:S(2)}, u32[]{:S(2)}) collective-permute-start(f32[128,128]{1,0:T(8,128)S(1)} %add.342), channel_id=1, source_target_pairs={{0,16},{4,20},{8,24},{12,28},{16,0},{20,4},{24,8},{28,12},{32,48},... | collective-permute-start | bytes 196616 | tf_op jit(solution)/shard_map/ppermute | solution.py:27
  88.2 9.5 %collective-permute-start.7 = (f32[160,128]{0,1:T(8,128)S(1)}, f32[160,128]{0,1:T(8,128)S(1)}, u32[]{:S(2)}, u32[]{:S(2)}) collective-permute-start(f32[160,128]{0,1:T(8,128)S(1)} %add.315), channel_id=1, source_target_pairs={{0,1},{1,0},{2,3},{3,2},{4,5},{5,4},{6,7},{7,6},{8,9},{9,8},{10,11... | collective-permute-start | bytes 245768 | tf_op jit(solution)/shard_map/ppermute | solution.py:27
  91.4 10.1 %collective-permute-start.20 = (f32[128,128]{1,0:T(8,128)S(1)}, f32[128,128]{1,0:T(8,128)S(1)}, u32[]{:S(2)}, u32[]{:S(2)}) collective-permute-start(f32[128,128]{1,0:T(8,128)S(1)} %add.343), channel_id=1, source_target_pairs={{0,32},{4,36},{8,40},{12,44},{16,48},{20,52},{24,56},{28,60},{32,0... | collective-permute-start | bytes 196616 | tf_op jit(solution)/shard_map/ppermute | solution.py:27
  97.8 8.5 %collective-permute-start.8 = (f32[160,128]{0,1:T(8,128)S(1)}, f32[160,128]{0,1:T(8,128)S(1)}, u32[]{:S(2)}, u32[]{:S(2)}) collective-permute-start(f32[160,128]{0,1:T(8,128)S(1)} %add.316), channel_id=1, source_target_pairs={{0,2},{1,3},{2,0},{3,1},{4,6},{5,7},{6,4},{7,5},{8,10},{9,11},{10,... | collective-permute-start | bytes 245768 | tf_op jit(solution)/shard_map/ppermute | solution.py:27
  101.5 8.3 %collective-permute-start.21 = (f32[128,128]{1,0:T(8,128)S(1)}, f32[128,128]{1,0:T(8,128)S(1)}, u32[]{:S(2)}, u32[]{:S(2)}) collective-permute-start(f32[128,128]{1,0:T(8,128)S(1)} %add.344), channel_id=1, source_target_pairs={{0,2},{1,3},{2,0},{3,1},{4,6},{5,7},{6,4},{7,5},{8,10},{9,11},{10,... | collective-permute-start | bytes 196616 | tf_op jit(solution)/shard_map/ppermute | solution.py:27
  106.3 9.2 %collective-permute-start.9 = (f32[160,128]{0,1:T(8,128)S(1)}, f32[160,128]{0,1:T(8,128)S(1)}, u32[]{:S(2)}, u32[]{:S(2)}) collective-permute-start(f32[160,128]{0,1:T(8,128)S(1)} %add.317), channel_id=1, source_target_pairs={{0,16},{4,20},{8,24},{12,28},{16,0},{20,4},{24,8},{28,12},{32,48},... | collective-permute-start | bytes 245768 | tf_op jit(solution)/shard_map/ppermute | solution.py:27
  109.9 7.6 %collective-permute-start.22 = (f32[256,128]{1,0:T(8,128)S(1)}, f32[256,128]{1,0:T(8,128)S(1)}, u32[]{:S(2)}, u32[]{:S(2)}) collective-permute-start(f32[256,128]{1,0:T(8,128)S(1)} %maximum_select_fusion.5), channel_id=1, source_target_pairs={{0,1},{1,0},{2,3},{3,2},{4,5},{5,4},{6,7},{7,6},{8,9},{9,8},{10,11... | collective-permute-start | bytes 393224 | tf_op jit(solution)/shard_map/ppermute | solution.py:27
  115.6 7.6 %collective-permute-start.10 = (f32[320,128]{0,1:T(8,128)S(1)}, f32[320,128]{0,1:T(8,128)S(1)}, u32[]{:S(2)}, u32[]{:S(2)}) collective-permute-start(f32[320,128]{0,1:T(8,128)S(1)} %maximum_select_fusion.4), channel_id=1, source_target_pairs={{0,8},{4,12},{8,0},{12,4},{16,24},{20,28},{24,16},{28,20},{32,40},... | collective-permute-start | bytes 491528 | tf_op jit(solution)/shard_map/ppermute | solution.py:27
  117.6 7.9 %collective-permute-start.23 = (f32[512,128]{1,0:T(8,128)S(1)}, f32[512,128]{1,0:T(8,128)S(1)}, u32[]{:S(2)}, u32[]{:S(2)}) collective-permute-start(f32[512,128]{1,0:T(8,128)S(1)} %maximum_select_fusion.3), channel_id=1, source_target_pairs={{0,4},{4,0},{8,12},{12,8},{16,20},{20,16},{24,28},{28,24},{32,36},... | collective-permute-start | bytes 786440 | tf_op jit(solution)/shard_map/ppermute | solution.py:27
  123.3 3.7 %collective-permute-start.11 = (f32[640,128]{0,1:T(8,128)S(1)}, f32[640,128]{0,1:T(8,128)S(1)}, u32[]{:S(2)}, u32[]{:S(2)}) collective-permute-start(f32[640,128]{0,1:T(8,128)S(1)} %maximum_select_fusion.2), channel_id=1, source_target_pairs={{0,4},{4,0},{8,12},{12,8},{16,20},{20,16},{24,28},{28,24},{32,36},... | collective-permute-start | bytes 983048 | tf_op jit(solution)/shard_map/ppermute | solution.py:27
  198.2 0.9 copy-start.2
  199.6 0.9 copy-start.1
  205.1 3.2 %collective-permute-start.24 = (f32[2,256]{1,0:T(2,128)S(1)}, f32[2,256]{1,0:T(2,128)S(1)}, u32[]{:S(2)}, u32[]{:S(2)}) collective-permute-start(f32[2,256]{1,0:T(2,128)S(1)} %pad_maximum_fusion.14), channel_id=1, source_target_pairs={{0,4},{4,0},{8,12},{12,8},{16,20},{20,16},{24,28},{28,24},{32,36},... | collective-permute-start | bytes 6152 | tf_op jit(solution)/shard_map/ppermute | solution.py:27
  208.3 5.5 %collective-permute-start.25 = (f32[2,256]{1,0:T(2,128)S(1)}, f32[2,256]{1,0:T(2,128)S(1)}, u32[]{:S(2)}, u32[]{:S(2)}) collective-permute-start(f32[2,256]{1,0:T(2,128)S(1)} %pad_maximum_fusion.15), channel_id=1, source_target_pairs={{0,8},{4,12},{8,0},{12,4},{16,24},{20,28},{24,16},{28,20},{32,40},... | collective-permute-start | bytes 6152 | tf_op jit(solution)/shard_map/ppermute | solution.py:27
  213.8 6.4 %collective-permute-start.26 = (f32[2,256]{1,0:T(2,128)S(1)}, f32[2,256]{1,0:T(2,128)S(1)}, u32[]{:S(2)}, u32[]{:S(2)}) collective-permute-start(f32[2,256]{1,0:T(2,128)S(1)} %pad_maximum_fusion.16), channel_id=1, source_target_pairs={{0,16},{4,20},{8,24},{12,28},{16,0},{20,4},{24,8},{28,12},{32,48},... | collective-permute-start | bytes 6152 | tf_op jit(solution)/shard_map/ppermute | solution.py:27
  220.2 9.4 %collective-permute-start.27 = (f32[2,256]{1,0:T(2,128)S(1)}, f32[2,256]{1,0:T(2,128)S(1)}, u32[]{:S(2)}, u32[]{:S(2)}) collective-permute-start(f32[2,256]{1,0:T(2,128)S(1)} %pad_maximum_fusion.17), channel_id=1, source_target_pairs={{0,32},{4,36},{8,40},{12,44},{16,48},{20,52},{24,56},{28,60},{32,0... | collective-permute-start | bytes 6152 | tf_op jit(solution)/shard_map/ppermute | solution.py:27
  229.6 5.5 %collective-permute-start.28 = (f32[2,256]{1,0:T(2,128)S(1)}, f32[2,256]{1,0:T(2,128)S(1)}, u32[]{:S(2)}, u32[]{:S(2)}) collective-permute-start(f32[2,256]{1,0:T(2,128)S(1)} %pad_maximum_fusion.18), channel_id=1, source_target_pairs={{0,64},{4,68},{8,72},{12,76},{16,80},{20,84},{24,88},{28,92},{32,9... | collective-permute-start | bytes 6152 | tf_op jit(solution)/shard_map/ppermute | solution.py:27
  235.1 6.4 %collective-permute-start.29 = (f32[2,256]{1,0:T(2,128)S(1)}, f32[2,256]{1,0:T(2,128)S(1)}, u32[]{:S(2)}, u32[]{:S(2)}) collective-permute-start(f32[2,256]{1,0:T(2,128)S(1)} %pad_maximum_fusion.19), channel_id=1, source_target_pairs={{0,128},{4,132},{8,136},{12,140},{16,144},{20,148},{24,152},{28,15... | collective-permute-start | bytes 6152 | tf_op jit(solution)/shard_map/ppermute | solution.py:27
  241.5 9.4 %collective-permute-start.30 = (f32[2,256]{1,0:T(2,128)S(1)}, f32[2,256]{1,0:T(2,128)S(1)}, u32[]{:S(2)}, u32[]{:S(2)}) collective-permute-start(f32[2,256]{1,0:T(2,128)S(1)} %pad_maximum_fusion.20), channel_id=1, source_target_pairs={{0,256},{4,260},{8,264},{12,268},{16,272},{20,276},{24,280},{28,28... | collective-permute-start | bytes 6152 | tf_op jit(solution)/shard_map/ppermute | solution.py:27
  250.9 5.5 %collective-permute-start.31 = (f32[2,256]{1,0:T(2,128)S(1)}, f32[2,256]{1,0:T(2,128)S(1)}, u32[]{:S(2)}, u32[]{:S(2)}) collective-permute-start(f32[2,256]{1,0:T(2,128)S(1)} %pad_maximum_fusion.21), channel_id=1, source_target_pairs={{0,1},{1,0},{2,3},{3,2},{4,5},{5,4},{6,7},{7,6},{8,9},{9,8},{10,11... | collective-permute-start | bytes 6152 | tf_op jit(solution)/shard_map/ppermute | solution.py:27
  256.4 7.0 %collective-permute-start.32 = (f32[2,256]{1,0:T(2,128)S(1)}, f32[2,256]{1,0:T(2,128)S(1)}, u32[]{:S(2)}, u32[]{:S(2)}) collective-permute-start(f32[2,256]{1,0:T(2,128)S(1)} %pad_maximum_fusion.22), channel_id=1, source_target_pairs={{0,2},{1,3},{2,0},{3,1},{4,6},{5,7},{6,4},{7,5},{8,10},{9,11},{10,... | collective-permute-start | bytes 6152 | tf_op jit(solution)/shard_map/ppermute | solution.py:27

commit v11 on v8

--- a/solution.py
+++ b/solution.py
@@ -139,7 +139,8 @@
     block_of = {}
     for n, (i, j) in enumerate((i, j) for i in range(nb) for j in range(i + 1)):
         block_of[(i, j)] = gram_sum[n]
-        block_of[(j, i)] = gram_sum[n].T
+        if j < i:
+            block_of[(j, i)] = jnp.zeros_like(gram_sum[n])
     gram = jnp.concatenate(
         [jnp.concatenate([block_of[(i, j)] for j in range(nb)], axis=1) for i in range(nb)],
         axis=0,

time: 262 us -> 254 us (0.969)
  starting transfers between devices: 129 us -> 117 us
  waiting for transfers between devices: 40.2 us -> 46.1 us
    ppermute x33, starting transfers between devices: 129 us -> 117 us  [partner(): return lax.ppermute(x, name, [(i, i ^ mask) for i in range(size)])]
    ppermute x33, waiting for transfers between devices: 40.2 us -> 46.1 us  [partner(): return lax.ppermute(x, name, [(i, i ^ mask) for i in range(size)])]
  transfers between devices with their start and end apart: 33 -> 33, of which waited for: 20 -> 22; matrix products, arithmetic and copies ran while one was open for 1% -> 2% of each run, Pallas kernels for 0% -> 0%
where the time goes in v11:
time: 254 us; the launch traced here: 252 us
  starting transfers between devices  117 us (46%)
  other arithmetic  55.4 us (22%)
  waiting for transfers between devices  46.1 us (18%)
  matrix products  22.9 us (9%)
  local copies, waits for them, and re-layouts  7.05 us (3%)
  between operations  2.92 us (1%)
    ppermute x33, starting transfers between devices, partner(): return lax.ppermute(x, name, [(i, i ^ mask) for i in range(size)])  117 us
    another operation x12, other arithmetic, blocked_cholesky(): head = lax.linalg.cholesky(trailing[:block, :block], symmetrize_input=False)  49.9 us
    ppermute x33, waiting for transfers between devices, partner(): return lax.ppermute(x, name, [(i, i ^ mask) for i in range(size)])  46.1 us
    dot_general x24, matrix products, triangular_inverse(): power = jnp.dot(power, power, precision=HIGHEST)  5.92 us
    dot_general x24, matrix products, triangular_inverse(): product = jnp.dot(product, eye + power, precision=HIGHEST)  5.89 us
  transfers between devices with their start and end apart: 33, of which 22 were waited for; matrix products, arithmetic and copies ran while one was open for 2% of the time, Pallas kernels for 0%

profile of v11, /device:TPU:6, one launch (start us, length us, event | category | flops | bytes accessed | tf_op | source)
XLA Modules:
  0.0 251.6 jit_solution(1122669141856840226)
XLA Ops:
  1.5 3.3 %fusion.1 = bf16[256,512]{1,0:T(8,128)(2,1)S(1)} fusion(bf16[256,1024]{1,0:T(8,128)(2,1)} %param.7, bf16[1024,512]{1,0:T(8,128)(2,1)S(1)} %copy-done, f32[512]{0:T(512)S(1)} %fusion.78), kind=kOutput, calls=%fused_computation.4 | convolution fusion | flops 268697600 | bytes 1837056 | tf_op jit(solution)/shard_map/dot_general | solution.py:119
  9.4 2.4 collective-permute-start
  13.0 3.5 %collective-permute-start.13 = (f32[256,128]{1,0:T(8,128)S(1)}, f32[256,128]{1,0:T(8,128)S(1)}, u32[]{:S(2)}, u32[]{:S(2)}) collective-permute-start(f32[256,128]{1,0:T(8,128)S(1)} %constant_dynamic-slice_fusion.1), channel_id=1, source_target_pairs={{0,64},{4,68},{8,72},{12,76},{16,80},{20,84},{24,88},{28,92},{32,9... | collective-permute-start | bytes 393224 | tf_op jit(solution)/shard_map/ppermute | solution.py:27
  16.6 4.3 %collective-permute-start.1 = (f32[320,128]{1,0:T(8,128)S(1)}, f32[320,128]{1,0:T(8,128)S(1)}, u32[]{:S(2)}, u32[]{:S(2)}) collective-permute-start(f32[320,128]{1,0:T(8,128)S(1)} %constant_dynamic-slice_fusion.4), channel_id=1, source_target_pairs={{0,8},{4,12},{8,0},{12,4},{16,24},{20,28},{24,16},{28,20},{32,40},... | collective-permute-start | bytes 491528 | tf_op jit(solution)/shard_map/ppermute | solution.py:27
  20.9 4.0 %collective-permute-done.1 = f32[320,128]{1,0:T(8,128)S(1)} collective-permute-done((f32[320,128]{1,0:T(8,128)S(1)}, f32[320,128]{1,0:T(8,128)S(1)}, u32[]{:S(2)}, u32[]{:S(2)}) %collective-permute-start.1) | collective-permute-done | bytes 163872 | tf_op jit(solution)/shard_map/ppermute | solution.py:27
  25.0 6.1 %collective-permute-start.2 = (f32[160,128]{1,0:T(8,128)S(1)}, f32[160,128]{1,0:T(8,128)S(1)}, u32[]{:S(2)}, u32[]{:S(2)}) collective-permute-start(f32[160,128]{1,0:T(8,128)S(1)} %constant_dynamic-slice_fusion.3), channel_id=1, source_target_pairs={{0,16},{4,20},{8,24},{12,28},{16,0},{20,4},{24,8},{28,12},{32,48},... | collective-permute-start | bytes 245768 | tf_op jit(solution)/shard_map/ppermute | solution.py:27
  31.1 4.5 %collective-permute-start.14 = (f32[128,128]{1,0:T(8,128)S(1)}, f32[128,128]{1,0:T(8,128)S(1)}, u32[]{:S(2)}, u32[]{:S(2)}) collective-permute-start(f32[128,128]{1,0:T(8,128)S(1)} %constant_dynamic-slice_fusion), channel_id=1, source_target_pairs={{0,128},{4,132},{8,136},{12,140},{16,144},{20,148},{24,152},{28,15... | collective-permute-start | bytes 196616 | tf_op jit(solution)/shard_map/ppermute | solution.py:27
  35.7 8.5 %collective-permute-start.3 = (f32[160,128]{1,0:T(8,128)S(1)}, f32[160,128]{1,0:T(8,128)S(1)}, u32[]{:S(2)}, u32[]{:S(2)}) collective-permute-start(f32[160,128]{1,0:T(8,128)S(1)} %dynamic-slice_add_fusion.4), channel_id=1, source_target_pairs={{0,32},{4,36},{8,40},{12,44},{16,48},{20,52},{24,56},{28,60},{32,0... | collective-permute-start | bytes 245768 | tf_op jit(solution)/shard_map/ppermute | solution.py:27
  44.2 5.2 %collective-permute-start.15 = (f32[128,128]{1,0:T(8,128)S(1)}, f32[128,128]{1,0:T(8,128)S(1)}, u32[]{:S(2)}, u32[]{:S(2)}) collective-permute-start(f32[128,128]{1,0:T(8,128)S(1)} %dynamic-slice_add_fusion.5), channel_id=1, source_target_pairs={{0,256},{4,260},{8,264},{12,268},{16,272},{20,276},{24,280},{28,28... | collective-permute-start | bytes 196616 | tf_op jit(solution)/shard_map/ppermute | solution.py:27
  49.5 3.3 %collective-permute-start.4 = (f32[160,128]{1,0:T(8,128)S(1)}, f32[160,128]{1,0:T(8,128)S(1)}, u32[]{:S(2)}, u32[]{:S(2)}) collective-permute-start(f32[160,128]{1,0:T(8,128)S(1)} %add.312), channel_id=1, source_target_pairs={{0,64},{4,68},{8,72},{12,76},{16,80},{20,84},{24,88},{28,92},{32,9... | collective-permute-start | bytes 245768 | tf_op jit(solution)/shard_map/ppermute | solution.py:27
  52.7 2.4 collective-permute-done.15
  55.1 3.4 %collective-permute-start.16 = (f32[128,128]{1,0:T(8,128)S(1)}, f32[128,128]{1,0:T(8,128)S(1)}, u32[]{:S(2)}, u32[]{:S(2)}) collective-permute-start(f32[128,128]{1,0:T(8,128)S(1)} %add.339), channel_id=1, source_target_pairs={{0,8},{4,12},{8,0},{12,4},{16,24},{20,28},{24,16},{28,20},{32,40},... | collective-permute-start | bytes 196616 | tf_op jit(solution)/shard_map/ppermute | solution.py:27
  58.5 2.2 collective-permute-start.5
  61.3 5.1 %collective-permute-start.17 = (f32[128,128]{1,0:T(8,128)S(1)}, f32[128,128]{1,0:T(8,128)S(1)}, u32[]{:S(2)}, u32[]{:S(2)}) collective-permute-start(f32[128,128]{1,0:T(8,128)S(1)} %add.340), channel_id=1, source_target_pairs={{0,16},{4,20},{8,24},{12,28},{16,0},{20,4},{24,8},{28,12},{32,48},... | collective-permute-start | bytes 196616 | tf_op jit(solution)/shard_map/ppermute | solution.py:27
  66.4 2.3 collective-permute-done.17
  68.8 4.5 %collective-permute-start.18 = (f32[128,128]{1,0:T(8,128)S(1)}, f32[128,128]{1,0:T(8,128)S(1)}, u32[]{:S(2)}, u32[]{:S(2)}) collective-permute-start(f32[128,128]{1,0:T(8,128)S(1)} %add.341), channel_id=1, source_target_pairs={{0,32},{4,36},{8,40},{12,44},{16,48},{20,52},{24,56},{28,60},{32,0... | collective-permute-start | bytes 196616 | tf_op jit(solution)/shard_map/ppermute | solution.py:27
  73.3 4.4 %collective-permute-start.6 = (f32[160,128]{1,0:T(8,128)S(1)}, f32[160,128]{1,0:T(8,128)S(1)}, u32[]{:S(2)}, u32[]{:S(2)}) collective-permute-start(f32[160,128]{1,0:T(8,128)S(1)} %add.314), channel_id=1, source_target_pairs={{0,256},{4,260},{8,264},{12,268},{16,272},{20,276},{24,280},{28,28... | collective-permute-start | bytes 245768 | tf_op jit(solution)/shard_map/ppermute | solution.py:27
  79.6 2.6 %collective-permute-start.19 = (f32[128,128]{1,0:T(8,128)S(1)}, f32[128,128]{1,0:T(8,128)S(1)}, u32[]{:S(2)}, u32[]{:S(2)}) collective-permute-start(f32[128,128]{1,0:T(8,128)S(1)} %add.342), channel_id=1, source_target_pairs={{0,1},{1,0},{2,3},{3,2},{4,5},{5,4},{6,7},{7,6},{8,9},{9,8},{10,11... | collective-permute-start | bytes 196616 | tf_op jit(solution)/shard_map/ppermute | solution.py:27
  83.6 2.7 %collective-permute-start.7 = (f32[160,128]{1,0:T(8,128)S(1)}, f32[160,128]{1,0:T(8,128)S(1)}, u32[]{:S(2)}, u32[]{:S(2)}) collective-permute-start(f32[160,128]{1,0:T(8,128)S(1)} %add.315), channel_id=1, source_target_pairs={{0,1},{1,0},{2,3},{3,2},{4,5},{5,4},{6,7},{7,6},{8,9},{9,8},{10,11... | collective-permute-start | bytes 245768 | tf_op jit(solution)/shard_map/ppermute | solution.py:27
  86.4 2.9 %collective-permute-start.20 = (f32[128,128]{1,0:T(8,128)S(1)}, f32[128,128]{1,0:T(8,128)S(1)}, u32[]{:S(2)}, u32[]{:S(2)}) collective-permute-start(f32[128,128]{1,0:T(8,128)S(1)} %add.343), channel_id=1, source_target_pairs={{0,2},{1,3},{2,0},{3,1},{4,6},{5,7},{6,4},{7,5},{8,10},{9,11},{10,... | collective-permute-start | bytes 196616 | tf_op jit(solution)/shard_map/ppermute | solution.py:27
  90.0 3.7 %collective-permute-start.8 = (f32[160,128]{1,0:T(8,128)S(1)}, f32[160,128]{1,0:T(8,128)S(1)}, u32[]{:S(2)}, u32[]{:S(2)}) collective-permute-start(f32[160,128]{1,0:T(8,128)S(1)} %add.316), channel_id=1, source_target_pairs={{0,2},{1,3},{2,0},{3,1},{4,6},{5,7},{6,4},{7,5},{8,10},{9,11},{10,... | collective-permute-start | bytes 245768 | tf_op jit(solution)/shard_map/ppermute | solution.py:27
  94.0 3.0 %collective-permute-start.21 = (f32[128,128]{1,0:T(8,128)S(1)}, f32[128,128]{1,0:T(8,128)S(1)}, u32[]{:S(2)}, u32[]{:S(2)}) collective-permute-start(f32[128,128]{1,0:T(8,128)S(1)} %add.344), channel_id=1, source_target_pairs={{0,128},{4,132},{8,136},{12,140},{16,144},{20,148},{24,152},{28,15... | collective-permute-start | bytes 196616 | tf_op jit(solution)/shard_map/ppermute | solution.py:27
  97.9 3.6 %collective-permute-start.9 = (f32[160,128]{1,0:T(8,128)S(1)}, f32[160,128]{1,0:T(8,128)S(1)}, u32[]{:S(2)}, u32[]{:S(2)}) collective-permute-start(f32[160,128]{1,0:T(8,128)S(1)} %add.317), channel_id=1, source_target_pairs={{0,16},{4,20},{8,24},{12,28},{16,0},{20,4},{24,8},{28,12},{32,48},... | collective-permute-start | bytes 245768 | tf_op jit(solution)/shard_map/ppermute | solution.py:27
  101.8 3.1 %collective-permute-start.22 = (f32[256,128]{1,0:T(8,128)S(1)}, f32[256,128]{1,0:T(8,128)S(1)}, u32[]{:S(2)}, u32[]{:S(2)}) collective-permute-start(f32[256,128]{1,0:T(8,128)S(1)} %maximum_select_fusion.5), channel_id=1, source_target_pairs={{0,64},{4,68},{8,72},{12,76},{16,80},{20,84},{24,88},{28,92},{32,9... | collective-permute-start | bytes 393224 | tf_op jit(solution)/shard_map/ppermute | solution.py:27
  106.0 1.9 collective-permute-start.10
  108.7 1.9 collective-permute-start.23
  111.3 1.9 collective-permute-done.10
  113.3 2.1 collective-permute-start.11
  117.9 11.7 %custom-call.6 = f32[128,128]{1,0:T(8,128)S(1)} custom-call(f32[128,128]{1,0:T(8,128)S(1)} %slice.265), custom_call_target="Cholesky" | custom-call | tf_op jit(solution)/shard_map/cholesky/custom-call.1 | solution.py:78
  134.8 11.7 %custom-call.7 = f32[128,128]{1,0:T(8,128)S(1)} custom-call(f32[128,128]{1,0:T(8,128)S(1)} %slice.269), custom_call_target="Cholesky" | custom-call | tf_op jit(solution)/shard_map/cholesky/custom-call.1 | solution.py:78
  151.7 11.7 %custom-call.8 = f32[128,128]{1,0:T(8,128)S(1)} custom-call(f32[128,128]{1,0:T(8,128)S(1)} %slice.274), custom_call_target="Cholesky" | custom-call | tf_op jit(solution)/shard_map/cholesky/custom-call.1 | solution.py:78
  168.2 11.7 %custom-call.9 = f32[128,128]{1,0:T(8,128)S(1)} custom-call(f32[128,128]{1,0:T(8,128)S(1)} %convolution_subtract_fusion.5), custom_call_target="Cholesky" | custom-call | tf_op jit(solution)/shard_map/cholesky/custom-call.1 | solution.py:78
  192.6 2.4 collective-permute-start.24
  197.8 3.6 %collective-permute-done.25 = f32[2,256]{1,0:T(2,128)S(1)} collective-permute-done((f32[2,256]{1,0:T(2,128)S(1)}, f32[2,256]{1,0:T(2,128)S(1)}, u32[]{:S(2)}, u32[]{:S(2)}) %collective-permute-start.25) | collective-permute-done | bytes 2080 | tf_op jit(solution)/shard_map/ppermute | solution.py:27
  201.4 3.1 %collective-permute-start.26 = (f32[2,256]{1,0:T(2,128)S(1)}, f32[2,256]{1,0:T(2,128)S(1)}, u32[]{:S(2)}, u32[]{:S(2)}) collective-permute-start(f32[2,256]{1,0:T(2,128)S(1)} %pad_maximum_fusion.15), channel_id=1, source_target_pairs={{0,16},{4,20},{8,24},{12,28},{16,0},{20,4},{24,8},{28,12},{32,48},... | collective-permute-start | bytes 6152 | tf_op jit(solution)/shard_map/ppermute | solution.py:27
  204.4 3.3 %collective-permute-done.26 = f32[2,256]{1,0:T(2,128)S(1)} collective-permute-done((f32[2,256]{1,0:T(2,128)S(1)}, f32[2,256]{1,0:T(2,128)S(1)}, u32[]{:S(2)}, u32[]{:S(2)}) %collective-permute-start.26) | collective-permute-done | bytes 2080 | tf_op jit(solution)/shard_map/ppermute | solution.py:27
  207.8 6.0 %collective-permute-start.27 = (f32[2,256]{1,0:T(2,128)S(1)}, f32[2,256]{1,0:T(2,128)S(1)}, u32[]{:S(2)}, u32[]{:S(2)}) collective-permute-start(f32[2,256]{1,0:T(2,128)S(1)} %pad_maximum_fusion.16), channel_id=1, source_target_pairs={{0,32},{4,36},{8,40},{12,44},{16,48},{20,52},{24,56},{28,60},{32,0... | collective-permute-start | bytes 6152 | tf_op jit(solution)/shard_map/ppermute | solution.py:27
  213.8 3.4 %collective-permute-done.27 = f32[2,256]{1,0:T(2,128)S(1)} collective-permute-done((f32[2,256]{1,0:T(2,128)S(1)}, f32[2,256]{1,0:T(2,128)S(1)}, u32[]{:S(2)}, u32[]{:S(2)}) %collective-permute-start.27) | collective-permute-done | bytes 2080 | tf_op jit(solution)/shard_map/ppermute | solution.py:27
  217.2 2.6 %collective-permute-start.28 = (f32[2,256]{1,0:T(2,128)S(1)}, f32[2,256]{1,0:T(2,128)S(1)}, u32[]{:S(2)}, u32[]{:S(2)}) collective-permute-start(f32[2,256]{1,0:T(2,128)S(1)} %pad_maximum_fusion.17), channel_id=1, source_target_pairs={{0,64},{4,68},{8,72},{12,76},{16,80},{20,84},{24,88},{28,92},{32,9... | collective-permute-start | bytes 6152 | tf_op jit(solution)/shard_map/ppermute | solution.py:27
  219.7 2.9 %collective-permute-done.28 = f32[2,256]{1,0:T(2,128)S(1)} collective-permute-done((f32[2,256]{1,0:T(2,128)S(1)}, f32[2,256]{1,0:T(2,128)S(1)}, u32[]{:S(2)}, u32[]{:S(2)}) %collective-permute-start.28) | collective-permute-done | bytes 2080 | tf_op jit(solution)/shard_map/ppermute | solution.py:27
  222.7 2.3 collective-permute-start.29
  225.0 4.1 %collective-permute-done.29 = f32[2,256]{1,0:T(2,128)S(1)} collective-permute-done((f32[2,256]{1,0:T(2,128)S(1)}, f32[2,256]{1,0:T(2,128)S(1)}, u32[]{:S(2)}, u32[]{:S(2)}) %collective-permute-start.29) | collective-permute-done | bytes 2080 | tf_op jit(solution)/shard_map/ppermute | solution.py:27
  229.1 5.7 %collective-permute-start.30 = (f32[2,256]{1,0:T(2,128)S(1)}, f32[2,256]{1,0:T(2,128)S(1)}, u32[]{:S(2)}, u32[]{:S(2)}) collective-permute-start(f32[2,256]{1,0:T(2,128)S(1)} %pad_maximum_fusion.19), channel_id=1, source_target_pairs={{0,256},{4,260},{8,264},{12,268},{16,272},{20,276},{24,280},{28,28... | collective-permute-start | bytes 6152 | tf_op jit(solution)/shard_map/ppermute | solution.py:27
  234.8 3.6 %collective-permute-done.30 = f32[2,256]{1,0:T(2,128)S(1)} collective-permute-done((f32[2,256]{1,0:T(2,128)S(1)}, f32[2,256]{1,0:T(2,128)S(1)}, u32[]{:S(2)}, u32[]{:S(2)}) %collective-permute-start.30) | collective-permute-done | bytes 2080 | tf_op jit(solution)/shard_map/ppermute | solution.py:27
  238.5 2.7 %collective-permute-start.31 = (f32[2,256]{1,0:T(2,128)S(1)}, f32[2,256]{1,0:T(2,128)S(1)}, u32[]{:S(2)}, u32[]{:S(2)}) collective-permute-start(f32[2,256]{1,0:T(2,128)S(1)} %pad_maximum_fusion.20), channel_id=1, source_target_pairs={{0,1},{1,0},{2,3},{3,2},{4,5},{5,4},{6,7},{7,6},{8,9},{9,8},{10,11... | collective-permute-start | bytes 6152 | tf_op jit(solution)/shard_map/ppermute | solution.py:27
  241.2 2.7 %collective-permute-done.31 = f32[2,256]{1,0:T(2,128)S(1)} collective-permute-done((f32[2,256]{1,0:T(2,128)S(1)}, f32[2,256]{1,0:T(2,128)S(1)}, u32[]{:S(2)}, u32[]{:S(2)}) %collective-permute-start.31) | collective-permute-done | bytes 2080 | tf_op jit(solution)/shard_map/ppermute | solution.py:27
  244.0 3.7 %collective-permute-start.32 = (f32[2,256]{1,0:T(2,128)S(1)}, f32[2,256]{1,0:T(2,128)S(1)}, u32[]{:S(2)}, u32[]{:S(2)}) collective-permute-start(f32[2,256]{1,0:T(2,128)S(1)} %pad_maximum_fusion.21), channel_id=1, source_target_pairs={{0,2},{1,3},{2,0},{3,1},{4,6},{5,7},{6,4},{7,5},{8,10},{9,11},{10,... | collective-permute-start | bytes 6152 | tf_op jit(solution)/shard_map/ppermute | solution.py:27
  247.7 3.3 %collective-permute-done.32 = f32[2,256]{1,0:T(2,128)S(1)} collective-permute-done((f32[2,256]{1,0:T(2,128)S(1)}, f32[2,256]{1,0:T(2,128)S(1)}, u32[]{:S(2)}, u32[]{:S(2)}) %collective-permute-start.32) | collective-permute-done | bytes 2080 | tf_op jit(solution)/shard_map/ppermute | solution.py:27
  (194 shorter events, 47.6 us)
Async XLA Ops:
  0.0 1.5 copy-start
  0.7 0.7 copy-start.5
  4.7 1.2 copy-start.4
  7.0 5.0 %collective-permute-start.12 = (f32[512,128]{1,0:T(8,128)}, f32[512,128]{1,0:T(8,128)}, u32[]{:S(2)}, u32[]{:S(2)}) collective-permute-start(f32[512,128]{1,0:T(8,128)} %constant_dynamic-slice_fusion.2), channel_id=1, source_target_pairs={{0,4},{4,0},{8,12},{12,8},{16,20},{20,16},{24,28},{28,24},{32,36},... | collective-permute-start | bytes 786440 | tf_op jit(solution)/shard_map/ppermute | solution.py:27
  9.4 7.1 %collective-permute-start = (f32[640,128]{1,0:T(8,128)S(1)}, f32[640,128]{1,0:T(8,128)S(1)}, u32[]{:S(2)}, u32[]{:S(2)}) collective-permute-start(f32[640,128]{1,0:T(8,128)S(1)} %constant_dynamic-slice_fusion.5), channel_id=1, source_target_pairs={{0,4},{4,0},{8,12},{12,8},{16,20},{20,16},{24,28},{28,24},{32,36},... | collective-permute-start | bytes 983048 | tf_op jit(solution)/shard_map/ppermute | solution.py:27
  13.0 7.9 %collective-permute-start.13 = (f32[256,128]{1,0:T(8,128)S(1)}, f32[256,128]{1,0:T(8,128)S(1)}, u32[]{:S(2)}, u32[]{:S(2)}) collective-permute-start(f32[256,128]{1,0:T(8,128)S(1)} %constant_dynamic-slice_fusion.1), channel_id=1, source_target_pairs={{0,64},{4,68},{8,72},{12,76},{16,80},{20,84},{24,88},{28,92},{32,9... | collective-permute-start | bytes 393224 | tf_op jit(solution)/shard_map/ppermute | solution.py:27
  16.6 8.4 %collective-permute-start.1 = (f32[320,128]{1,0:T(8,128)S(1)}, f32[320,128]{1,0:T(8,128)S(1)}, u32[]{:S(2)}, u32[]{:S(2)}) collective-permute-start(f32[320,128]{1,0:T(8,128)S(1)} %constant_dynamic-slice_fusion.4), channel_id=1, source_target_pairs={{0,8},{4,12},{8,0},{12,4},{16,24},{20,28},{24,16},{28,20},{32,40},... | collective-permute-start | bytes 491528 | tf_op jit(solution)/shard_map/ppermute | solution.py:27
  25.0 10.6 %collective-permute-start.2 = (f32[160,128]{1,0:T(8,128)S(1)}, f32[160,128]{1,0:T(8,128)S(1)}, u32[]{:S(2)}, u32[]{:S(2)}) collective-permute-start(f32[160,128]{1,0:T(8,128)S(1)} %constant_dynamic-slice_fusion.3), channel_id=1, source_target_pairs={{0,16},{4,20},{8,24},{12,28},{16,0},{20,4},{24,8},{28,12},{32,48},... | collective-permute-start | bytes 245768 | tf_op jit(solution)/shard_map/ppermute | solution.py:27
  31.1 13.0 %collective-permute-start.14 = (f32[128,128]{1,0:T(8,128)S(1)}, f32[128,128]{1,0:T(8,128)S(1)}, u32[]{:S(2)}, u32[]{:S(2)}) collective-permute-start(f32[128,128]{1,0:T(8,128)S(1)} %constant_dynamic-slice_fusion), channel_id=1, source_target_pairs={{0,128},{4,132},{8,136},{12,140},{16,144},{20,148},{24,152},{28,15... | collective-permute-start | bytes 196616 | tf_op jit(solution)/shard_map/ppermute | solution.py:27
  35.7 13.8 %collective-permute-start.3 = (f32[160,128]{1,0:T(8,128)S(1)}, f32[160,128]{1,0:T(8,128)S(1)}, u32[]{:S(2)}, u32[]{:S(2)}) collective-permute-start(f32[160,128]{1,0:T(8,128)S(1)} %dynamic-slice_add_fusion.4), channel_id=1, source_target_pairs={{0,32},{4,36},{8,40},{12,44},{16,48},{20,52},{24,56},{28,60},{32,0... | collective-permute-start | bytes 245768 | tf_op jit(solution)/shard_map/ppermute | solution.py:27
  44.2 10.9 %collective-permute-start.15 = (f32[128,128]{1,0:T(8,128)S(1)}, f32[128,128]{1,0:T(8,128)S(1)}, u32[]{:S(2)}, u32[]{:S(2)}) collective-permute-start(f32[128,128]{1,0:T(8,128)S(1)} %dynamic-slice_add_fusion.5), channel_id=1, source_target_pairs={{0,256},{4,260},{8,264},{12,268},{16,272},{20,276},{24,280},{28,28... | collective-permute-start | bytes 196616 | tf_op jit(solution)/shard_map/ppermute | solution.py:27
  49.5 9.0 %collective-permute-start.4 = (f32[160,128]{1,0:T(8,128)S(1)}, f32[160,128]{1,0:T(8,128)S(1)}, u32[]{:S(2)}, u32[]{:S(2)}) collective-permute-start(f32[160,128]{1,0:T(8,128)S(1)} %add.312), channel_id=1, source_target_pairs={{0,64},{4,68},{8,72},{12,76},{16,80},{20,84},{24,88},{28,92},{32,9... | collective-permute-start | bytes 245768 | tf_op jit(solution)/shard_map/ppermute | solution.py:27
  55.1 6.2 %collective-permute-start.16 = (f32[128,128]{1,0:T(8,128)S(1)}, f32[128,128]{1,0:T(8,128)S(1)}, u32[]{:S(2)}, u32[]{:S(2)}) collective-permute-start(f32[128,128]{1,0:T(8,128)S(1)} %add.339), channel_id=1, source_target_pairs={{0,8},{4,12},{8,0},{12,4},{16,24},{20,28},{24,16},{28,20},{32,40},... | collective-permute-start | bytes 196616 | tf_op jit(solution)/shard_map/ppermute | solution.py:27
  58.5 14.8 %collective-permute-start.5 = (f32[160,128]{1,0:T(8,128)S(1)}, f32[160,128]{1,0:T(8,128)S(1)}, u32[]{:S(2)}, u32[]{:S(2)}) collective-permute-start(f32[160,128]{1,0:T(8,128)S(1)} %add.313), channel_id=1, source_target_pairs={{0,128},{4,132},{8,136},{12,140},{16,144},{20,148},{24,152},{28,15... | collective-permute-start | bytes 245768 | tf_op jit(solution)/shard_map/ppermute | solution.py:27
  61.3 7.5 %collective-permute-start.17 = (f32[128,128]{1,0:T(8,128)S(1)}, f32[128,128]{1,0:T(8,128)S(1)}, u32[]{:S(2)}, u32[]{:S(2)}) collective-permute-start(f32[128,128]{1,0:T(8,128)S(1)} %add.340), channel_id=1, source_target_pairs={{0,16},{4,20},{8,24},{12,28},{16,0},{20,4},{24,8},{28,12},{32,48},... | collective-permute-start | bytes 196616 | tf_op jit(solution)/shard_map/ppermute | solution.py:27
  68.8 10.9 %collective-permute-start.18 = (f32[128,128]{1,0:T(8,128)S(1)}, f32[128,128]{1,0:T(8,128)S(1)}, u32[]{:S(2)}, u32[]{:S(2)}) collective-permute-start(f32[128,128]{1,0:T(8,128)S(1)} %add.341), channel_id=1, source_target_pairs={{0,32},{4,36},{8,40},{12,44},{16,48},{20,52},{24,56},{28,60},{32,0... | collective-permute-start | bytes 196616 | tf_op jit(solution)/shard_map/ppermute | solution.py:27
  73.3 10.2 %collective-permute-start.6 = (f32[160,128]{1,0:T(8,128)S(1)}, f32[160,128]{1,0:T(8,128)S(1)}, u32[]{:S(2)}, u32[]{:S(2)}) collective-permute-start(f32[160,128]{1,0:T(8,128)S(1)} %add.314), channel_id=1, source_target_pairs={{0,256},{4,260},{8,264},{12,268},{16,272},{20,276},{24,280},{28,28... | collective-permute-start | bytes 245768 | tf_op jit(solution)/shard_map/ppermute | solution.py:27
  79.6 6.7 %collective-permute-start.19 = (f32[128,128]{1,0:T(8,128)S(1)}, f32[128,128]{1,0:T(8,128)S(1)}, u32[]{:S(2)}, u32[]{:S(2)}) collective-permute-start(f32[128,128]{1,0:T(8,128)S(1)} %add.342), channel_id=1, source_target_pairs={{0,1},{1,0},{2,3},{3,2},{4,5},{5,4},{6,7},{7,6},{8,9},{9,8},{10,11... | collective-permute-start | bytes 196616 | tf_op jit(solution)/shard_map/ppermute | solution.py:27
  83.6 6.4 %collective-permute-start.7 = (f32[160,128]{1,0:T(8,128)S(1)}, f32[160,128]{1,0:T(8,128)S(1)}, u32[]{:S(2)}, u32[]{:S(2)}) collective-permute-start(f32[160,128]{1,0:T(8,128)S(1)} %add.315), channel_id=1, source_target_pairs={{0,1},{1,0},{2,3},{3,2},{4,5},{5,4},{6,7},{7,6},{8,9},{9,8},{10,11... | collective-permute-start | bytes 245768 | tf_op jit(solution)/shard_map/ppermute | solution.py:27
  86.4 7.7 %collective-permute-start.20 = (f32[128,128]{1,0:T(8,128)S(1)}, f32[128,128]{1,0:T(8,128)S(1)}, u32[]{:S(2)}, u32[]{:S(2)}) collective-permute-start(f32[128,128]{1,0:T(8,128)S(1)} %add.343), channel_id=1, source_target_pairs={{0,2},{1,3},{2,0},{3,1},{4,6},{5,7},{6,4},{7,5},{8,10},{9,11},{10,... | collective-permute-start | bytes 196616 | tf_op jit(solution)/shard_map/ppermute | solution.py:27
  90.0 7.8 %collective-permute-start.8 = (f32[160,128]{1,0:T(8,128)S(1)}, f32[160,128]{1,0:T(8,128)S(1)}, u32[]{:S(2)}, u32[]{:S(2)}) collective-permute-start(f32[160,128]{1,0:T(8,128)S(1)} %add.316), channel_id=1, source_target_pairs={{0,2},{1,3},{2,0},{3,1},{4,6},{5,7},{6,4},{7,5},{8,10},{9,11},{10,... | collective-permute-start | bytes 245768 | tf_op jit(solution)/shard_map/ppermute | solution.py:27
  94.0 7.8 %collective-permute-start.21 = (f32[128,128]{1,0:T(8,128)S(1)}, f32[128,128]{1,0:T(8,128)S(1)}, u32[]{:S(2)}, u32[]{:S(2)}) collective-permute-start(f32[128,128]{1,0:T(8,128)S(1)} %add.344), channel_id=1, source_target_pairs={{0,128},{4,132},{8,136},{12,140},{16,144},{20,148},{24,152},{28,15... | collective-permute-start | bytes 196616 | tf_op jit(solution)/shard_map/ppermute | solution.py:27
  97.9 8.1 %collective-permute-start.9 = (f32[160,128]{1,0:T(8,128)S(1)}, f32[160,128]{1,0:T(8,128)S(1)}, u32[]{:S(2)}, u32[]{:S(2)}) collective-permute-start(f32[160,128]{1,0:T(8,128)S(1)} %add.317), channel_id=1, source_target_pairs={{0,16},{4,20},{8,24},{12,28},{16,0},{20,4},{24,8},{28,12},{32,48},... | collective-permute-start | bytes 245768 | tf_op jit(solution)/shard_map/ppermute | solution.py:27
  101.8 6.9 %collective-permute-start.22 = (f32[256,128]{1,0:T(8,128)S(1)}, f32[256,128]{1,0:T(8,128)S(1)}, u32[]{:S(2)}, u32[]{:S(2)}) collective-permute-start(f32[256,128]{1,0:T(8,128)S(1)} %maximum_select_fusion.5), channel_id=1, source_target_pairs={{0,64},{4,68},{8,72},{12,76},{16,80},{20,84},{24,88},{28,92},{32,9... | collective-permute-start | bytes 393224 | tf_op jit(solution)/shard_map/ppermute | solution.py:27
  106.0 7.2 %collective-permute-start.10 = (f32[320,128]{1,0:T(8,128)S(1)}, f32[320,128]{1,0:T(8,128)S(1)}, u32[]{:S(2)}, u32[]{:S(2)}) collective-permute-start(f32[320,128]{1,0:T(8,128)S(1)} %maximum_select_fusion.4), channel_id=1, source_target_pairs={{0,8},{4,12},{8,0},{12,4},{16,24},{20,28},{24,16},{28,20},{32,40},... | collective-permute-start | bytes 491528 | tf_op jit(solution)/shard_map/ppermute | solution.py:27
  108.7 6.7 %collective-permute-start.23 = (f32[512,128]{1,0:T(8,128)S(1)}, f32[512,128]{1,0:T(8,128)S(1)}, u32[]{:S(2)}, u32[]{:S(2)}) collective-permute-start(f32[512,128]{1,0:T(8,128)S(1)} %maximum_select_fusion.3), channel_id=1, source_target_pairs={{0,4},{4,0},{8,12},{12,8},{16,20},{20,16},{24,28},{28,24},{32,36},... | collective-permute-start | bytes 786440 | tf_op jit(solution)/shard_map/ppermute | solution.py:27
  113.3 4.3 %collective-permute-start.11 = (f32[640,128]{1,0:T(8,128)S(1)}, f32[640,128]{1,0:T(8,128)S(1)}, u32[]{:S(2)}, u32[]{:S(2)}) collective-permute-start(f32[640,128]{1,0:T(8,128)S(1)} %maximum_select_fusion.2), channel_id=1, source_target_pairs={{0,4},{4,0},{8,12},{12,8},{16,20},{20,16},{24,28},{28,24},{32,36},... | collective-permute-start | bytes 983048 | tf_op jit(solution)/shard_map/ppermute | solution.py:27
  185.1 0.9 copy-start.3
  186.3 0.9 copy-start.2
  187.8 0.9 copy-start.1
  192.6 3.2 %collective-permute-start.24 = (f32[2,256]{1,0:T(2,128)S(1)}, f32[2,256]{1,0:T(2,128)S(1)}, u32[]{:S(2)}, u32[]{:S(2)}) collective-permute-start(f32[2,256]{1,0:T(2,128)S(1)} %pad_maximum_fusion.13), channel_id=1, source_target_pairs={{0,4},{4,0},{8,12},{12,8},{16,20},{20,16},{24,28},{28,24},{32,36},... | collective-permute-start | bytes 6152 | tf_op jit(solution)/shard_map/ppermute | solution.py:27
  195.9 5.5 %collective-permute-start.25 = (f32[2,256]{1,0:T(2,128)S(1)}, f32[2,256]{1,0:T(2,128)S(1)}, u32[]{:S(2)}, u32[]{:S(2)}) collective-permute-start(f32[2,256]{1,0:T(2,128)S(1)} %pad_maximum_fusion.14), channel_id=1, source_target_pairs={{0,8},{4,12},{8,0},{12,4},{16,24},{20,28},{24,16},{28,20},{32,40},... | collective-permute-start | bytes 6152 | tf_op jit(solution)/shard_map/ppermute | solution.py:27
  201.4 6.4 %collective-permute-start.26 = (f32[2,256]{1,0:T(2,128)S(1)}, f32[2,256]{1,0:T(2,128)S(1)}, u32[]{:S(2)}, u32[]{:S(2)}) collective-permute-start(f32[2,256]{1,0:T(2,128)S(1)} %pad_maximum_fusion.15), channel_id=1, source_target_pairs={{0,16},{4,20},{8,24},{12,28},{16,0},{20,4},{24,8},{28,12},{32,48},... | collective-permute-start | bytes 6152 | tf_op jit(solution)/shard_map/ppermute | solution.py:27
  207.8 9.4 %collective-permute-start.27 = (f32[2,256]{1,0:T(2,128)S(1)}, f32[2,256]{1,0:T(2,128)S(1)}, u32[]{:S(2)}, u32[]{:S(2)}) collective-permute-start(f32[2,256]{1,0:T(2,128)S(1)} %pad_maximum_fusion.16), channel_id=1, source_target_pairs={{0,32},{4,36},{8,40},{12,44},{16,48},{20,52},{24,56},{28,60},{32,0... | collective-permute-start | bytes 6152 | tf_op jit(solution)/shard_map/ppermute | solution.py:27
  217.2 5.5 %collective-permute-start.28 = (f32[2,256]{1,0:T(2,128)S(1)}, f32[2,256]{1,0:T(2,128)S(1)}, u32[]{:S(2)}, u32[]{:S(2)}) collective-permute-start(f32[2,256]{1,0:T(2,128)S(1)} %pad_maximum_fusion.17), channel_id=1, source_target_pairs={{0,64},{4,68},{8,72},{12,76},{16,80},{20,84},{24,88},{28,92},{32,9... | collective-permute-start | bytes 6152 | tf_op jit(solution)/shard_map/ppermute | solution.py:27
  222.7 6.4 %collective-permute-start.29 = (f32[2,256]{1,0:T(2,128)S(1)}, f32[2,256]{1,0:T(2,128)S(1)}, u32[]{:S(2)}, u32[]{:S(2)}) collective-permute-start(f32[2,256]{1,0:T(2,128)S(1)} %pad_maximum_fusion.18), channel_id=1, source_target_pairs={{0,128},{4,132},{8,136},{12,140},{16,144},{20,148},{24,152},{28,15... | collective-permute-start | bytes 6152 | tf_op jit(solution)/shard_map/ppermute | solution.py:27
  229.1 9.4 %collective-permute-start.30 = (f32[2,256]{1,0:T(2,128)S(1)}, f32[2,256]{1,0:T(2,128)S(1)}, u32[]{:S(2)}, u32[]{:S(2)}) collective-permute-start(f32[2,256]{1,0:T(2,128)S(1)} %pad_maximum_fusion.19), channel_id=1, source_target_pairs={{0,256},{4,260},{8,264},{12,268},{16,272},{20,276},{24,280},{28,28... | collective-permute-start | bytes 6152 | tf_op jit(solution)/shard_map/ppermute | solution.py:27
  238.5 5.5 %collective-permute-start.31 = (f32[2,256]{1,0:T(2,128)S(1)}, f32[2,256]{1,0:T(2,128)S(1)}, u32[]{:S(2)}, u32[]{:S(2)}) collective-permute-start(f32[2,256]{1,0:T(2,128)S(1)} %pad_maximum_fusion.20), channel_id=1, source_target_pairs={{0,1},{1,0},{2,3},{3,2},{4,5},{5,4},{6,7},{7,6},{8,9},{9,8},{10,11... | collective-permute-start | bytes 6152 | tf_op jit(solution)/shard_map/ppermute | solution.py:27
  244.0 7.0 %collective-permute-start.32 = (f32[2,256]{1,0:T(2,128)S(1)}, f32[2,256]{1,0:T(2,128)S(1)}, u32[]{:S(2)}, u32[]{:S(2)}) collective-permute-start(f32[2,256]{1,0:T(2,128)S(1)} %pad_maximum_fusion.21), channel_id=1, source_target_pairs={{0,2},{1,3},{2,0},{3,1},{4,6},{5,7},{6,4},{7,5},{8,10},{9,11},{10,... | collective-permute-start | bytes 6152 | tf_op jit(solution)/shard_map/ppermute | solution.py:27

commit v12 on v11

--- a/solution.py
+++ b/solution.py
@@ -133,9 +133,9 @@
         for j in range(i + 1)
     ]
     gram_flat = jnp.concatenate(lower_blocks, axis=0).reshape(-1, 128)
-    gram_sum = tree_sum(gram_flat, bits, 3).reshape(len(lower_blocks), block, block)
+    gram_sum = tree_sum(gram_flat, bits, 4).reshape(len(lower_blocks), block, block)
     cross_bits = bits[:1] + bits[4:7] + bits[1:4] + bits[7:]
-    cross = tree_sum(cross_part.reshape(-1, 128), cross_bits, 3).reshape(width, attrs)
+    cross = tree_sum(cross_part.reshape(-1, 128), cross_bits, 4).reshape(width, attrs)
     block_of = {}
     for n, (i, j) in enumerate((i, j) for i in range(nb) for j in range(i + 1)):
         block_of[(i, j)] = gram_sum[n]

time: 254 us -> 262 us (1.031)
  starting transfers between devices: 117 us -> 135 us
  waiting for transfers between devices: 46.1 us -> 37.8 us
    ppermute x33 -> x35, starting transfers between devices: 117 us -> 135 us  [partner(): return lax.ppermute(x, name, [(i, i ^ mask) for i in range(size)])]
    ppermute x33 -> x35, waiting for transfers between devices: 46.1 us -> 37.8 us  [partner(): return lax.ppermute(x, name, [(i, i ^ mask) for i in range(size)])]
  transfers between devices with their start and end apart: 33 -> 35, of which waited for: 22 -> 16; matrix products, arithmetic and copies ran while one was open for 2% -> 2% of each run, Pallas kernels for 0% -> 0%
where the time goes in v12:
time: 262 us; the launch traced here: 261 us
  starting transfers between devices  135 us (52%)
  other arithmetic  55.1 us (21%)
  waiting for transfers between devices  37.8 us (14%)
  matrix products  22.8 us (9%)
  local copies, waits for them, and re-layouts  7.05 us (3%)
  between operations  3.12 us (1%)
    ppermute x35, starting transfers between devices, partner(): return lax.ppermute(x, name, [(i, i ^ mask) for i in range(size)])  135 us
    another operation x12, other arithmetic, blocked_cholesky(): head = lax.linalg.cholesky(trailing[:block, :block], symmetrize_input=False)  49.8 us
    ppermute x35, waiting for transfers between devices, partner(): return lax.ppermute(x, name, [(i, i ^ mask) for i in range(size)])  37.8 us
    dot_general x24, matrix products, triangular_inverse(): power = jnp.dot(power, power, precision=HIGHEST)  5.86 us
    dot_general x24, matrix products, triangular_inverse(): product = jnp.dot(product, eye + power, precision=HIGHEST)  5.83 us
  transfers between devices with their start and end apart: 35, of which 16 were waited for; matrix products, arithmetic and copies ran while one was open for 2% of the time, Pallas kernels for 0%

profile of v12, /device:TPU:6, one launch (start us, length us, event | category | flops | bytes accessed | tf_op | source)
XLA Modules:
  0.0 260.5 jit_solution(9935111589001282349)
XLA Ops:
  1.5 3.3 %fusion.1 = bf16[256,512]{1,0:T(8,128)(2,1)S(1)} fusion(bf16[256,1024]{1,0:T(8,128)(2,1)} %param.7, bf16[1024,512]{1,0:T(8,128)(2,1)S(1)} %copy-done, f32[512]{0:T(512)S(1)} %fusion.78), kind=kOutput, calls=%fused_computation.4 | convolution fusion | flops 268697600 | bytes 1837056 | tf_op jit(solution)/shard_map/dot_general | solution.py:119
  9.4 2.4 collective-permute-start
  13.1 3.5 %collective-permute-start.14 = (f32[256,128]{1,0:T(8,128)S(1)}, f32[256,128]{1,0:T(8,128)S(1)}, u32[]{:S(2)}, u32[]{:S(2)}) collective-permute-start(f32[256,128]{1,0:T(8,128)S(1)} %constant_dynamic-slice_fusion.2), channel_id=1, source_target_pairs={{0,64},{4,68},{8,72},{12,76},{16,80},{20,84},{24,88},{28,92},{32,9... | collective-permute-start | bytes 393224 | tf_op jit(solution)/shard_map/ppermute | solution.py:27
  16.7 4.3 %collective-permute-start.1 = (f32[320,128]{1,0:T(8,128)S(1)}, f32[320,128]{1,0:T(8,128)S(1)}, u32[]{:S(2)}, u32[]{:S(2)}) collective-permute-start(f32[320,128]{1,0:T(8,128)S(1)} %constant_dynamic-slice_fusion.6), channel_id=1, source_target_pairs={{0,8},{4,12},{8,0},{12,4},{16,24},{20,28},{24,16},{28,20},{32,40},... | collective-permute-start | bytes 491528 | tf_op jit(solution)/shard_map/ppermute | solution.py:27
  21.0 4.5 %collective-permute-start.15 = (f32[128,128]{1,0:T(8,128)S(1)}, f32[128,128]{1,0:T(8,128)S(1)}, u32[]{:S(2)}, u32[]{:S(2)}) collective-permute-start(f32[128,128]{1,0:T(8,128)S(1)} %constant_dynamic-slice_fusion.1), channel_id=1, source_target_pairs={{0,128},{4,132},{8,136},{12,140},{16,144},{20,148},{24,152},{28,15... | collective-permute-start | bytes 196616 | tf_op jit(solution)/shard_map/ppermute | solution.py:27
  25.6 6.1 %collective-permute-start.2 = (f32[160,128]{1,0:T(8,128)S(1)}, f32[160,128]{1,0:T(8,128)S(1)}, u32[]{:S(2)}, u32[]{:S(2)}) collective-permute-start(f32[160,128]{1,0:T(8,128)S(1)} %constant_dynamic-slice_fusion.5), channel_id=1, source_target_pairs={{0,16},{4,20},{8,24},{12,28},{16,0},{20,4},{24,8},{28,12},{32,48},... | collective-permute-start | bytes 245768 | tf_op jit(solution)/shard_map/ppermute | solution.py:27
  31.7 2.7 %collective-permute-done.2 = f32[160,128]{1,0:T(8,128)S(1)} collective-permute-done((f32[160,128]{1,0:T(8,128)S(1)}, f32[160,128]{1,0:T(8,128)S(1)}, u32[]{:S(2)}, u32[]{:S(2)}) %collective-permute-start.2) | collective-permute-done | bytes 81952 | tf_op jit(solution)/shard_map/ppermute | solution.py:27
  34.4 8.8 %collective-permute-start.3 = (f32[80,128]{1,0:T(8,128)S(1)}, f32[80,128]{1,0:T(8,128)S(1)}, u32[]{:S(2)}, u32[]{:S(2)}) collective-permute-start(f32[80,128]{1,0:T(8,128)S(1)} %constant_dynamic-slice_fusion.4), channel_id=1, source_target_pairs={{0,32},{4,36},{8,40},{12,44},{16,48},{20,52},{24,56},{28,60},{32,0... | collective-permute-start | bytes 122888 | tf_op jit(solution)/shard_map/ppermute | solution.py:27
  43.2 6.3 %collective-permute-start.16 = (f32[64,128]{1,0:T(8,128)S(1)}, f32[64,128]{1,0:T(8,128)S(1)}, u32[]{:S(2)}, u32[]{:S(2)}) collective-permute-start(f32[64,128]{1,0:T(8,128)S(1)} %constant_dynamic-slice_fusion), channel_id=1, source_target_pairs={{0,256},{4,260},{8,264},{12,268},{16,272},{20,276},{24,280},{28,28... | collective-permute-start | bytes 98312 | tf_op jit(solution)/shard_map/ppermute | solution.py:27
  49.5 3.3 %collective-permute-start.4 = (f32[80,128]{1,0:T(8,128)S(1)}, f32[80,128]{1,0:T(8,128)S(1)}, u32[]{:S(2)}, u32[]{:S(2)}) collective-permute-start(f32[80,128]{1,0:T(8,128)S(1)} %dynamic-slice_add_fusion.6), channel_id=1, source_target_pairs={{0,64},{4,68},{8,72},{12,76},{16,80},{20,84},{24,88},{28,92},{32,9... | collective-permute-start | bytes 122888 | tf_op jit(solution)/shard_map/ppermute | solution.py:27
  53.4 3.5 %collective-permute-start.17 = (f32[64,128]{1,0:T(8,128)S(1)}, f32[64,128]{1,0:T(8,128)S(1)}, u32[]{:S(2)}, u32[]{:S(2)}) collective-permute-start(f32[64,128]{1,0:T(8,128)S(1)} %dynamic-slice_add_fusion.7), channel_id=1, source_target_pairs={{0,8},{4,12},{8,0},{12,4},{16,24},{20,28},{24,16},{28,20},{32,40},... | collective-permute-start | bytes 98312 | tf_op jit(solution)/shard_map/ppermute | solution.py:27
  56.9 3.3 %collective-permute-start.5 = (f32[80,128]{1,0:T(8,128)S(1)}, f32[80,128]{1,0:T(8,128)S(1)}, u32[]{:S(2)}, u32[]{:S(2)}) collective-permute-start(f32[80,128]{1,0:T(8,128)S(1)} %add.338), channel_id=1, source_target_pairs={{0,128},{4,132},{8,136},{12,140},{16,144},{20,148},{24,152},{28,15... | collective-permute-start | bytes 122888 | tf_op jit(solution)/shard_map/ppermute | solution.py:27
  60.3 5.2 %collective-permute-start.18 = (f32[64,128]{1,0:T(8,128)S(1)}, f32[64,128]{1,0:T(8,128)S(1)}, u32[]{:S(2)}, u32[]{:S(2)}) collective-permute-start(f32[64,128]{1,0:T(8,128)S(1)} %add.368), channel_id=1, source_target_pairs={{0,16},{4,20},{8,24},{12,28},{16,0},{20,4},{24,8},{28,12},{32,48},... | collective-permute-start | bytes 98312 | tf_op jit(solution)/shard_map/ppermute | solution.py:27
  65.5 2.1 collective-permute-done.18
  67.6 2.4 collective-permute-start.19
  70.0 6.1 %collective-permute-start.6 = (f32[80,128]{1,0:T(8,128)S(1)}, f32[80,128]{1,0:T(8,128)S(1)}, u32[]{:S(2)}, u32[]{:S(2)}) collective-permute-start(f32[80,128]{1,0:T(8,128)S(1)} %add.339), channel_id=1, source_target_pairs={{0,256},{4,260},{8,264},{12,268},{16,272},{20,276},{24,280},{28,28... | collective-permute-start | bytes 122888 | tf_op jit(solution)/shard_map/ppermute | solution.py:27
  77.3 2.7 %collective-permute-start.20 = (f32[64,128]{1,0:T(8,128)S(1)}, f32[64,128]{1,0:T(8,128)S(1)}, u32[]{:S(2)}, u32[]{:S(2)}) collective-permute-start(f32[64,128]{1,0:T(8,128)S(1)} %add.370), channel_id=1, source_target_pairs={{0,1},{1,0},{2,3},{3,2},{4,5},{5,4},{6,7},{7,6},{8,9},{9,8},{10,11... | collective-permute-start | bytes 98312 | tf_op jit(solution)/shard_map/ppermute | solution.py:27
  80.0 3.1 %collective-permute-start.7 = (f32[80,128]{1,0:T(8,128)S(1)}, f32[80,128]{1,0:T(8,128)S(1)}, u32[]{:S(2)}, u32[]{:S(2)}) collective-permute-start(f32[80,128]{1,0:T(8,128)S(1)} %add.340), channel_id=1, source_target_pairs={{0,1},{1,0},{2,3},{3,2},{4,5},{5,4},{6,7},{7,6},{8,9},{9,8},{10,11... | collective-permute-start | bytes 122888 | tf_op jit(solution)/shard_map/ppermute | solution.py:27
  83.2 3.4 %collective-permute-start.21 = (f32[64,128]{1,0:T(8,128)S(1)}, f32[64,128]{1,0:T(8,128)S(1)}, u32[]{:S(2)}, u32[]{:S(2)}) collective-permute-start(f32[64,128]{1,0:T(8,128)S(1)} %add.371), channel_id=1, source_target_pairs={{0,2},{1,3},{2,0},{3,1},{4,6},{5,7},{6,4},{7,5},{8,10},{9,11},{10,... | collective-permute-start | bytes 98312 | tf_op jit(solution)/shard_map/ppermute | solution.py:27
  86.6 3.9 %collective-permute-start.8 = (f32[80,128]{1,0:T(8,128)S(1)}, f32[80,128]{1,0:T(8,128)S(1)}, u32[]{:S(2)}, u32[]{:S(2)}) collective-permute-start(f32[80,128]{1,0:T(8,128)S(1)} %add.341), channel_id=1, source_target_pairs={{0,2},{1,3},{2,0},{3,1},{4,6},{5,7},{6,4},{7,5},{8,10},{9,11},{10,... | collective-permute-start | bytes 122888 | tf_op jit(solution)/shard_map/ppermute | solution.py:27
  90.6 6.0 %collective-permute-start.22 = (f32[64,128]{1,0:T(8,128)S(1)}, f32[64,128]{1,0:T(8,128)S(1)}, u32[]{:S(2)}, u32[]{:S(2)}) collective-permute-start(f32[64,128]{1,0:T(8,128)S(1)} %add.372), channel_id=1, source_target_pairs={{0,256},{4,260},{8,264},{12,268},{16,272},{20,276},{24,280},{28,28... | collective-permute-start | bytes 98312 | tf_op jit(solution)/shard_map/ppermute | solution.py:27
  96.6 6.7 %collective-permute-start.9 = (f32[80,128]{1,0:T(8,128)S(1)}, f32[80,128]{1,0:T(8,128)S(1)}, u32[]{:S(2)}, u32[]{:S(2)}) collective-permute-start(f32[80,128]{1,0:T(8,128)S(1)} %add.342), channel_id=1, source_target_pairs={{0,32},{4,36},{8,40},{12,44},{16,48},{20,52},{24,56},{28,60},{32,0... | collective-permute-start | bytes 122888 | tf_op jit(solution)/shard_map/ppermute | solution.py:27
  103.4 3.3 %collective-permute-start.23 = (f32[128,128]{1,0:T(8,128)S(1)}, f32[128,128]{1,0:T(8,128)S(1)}, u32[]{:S(2)}, u32[]{:S(2)}) collective-permute-start(f32[128,128]{1,0:T(8,128)S(1)} %maximum_select_fusion.7), channel_id=1, source_target_pairs={{0,128},{4,132},{8,136},{12,140},{16,144},{20,148},{24,152},{28,15... | collective-permute-start | bytes 196616 | tf_op jit(solution)/shard_map/ppermute | solution.py:27
  106.7 5.3 %collective-permute-start.10 = (f32[160,128]{1,0:T(8,128)S(1)}, f32[160,128]{1,0:T(8,128)S(1)}, u32[]{:S(2)}, u32[]{:S(2)}) collective-permute-start(f32[160,128]{1,0:T(8,128)S(1)} %maximum_select_fusion.6), channel_id=1, source_target_pairs={{0,16},{4,20},{8,24},{12,28},{16,0},{20,4},{24,8},{28,12},{32,48},... | collective-permute-start | bytes 245768 | tf_op jit(solution)/shard_map/ppermute | solution.py:27
  112.0 2.8 %collective-permute-start.24 = (f32[256,128]{1,0:T(8,128)S(1)}, f32[256,128]{1,0:T(8,128)S(1)}, u32[]{:S(2)}, u32[]{:S(2)}) collective-permute-start(f32[256,128]{1,0:T(8,128)S(1)} %maximum_select_fusion.5), channel_id=1, source_target_pairs={{0,64},{4,68},{8,72},{12,76},{16,80},{20,84},{24,88},{28,92},{32,9... | collective-permute-start | bytes 393224 | tf_op jit(solution)/shard_map/ppermute | solution.py:27
  115.3 1.9 collective-permute-start.11
  118.9 1.9 collective-permute-start.25
  122.6 2.1 collective-permute-start.12
  127.1 11.7 %custom-call.6 = f32[128,128]{1,0:T(8,128)S(1)} custom-call(f32[128,128]{1,0:T(8,128)S(1)} %slice.265), custom_call_target="Cholesky" | custom-call | tf_op jit(solution)/shard_map/cholesky/custom-call.1 | solution.py:78
  144.0 11.7 %custom-call.7 = f32[128,128]{1,0:T(8,128)S(1)} custom-call(f32[128,128]{1,0:T(8,128)S(1)} %slice.269), custom_call_target="Cholesky" | custom-call | tf_op jit(solution)/shard_map/cholesky/custom-call.1 | solution.py:78
  160.8 11.7 %custom-call.8 = f32[128,128]{1,0:T(8,128)S(1)} custom-call(f32[128,128]{1,0:T(8,128)S(1)} %slice.274), custom_call_target="Cholesky" | custom-call | tf_op jit(solution)/shard_map/cholesky/custom-call.1 | solution.py:78
  177.3 11.7 %custom-call.9 = f32[128,128]{1,0:T(8,128)S(1)} custom-call(f32[128,128]{1,0:T(8,128)S(1)} %convolution_subtract_fusion.5), custom_call_target="Cholesky" | custom-call | tf_op jit(solution)/shard_map/cholesky/custom-call.1 | solution.py:78
  201.5 2.4 collective-permute-start.26
  206.7 3.6 %collective-permute-done.27 = f32[2,256]{1,0:T(2,128)S(1)} collective-permute-done((f32[2,256]{1,0:T(2,128)S(1)}, f32[2,256]{1,0:T(2,128)S(1)}, u32[]{:S(2)}, u32[]{:S(2)}) %collective-permute-start.27) | collective-permute-done | bytes 2080 | tf_op jit(solution)/shard_map/ppermute | solution.py:27
  210.3 3.9 %collective-permute-start.28 = (f32[2,256]{1,0:T(2,128)S(1)}, f32[2,256]{1,0:T(2,128)S(1)}, u32[]{:S(2)}, u32[]{:S(2)}) collective-permute-start(f32[2,256]{1,0:T(2,128)S(1)} %pad_maximum_fusion.15), channel_id=1, source_target_pairs={{0,16},{4,20},{8,24},{12,28},{16,0},{20,4},{24,8},{28,12},{32,48},... | collective-permute-start | bytes 6152 | tf_op jit(solution)/shard_map/ppermute | solution.py:27
  214.2 2.4 collective-permute-done.28
  216.7 6.1 %collective-permute-start.29 = (f32[2,256]{1,0:T(2,128)S(1)}, f32[2,256]{1,0:T(2,128)S(1)}, u32[]{:S(2)}, u32[]{:S(2)}) collective-permute-start(f32[2,256]{1,0:T(2,128)S(1)} %pad_maximum_fusion.16), channel_id=1, source_target_pairs={{0,32},{4,36},{8,40},{12,44},{16,48},{20,52},{24,56},{28,60},{32,0... | collective-permute-start | bytes 6152 | tf_op jit(solution)/shard_map/ppermute | solution.py:27
  222.8 3.2 %collective-permute-done.29 = f32[2,256]{1,0:T(2,128)S(1)} collective-permute-done((f32[2,256]{1,0:T(2,128)S(1)}, f32[2,256]{1,0:T(2,128)S(1)}, u32[]{:S(2)}, u32[]{:S(2)}) %collective-permute-start.29) | collective-permute-done | bytes 2080 | tf_op jit(solution)/shard_map/ppermute | solution.py:27
  226.1 2.7 %collective-permute-start.30 = (f32[2,256]{1,0:T(2,128)S(1)}, f32[2,256]{1,0:T(2,128)S(1)}, u32[]{:S(2)}, u32[]{:S(2)}) collective-permute-start(f32[2,256]{1,0:T(2,128)S(1)} %pad_maximum_fusion.17), channel_id=1, source_target_pairs={{0,64},{4,68},{8,72},{12,76},{16,80},{20,84},{24,88},{28,92},{32,9... | collective-permute-start | bytes 6152 | tf_op jit(solution)/shard_map/ppermute | solution.py:27
  228.7 2.8 %collective-permute-done.30 = f32[2,256]{1,0:T(2,128)S(1)} collective-permute-done((f32[2,256]{1,0:T(2,128)S(1)}, f32[2,256]{1,0:T(2,128)S(1)}, u32[]{:S(2)}, u32[]{:S(2)}) %collective-permute-start.30) | collective-permute-done | bytes 2080 | tf_op jit(solution)/shard_map/ppermute | solution.py:27
  231.6 3.1 %collective-permute-start.31 = (f32[2,256]{1,0:T(2,128)S(1)}, f32[2,256]{1,0:T(2,128)S(1)}, u32[]{:S(2)}, u32[]{:S(2)}) collective-permute-start(f32[2,256]{1,0:T(2,128)S(1)} %pad_maximum_fusion.18), channel_id=1, source_target_pairs={{0,128},{4,132},{8,136},{12,140},{16,144},{20,148},{24,152},{28,15... | collective-permute-start | bytes 6152 | tf_op jit(solution)/shard_map/ppermute | solution.py:27
  234.6 3.3 %collective-permute-done.31 = f32[2,256]{1,0:T(2,128)S(1)} collective-permute-done((f32[2,256]{1,0:T(2,128)S(1)}, f32[2,256]{1,0:T(2,128)S(1)}, u32[]{:S(2)}, u32[]{:S(2)}) %collective-permute-start.31) | collective-permute-done | bytes 2080 | tf_op jit(solution)/shard_map/ppermute | solution.py:27
  237.9 3.9 %collective-permute-start.32 = (f32[2,256]{1,0:T(2,128)S(1)}, f32[2,256]{1,0:T(2,128)S(1)}, u32[]{:S(2)}, u32[]{:S(2)}) collective-permute-start(f32[2,256]{1,0:T(2,128)S(1)} %pad_maximum_fusion.19), channel_id=1, source_target_pairs={{0,256},{4,260},{8,264},{12,268},{16,272},{20,276},{24,280},{28,28... | collective-permute-start | bytes 6152 | tf_op jit(solution)/shard_map/ppermute | solution.py:27
  241.8 5.5 %collective-permute-done.32 = f32[2,256]{1,0:T(2,128)S(1)} collective-permute-done((f32[2,256]{1,0:T(2,128)S(1)}, f32[2,256]{1,0:T(2,128)S(1)}, u32[]{:S(2)}, u32[]{:S(2)}) %collective-permute-start.32) | collective-permute-done | bytes 2080 | tf_op jit(solution)/shard_map/ppermute | solution.py:27
  247.4 2.7 %collective-permute-start.33 = (f32[2,256]{1,0:T(2,128)S(1)}, f32[2,256]{1,0:T(2,128)S(1)}, u32[]{:S(2)}, u32[]{:S(2)}) collective-permute-start(f32[2,256]{1,0:T(2,128)S(1)} %pad_maximum_fusion.20), channel_id=1, source_target_pairs={{0,1},{1,0},{2,3},{3,2},{4,5},{5,4},{6,7},{7,6},{8,9},{9,8},{10,11... | collective-permute-start | bytes 6152 | tf_op jit(solution)/shard_map/ppermute | solution.py:27
  250.1 2.7 %collective-permute-done.33 = f32[2,256]{1,0:T(2,128)S(1)} collective-permute-done((f32[2,256]{1,0:T(2,128)S(1)}, f32[2,256]{1,0:T(2,128)S(1)}, u32[]{:S(2)}, u32[]{:S(2)}) %collective-permute-start.33) | collective-permute-done | bytes 2080 | tf_op jit(solution)/shard_map/ppermute | solution.py:27
  252.8 3.1 %collective-permute-start.34 = (f32[2,256]{1,0:T(2,128)S(1)}, f32[2,256]{1,0:T(2,128)S(1)}, u32[]{:S(2)}, u32[]{:S(2)}) collective-permute-start(f32[2,256]{1,0:T(2,128)S(1)} %pad_maximum_fusion.21), channel_id=1, source_target_pairs={{0,2},{1,3},{2,0},{3,1},{4,6},{5,7},{6,4},{7,5},{8,10},{9,11},{10,... | collective-permute-start | bytes 6152 | tf_op jit(solution)/shard_map/ppermute | solution.py:27
  255.9 3.9 %collective-permute-done.34 = f32[2,256]{1,0:T(2,128)S(1)} collective-permute-done((f32[2,256]{1,0:T(2,128)S(1)}, f32[2,256]{1,0:T(2,128)S(1)}, u32[]{:S(2)}, u32[]{:S(2)}) %collective-permute-start.34) | collective-permute-done | bytes 2080 | tf_op jit(solution)/shard_map/ppermute | solution.py:27
  (202 shorter events, 44.3 us)
Async XLA Ops:
  0.0 1.5 copy-start
  0.7 0.7 copy-start.5
  4.7 1.2 copy-start.4
  7.0 5.1 %collective-permute-start.13 = (f32[512,128]{1,0:T(8,128)}, f32[512,128]{1,0:T(8,128)}, u32[]{:S(2)}, u32[]{:S(2)}) collective-permute-start(f32[512,128]{1,0:T(8,128)} %constant_dynamic-slice_fusion.3), channel_id=1, source_target_pairs={{0,4},{4,0},{8,12},{12,8},{16,20},{20,16},{24,28},{28,24},{32,36},... | collective-permute-start | bytes 786440 | tf_op jit(solution)/shard_map/ppermute | solution.py:27
  9.4 7.2 %collective-permute-start = (f32[640,128]{1,0:T(8,128)S(1)}, f32[640,128]{1,0:T(8,128)S(1)}, u32[]{:S(2)}, u32[]{:S(2)}) collective-permute-start(f32[640,128]{1,0:T(8,128)S(1)} %constant_dynamic-slice_fusion.7), channel_id=1, source_target_pairs={{0,4},{4,0},{8,12},{12,8},{16,20},{20,16},{24,28},{28,24},{32,36},... | collective-permute-start | bytes 983048 | tf_op jit(solution)/shard_map/ppermute | solution.py:27
  13.1 7.9 %collective-permute-start.14 = (f32[256,128]{1,0:T(8,128)S(1)}, f32[256,128]{1,0:T(8,128)S(1)}, u32[]{:S(2)}, u32[]{:S(2)}) collective-permute-start(f32[256,128]{1,0:T(8,128)S(1)} %constant_dynamic-slice_fusion.2), channel_id=1, source_target_pairs={{0,64},{4,68},{8,72},{12,76},{16,80},{20,84},{24,88},{28,92},{32,9... | collective-permute-start | bytes 393224 | tf_op jit(solution)/shard_map/ppermute | solution.py:27
  16.7 8.9 %collective-permute-start.1 = (f32[320,128]{1,0:T(8,128)S(1)}, f32[320,128]{1,0:T(8,128)S(1)}, u32[]{:S(2)}, u32[]{:S(2)}) collective-permute-start(f32[320,128]{1,0:T(8,128)S(1)} %constant_dynamic-slice_fusion.6), channel_id=1, source_target_pairs={{0,8},{4,12},{8,0},{12,4},{16,24},{20,28},{24,16},{28,20},{32,40},... | collective-permute-start | bytes 491528 | tf_op jit(solution)/shard_map/ppermute | solution.py:27
  21.0 10.7 %collective-permute-start.15 = (f32[128,128]{1,0:T(8,128)S(1)}, f32[128,128]{1,0:T(8,128)S(1)}, u32[]{:S(2)}, u32[]{:S(2)}) collective-permute-start(f32[128,128]{1,0:T(8,128)S(1)} %constant_dynamic-slice_fusion.1), channel_id=1, source_target_pairs={{0,128},{4,132},{8,136},{12,140},{16,144},{20,148},{24,152},{28,15... | collective-permute-start | bytes 196616 | tf_op jit(solution)/shard_map/ppermute | solution.py:27
  25.6 8.8 %collective-permute-start.2 = (f32[160,128]{1,0:T(8,128)S(1)}, f32[160,128]{1,0:T(8,128)S(1)}, u32[]{:S(2)}, u32[]{:S(2)}) collective-permute-start(f32[160,128]{1,0:T(8,128)S(1)} %constant_dynamic-slice_fusion.5), channel_id=1, source_target_pairs={{0,16},{4,20},{8,24},{12,28},{16,0},{20,4},{24,8},{28,12},{32,48},... | collective-permute-start | bytes 245768 | tf_op jit(solution)/shard_map/ppermute | solution.py:27
  34.4 15.1 %collective-permute-start.3 = (f32[80,128]{1,0:T(8,128)S(1)}, f32[80,128]{1,0:T(8,128)S(1)}, u32[]{:S(2)}, u32[]{:S(2)}) collective-permute-start(f32[80,128]{1,0:T(8,128)S(1)} %constant_dynamic-slice_fusion.4), channel_id=1, source_target_pairs={{0,32},{4,36},{8,40},{12,44},{16,48},{20,52},{24,56},{28,60},{32,0... | collective-permute-start | bytes 122888 | tf_op jit(solution)/shard_map/ppermute | solution.py:27
  43.2 10.2 %collective-permute-start.16 = (f32[64,128]{1,0:T(8,128)S(1)}, f32[64,128]{1,0:T(8,128)S(1)}, u32[]{:S(2)}, u32[]{:S(2)}) collective-permute-start(f32[64,128]{1,0:T(8,128)S(1)} %constant_dynamic-slice_fusion), channel_id=1, source_target_pairs={{0,256},{4,260},{8,264},{12,268},{16,272},{20,276},{24,280},{28,28... | collective-permute-start | bytes 98312 | tf_op jit(solution)/shard_map/ppermute | solution.py:27
  49.5 7.4 %collective-permute-start.4 = (f32[80,128]{1,0:T(8,128)S(1)}, f32[80,128]{1,0:T(8,128)S(1)}, u32[]{:S(2)}, u32[]{:S(2)}) collective-permute-start(f32[80,128]{1,0:T(8,128)S(1)} %dynamic-slice_add_fusion.6), channel_id=1, source_target_pairs={{0,64},{4,68},{8,72},{12,76},{16,80},{20,84},{24,88},{28,92},{32,9... | collective-permute-start | bytes 122888 | tf_op jit(solution)/shard_map/ppermute | solution.py:27
  53.4 6.9 %collective-permute-start.17 = (f32[64,128]{1,0:T(8,128)S(1)}, f32[64,128]{1,0:T(8,128)S(1)}, u32[]{:S(2)}, u32[]{:S(2)}) collective-permute-start(f32[64,128]{1,0:T(8,128)S(1)} %dynamic-slice_add_fusion.7), channel_id=1, source_target_pairs={{0,8},{4,12},{8,0},{12,4},{16,24},{20,28},{24,16},{28,20},{32,40},... | collective-permute-start | bytes 98312 | tf_op jit(solution)/shard_map/ppermute | solution.py:27
  56.9 13.1 %collective-permute-start.5 = (f32[80,128]{1,0:T(8,128)S(1)}, f32[80,128]{1,0:T(8,128)S(1)}, u32[]{:S(2)}, u32[]{:S(2)}) collective-permute-start(f32[80,128]{1,0:T(8,128)S(1)} %add.338), channel_id=1, source_target_pairs={{0,128},{4,132},{8,136},{12,140},{16,144},{20,148},{24,152},{28,15... | collective-permute-start | bytes 122888 | tf_op jit(solution)/shard_map/ppermute | solution.py:27
  60.3 7.2 %collective-permute-start.18 = (f32[64,128]{1,0:T(8,128)S(1)}, f32[64,128]{1,0:T(8,128)S(1)}, u32[]{:S(2)}, u32[]{:S(2)}) collective-permute-start(f32[64,128]{1,0:T(8,128)S(1)} %add.368), channel_id=1, source_target_pairs={{0,16},{4,20},{8,24},{12,28},{16,0},{20,4},{24,8},{28,12},{32,48},... | collective-permute-start | bytes 98312 | tf_op jit(solution)/shard_map/ppermute | solution.py:27
  67.6 9.7 %collective-permute-start.19 = (f32[64,128]{1,0:T(8,128)S(1)}, f32[64,128]{1,0:T(8,128)S(1)}, u32[]{:S(2)}, u32[]{:S(2)}) collective-permute-start(f32[64,128]{1,0:T(8,128)S(1)} %add.369), channel_id=1, source_target_pairs={{0,32},{4,36},{8,40},{12,44},{16,48},{20,52},{24,56},{28,60},{32,0... | collective-permute-start | bytes 98312 | tf_op jit(solution)/shard_map/ppermute | solution.py:27
  70.0 10.0 %collective-permute-start.6 = (f32[80,128]{1,0:T(8,128)S(1)}, f32[80,128]{1,0:T(8,128)S(1)}, u32[]{:S(2)}, u32[]{:S(2)}) collective-permute-start(f32[80,128]{1,0:T(8,128)S(1)} %add.339), channel_id=1, source_target_pairs={{0,256},{4,260},{8,264},{12,268},{16,272},{20,276},{24,280},{28,28... | collective-permute-start | bytes 122888 | tf_op jit(solution)/shard_map/ppermute | solution.py:27
  77.3 5.9 %collective-permute-start.20 = (f32[64,128]{1,0:T(8,128)S(1)}, f32[64,128]{1,0:T(8,128)S(1)}, u32[]{:S(2)}, u32[]{:S(2)}) collective-permute-start(f32[64,128]{1,0:T(8,128)S(1)} %add.370), channel_id=1, source_target_pairs={{0,1},{1,0},{2,3},{3,2},{4,5},{5,4},{6,7},{7,6},{8,9},{9,8},{10,11... | collective-permute-start | bytes 98312 | tf_op jit(solution)/shard_map/ppermute | solution.py:27
  80.0 6.6 %collective-permute-start.7 = (f32[80,128]{1,0:T(8,128)S(1)}, f32[80,128]{1,0:T(8,128)S(1)}, u32[]{:S(2)}, u32[]{:S(2)}) collective-permute-start(f32[80,128]{1,0:T(8,128)S(1)} %add.340), channel_id=1, source_target_pairs={{0,1},{1,0},{2,3},{3,2},{4,5},{5,4},{6,7},{7,6},{8,9},{9,8},{10,11... | collective-permute-start | bytes 122888 | tf_op jit(solution)/shard_map/ppermute | solution.py:27
  83.2 7.4 %collective-permute-start.21 = (f32[64,128]{1,0:T(8,128)S(1)}, f32[64,128]{1,0:T(8,128)S(1)}, u32[]{:S(2)}, u32[]{:S(2)}) collective-permute-start(f32[64,128]{1,0:T(8,128)S(1)} %add.371), channel_id=1, source_target_pairs={{0,2},{1,3},{2,0},{3,1},{4,6},{5,7},{6,4},{7,5},{8,10},{9,11},{10,... | collective-permute-start | bytes 98312 | tf_op jit(solution)/shard_map/ppermute | solution.py:27
  86.6 9.9 %collective-permute-start.8 = (f32[80,128]{1,0:T(8,128)S(1)}, f32[80,128]{1,0:T(8,128)S(1)}, u32[]{:S(2)}, u32[]{:S(2)}) collective-permute-start(f32[80,128]{1,0:T(8,128)S(1)} %add.341), channel_id=1, source_target_pairs={{0,2},{1,3},{2,0},{3,1},{4,6},{5,7},{6,4},{7,5},{8,10},{9,11},{10,... | collective-permute-start | bytes 122888 | tf_op jit(solution)/shard_map/ppermute | solution.py:27
  90.6 12.7 %collective-permute-start.22 = (f32[64,128]{1,0:T(8,128)S(1)}, f32[64,128]{1,0:T(8,128)S(1)}, u32[]{:S(2)}, u32[]{:S(2)}) collective-permute-start(f32[64,128]{1,0:T(8,128)S(1)} %add.372), channel_id=1, source_target_pairs={{0,256},{4,260},{8,264},{12,268},{16,272},{20,276},{24,280},{28,28... | collective-permute-start | bytes 98312 | tf_op jit(solution)/shard_map/ppermute | solution.py:27
  96.6 10.1 %collective-permute-start.9 = (f32[80,128]{1,0:T(8,128)S(1)}, f32[80,128]{1,0:T(8,128)S(1)}, u32[]{:S(2)}, u32[]{:S(2)}) collective-permute-start(f32[80,128]{1,0:T(8,128)S(1)} %add.342), channel_id=1, source_target_pairs={{0,32},{4,36},{8,40},{12,44},{16,48},{20,52},{24,56},{28,60},{32,0... | collective-permute-start | bytes 122888 | tf_op jit(solution)/shard_map/ppermute | solution.py:27
  103.4 8.7 %collective-permute-start.23 = (f32[128,128]{1,0:T(8,128)S(1)}, f32[128,128]{1,0:T(8,128)S(1)}, u32[]{:S(2)}, u32[]{:S(2)}) collective-permute-start(f32[128,128]{1,0:T(8,128)S(1)} %maximum_select_fusion.7), channel_id=1, source_target_pairs={{0,128},{4,132},{8,136},{12,140},{16,144},{20,148},{24,152},{28,15... | collective-permute-start | bytes 196616 | tf_op jit(solution)/shard_map/ppermute | solution.py:27
  106.7 8.6 %collective-permute-start.10 = (f32[160,128]{1,0:T(8,128)S(1)}, f32[160,128]{1,0:T(8,128)S(1)}, u32[]{:S(2)}, u32[]{:S(2)}) collective-permute-start(f32[160,128]{1,0:T(8,128)S(1)} %maximum_select_fusion.6), channel_id=1, source_target_pairs={{0,16},{4,20},{8,24},{12,28},{16,0},{20,4},{24,8},{28,12},{32,48},... | collective-permute-start | bytes 245768 | tf_op jit(solution)/shard_map/ppermute | solution.py:27
  112.0 6.9 %collective-permute-start.24 = (f32[256,128]{1,0:T(8,128)S(1)}, f32[256,128]{1,0:T(8,128)S(1)}, u32[]{:S(2)}, u32[]{:S(2)}) collective-permute-start(f32[256,128]{1,0:T(8,128)S(1)} %maximum_select_fusion.5), channel_id=1, source_target_pairs={{0,64},{4,68},{8,72},{12,76},{16,80},{20,84},{24,88},{28,92},{32,9... | collective-permute-start | bytes 393224 | tf_op jit(solution)/shard_map/ppermute | solution.py:27
  115.3 7.2 %collective-permute-start.11 = (f32[320,128]{1,0:T(8,128)S(1)}, f32[320,128]{1,0:T(8,128)S(1)}, u32[]{:S(2)}, u32[]{:S(2)}) collective-permute-start(f32[320,128]{1,0:T(8,128)S(1)} %maximum_select_fusion.4), channel_id=1, source_target_pairs={{0,8},{4,12},{8,0},{12,4},{16,24},{20,28},{24,16},{28,20},{32,40},... | collective-permute-start | bytes 491528 | tf_op jit(solution)/shard_map/ppermute | solution.py:27
  118.9 5.7 %collective-permute-start.25 = (f32[512,128]{1,0:T(8,128)S(1)}, f32[512,128]{1,0:T(8,128)S(1)}, u32[]{:S(2)}, u32[]{:S(2)}) collective-permute-start(f32[512,128]{1,0:T(8,128)S(1)} %maximum_select_fusion.3), channel_id=1, source_target_pairs={{0,4},{4,0},{8,12},{12,8},{16,20},{20,16},{24,28},{28,24},{32,36},... | collective-permute-start | bytes 786440 | tf_op jit(solution)/shard_map/ppermute | solution.py:27
  122.6 4.3 %collective-permute-start.12 = (f32[640,128]{1,0:T(8,128)S(1)}, f32[640,128]{1,0:T(8,128)S(1)}, u32[]{:S(2)}, u32[]{:S(2)}) collective-permute-start(f32[640,128]{1,0:T(8,128)S(1)} %maximum_select_fusion.2), channel_id=1, source_target_pairs={{0,4},{4,0},{8,12},{12,8},{16,20},{20,16},{24,28},{28,24},{32,36},... | collective-permute-start | bytes 983048 | tf_op jit(solution)/shard_map/ppermute | solution.py:27
  194.0 0.9 copy-start.3
  195.2 0.9 copy-start.2
  196.7 0.9 copy-start.1
  201.5 3.2 %collective-permute-start.26 = (f32[2,256]{1,0:T(2,128)S(1)}, f32[2,256]{1,0:T(2,128)S(1)}, u32[]{:S(2)}, u32[]{:S(2)}) collective-permute-start(f32[2,256]{1,0:T(2,128)S(1)} %pad_maximum_fusion.13), channel_id=1, source_target_pairs={{0,4},{4,0},{8,12},{12,8},{16,20},{20,16},{24,28},{28,24},{32,36},... | collective-permute-start | bytes 6152 | tf_op jit(solution)/shard_map/ppermute | solution.py:27
  204.8 5.5 %collective-permute-start.27 = (f32[2,256]{1,0:T(2,128)S(1)}, f32[2,256]{1,0:T(2,128)S(1)}, u32[]{:S(2)}, u32[]{:S(2)}) collective-permute-start(f32[2,256]{1,0:T(2,128)S(1)} %pad_maximum_fusion.14), channel_id=1, source_target_pairs={{0,8},{4,12},{8,0},{12,4},{16,24},{20,28},{24,16},{28,20},{32,40},... | collective-permute-start | bytes 6152 | tf_op jit(solution)/shard_map/ppermute | solution.py:27
  210.3 6.4 %collective-permute-start.28 = (f32[2,256]{1,0:T(2,128)S(1)}, f32[2,256]{1,0:T(2,128)S(1)}, u32[]{:S(2)}, u32[]{:S(2)}) collective-permute-start(f32[2,256]{1,0:T(2,128)S(1)} %pad_maximum_fusion.15), channel_id=1, source_target_pairs={{0,16},{4,20},{8,24},{12,28},{16,0},{20,4},{24,8},{28,12},{32,48},... | collective-permute-start | bytes 6152 | tf_op jit(solution)/shard_map/ppermute | solution.py:27
  216.7 9.4 %collective-permute-start.29 = (f32[2,256]{1,0:T(2,128)S(1)}, f32[2,256]{1,0:T(2,128)S(1)}, u32[]{:S(2)}, u32[]{:S(2)}) collective-permute-start(f32[2,256]{1,0:T(2,128)S(1)} %pad_maximum_fusion.16), channel_id=1, source_target_pairs={{0,32},{4,36},{8,40},{12,44},{16,48},{20,52},{24,56},{28,60},{32,0... | collective-permute-start | bytes 6152 | tf_op jit(solution)/shard_map/ppermute | solution.py:27
  226.1 5.5 %collective-permute-start.30 = (f32[2,256]{1,0:T(2,128)S(1)}, f32[2,256]{1,0:T(2,128)S(1)}, u32[]{:S(2)}, u32[]{:S(2)}) collective-permute-start(f32[2,256]{1,0:T(2,128)S(1)} %pad_maximum_fusion.17), channel_id=1, source_target_pairs={{0,64},{4,68},{8,72},{12,76},{16,80},{20,84},{24,88},{28,92},{32,9... | collective-permute-start | bytes 6152 | tf_op jit(solution)/shard_map/ppermute | solution.py:27
  231.6 6.4 %collective-permute-start.31 = (f32[2,256]{1,0:T(2,128)S(1)}, f32[2,256]{1,0:T(2,128)S(1)}, u32[]{:S(2)}, u32[]{:S(2)}) collective-permute-start(f32[2,256]{1,0:T(2,128)S(1)} %pad_maximum_fusion.18), channel_id=1, source_target_pairs={{0,128},{4,132},{8,136},{12,140},{16,144},{20,148},{24,152},{28,15... | collective-permute-start | bytes 6152 | tf_op jit(solution)/shard_map/ppermute | solution.py:27
  237.9 9.4 %collective-permute-start.32 = (f32[2,256]{1,0:T(2,128)S(1)}, f32[2,256]{1,0:T(2,128)S(1)}, u32[]{:S(2)}, u32[]{:S(2)}) collective-permute-start(f32[2,256]{1,0:T(2,128)S(1)} %pad_maximum_fusion.19), channel_id=1, source_target_pairs={{0,256},{4,260},{8,264},{12,268},{16,272},{20,276},{24,280},{28,28... | collective-permute-start | bytes 6152 | tf_op jit(solution)/shard_map/ppermute | solution.py:27
  247.4 5.5 %collective-permute-start.33 = (f32[2,256]{1,0:T(2,128)S(1)}, f32[2,256]{1,0:T(2,128)S(1)}, u32[]{:S(2)}, u32[]{:S(2)}) collective-permute-start(f32[2,256]{1,0:T(2,128)S(1)} %pad_maximum_fusion.20), channel_id=1, source_target_pairs={{0,1},{1,0},{2,3},{3,2},{4,5},{5,4},{6,7},{7,6},{8,9},{9,8},{10,11... | collective-permute-start | bytes 6152 | tf_op jit(solution)/shard_map/ppermute | solution.py:27
  252.8 7.0 %collective-permute-start.34 = (f32[2,256]{1,0:T(2,128)S(1)}, f32[2,256]{1,0:T(2,128)S(1)}, u32[]{:S(2)}, u32[]{:S(2)}) collective-permute-start(f32[2,256]{1,0:T(2,128)S(1)} %pad_maximum_fusion.21), channel_id=1, source_target_pairs={{0,2},{1,3},{2,0},{3,1},{4,6},{5,7},{6,4},{7,5},{8,10},{9,11},{10,... | collective-permute-start | bytes 6152 | tf_op jit(solution)/shard_map/ppermute | solution.py:27

commit v13 on v11

--- a/solution.py
+++ b/solution.py
@@ -69,18 +69,20 @@
     return product / pivots[None, :]
 
 
-def blocked_cholesky(system, block):
+def blocked_cholesky(system, block, first_head, first_column):
     count = system.shape[0] // block
     trailing = system
     columns = []
     inverses = []
     for k in range(count):
-        head = lax.linalg.cholesky(trailing[:block, :block], symmetrize_input=False)
+        corner = first_head if k == 0 else trailing[:block, :block]
+        head = lax.linalg.cholesky(corner, symmetrize_input=False)
         inverse = triangular_inverse(head)
         inverses.append(inverse)
         above = [jnp.zeros((k * block, block), system.dtype)] if k else []
         if k < count - 1:
-            panel = jnp.dot(trailing[block:, :block], inverse.T, precision=HIGHEST)
+            below = first_column if k == 0 else trailing[block:, :block]
+            panel = jnp.dot(below, inverse.T, precision=HIGHEST)
             trailing = trailing[block:, block:] - jnp.dot(panel, panel.T, precision=HIGHEST)
             columns.append(jnp.concatenate(above + [head, panel]))
         else:
@@ -148,7 +150,9 @@
     total_rows = embeddings.shape[0] * lax.axis_size("docs") * lax.axis_size("grp")
     ridge_shift = penalty[0].astype(jnp.float32) * jnp.float32(total_rows / 8.0)
     system = gram + ridge_shift * jnp.eye(width, dtype=jnp.float32)
-    factor, inverses = blocked_cholesky(system, block)
+    first_head = gram_sum[0] + ridge_shift * jnp.eye(block, dtype=jnp.float32)
+    first_column = jnp.concatenate([block_of[(i, 0)] for i in range(1, nb)], axis=0)
+    factor, inverses = blocked_cholesky(system, block, first_head, first_column)
     coeffs = cholesky_solve(factor, inverses, cross, block).astype(jnp.bfloat16)
     scores = jnp.dot(features, coeffs, preferred_element_type=jnp.float32)
     peak_local = jnp.max(jnp.abs(scores), axis=0)

time: 254 us -> 252 us (level)
  local copies, waits for them, and re-layouts: 7.05 us -> 3.84 us
  transfers between devices with their start and end apart: 33 -> 33, of which waited for: 22 -> 23; matrix products, arithmetic and copies ran while one was open for 2% -> 1% of each run, Pallas kernels for 0% -> 0%
where the time goes in v13:
time: 252 us; the launch traced here: 249 us
  starting transfers between devices  117 us (46%)
  other arithmetic  55.5 us (22%)
  waiting for transfers between devices  47.2 us (19%)
  matrix products  22.9 us (9%)
  local copies, waits for them, and re-layouts  3.84 us (2%)
  between operations  2.9 us (1%)
    ppermute x33, starting transfers between devices, partner(): return lax.ppermute(x, name, [(i, i ^ mask) for i in range(size)])  117 us
    another operation x12, other arithmetic, blocked_cholesky(): head = lax.linalg.cholesky(corner, symmetrize_input=False)  49.6 us
    ppermute x33, waiting for transfers between devices, partner(): return lax.ppermute(x, name, [(i, i ^ mask) for i in range(size)])  47.2 us
    dot_general x24, matrix products, triangular_inverse(): power = jnp.dot(power, power, precision=HIGHEST)  5.87 us
    dot_general x24, matrix products, triangular_inverse(): product = jnp.dot(product, eye + power, precision=HIGHEST)  5.84 us
  transfers between devices with their start and end apart: 33, of which 23 were waited for; matrix products, arithmetic and copies ran while one was open for 1% of the time, Pallas kernels for 0%

profile of v13, /device:TPU:6, one launch (start us, length us, event | category | flops | bytes accessed | tf_op | source)
XLA Modules:
  0.0 249.4 jit_solution(14694744011622807192)
XLA Ops:
  1.5 3.3 %fusion.1 = bf16[256,512]{1,0:T(8,128)(2,1)S(1)} fusion(bf16[256,1024]{1,0:T(8,128)(2,1)} %param.7, bf16[1024,512]{1,0:T(8,128)(2,1)S(1)} %copy-done, f32[512]{0:T(512)S(1)} %fusion.86), kind=kOutput, calls=%fused_computation.4 | convolution fusion | flops 268697600 | bytes 1837056 | tf_op jit(solution)/shard_map/dot_general | solution.py:121
  9.4 2.4 collective-permute-start
  13.0 3.5 %collective-permute-start.13 = (f32[256,128]{1,0:T(8,128)S(1)}, f32[256,128]{1,0:T(8,128)S(1)}, u32[]{:S(2)}, u32[]{:S(2)}) collective-permute-start(f32[256,128]{1,0:T(8,128)S(1)} %constant_dynamic-slice_fusion.1), channel_id=1, source_target_pairs={{0,64},{4,68},{8,72},{12,76},{16,80},{20,84},{24,88},{28,92},{32,9... | collective-permute-start | bytes 393224 | tf_op jit(solution)/shard_map/ppermute | solution.py:27
  16.6 4.3 %collective-permute-start.1 = (f32[320,128]{1,0:T(8,128)S(1)}, f32[320,128]{1,0:T(8,128)S(1)}, u32[]{:S(2)}, u32[]{:S(2)}) collective-permute-start(f32[320,128]{1,0:T(8,128)S(1)} %constant_dynamic-slice_fusion.4), channel_id=1, source_target_pairs={{0,8},{4,12},{8,0},{12,4},{16,24},{20,28},{24,16},{28,20},{32,40},... | collective-permute-start | bytes 491528 | tf_op jit(solution)/shard_map/ppermute | solution.py:27
  20.9 4.0 %collective-permute-done.1 = f32[320,128]{1,0:T(8,128)S(1)} collective-permute-done((f32[320,128]{1,0:T(8,128)S(1)}, f32[320,128]{1,0:T(8,128)S(1)}, u32[]{:S(2)}, u32[]{:S(2)}) %collective-permute-start.1) | collective-permute-done | bytes 163872 | tf_op jit(solution)/shard_map/ppermute | solution.py:27
  25.0 6.1 %collective-permute-start.2 = (f32[160,128]{1,0:T(8,128)S(1)}, f32[160,128]{1,0:T(8,128)S(1)}, u32[]{:S(2)}, u32[]{:S(2)}) collective-permute-start(f32[160,128]{1,0:T(8,128)S(1)} %constant_dynamic-slice_fusion.3), channel_id=1, source_target_pairs={{0,16},{4,20},{8,24},{12,28},{16,0},{20,4},{24,8},{28,12},{32,48},... | collective-permute-start | bytes 245768 | tf_op jit(solution)/shard_map/ppermute | solution.py:27
  31.1 4.5 %collective-permute-start.14 = (f32[128,128]{1,0:T(8,128)S(1)}, f32[128,128]{1,0:T(8,128)S(1)}, u32[]{:S(2)}, u32[]{:S(2)}) collective-permute-start(f32[128,128]{1,0:T(8,128)S(1)} %constant_dynamic-slice_fusion), channel_id=1, source_target_pairs={{0,128},{4,132},{8,136},{12,140},{16,144},{20,148},{24,152},{28,15... | collective-permute-start | bytes 196616 | tf_op jit(solution)/shard_map/ppermute | solution.py:27
  35.7 8.5 %collective-permute-start.3 = (f32[160,128]{1,0:T(8,128)S(1)}, f32[160,128]{1,0:T(8,128)S(1)}, u32[]{:S(2)}, u32[]{:S(2)}) collective-permute-start(f32[160,128]{1,0:T(8,128)S(1)} %dynamic-slice_add_fusion.4), channel_id=1, source_target_pairs={{0,32},{4,36},{8,40},{12,44},{16,48},{20,52},{24,56},{28,60},{32,0... | collective-permute-start | bytes 245768 | tf_op jit(solution)/shard_map/ppermute | solution.py:27
  44.2 5.2 %collective-permute-start.15 = (f32[128,128]{1,0:T(8,128)S(1)}, f32[128,128]{1,0:T(8,128)S(1)}, u32[]{:S(2)}, u32[]{:S(2)}) collective-permute-start(f32[128,128]{1,0:T(8,128)S(1)} %dynamic-slice_add_fusion.5), channel_id=1, source_target_pairs={{0,256},{4,260},{8,264},{12,268},{16,272},{20,276},{24,280},{28,28... | collective-permute-start | bytes 196616 | tf_op jit(solution)/shard_map/ppermute | solution.py:27
  49.5 3.3 %collective-permute-start.4 = (f32[160,128]{1,0:T(8,128)S(1)}, f32[160,128]{1,0:T(8,128)S(1)}, u32[]{:S(2)}, u32[]{:S(2)}) collective-permute-start(f32[160,128]{1,0:T(8,128)S(1)} %add.315), channel_id=1, source_target_pairs={{0,64},{4,68},{8,72},{12,76},{16,80},{20,84},{24,88},{28,92},{32,9... | collective-permute-start | bytes 245768 | tf_op jit(solution)/shard_map/ppermute | solution.py:27
  52.7 2.4 collective-permute-done.15
  55.1 3.4 %collective-permute-start.16 = (f32[128,128]{1,0:T(8,128)S(1)}, f32[128,128]{1,0:T(8,128)S(1)}, u32[]{:S(2)}, u32[]{:S(2)}) collective-permute-start(f32[128,128]{1,0:T(8,128)S(1)} %add.342), channel_id=1, source_target_pairs={{0,8},{4,12},{8,0},{12,4},{16,24},{20,28},{24,16},{28,20},{32,40},... | collective-permute-start | bytes 196616 | tf_op jit(solution)/shard_map/ppermute | solution.py:27
  58.5 2.2 collective-permute-start.5
  61.3 5.1 %collective-permute-start.17 = (f32[128,128]{1,0:T(8,128)S(1)}, f32[128,128]{1,0:T(8,128)S(1)}, u32[]{:S(2)}, u32[]{:S(2)}) collective-permute-start(f32[128,128]{1,0:T(8,128)S(1)} %add.343), channel_id=1, source_target_pairs={{0,16},{4,20},{8,24},{12,28},{16,0},{20,4},{24,8},{28,12},{32,48},... | collective-permute-start | bytes 196616 | tf_op jit(solution)/shard_map/ppermute | solution.py:27
  66.4 2.3 collective-permute-done.17
  68.8 4.5 %collective-permute-start.18 = (f32[128,128]{1,0:T(8,128)S(1)}, f32[128,128]{1,0:T(8,128)S(1)}, u32[]{:S(2)}, u32[]{:S(2)}) collective-permute-start(f32[128,128]{1,0:T(8,128)S(1)} %add.344), channel_id=1, source_target_pairs={{0,32},{4,36},{8,40},{12,44},{16,48},{20,52},{24,56},{28,60},{32,0... | collective-permute-start | bytes 196616 | tf_op jit(solution)/shard_map/ppermute | solution.py:27
  73.3 4.4 %collective-permute-start.6 = (f32[160,128]{1,0:T(8,128)S(1)}, f32[160,128]{1,0:T(8,128)S(1)}, u32[]{:S(2)}, u32[]{:S(2)}) collective-permute-start(f32[160,128]{1,0:T(8,128)S(1)} %add.317), channel_id=1, source_target_pairs={{0,256},{4,260},{8,264},{12,268},{16,272},{20,276},{24,280},{28,28... | collective-permute-start | bytes 245768 | tf_op jit(solution)/shard_map/ppermute | solution.py:27
  79.6 2.6 %collective-permute-start.19 = (f32[128,128]{1,0:T(8,128)S(1)}, f32[128,128]{1,0:T(8,128)S(1)}, u32[]{:S(2)}, u32[]{:S(2)}) collective-permute-start(f32[128,128]{1,0:T(8,128)S(1)} %add.345), channel_id=1, source_target_pairs={{0,1},{1,0},{2,3},{3,2},{4,5},{5,4},{6,7},{7,6},{8,9},{9,8},{10,11... | collective-permute-start | bytes 196616 | tf_op jit(solution)/shard_map/ppermute | solution.py:27
  83.6 2.7 %collective-permute-start.7 = (f32[160,128]{1,0:T(8,128)S(1)}, f32[160,128]{1,0:T(8,128)S(1)}, u32[]{:S(2)}, u32[]{:S(2)}) collective-permute-start(f32[160,128]{1,0:T(8,128)S(1)} %add.318), channel_id=1, source_target_pairs={{0,1},{1,0},{2,3},{3,2},{4,5},{5,4},{6,7},{7,6},{8,9},{9,8},{10,11... | collective-permute-start | bytes 245768 | tf_op jit(solution)/shard_map/ppermute | solution.py:27
  86.4 2.9 %collective-permute-start.20 = (f32[128,128]{1,0:T(8,128)S(1)}, f32[128,128]{1,0:T(8,128)S(1)}, u32[]{:S(2)}, u32[]{:S(2)}) collective-permute-start(f32[128,128]{1,0:T(8,128)S(1)} %add.346), channel_id=1, source_target_pairs={{0,2},{1,3},{2,0},{3,1},{4,6},{5,7},{6,4},{7,5},{8,10},{9,11},{10,... | collective-permute-start | bytes 196616 | tf_op jit(solution)/shard_map/ppermute | solution.py:27
  90.0 3.7 %collective-permute-start.8 = (f32[160,128]{1,0:T(8,128)S(1)}, f32[160,128]{1,0:T(8,128)S(1)}, u32[]{:S(2)}, u32[]{:S(2)}) collective-permute-start(f32[160,128]{1,0:T(8,128)S(1)} %add.319), channel_id=1, source_target_pairs={{0,2},{1,3},{2,0},{3,1},{4,6},{5,7},{6,4},{7,5},{8,10},{9,11},{10,... | collective-permute-start | bytes 245768 | tf_op jit(solution)/shard_map/ppermute | solution.py:27
  94.0 3.0 %collective-permute-start.21 = (f32[128,128]{1,0:T(8,128)S(1)}, f32[128,128]{1,0:T(8,128)S(1)}, u32[]{:S(2)}, u32[]{:S(2)}) collective-permute-start(f32[128,128]{1,0:T(8,128)S(1)} %add.347), channel_id=1, source_target_pairs={{0,128},{4,132},{8,136},{12,140},{16,144},{20,148},{24,152},{28,15... | collective-permute-start | bytes 196616 | tf_op jit(solution)/shard_map/ppermute | solution.py:27
  97.9 3.7 %collective-permute-start.9 = (f32[160,128]{1,0:T(8,128)S(1)}, f32[160,128]{1,0:T(8,128)S(1)}, u32[]{:S(2)}, u32[]{:S(2)}) collective-permute-start(f32[160,128]{1,0:T(8,128)S(1)} %add.320), channel_id=1, source_target_pairs={{0,16},{4,20},{8,24},{12,28},{16,0},{20,4},{24,8},{28,12},{32,48},... | collective-permute-start | bytes 245768 | tf_op jit(solution)/shard_map/ppermute | solution.py:27
  101.8 3.1 %collective-permute-start.22 = (f32[256,128]{1,0:T(8,128)S(1)}, f32[256,128]{1,0:T(8,128)S(1)}, u32[]{:S(2)}, u32[]{:S(2)}) collective-permute-start(f32[256,128]{1,0:T(8,128)S(1)} %maximum_select_fusion.5), channel_id=1, source_target_pairs={{0,64},{4,68},{8,72},{12,76},{16,80},{20,84},{24,88},{28,92},{32,9... | collective-permute-start | bytes 393224 | tf_op jit(solution)/shard_map/ppermute | solution.py:27
  106.0 1.9 collective-permute-start.10
  111.3 1.9 collective-permute-done.10
  113.3 2.1 collective-permute-start.11
  117.5 11.7 %custom-call.6 = f32[128,128]{1,0:T(8,128)S(1)} custom-call(f32[128,128]{1,0:T(8,128)S(1)} %get-tuple-element.15), custom_call_target="Cholesky" | custom-call | tf_op jit(solution)/shard_map/cholesky/custom-call.1 | solution.py:79
  135.2 11.7 %custom-call.7 = f32[128,128]{1,0:T(8,128)S(1)} custom-call(f32[128,128]{1,0:T(8,128)S(1)} %slice.259), custom_call_target="Cholesky" | custom-call | tf_op jit(solution)/shard_map/cholesky/custom-call.1 | solution.py:79
  152.0 11.7 %custom-call.8 = f32[128,128]{1,0:T(8,128)S(1)} custom-call(f32[128,128]{1,0:T(8,128)S(1)} %slice.264), custom_call_target="Cholesky" | custom-call | tf_op jit(solution)/shard_map/cholesky/custom-call.1 | solution.py:79
  168.4 11.7 %custom-call.9 = f32[128,128]{1,0:T(8,128)S(1)} custom-call(f32[128,128]{1,0:T(8,128)S(1)} %convolution_subtract_fusion.5), custom_call_target="Cholesky" | custom-call | tf_op jit(solution)/shard_map/cholesky/custom-call.1 | solution.py:79
  190.6 2.0 collective-permute-start.24
  193.6 1.9 collective-permute-start.25
  195.6 3.5 %collective-permute-done.25 = f32[2,256]{1,0:T(2,128)S(1)} collective-permute-done((f32[2,256]{1,0:T(2,128)S(1)}, f32[2,256]{1,0:T(2,128)S(1)}, u32[]{:S(2)}, u32[]{:S(2)}) %collective-permute-start.25) | collective-permute-done | bytes 2080 | tf_op jit(solution)/shard_map/ppermute | solution.py:27
  199.1 3.1 %collective-permute-start.26 = (f32[2,256]{1,0:T(2,128)S(1)}, f32[2,256]{1,0:T(2,128)S(1)}, u32[]{:S(2)}, u32[]{:S(2)}) collective-permute-start(f32[2,256]{1,0:T(2,128)S(1)} %pad_maximum_fusion.25), channel_id=1, source_target_pairs={{0,16},{4,20},{8,24},{12,28},{16,0},{20,4},{24,8},{28,12},{32,48},... | collective-permute-start | bytes 6152 | tf_op jit(solution)/shard_map/ppermute | solution.py:27
  202.2 3.3 %collective-permute-done.26 = f32[2,256]{1,0:T(2,128)S(1)} collective-permute-done((f32[2,256]{1,0:T(2,128)S(1)}, f32[2,256]{1,0:T(2,128)S(1)}, u32[]{:S(2)}, u32[]{:S(2)}) %collective-permute-start.26) | collective-permute-done | bytes 2080 | tf_op jit(solution)/shard_map/ppermute | solution.py:27
  205.5 6.0 %collective-permute-start.27 = (f32[2,256]{1,0:T(2,128)S(1)}, f32[2,256]{1,0:T(2,128)S(1)}, u32[]{:S(2)}, u32[]{:S(2)}) collective-permute-start(f32[2,256]{1,0:T(2,128)S(1)} %pad_maximum_fusion.26), channel_id=1, source_target_pairs={{0,32},{4,36},{8,40},{12,44},{16,48},{20,52},{24,56},{28,60},{32,0... | collective-permute-start | bytes 6152 | tf_op jit(solution)/shard_map/ppermute | solution.py:27
  211.5 3.4 %collective-permute-done.27 = f32[2,256]{1,0:T(2,128)S(1)} collective-permute-done((f32[2,256]{1,0:T(2,128)S(1)}, f32[2,256]{1,0:T(2,128)S(1)}, u32[]{:S(2)}, u32[]{:S(2)}) %collective-permute-start.27) | collective-permute-done | bytes 2080 | tf_op jit(solution)/shard_map/ppermute | solution.py:27
  214.9 2.6 %collective-permute-start.28 = (f32[2,256]{1,0:T(2,128)S(1)}, f32[2,256]{1,0:T(2,128)S(1)}, u32[]{:S(2)}, u32[]{:S(2)}) collective-permute-start(f32[2,256]{1,0:T(2,128)S(1)} %pad_maximum_fusion.27), channel_id=1, source_target_pairs={{0,64},{4,68},{8,72},{12,76},{16,80},{20,84},{24,88},{28,92},{32,9... | collective-permute-start | bytes 6152 | tf_op jit(solution)/shard_map/ppermute | solution.py:27
  217.5 2.9 %collective-permute-done.28 = f32[2,256]{1,0:T(2,128)S(1)} collective-permute-done((f32[2,256]{1,0:T(2,128)S(1)}, f32[2,256]{1,0:T(2,128)S(1)}, u32[]{:S(2)}, u32[]{:S(2)}) %collective-permute-start.28) | collective-permute-done | bytes 2080 | tf_op jit(solution)/shard_map/ppermute | solution.py:27
  220.4 2.3 collective-permute-start.29
  222.7 4.1 %collective-permute-done.29 = f32[2,256]{1,0:T(2,128)S(1)} collective-permute-done((f32[2,256]{1,0:T(2,128)S(1)}, f32[2,256]{1,0:T(2,128)S(1)}, u32[]{:S(2)}, u32[]{:S(2)}) %collective-permute-start.29) | collective-permute-done | bytes 2080 | tf_op jit(solution)/shard_map/ppermute | solution.py:27
  226.8 5.7 %collective-permute-start.30 = (f32[2,256]{1,0:T(2,128)S(1)}, f32[2,256]{1,0:T(2,128)S(1)}, u32[]{:S(2)}, u32[]{:S(2)}) collective-permute-start(f32[2,256]{1,0:T(2,128)S(1)} %pad_maximum_fusion.29), channel_id=1, source_target_pairs={{0,256},{4,260},{8,264},{12,268},{16,272},{20,276},{24,280},{28,28... | collective-permute-start | bytes 6152 | tf_op jit(solution)/shard_map/ppermute | solution.py:27
  232.6 3.6 %collective-permute-done.30 = f32[2,256]{1,0:T(2,128)S(1)} collective-permute-done((f32[2,256]{1,0:T(2,128)S(1)}, f32[2,256]{1,0:T(2,128)S(1)}, u32[]{:S(2)}, u32[]{:S(2)}) %collective-permute-start.30) | collective-permute-done | bytes 2080 | tf_op jit(solution)/shard_map/ppermute | solution.py:27
  236.2 2.7 %collective-permute-start.31 = (f32[2,256]{1,0:T(2,128)S(1)}, f32[2,256]{1,0:T(2,128)S(1)}, u32[]{:S(2)}, u32[]{:S(2)}) collective-permute-start(f32[2,256]{1,0:T(2,128)S(1)} %pad_maximum_fusion.30), channel_id=1, source_target_pairs={{0,1},{1,0},{2,3},{3,2},{4,5},{5,4},{6,7},{7,6},{8,9},{9,8},{10,11... | collective-permute-start | bytes 6152 | tf_op jit(solution)/shard_map/ppermute | solution.py:27
  239.0 2.7 %collective-permute-done.31 = f32[2,256]{1,0:T(2,128)S(1)} collective-permute-done((f32[2,256]{1,0:T(2,128)S(1)}, f32[2,256]{1,0:T(2,128)S(1)}, u32[]{:S(2)}, u32[]{:S(2)}) %collective-permute-start.31) | collective-permute-done | bytes 2080 | tf_op jit(solution)/shard_map/ppermute | solution.py:27
  241.7 3.7 %collective-permute-start.32 = (f32[2,256]{1,0:T(2,128)S(1)}, f32[2,256]{1,0:T(2,128)S(1)}, u32[]{:S(2)}, u32[]{:S(2)}) collective-permute-start(f32[2,256]{1,0:T(2,128)S(1)} %pad_maximum_fusion.31), channel_id=1, source_target_pairs={{0,2},{1,3},{2,0},{3,1},{4,6},{5,7},{6,4},{7,5},{8,10},{9,11},{10,... | collective-permute-start | bytes 6152 | tf_op jit(solution)/shard_map/ppermute | solution.py:27
  245.4 3.3 %collective-permute-done.32 = f32[2,256]{1,0:T(2,128)S(1)} collective-permute-done((f32[2,256]{1,0:T(2,128)S(1)}, f32[2,256]{1,0:T(2,128)S(1)}, u32[]{:S(2)}, u32[]{:S(2)}) %collective-permute-start.32) | collective-permute-done | bytes 2080 | tf_op jit(solution)/shard_map/ppermute | solution.py:27
  (188 shorter events, 45.7 us)
Async XLA Ops:
  0.0 1.5 copy-start
  0.7 0.7 copy-start.3
  4.7 1.2 copy-start.1
  7.0 5.0 %collective-permute-start.12 = (f32[512,128]{1,0:T(8,128)}, f32[512,128]{1,0:T(8,128)}, u32[]{:S(2)}, u32[]{:S(2)}) collective-permute-start(f32[512,128]{1,0:T(8,128)} %constant_dynamic-slice_fusion.2), channel_id=1, source_target_pairs={{0,4},{4,0},{8,12},{12,8},{16,20},{20,16},{24,28},{28,24},{32,36},... | collective-permute-start | bytes 786440 | tf_op jit(solution)/shard_map/ppermute | solution.py:27
  9.4 7.1 %collective-permute-start = (f32[640,128]{1,0:T(8,128)S(1)}, f32[640,128]{1,0:T(8,128)S(1)}, u32[]{:S(2)}, u32[]{:S(2)}) collective-permute-start(f32[640,128]{1,0:T(8,128)S(1)} %constant_dynamic-slice_fusion.5), channel_id=1, source_target_pairs={{0,4},{4,0},{8,12},{12,8},{16,20},{20,16},{24,28},{28,24},{32,36},... | collective-permute-start | bytes 983048 | tf_op jit(solution)/shard_map/ppermute | solution.py:27
  13.0 7.9 %collective-permute-start.13 = (f32[256,128]{1,0:T(8,128)S(1)}, f32[256,128]{1,0:T(8,128)S(1)}, u32[]{:S(2)}, u32[]{:S(2)}) collective-permute-start(f32[256,128]{1,0:T(8,128)S(1)} %constant_dynamic-slice_fusion.1), channel_id=1, source_target_pairs={{0,64},{4,68},{8,72},{12,76},{16,80},{20,84},{24,88},{28,92},{32,9... | collective-permute-start | bytes 393224 | tf_op jit(solution)/shard_map/ppermute | solution.py:27
  16.6 8.4 %collective-permute-start.1 = (f32[320,128]{1,0:T(8,128)S(1)}, f32[320,128]{1,0:T(8,128)S(1)}, u32[]{:S(2)}, u32[]{:S(2)}) collective-permute-start(f32[320,128]{1,0:T(8,128)S(1)} %constant_dynamic-slice_fusion.4), channel_id=1, source_target_pairs={{0,8},{4,12},{8,0},{12,4},{16,24},{20,28},{24,16},{28,20},{32,40},... | collective-permute-start | bytes 491528 | tf_op jit(solution)/shard_map/ppermute | solution.py:27
  25.0 10.6 %collective-permute-start.2 = (f32[160,128]{1,0:T(8,128)S(1)}, f32[160,128]{1,0:T(8,128)S(1)}, u32[]{:S(2)}, u32[]{:S(2)}) collective-permute-start(f32[160,128]{1,0:T(8,128)S(1)} %constant_dynamic-slice_fusion.3), channel_id=1, source_target_pairs={{0,16},{4,20},{8,24},{12,28},{16,0},{20,4},{24,8},{28,12},{32,48},... | collective-permute-start | bytes 245768 | tf_op jit(solution)/shard_map/ppermute | solution.py:27
  31.1 13.0 %collective-permute-start.14 = (f32[128,128]{1,0:T(8,128)S(1)}, f32[128,128]{1,0:T(8,128)S(1)}, u32[]{:S(2)}, u32[]{:S(2)}) collective-permute-start(f32[128,128]{1,0:T(8,128)S(1)} %constant_dynamic-slice_fusion), channel_id=1, source_target_pairs={{0,128},{4,132},{8,136},{12,140},{16,144},{20,148},{24,152},{28,15... | collective-permute-start | bytes 196616 | tf_op jit(solution)/shard_map/ppermute | solution.py:27
  35.7 13.8 %collective-permute-start.3 = (f32[160,128]{1,0:T(8,128)S(1)}, f32[160,128]{1,0:T(8,128)S(1)}, u32[]{:S(2)}, u32[]{:S(2)}) collective-permute-start(f32[160,128]{1,0:T(8,128)S(1)} %dynamic-slice_add_fusion.4), channel_id=1, source_target_pairs={{0,32},{4,36},{8,40},{12,44},{16,48},{20,52},{24,56},{28,60},{32,0... | collective-permute-start | bytes 245768 | tf_op jit(solution)/shard_map/ppermute | solution.py:27
  44.2 10.9 %collective-permute-start.15 = (f32[128,128]{1,0:T(8,128)S(1)}, f32[128,128]{1,0:T(8,128)S(1)}, u32[]{:S(2)}, u32[]{:S(2)}) collective-permute-start(f32[128,128]{1,0:T(8,128)S(1)} %dynamic-slice_add_fusion.5), channel_id=1, source_target_pairs={{0,256},{4,260},{8,264},{12,268},{16,272},{20,276},{24,280},{28,28... | collective-permute-start | bytes 196616 | tf_op jit(solution)/shard_map/ppermute | solution.py:27
  49.5 9.0 %collective-permute-start.4 = (f32[160,128]{1,0:T(8,128)S(1)}, f32[160,128]{1,0:T(8,128)S(1)}, u32[]{:S(2)}, u32[]{:S(2)}) collective-permute-start(f32[160,128]{1,0:T(8,128)S(1)} %add.315), channel_id=1, source_target_pairs={{0,64},{4,68},{8,72},{12,76},{16,80},{20,84},{24,88},{28,92},{32,9... | collective-permute-start | bytes 245768 | tf_op jit(solution)/shard_map/ppermute | solution.py:27
  55.1 6.2 %collective-permute-start.16 = (f32[128,128]{1,0:T(8,128)S(1)}, f32[128,128]{1,0:T(8,128)S(1)}, u32[]{:S(2)}, u32[]{:S(2)}) collective-permute-start(f32[128,128]{1,0:T(8,128)S(1)} %add.342), channel_id=1, source_target_pairs={{0,8},{4,12},{8,0},{12,4},{16,24},{20,28},{24,16},{28,20},{32,40},... | collective-permute-start | bytes 196616 | tf_op jit(solution)/shard_map/ppermute | solution.py:27
  58.5 14.8 %collective-permute-start.5 = (f32[160,128]{1,0:T(8,128)S(1)}, f32[160,128]{1,0:T(8,128)S(1)}, u32[]{:S(2)}, u32[]{:S(2)}) collective-permute-start(f32[160,128]{1,0:T(8,128)S(1)} %add.316), channel_id=1, source_target_pairs={{0,128},{4,132},{8,136},{12,140},{16,144},{20,148},{24,152},{28,15... | collective-permute-start | bytes 245768 | tf_op jit(solution)/shard_map/ppermute | solution.py:27
  61.3 7.5 %collective-permute-start.17 = (f32[128,128]{1,0:T(8,128)S(1)}, f32[128,128]{1,0:T(8,128)S(1)}, u32[]{:S(2)}, u32[]{:S(2)}) collective-permute-start(f32[128,128]{1,0:T(8,128)S(1)} %add.343), channel_id=1, source_target_pairs={{0,16},{4,20},{8,24},{12,28},{16,0},{20,4},{24,8},{28,12},{32,48},... | collective-permute-start | bytes 196616 | tf_op jit(solution)/shard_map/ppermute | solution.py:27
  68.8 10.9 %collective-permute-start.18 = (f32[128,128]{1,0:T(8,128)S(1)}, f32[128,128]{1,0:T(8,128)S(1)}, u32[]{:S(2)}, u32[]{:S(2)}) collective-permute-start(f32[128,128]{1,0:T(8,128)S(1)} %add.344), channel_id=1, source_target_pairs={{0,32},{4,36},{8,40},{12,44},{16,48},{20,52},{24,56},{28,60},{32,0... | collective-permute-start | bytes 196616 | tf_op jit(solution)/shard_map/ppermute | solution.py:27
  73.3 10.2 %collective-permute-start.6 = (f32[160,128]{1,0:T(8,128)S(1)}, f32[160,128]{1,0:T(8,128)S(1)}, u32[]{:S(2)}, u32[]{:S(2)}) collective-permute-start(f32[160,128]{1,0:T(8,128)S(1)} %add.317), channel_id=1, source_target_pairs={{0,256},{4,260},{8,264},{12,268},{16,272},{20,276},{24,280},{28,28... | collective-permute-start | bytes 245768 | tf_op jit(solution)/shard_map/ppermute | solution.py:27
  79.6 6.7 %collective-permute-start.19 = (f32[128,128]{1,0:T(8,128)S(1)}, f32[128,128]{1,0:T(8,128)S(1)}, u32[]{:S(2)}, u32[]{:S(2)}) collective-permute-start(f32[128,128]{1,0:T(8,128)S(1)} %add.345), channel_id=1, source_target_pairs={{0,1},{1,0},{2,3},{3,2},{4,5},{5,4},{6,7},{7,6},{8,9},{9,8},{10,11... | collective-permute-start | bytes 196616 | tf_op jit(solution)/shard_map/ppermute | solution.py:27
  83.6 6.4 %collective-permute-start.7 = (f32[160,128]{1,0:T(8,128)S(1)}, f32[160,128]{1,0:T(8,128)S(1)}, u32[]{:S(2)}, u32[]{:S(2)}) collective-permute-start(f32[160,128]{1,0:T(8,128)S(1)} %add.318), channel_id=1, source_target_pairs={{0,1},{1,0},{2,3},{3,2},{4,5},{5,4},{6,7},{7,6},{8,9},{9,8},{10,11... | collective-permute-start | bytes 245768 | tf_op jit(solution)/shard_map/ppermute | solution.py:27
  86.4 7.7 %collective-permute-start.20 = (f32[128,128]{1,0:T(8,128)S(1)}, f32[128,128]{1,0:T(8,128)S(1)}, u32[]{:S(2)}, u32[]{:S(2)}) collective-permute-start(f32[128,128]{1,0:T(8,128)S(1)} %add.346), channel_id=1, source_target_pairs={{0,2},{1,3},{2,0},{3,1},{4,6},{5,7},{6,4},{7,5},{8,10},{9,11},{10,... | collective-permute-start | bytes 196616 | tf_op jit(solution)/shard_map/ppermute | solution.py:27
  90.0 7.8 %collective-permute-start.8 = (f32[160,128]{1,0:T(8,128)S(1)}, f32[160,128]{1,0:T(8,128)S(1)}, u32[]{:S(2)}, u32[]{:S(2)}) collective-permute-start(f32[160,128]{1,0:T(8,128)S(1)} %add.319), channel_id=1, source_target_pairs={{0,2},{1,3},{2,0},{3,1},{4,6},{5,7},{6,4},{7,5},{8,10},{9,11},{10,... | collective-permute-start | bytes 245768 | tf_op jit(solution)/shard_map/ppermute | solution.py:27
  94.0 7.8 %collective-permute-start.21 = (f32[128,128]{1,0:T(8,128)S(1)}, f32[128,128]{1,0:T(8,128)S(1)}, u32[]{:S(2)}, u32[]{:S(2)}) collective-permute-start(f32[128,128]{1,0:T(8,128)S(1)} %add.347), channel_id=1, source_target_pairs={{0,128},{4,132},{8,136},{12,140},{16,144},{20,148},{24,152},{28,15... | collective-permute-start | bytes 196616 | tf_op jit(solution)/shard_map/ppermute | solution.py:27
  97.9 8.1 %collective-permute-start.9 = (f32[160,128]{1,0:T(8,128)S(1)}, f32[160,128]{1,0:T(8,128)S(1)}, u32[]{:S(2)}, u32[]{:S(2)}) collective-permute-start(f32[160,128]{1,0:T(8,128)S(1)} %add.320), channel_id=1, source_target_pairs={{0,16},{4,20},{8,24},{12,28},{16,0},{20,4},{24,8},{28,12},{32,48},... | collective-permute-start | bytes 245768 | tf_op jit(solution)/shard_map/ppermute | solution.py:27
  101.8 6.9 %collective-permute-start.22 = (f32[256,128]{1,0:T(8,128)S(1)}, f32[256,128]{1,0:T(8,128)S(1)}, u32[]{:S(2)}, u32[]{:S(2)}) collective-permute-start(f32[256,128]{1,0:T(8,128)S(1)} %maximum_select_fusion.5), channel_id=1, source_target_pairs={{0,64},{4,68},{8,72},{12,76},{16,80},{20,84},{24,88},{28,92},{32,9... | collective-permute-start | bytes 393224 | tf_op jit(solution)/shard_map/ppermute | solution.py:27
  106.0 7.2 %collective-permute-start.10 = (f32[320,128]{1,0:T(8,128)S(1)}, f32[320,128]{1,0:T(8,128)S(1)}, u32[]{:S(2)}, u32[]{:S(2)}) collective-permute-start(f32[320,128]{1,0:T(8,128)S(1)} %maximum_select_fusion.4), channel_id=1, source_target_pairs={{0,8},{4,12},{8,0},{12,4},{16,24},{20,28},{24,16},{28,20},{32,40},... | collective-permute-start | bytes 491528 | tf_op jit(solution)/shard_map/ppermute | solution.py:27
  108.7 6.7 %collective-permute-start.23 = (f32[512,128]{1,0:T(8,128)S(1)}, f32[512,128]{1,0:T(8,128)S(1)}, u32[]{:S(2)}, u32[]{:S(2)}) collective-permute-start(f32[512,128]{1,0:T(8,128)S(1)} %maximum_select_fusion.3), channel_id=1, source_target_pairs={{0,4},{4,0},{8,12},{12,8},{16,20},{20,16},{24,28},{28,24},{32,36},... | collective-permute-start | bytes 786440 | tf_op jit(solution)/shard_map/ppermute | solution.py:27
  113.3 3.5 %collective-permute-start.11 = (f32[640,128]{1,0:T(8,128)S(1)}, f32[640,128]{1,0:T(8,128)S(1)}, u32[]{:S(2)}, u32[]{:S(2)}) collective-permute-start(f32[640,128]{1,0:T(8,128)S(1)} %maximum_select_fusion.2), channel_id=1, source_target_pairs={{0,4},{4,0},{8,12},{12,8},{16,20},{20,16},{24,28},{28,24},{32,36},... | collective-permute-start | bytes 983048 | tf_op jit(solution)/shard_map/ppermute | solution.py:27
  133.7 0.8 copy-start.2
  190.6 3.1 %collective-permute-start.24 = (f32[2,256]{1,0:T(2,128)S(1)}, f32[2,256]{1,0:T(2,128)S(1)}, u32[]{:S(2)}, u32[]{:S(2)}) collective-permute-start(f32[2,256]{1,0:T(2,128)S(1)} %pad_maximum_fusion.23), channel_id=1, source_target_pairs={{0,4},{4,0},{8,12},{12,8},{16,20},{20,16},{24,28},{28,24},{32,36},... | collective-permute-start | bytes 6152 | tf_op jit(solution)/shard_map/ppermute | solution.py:27
  193.6 5.5 %collective-permute-start.25 = (f32[2,256]{1,0:T(2,128)S(1)}, f32[2,256]{1,0:T(2,128)S(1)}, u32[]{:S(2)}, u32[]{:S(2)}) collective-permute-start(f32[2,256]{1,0:T(2,128)S(1)} %pad_maximum_fusion.24), channel_id=1, source_target_pairs={{0,8},{4,12},{8,0},{12,4},{16,24},{20,28},{24,16},{28,20},{32,40},... | collective-permute-start | bytes 6152 | tf_op jit(solution)/shard_map/ppermute | solution.py:27
  199.1 6.4 %collective-permute-start.26 = (f32[2,256]{1,0:T(2,128)S(1)}, f32[2,256]{1,0:T(2,128)S(1)}, u32[]{:S(2)}, u32[]{:S(2)}) collective-permute-start(f32[2,256]{1,0:T(2,128)S(1)} %pad_maximum_fusion.25), channel_id=1, source_target_pairs={{0,16},{4,20},{8,24},{12,28},{16,0},{20,4},{24,8},{28,12},{32,48},... | collective-permute-start | bytes 6152 | tf_op jit(solution)/shard_map/ppermute | solution.py:27
  205.5 9.4 %collective-permute-start.27 = (f32[2,256]{1,0:T(2,128)S(1)}, f32[2,256]{1,0:T(2,128)S(1)}, u32[]{:S(2)}, u32[]{:S(2)}) collective-permute-start(f32[2,256]{1,0:T(2,128)S(1)} %pad_maximum_fusion.26), channel_id=1, source_target_pairs={{0,32},{4,36},{8,40},{12,44},{16,48},{20,52},{24,56},{28,60},{32,0... | collective-permute-start | bytes 6152 | tf_op jit(solution)/shard_map/ppermute | solution.py:27
  214.9 5.5 %collective-permute-start.28 = (f32[2,256]{1,0:T(2,128)S(1)}, f32[2,256]{1,0:T(2,128)S(1)}, u32[]{:S(2)}, u32[]{:S(2)}) collective-permute-start(f32[2,256]{1,0:T(2,128)S(1)} %pad_maximum_fusion.27), channel_id=1, source_target_pairs={{0,64},{4,68},{8,72},{12,76},{16,80},{20,84},{24,88},{28,92},{32,9... | collective-permute-start | bytes 6152 | tf_op jit(solution)/shard_map/ppermute | solution.py:27
  220.4 6.4 %collective-permute-start.29 = (f32[2,256]{1,0:T(2,128)S(1)}, f32[2,256]{1,0:T(2,128)S(1)}, u32[]{:S(2)}, u32[]{:S(2)}) collective-permute-start(f32[2,256]{1,0:T(2,128)S(1)} %pad_maximum_fusion.28), channel_id=1, source_target_pairs={{0,128},{4,132},{8,136},{12,140},{16,144},{20,148},{24,152},{28,15... | collective-permute-start | bytes 6152 | tf_op jit(solution)/shard_map/ppermute | solution.py:27
  226.8 9.4 %collective-permute-start.30 = (f32[2,256]{1,0:T(2,128)S(1)}, f32[2,256]{1,0:T(2,128)S(1)}, u32[]{:S(2)}, u32[]{:S(2)}) collective-permute-start(f32[2,256]{1,0:T(2,128)S(1)} %pad_maximum_fusion.29), channel_id=1, source_target_pairs={{0,256},{4,260},{8,264},{12,268},{16,272},{20,276},{24,280},{28,28... | collective-permute-start | bytes 6152 | tf_op jit(solution)/shard_map/ppermute | solution.py:27
  236.2 5.5 %collective-permute-start.31 = (f32[2,256]{1,0:T(2,128)S(1)}, f32[2,256]{1,0:T(2,128)S(1)}, u32[]{:S(2)}, u32[]{:S(2)}) collective-permute-start(f32[2,256]{1,0:T(2,128)S(1)} %pad_maximum_fusion.30), channel_id=1, source_target_pairs={{0,1},{1,0},{2,3},{3,2},{4,5},{5,4},{6,7},{7,6},{8,9},{9,8},{10,11... | collective-permute-start | bytes 6152 | tf_op jit(solution)/shard_map/ppermute | solution.py:27
  241.7 7.0 %collective-permute-start.32 = (f32[2,256]{1,0:T(2,128)S(1)}, f32[2,256]{1,0:T(2,128)S(1)}, u32[]{:S(2)}, u32[]{:S(2)}) collective-permute-start(f32[2,256]{1,0:T(2,128)S(1)} %pad_maximum_fusion.31), channel_id=1, source_target_pairs={{0,2},{1,3},{2,0},{3,1},{4,6},{5,7},{6,4},{7,5},{8,10},{9,11},{10,... | collective-permute-start | bytes 6152 | tf_op jit(solution)/shard_map/ppermute | solution.py:27
